TPU v7x, 32 devices: a whole 2x2x4 slice. The times are simulated.
32 devices in a mesh: dp: 8 (over y, x, core), tensor: 4 (over z).
Axes of the slice: x: 2, y: 2, z: 4, core: 2. Of those that a mesh axis runs over, the one named last changes fastest.
Arguments:
- tokens: bfloat16 [2, 8, 1216, 2048], P(None, 'dp', 'tensor'), may hold values from -6 to 6
- cotangent: bfloat16 [2, 8, 1216, 2048], P(None, 'dp', 'tensor'), may hold values from -6 to 6
- cont_lengths: int32 [2, 8, 3], P(None, 'dp'), may hold values from 1 to 128, 192 in all within a row
- query_weight: float32 [2048, 2048], P('dp', 'tensor'), may hold values from -0.5 to 0.5
- keyval_weight: float32 [2048, 8, 128], P('dp', 'tensor'), may hold values from -0.5 to 0.5
- output_weight: float32 [2048, 2048], P('tensor', 'dp'), may hold values from -0.125 to 0.125
- gateup_weight: float32 [2048, 2, 8192], P('dp', None, 'tensor'), may hold values from -0.125 to 0.125
- down_weight: float32 [8192, 2048], P('tensor', 'dp'), may hold values from -0.0625 to 0.0625
- norm_gains: float32 [2, 2048], P(None, 'dp'), may hold values from 0.5 to 1.5
- query_moment: float32 [2048, 2048], P('dp', 'tensor'), may hold values from -128 to 128
- keyval_moment: float32 [2048, 8, 128], P('dp', 'tensor'), may hold values from -128 to 128
- output_moment: float32 [2048, 2048], P('tensor', 'dp'), may hold values from -256 to 256
- gateup_moment: float32 [2048, 2, 8192], P('dp', None, 'tensor'), may hold values from -64 to 64
- down_moment: float32 [8192, 2048], P('tensor', 'dp'), may hold values from -160 to 160
- gains_moment: float32 [2, 2048], P(None, 'dp'), may hold values from -320 to 320
- query_square: float32 [2048, 2048], P('dp', 'tensor'), may hold values from 100 to 1000
- keyval_square: float32 [2048, 8, 128], P('dp', 'tensor'), may hold values from 100 to 1000
- output_square: float32 [2048, 2048], P('tensor', 'dp'), may hold values from 400 to 4000
- gateup_square: float32 [2048, 2, 8192], P('dp', None, 'tensor'), may hold values from 40 to 400
- down_square: float32 [8192, 2048], P('tensor', 'dp'), may hold values from 200 to 2000
- gains_square: float32 [2, 2048], P(None, 'dp'), may hold values from 700 to 7000
Outputs:
- layer_output: bfloat16 [2, 8, 1216, 2048], P(None, 'dp', 'tensor')
- input_grad: float32 [2, 8, 1216, 2048], P(None, 'dp', 'tensor')
- new_query: float32 [2048, 2048], P('dp', 'tensor')
- new_keyval: float32 [2048, 8, 128], P('dp', 'tensor')
- new_output: float32 [2048, 2048], P('tensor', 'dp')
- new_gateup: float32 [2048, 2, 8192], P('dp', None, 'tensor')
- new_down: float32 [8192, 2048], P('tensor', 'dp')
- new_gains: float32 [2, 2048], P(None, 'dp')
- next_query_moment: float32 [2048, 2048], P('dp', 'tensor')
- next_keyval_moment: float32 [2048, 8, 128], P('dp', 'tensor')
- next_output_moment: float32 [2048, 2048], P('tensor', 'dp')
- next_gateup_moment: float32 [2048, 2, 8192], P('dp', None, 'tensor')
- next_down_moment: float32 [8192, 2048], P('tensor', 'dp')
- next_gains_moment: float32 [2, 2048], P(None, 'dp')
- next_query_square: float32 [2048, 2048], P('dp', 'tensor')
- next_keyval_square: float32 [2048, 8, 128], P('dp', 'tensor')
- next_output_square: float32 [2048, 2048], P('tensor', 'dp')
- next_gateup_square: float32 [2048, 2, 8192], P('dp', None, 'tensor')
- next_down_square: float32 [8192, 2048], P('tensor', 'dp')
- next_gains_square: float32 [2, 2048], P(None, 'dp')
- trust_norms: float32 [2, 7], replicated
Inputs may be any that keep to these rules, and one draw needn't show every extreme that they name: `cont_lengths`: each group's 3 continuation lengths sum to 192, and the longest is exactly 128.
All inputs are finite; a program needn't handle non-finite values.
Results may differ from a plain program's by a relative error of at most 0.025.
Values may be sent and summed in bfloat16 or wider, within the bound.
No kernel may reach another device: no remote copies, remote signals or barrier semaphores. Data moves between devices by JAX's collectives and lax.ppermute only.
A program may use at most 448 MiB of HBM per device.

v0:
```python
import jax
import jax.numpy as jnp
from jax import lax
from jax.sharding import PartitionSpec as P

HD = 64
PROMPT = 1024
CONTS = 3
STEP = 3
GROUP = 1216


norm_eps = 1e-05
branch_scale = 0.22
score_scale = 0.015625
rope_base = 10000000.0
moment_decay = 0.5
learn_rate = 0.25
ratio_eps = 1e-06
masked_fill = -1e30


def layout(lengths):
    row_index = jnp.arange(GROUP, dtype=jnp.int32)
    ends = jnp.cumsum(lengths)
    starts = ends - lengths
    within = row_index - PROMPT
    inside = (within[:, None] >= starts[None, :]) & (within[:, None] < ends[None, :])
    labels = jnp.arange(1, CONTS + 1, dtype=jnp.int32)
    segment = jnp.sum(jnp.where(inside, labels[None, :], 0), axis=1)
    offsets = jnp.sum(jnp.where(inside, starts[None, :], 0), axis=1)
    position = row_index - offsets
    causal = row_index[None, :] <= row_index[:, None]
    shared = (segment[None, :] == segment[:, None]) | (segment[None, :] == 0)
    return (causal & shared, position)


def rope_tables(position):
    half_size = HD // 2
    inverse = rope_base ** (-2.0 * jnp.arange(half_size, dtype=jnp.float32) / HD)
    angle = position.astype(jnp.float32)[:, None] * inverse[None, :]
    return (jnp.cos(angle)[:, None, :], jnp.sin(angle)[:, None, :])


def rotate(field, cos_table, sin_table):
    half_size = field.shape[-1] // 2
    first_half = field[..., :half_size]
    second_half = field[..., half_size:]
    return jnp.concatenate(
        [
            first_half * cos_table - second_half * sin_table,
            second_half * cos_table + first_half * sin_table,
        ],
        axis=-1,
    )


def rotate_back(grad_field, cos_table, sin_table):
    half_size = grad_field.shape[-1] // 2
    first_half = grad_field[..., :half_size]
    second_half = grad_field[..., half_size:]
    return jnp.concatenate(
        [
            first_half * cos_table + second_half * sin_table,
            second_half * cos_table - first_half * sin_table,
        ],
        axis=-1,
    )


def attend(queries, key_rows, values, visible, block_rows):
    outputs = []
    log_totals = []
    for block in range(2):
        begin = block * block_rows
        stop = begin + block_rows
        scores = (
            jnp.einsum(
                "ikrd,jkd->krij",
                queries[begin:stop],
                key_rows[:stop],
                preferred_element_type=jnp.float32,
            )
            * score_scale
        )
        scores = jnp.where(visible[begin:stop, :stop][None, None], scores, masked_fill)
        row_peak = jnp.max(scores, axis=-1, keepdims=True)
        shifted_exp = jnp.exp(scores - row_peak)
        row_total = jnp.sum(shifted_exp, axis=-1, keepdims=True)
        attn_prob = (shifted_exp / row_total).astype(jnp.bfloat16)
        outputs.append(
            jnp.einsum(
                "krij,jkd->ikrd", attn_prob, values[:stop], preferred_element_type=jnp.float32
            )
        )
        log_totals.append(row_peak + jnp.log(row_total))
    return (jnp.concatenate(outputs, axis=0), jnp.concatenate(log_totals, axis=2))


def attend_back(queries, key_rows, values, visible, log_totals, mixed_grad, block_rows):
    query_grads = []
    key_grad = jnp.zeros(key_rows.shape, jnp.float32)
    value_grad = jnp.zeros(values.shape, jnp.float32)
    for block in range(2):
        begin = block * block_rows
        stop = begin + block_rows
        query_block = queries[begin:stop]
        grad_block = mixed_grad[begin:stop]
        scores = (
            jnp.einsum(
                "ikrd,jkd->krij", query_block, key_rows[:stop], preferred_element_type=jnp.float32
            )
            * score_scale
        )
        attn_prob = jnp.where(
            visible[begin:stop, :stop][None, None],
            jnp.exp(scores - log_totals[:, :, begin:stop]),
            0.0,
        )
        prob_grad = jnp.einsum(
            "ikrd,jkd->krij", grad_block, values[:stop], preferred_element_type=jnp.float32
        )
        row_dot = jnp.sum(attn_prob * prob_grad, axis=-1, keepdims=True)
        score_grad = (attn_prob * (prob_grad - row_dot)).astype(jnp.bfloat16)
        query_grads.append(
            jnp.einsum(
                "krij,jkd->ikrd", score_grad, key_rows[:stop], preferred_element_type=jnp.float32
            )
            * score_scale
        )
        key_grad = key_grad.at[:stop].add(
            jnp.einsum(
                "krij,ikrd->jkd", score_grad, query_block, preferred_element_type=jnp.float32
            )
            * score_scale
        )
        value_grad = value_grad.at[:stop].add(
            jnp.einsum(
                "krij,ikrd->jkd",
                attn_prob.astype(jnp.bfloat16),
                grad_block,
                preferred_element_type=jnp.float32,
            )
        )
    return (jnp.concatenate(query_grads, axis=0), key_grad, value_grad)


def norm_back(upstream, normed_hat, scale_rows, gain_row):
    scaled = upstream * gain_row[None, :]
    through = scale_rows * (
        scaled - normed_hat * jnp.mean(scaled * normed_hat, axis=1, keepdims=True)
    )
    return (through, jnp.sum(upstream * normed_hat, axis=0))


def contract_rows(left, right):
    return lax.dot_general(
        left, right, (((0,), (0,)), ((), ())), preferred_element_type=jnp.float32
    )


def contract_cols(left, right):
    return lax.dot_general(
        left, right, (((1,), (1,)), ((), ())), preferred_element_type=jnp.float32
    )


def per_device(
    tokens,
    cotangent,
    cont_lengths,
    query_weight,
    keyval_weight,
    output_weight,
    gateup_weight,
    down_weight,
    norm_gains,
    query_moment,
    keyval_moment,
    output_moment,
    gateup_moment,
    down_moment,
    gains_moment,
    query_square,
    keyval_square,
    output_square,
    gateup_square,
    down_square,
    gains_square,
):
    masters = (query_weight, keyval_weight, output_weight, gateup_weight, down_weight, norm_gains)
    firsts = (query_moment, keyval_moment, output_moment, gateup_moment, down_moment, gains_moment)
    seconds = (query_square, keyval_square, output_square, gateup_square, down_square, gains_square)
    rounded = tuple((master.astype(jnp.bfloat16) for master in masters))
    gathered = (
        lax.all_gather(rounded[0], "dp", axis=0, tiled=True),
        lax.all_gather(rounded[1], "dp", axis=0, tiled=True),
        lax.all_gather(rounded[2], "dp", axis=1, tiled=True),
        lax.all_gather(rounded[3], "dp", axis=0, tiled=True),
        lax.all_gather(rounded[4], "dp", axis=1, tiled=True),
        lax.all_gather(rounded[5], "dp", axis=1, tiled=True),
    )
    full_query, full_keyval, full_output, full_gateup, full_down, full_gains = gathered
    gain_values = full_gains.astype(jnp.float32)
    tensor_count = lax.axis_size("tensor")
    block_rows = GROUP // 2
    keyval_heads = full_keyval.shape[1]
    query_heads = full_query.shape[1] // HD
    head_repeat = query_heads // keyval_heads

    def micro_step(token_rows, cot_rows, lengths):
        visible, position = layout(lengths)
        cos_table, sin_table = rope_tables(position)
        start_rows = token_rows.astype(jnp.float32)
        scale_one = lax.rsqrt(jnp.mean(start_rows * start_rows, axis=1, keepdims=True) + norm_eps)
        hat_one = start_rows * scale_one
        normed_one = (hat_one * gain_values[0][None, :]).astype(jnp.bfloat16)
        rows_one = lax.all_gather(normed_one, "tensor", axis=0, tiled=True)
        query_raw = jnp.dot(rows_one, full_query, preferred_element_type=jnp.float32).reshape(
            GROUP, query_heads, HD
        )
        keyval_raw = jnp.einsum(
            "rd,dhk->rhk", rows_one, full_keyval, preferred_element_type=jnp.float32
        )
        queries = (
            rotate(query_raw, cos_table, sin_table)
            .astype(jnp.bfloat16)
            .reshape(GROUP, keyval_heads, head_repeat, HD)
        )
        key_rows = rotate(keyval_raw[:, :, :HD], cos_table, sin_table).astype(jnp.bfloat16)
        values = keyval_raw[:, :, HD:].astype(jnp.bfloat16)
        mixed_full, log_totals = attend(queries, key_rows, values, visible, block_rows)
        mixed = mixed_full.astype(jnp.bfloat16).reshape(GROUP, query_heads * HD)
        attn_branch = lax.psum_scatter(
            jnp.dot(mixed, full_output, preferred_element_type=jnp.float32).astype(jnp.bfloat16),
            "tensor",
            scatter_dimension=0,
            tiled=True,
        ).astype(jnp.float32)
        middle = start_rows + branch_scale * attn_branch
        scale_two = lax.rsqrt(jnp.mean(middle * middle, axis=1, keepdims=True) + norm_eps)
        hat_two = middle * scale_two
        normed_two = (hat_two * gain_values[1][None, :]).astype(jnp.bfloat16)
        rows_two = lax.all_gather(normed_two, "tensor", axis=0, tiled=True)
        gate_up = jnp.einsum(
            "rd,dcf->rcf", rows_two, full_gateup, preferred_element_type=jnp.float32
        )
        gate_part = gate_up[:, 0]
        up_part = gate_up[:, 1]
        sigmoid_gate = jax.nn.sigmoid(gate_part)
        silu_gate = gate_part * sigmoid_gate
        hidden_state = (silu_gate * up_part).astype(jnp.bfloat16)
        ffn_branch = lax.psum_scatter(
            jnp.dot(hidden_state, full_down, preferred_element_type=jnp.float32).astype(
                jnp.bfloat16
            ),
            "tensor",
            scatter_dimension=0,
            tiled=True,
        ).astype(jnp.float32)
        layer_rows = (middle + branch_scale * ffn_branch).astype(jnp.bfloat16)
        upstream = cot_rows.astype(jnp.float32)
        ffn_grad = (branch_scale * upstream).astype(jnp.bfloat16)
        ffn_grad_all = lax.all_gather(ffn_grad, "tensor", axis=0, tiled=True)
        grad_down = contract_rows(hidden_state, ffn_grad_all)
        hidden_grad = contract_cols(ffn_grad_all, full_down)
        gate_grad = hidden_grad * up_part * sigmoid_gate * (1.0 + gate_part * (1.0 - sigmoid_gate))
        up_grad = hidden_grad * silu_gate
        gateup_grad = jnp.stack([gate_grad, up_grad], axis=1).astype(jnp.bfloat16)
        grad_gateup = jnp.einsum(
            "rd,rcf->dcf", rows_two, gateup_grad, preferred_element_type=jnp.float32
        )
        normed_two_grad = lax.psum_scatter(
            jnp.einsum(
                "rcf,dcf->rd", gateup_grad, full_gateup, preferred_element_type=jnp.float32
            ).astype(jnp.bfloat16),
            "tensor",
            scatter_dimension=0,
            tiled=True,
        ).astype(jnp.float32)
        middle_back, gain_two = norm_back(normed_two_grad, hat_two, scale_two, gain_values[1])
        middle_grad = upstream + middle_back
        attn_grad = (branch_scale * middle_grad).astype(jnp.bfloat16)
        attn_grad_all = lax.all_gather(attn_grad, "tensor", axis=0, tiled=True)
        grad_output = contract_rows(mixed, attn_grad_all)
        mixed_grad = (
            contract_cols(attn_grad_all, full_output)
            .astype(jnp.bfloat16)
            .reshape(GROUP, keyval_heads, head_repeat, HD)
        )
        query_grad, key_grad, value_grad = attend_back(
            queries, key_rows, values, visible, log_totals, mixed_grad, block_rows
        )
        query_raw_grad = (
            rotate_back(query_grad.reshape(GROUP, query_heads, HD), cos_table, sin_table)
            .astype(jnp.bfloat16)
            .reshape(GROUP, query_heads * HD)
        )
        keyval_raw_grad = jnp.concatenate(
            [rotate_back(key_grad, cos_table, sin_table), value_grad], axis=2
        ).astype(jnp.bfloat16)
        grad_query = contract_rows(rows_one, query_raw_grad)
        grad_keyval = jnp.einsum(
            "rd,rhk->dhk", rows_one, keyval_raw_grad, preferred_element_type=jnp.float32
        )
        normed_one_grad = lax.psum_scatter(
            (
                contract_cols(query_raw_grad, full_query)
                + jnp.einsum(
                    "rhk,dhk->rd", keyval_raw_grad, full_keyval, preferred_element_type=jnp.float32
                )
            ).astype(jnp.bfloat16),
            "tensor",
            scatter_dimension=0,
            tiled=True,
        ).astype(jnp.float32)
        start_back, gain_one = norm_back(normed_one_grad, hat_one, scale_one, gain_values[0])
        input_rows = middle_grad + start_back
        gain_grad = lax.psum(jnp.stack([gain_one, gain_two]), "tensor")
        return (
            layer_rows,
            input_rows,
            (grad_query, grad_keyval, grad_output, grad_gateup, grad_down, gain_grad),
        )

    totals_init = tuple((jnp.zeros(piece_full.shape, jnp.float32) for piece_full in gathered))

    def run_micro(step_index, carry):
        out_rows, grad_rows, totals = carry
        token_rows = lax.dynamic_index_in_dim(tokens, step_index, 0, keepdims=False)[0]
        cot_rows = lax.dynamic_index_in_dim(cotangent, step_index, 0, keepdims=False)[0]
        lengths = lax.dynamic_index_in_dim(cont_lengths, step_index, 0, keepdims=False)[0]
        layer_rows, input_rows, grads = micro_step(token_rows, cot_rows, lengths)
        totals = tuple((old_sum + new_term for old_sum, new_term in zip(totals, grads)))
        out_rows = lax.dynamic_update_index_in_dim(out_rows, layer_rows[None], step_index, 0)
        grad_rows = lax.dynamic_update_index_in_dim(grad_rows, input_rows[None], step_index, 0)
        return (out_rows, grad_rows, totals)

    initial = (
        jnp.zeros(tokens.shape, jnp.bfloat16),
        jnp.zeros(tokens.shape, jnp.float32),
        totals_init,
    )
    layer_output, input_grad, totals = lax.fori_loop(0, tokens.shape[0], run_micro, initial)
    summed = (
        lax.psum_scatter(
            totals[0].astype(jnp.bfloat16), "dp", scatter_dimension=0, tiled=True
        ).astype(jnp.float32),
        lax.psum_scatter(
            totals[1].astype(jnp.bfloat16), "dp", scatter_dimension=0, tiled=True
        ).astype(jnp.float32),
        lax.psum_scatter(
            totals[2].astype(jnp.bfloat16), "dp", scatter_dimension=1, tiled=True
        ).astype(jnp.float32),
        lax.psum_scatter(
            totals[3].astype(jnp.bfloat16), "dp", scatter_dimension=0, tiled=True
        ).astype(jnp.float32),
        lax.psum_scatter(
            totals[4].astype(jnp.bfloat16), "dp", scatter_dimension=1, tiled=True
        ).astype(jnp.float32),
        lax.psum_scatter(
            totals[5].astype(jnp.bfloat16), "dp", scatter_dimension=1, tiled=True
        ).astype(jnp.float32),
    )
    correction = 1.0 - moment_decay**STEP
    new_firsts = []
    new_seconds = []
    directions = []
    for grad, first, second in zip(summed, firsts, seconds):
        first_new = moment_decay * first + (1.0 - moment_decay) * grad
        second_new = moment_decay * second + (1.0 - moment_decay) * grad * grad
        direction = first_new / correction / (jnp.sqrt(second_new / correction) + ratio_eps)
        new_firsts.append(first_new)
        new_seconds.append(second_new)
        directions.append(direction)
    weight_part = jnp.concatenate(
        [
            jnp.stack([jnp.sum(masters[slot] * masters[slot]) for slot in range(5)]),
            jnp.sum(norm_gains * norm_gains, axis=1) / tensor_count,
        ]
    )
    update_part = jnp.concatenate(
        [
            jnp.stack([jnp.sum(directions[slot] * directions[slot]) for slot in range(5)]),
            jnp.sum(directions[5] * directions[5], axis=1) / tensor_count,
        ]
    )
    square_totals = lax.psum(jnp.stack([weight_part, update_part]), ("dp", "tensor"))
    trust_norms = jnp.sqrt(square_totals)
    ratio = trust_norms[0] / (trust_norms[1] + ratio_eps)
    new_weights = [masters[slot] - learn_rate * ratio[slot] * directions[slot] for slot in range(5)]
    new_gains = norm_gains - learn_rate * ratio[5:7][:, None] * directions[5]
    return (
        layer_output,
        input_grad,
        new_weights[0],
        new_weights[1],
        new_weights[2],
        new_weights[3],
        new_weights[4],
        new_gains,
        new_firsts[0],
        new_firsts[1],
        new_firsts[2],
        new_firsts[3],
        new_firsts[4],
        new_firsts[5],
        new_seconds[0],
        new_seconds[1],
        new_seconds[2],
        new_seconds[3],
        new_seconds[4],
        new_seconds[5],
        trust_norms,
    )


def solution(mesh):
    return jax.shard_map(
        per_device,
        mesh=mesh,
        in_specs=(
            P(None, "dp", "tensor", None),
            P(None, "dp", "tensor", None),
            P(None, "dp", None),
            P("dp", "tensor"),
            P("dp", "tensor", None),
            P("tensor", "dp"),
            P("dp", None, "tensor"),
            P("tensor", "dp"),
            P(None, "dp"),
            P("dp", "tensor"),
            P("dp", "tensor", None),
            P("tensor", "dp"),
            P("dp", None, "tensor"),
            P("tensor", "dp"),
            P(None, "dp"),
            P("dp", "tensor"),
            P("dp", "tensor", None),
            P("tensor", "dp"),
            P("dp", None, "tensor"),
            P("tensor", "dp"),
            P(None, "dp"),
        ),
        out_specs=(
            P(None, "dp", "tensor", None),
            P(None, "dp", "tensor", None),
            P("dp", "tensor"),
            P("dp", "tensor", None),
            P("tensor", "dp"),
            P("dp", None, "tensor"),
            P("tensor", "dp"),
            P(None, "dp"),
            P("dp", "tensor"),
            P("dp", "tensor", None),
            P("tensor", "dp"),
            P("dp", None, "tensor"),
            P("tensor", "dp"),
            P(None, "dp"),
            P("dp", "tensor"),
            P("dp", "tensor", None),
            P("tensor", "dp"),
            P("dp", None, "tensor"),
            P("tensor", "dp"),
            P(None, "dp"),
            P(),
        ),
        check_vma=False,
    )
```

profile of v0, /device:TPU:0, one launch (start us, length us, event | category | flops | bytes accessed | tf_op | source)
XLA Modules:
  0.0 2580.6 jit_solution(2954414390696849672)
XLA Ops:
  18.7 6.0 copy.230
  25.4 10.5 all_gather.58
  36.6 30.2 %all-gather.12.cloned.1.call-done = bf16[2048,512]{1,0:T(8,128)(2,1)} async-done(((bf16[256,512]{1,0:T(8,128)(2,1)}), bf16[2048,512]{1,0:T(8,128)(2,1)}) %all-gather.12.cloned.1.call-update) | async-done | bytes 2097168 | tf_op jit(solution)/shard_map/all_gather | solution.py:196
  66.9 30.6 %all-gather.14.cloned.1.call-done = bf16[512,2048]{1,0:T(8,128)(2,1)} async-done(((bf16[512,256]{1,0:T(8,128)(2,1)}), bf16[512,2048]{1,0:T(8,128)(2,1)}) %all-gather.14.cloned.1.call-update) | async-done | bytes 2097168 | tf_op jit(solution)/shard_map/all_gather | solution.py:198
  97.5 58.2 %all-gather.18.cloned.1.call-done = bf16[2048,2048]{1,0:T(8,128)(2,1)} async-done(((bf16[2048,256]{1,0:T(8,128)(2,1)}), bf16[2048,2048]{1,0:T(8,128)(2,1)}) %all-gather.18.cloned.1.call-update) | async-done | bytes 8388624 | tf_op jit(solution)/shard_map/all_gather | solution.py:200
  155.7 92.1 %all-gather.16.cloned.1.call-done = bf16[2048,2,2048]{2,0,1:T(8,128)(2,1)} async-done(((bf16[256,2,2048]{2,0,1:T(8,128)(2,1)}), bf16[2048,2,2048]{2,0,1:T(8,128)(2,1)}) %all-gather.16.cloned.1.call-update) | async-done | bytes 16777232 | tf_op jit(solution)/shard_map/all_gather | solution.py:199
  247.8 1825.9 %while.50 = (s32[]{:T(128)}, bf16[2,1,304,2048]{3,2,1,0:T(8,128)(2,1)}, f32[2,1,304,2048]{3,2,1,0:T(8,128)}, f32[2048,512]{1,0:T(8,128)}, f32[2048,2,128]{2,0,1:...) while((s32[]{:T(128)}, ...), condition=%wide.region_21.22_spmd.clone, body=%wide.region_0.21_spmd.clone.sunk | while | flops 118172196864 | bytes 1438253696 | solution.py:344
  256.1 88.4 %all-gather.20.cloned.1.call-done = bf16[1216,2048]{1,0:T(8,128)(2,1)} async-done(((bf16[304,2048]{1,0:T(8,128)(2,1)}), bf16[1216,2048]{1,0:T(8,128)(2,1)}) %all-gather.20.cloned.1.call-update) | async-done | bytes 4980752 | tf_op jit(solution)/shard_map/while/body/eval_jaxpr/all_gather | solution.py:218
  354.6 6.2 fusion.282
  379.8 8.2 copy-done
  393.8 12.1 fusion.288
  412.1 88.0 %reduce-scatter.19.cloned.1.call-done = bf16[304,2048]{1,0:T(8,128)(2,1)} async-done(((bf16[1216,2048]{1,0:T(8,128)(2,1)}), bf16[304,2048]{1,0:T(8,128)(2,1)}) %reduce-scatter.19.cloned.1.call-update) | async-done | bytes 1245200 | tf_op jit(solution)/shard_map/while/body/eval_jaxpr/reduce_scatter | solution.py:234
  507.7 91.6 %all-gather.22.cloned.1.call-done = bf16[1216,2048]{1,0:T(8,128)(2,1)} async-done(((bf16[304,2048]{1,0:T(8,128)(2,1)}), bf16[1216,2048]{1,0:T(8,128)(2,1)}) %all-gather.22.cloned.1.call-update) | async-done | bytes 4980752 | tf_op jit(solution)/shard_map/while/body/eval_jaxpr/all_gather | solution.py:244
  599.4 27.4 %fusion.292 = f32[1216,2,2048]{2,0,1:T(8,128)} fusion(bf16[2048,2,2048]{2,0,1:T(8,128)(2,1)} %get-tuple-element.974, bf16[1216,2048]{1,0:T(8,128)(2,1)} %all-gather.22.cloned.1.call-done), kind=kOutput, calls=%fused_computation.53.clone.1 | convolution fusion | flops 20401094656 | bytes 41680896 | tf_op jit(solution)/shard_map/while/body/eval_jaxpr/rd,dcf->rcf/dot_general | solution.py:245
  626.7 66.9 %all-gather.24.cloned.1.call-done = bf16[1216,2048]{1,0:T(8,128)(2,1)} async-done(((bf16[304,2048]{1,0:T(8,128)(2,1)}), bf16[1216,2048]{1,0:T(8,128)(2,1)}) %all-gather.24.cloned.1.call-update) | async-done | bytes 4980752 | tf_op jit(solution)/shard_map/while/body/eval_jaxpr/all_gather | solution.py:264
  693.6 25.7 fusion.294
  719.3 28.1 %bitcast_convert_fusion.2 = bf16[1216,2048]{1,0:T(8,128)(2,1)} fusion(bf16[2048,2,2048]{2,0,1:T(8,128)(2,1)} %get-tuple-element.974, bf16[1216,1,2048]{2,0,1:T(8,128)(2,1)} %get-tuple-element.903, bf16[1216,1,2048]{2,0,1:T(8,128)(2,1)} %get-tuple-element.904), kind=kOutput, calls=%fused_computation.36.clone.1 | convolution fusion | flops 20408565760 | bytes 31719424 | tf_op jit(solution)/shard_map/while/body/eval_jaxpr/rcf,dcf->rd/dot_general | solution.py:274
  747.6 88.0 %reduce-scatter.23.cloned.1.call-done = bf16[304,2048]{1,0:T(8,128)(2,1)} async-done(((bf16[1216,2048]{1,0:T(8,128)(2,1)}), bf16[304,2048]{1,0:T(8,128)(2,1)}) %reduce-scatter.23.cloned.1.call-update) | async-done | bytes 1245200 | tf_op jit(solution)/shard_map/while/body/eval_jaxpr/reduce_scatter | solution.py:273
  843.1 15.9 convolution_convert_fusion.7
  859.1 18.1 select_add_fusion.13
  877.2 60.2 %all-gather.26.cloned.1.call-done = bf16[1216,2048]{1,0:T(8,128)(2,1)} async-done(((bf16[304,2048]{1,0:T(8,128)(2,1)}), bf16[1216,2048]{1,0:T(8,128)(2,1)}) %all-gather.26.cloned.1.call-update) | async-done | bytes 4980752 | tf_op jit(solution)/shard_map/while/body/eval_jaxpr/all_gather | solution.py:284
  944.1 11.5 fusion.302
  957.0 7.2 fusion.303
  969.2 18.1 fusion.300
  987.4 17.0 fusion.301
  1014.2 8.5 fusion.305
  1025.6 11.2 fusion.299
  1043.8 30.5 %select_add_fusion.12 = f32[2048,2,2048]{2,0,1:T(8,128)} fusion(f32[2048,2,2048]{2,0,1:T(8,128)} %get-tuple-element.945, pred[]{:T(512)S(6)} %compare.47, bf16[1216,1,2048]{2,0,1:T(8,128)(2,1)} %get-tuple-element.903, bf16[1216,1,2048]{2,0,1:T(8,128)(2,1)} %get-tuple-element.904, bf16[1216,2048]{1,0:T(8,128)(2,1)} %all-gather.22.cloned.1.call-done), kind=kOutput, calls=%fused_computation.clone.1 | convolution fusion | flops 20437794816 | bytes 82051072 | tf_op jit(solution)/shard_map/while/body/eval_jaxpr/rd,rcf->dcf/dot_general | solution.py:270
  1095.5 37.1 %reduce-scatter.25.cloned.1.call-done = bf16[304,2048]{1,0:T(8,128)(2,1)} async-done(((bf16[1216,2048]{1,0:T(8,128)(2,1)}), bf16[304,2048]{1,0:T(8,128)(2,1)}) %reduce-scatter.25.cloned.1.call-update) | async-done | bytes 1245200 | tf_op jit(solution)/shard_map/while/body/eval_jaxpr/reduce_scatter | solution.py:306
  1134.9 18.0 psum.24
  1167.3 86.7 %all-gather.20.cloned.1.call-done = bf16[1216,2048]{1,0:T(8,128)(2,1)} async-done(((bf16[304,2048]{1,0:T(8,128)(2,1)}), bf16[1216,2048]{1,0:T(8,128)(2,1)}) %all-gather.20.cloned.1.call-update) | async-done | bytes 4980752 | tf_op jit(solution)/shard_map/while/body/eval_jaxpr/all_gather | solution.py:218
  1264.2 6.2 fusion.282
  1289.3 8.2 copy-done
  1303.3 12.1 fusion.288
  1321.7 88.0 %reduce-scatter.19.cloned.1.call-done = bf16[304,2048]{1,0:T(8,128)(2,1)} async-done(((bf16[1216,2048]{1,0:T(8,128)(2,1)}), bf16[304,2048]{1,0:T(8,128)(2,1)}) %reduce-scatter.19.cloned.1.call-update) | async-done | bytes 1245200 | tf_op jit(solution)/shard_map/while/body/eval_jaxpr/reduce_scatter | solution.py:234
  1417.3 91.7 %all-gather.22.cloned.1.call-done = bf16[1216,2048]{1,0:T(8,128)(2,1)} async-done(((bf16[304,2048]{1,0:T(8,128)(2,1)}), bf16[1216,2048]{1,0:T(8,128)(2,1)}) %all-gather.22.cloned.1.call-update) | async-done | bytes 4980752 | tf_op jit(solution)/shard_map/while/body/eval_jaxpr/all_gather | solution.py:244
  1508.9 27.4 %fusion.292 = f32[1216,2,2048]{2,0,1:T(8,128)} fusion(bf16[2048,2,2048]{2,0,1:T(8,128)(2,1)} %get-tuple-element.974, bf16[1216,2048]{1,0:T(8,128)(2,1)} %all-gather.22.cloned.1.call-done), kind=kOutput, calls=%fused_computation.53.clone.1 | convolution fusion | flops 20401094656 | bytes 41680896 | tf_op jit(solution)/shard_map/while/body/eval_jaxpr/rd,dcf->rcf/dot_general | solution.py:245
  1536.3 66.7 %all-gather.24.cloned.1.call-done = bf16[1216,2048]{1,0:T(8,128)(2,1)} async-done(((bf16[304,2048]{1,0:T(8,128)(2,1)}), bf16[1216,2048]{1,0:T(8,128)(2,1)}) %all-gather.24.cloned.1.call-update) | async-done | bytes 4980752 | tf_op jit(solution)/shard_map/while/body/eval_jaxpr/all_gather | solution.py:264
  1603.1 25.7 fusion.294
  1628.8 28.2 %bitcast_convert_fusion.2 = bf16[1216,2048]{1,0:T(8,128)(2,1)} fusion(bf16[2048,2,2048]{2,0,1:T(8,128)(2,1)} %get-tuple-element.974, bf16[1216,1,2048]{2,0,1:T(8,128)(2,1)} %get-tuple-element.903, bf16[1216,1,2048]{2,0,1:T(8,128)(2,1)} %get-tuple-element.904), kind=kOutput, calls=%fused_computation.36.clone.1 | convolution fusion | flops 20408565760 | bytes 31719424 | tf_op jit(solution)/shard_map/while/body/eval_jaxpr/rcf,dcf->rd/dot_general | solution.py:274
  1657.1 88.0 %reduce-scatter.23.cloned.1.call-done = bf16[304,2048]{1,0:T(8,128)(2,1)} async-done(((bf16[1216,2048]{1,0:T(8,128)(2,1)}), bf16[304,2048]{1,0:T(8,128)(2,1)}) %reduce-scatter.23.cloned.1.call-update) | async-done | bytes 1245200 | tf_op jit(solution)/shard_map/while/body/eval_jaxpr/reduce_scatter | solution.py:273
  1752.6 15.9 convolution_convert_fusion.7
  1768.6 20.5 select_add_fusion.13
  1789.1 57.8 %all-gather.26.cloned.1.call-done = bf16[1216,2048]{1,0:T(8,128)(2,1)} async-done(((bf16[304,2048]{1,0:T(8,128)(2,1)}), bf16[1216,2048]{1,0:T(8,128)(2,1)}) %all-gather.26.cloned.1.call-update) | async-done | bytes 4980752 | tf_op jit(solution)/shard_map/while/body/eval_jaxpr/all_gather | solution.py:284
  1853.6 11.5 fusion.302
  1866.5 7.2 fusion.303
  1878.7 18.1 fusion.300
  1896.8 17.0 fusion.301
  1923.7 8.5 fusion.305
  1935.1 11.2 fusion.299
  1953.3 35.2 %select_add_fusion.12 = f32[2048,2,2048]{2,0,1:T(8,128)} fusion(f32[2048,2,2048]{2,0,1:T(8,128)} %get-tuple-element.945, pred[]{:T(512)S(6)} %compare.47, bf16[1216,1,2048]{2,0,1:T(8,128)(2,1)} %get-tuple-element.903, bf16[1216,1,2048]{2,0,1:T(8,128)(2,1)} %get-tuple-element.904, bf16[1216,2048]{1,0:T(8,128)(2,1)} %all-gather.22.cloned.1.call-done), kind=kOutput, calls=%fused_computation.clone.1 | convolution fusion | flops 20437794816 | bytes 82051072 | tf_op jit(solution)/shard_map/while/body/eval_jaxpr/rd,rcf->dcf/dot_general | solution.py:270
  2004.9 6.5 select_add_fusion.10
  2011.3 30.8 %reduce-scatter.25.cloned.1.call-done = bf16[304,2048]{1,0:T(8,128)(2,1)} async-done(((bf16[1216,2048]{1,0:T(8,128)(2,1)}), bf16[304,2048]{1,0:T(8,128)(2,1)}) %reduce-scatter.25.cloned.1.call-update) | async-done | bytes 1245200 | tf_op jit(solution)/shard_map/while/body/eval_jaxpr/reduce_scatter | solution.py:306
  2044.5 18.0 psum.24
  2083.5 8.4 copy.231
  2091.9 54.9 %copy.229 = bf16[2048,2,2048]{2,1,0:T(2,128)(2,1)} copy(f32[2048,2,2048]{2,0,1:T(8,128)} %get-tuple-element.1006) | data formatting | bytes 50331648 | tf_op jit(solution)/shard_map/while | solution.py:344
  2146.8 9.5 convert_element_type.383
  2159.1 7.1 multiply_reduce_fusion.2
  2173.1 27.5 %reduce-scatter.13.cloned.1.call-done = bf16[512,256]{1,0:T(8,128)(2,1)} async-done(((bf16[512,2048]{1,0:T(8,128)(2,1)}), bf16[512,256]{1,0:T(8,128)(2,1)}) %reduce-scatter.13.cloned.1.call-update) | async-done | bytes 262160 | tf_op jit(solution)/shard_map/reduce_scatter | solution.py:352
  2203.4 230.5 %all-reduce.7.cloned.1.call-done = (bf16[2048,2,128]{2,1,0:T(2,128)(2,1)}, bf16[2048,2,2048]{2,1,0:T(2,128)(2,1)}) async-done(((bf16[2048,2,128]{2,1,0:T(2,128)(2,1)}, bf16[2048,2,2048]{2,1,0:T(2,128)(2,1)}), (bf16[2048,2,128]{2,1,0:T(2,128)(2,1)}, bf16[2048,2,2048]{2,1,0:T(2,128)(2,1)})) %all-reduce.7.cloned.1.call-update) | async-done | bytes 17825808
  2437.1 17.0 multiply_reduce_fusion.1
  2454.1 54.4 %reduce-scatter.15.cloned.1.call-done = bf16[2048,256]{1,0:T(8,128)(2,1)} async-done(((bf16[2048,2048]{1,0:T(8,128)(2,1)}), bf16[2048,256]{1,0:T(8,128)(2,1)}) %reduce-scatter.15.cloned.1.call-update) | async-done | bytes 1048592 | tf_op jit(solution)/shard_map/reduce_scatter | solution.py:358
  2517.7 39.6 %psum.21 = f32[2,7]{1,0:T(2,128)S(1)} all-reduce(f32[2,7]{1,0:T(2,128)S(1)} %pad_maximum_fusion.14), channel_id=1, replica_groups=mesh['dp'=8,'tensor'=4] {'dp','tensor'}, use_global_device_ids=true, to_apply=%region_40.41 | all-reduce | flops 14 | bytes 112 | tf_op jit(solution)/shard_map/psum | solution.py:388
  2561.8 6.8 multiply_subtract_fusion
  (574 shorter events, 300.0 us)
Async XLA Ops:
  7.2 29.4 %all-gather.10.cloned.1.call-start = ((), (), s32[]{:S(2)}) async-start(), calls=%async_computation.8 | async-start | bytes 1179648 | tf_op jit(solution)/shard_map/all_gather | solution.py:197
  8.9 58.0 %all-gather.12.cloned.1.call-start = ((), (), s32[]{:S(2)}) async-start(), calls=%async_computation.9 | async-start | bytes 2359296 | tf_op jit(solution)/shard_map/all_gather | solution.py:196
  11.6 85.9 %all-gather.14.cloned.1.call-start = ((), (), s32[]{:S(2)}) async-start(), calls=%async_computation.10 | async-start | bytes 2359296 | tf_op jit(solution)/shard_map/all_gather | solution.py:198
  14.3 141.4 %all-gather.18.cloned.1.call-start = ((), (), s32[]{:S(2)}) async-start(), calls=%async_computation.12 | async-start | bytes 9437184 | tf_op jit(solution)/shard_map/all_gather | solution.py:200
  18.6 229.2 %copy-start.4 = (bf16[2,1,304,2048]{3,2,1,0:T(8,128)(2,1)S(1)}, bf16[2,1,304,2048]{3,2,1,0:T(8,128)(2,1)}, u32[]{:S(2)}) copy-start(bf16[2,1,304,2048]{3,2,1,0:T(8,128)(2,1)} %param.35) | copy-start | bytes 7471108
  18.6 229.1 %all-gather.16.cloned.1.call-start = ((), (), s32[]{:S(2)}) async-start(), calls=%async_computation.11 | async-start | bytes 18874368 | tf_op jit(solution)/shard_map/all_gather | solution.py:199
  247.9 96.5 %all-gather.20.cloned.1.call-start = ((), (), s32[]{:S(2)}) async-start(), calls=%async_computation.18 | async-start | bytes 6225920 | tf_op jit(solution)/shard_map/while/body/eval_jaxpr/all_gather | solution.py:218
  249.2 100.3 %copy-start.47 = (f32[1,2048]{1,0:T(1,128)}, f32[1,2048]{1,0:T(1,128)S(1)}, u32[]{:S(2)}) copy-start(f32[1,2048]{1,0:T(1,128)S(1)} %get-tuple-element.884) | copy-start | bytes 24580 | tf_op jit(solution)/shard_map/while
  249.2 590.0 %copy-start.39 = (f32[1,2048]{1,0:T(1,128)}, f32[1,2048]{1,0:T(1,128)S(1)}, u32[]{:S(2)}) copy-start(f32[1,2048]{1,0:T(1,128)S(1)} %get-tuple-element.882) | copy-start | bytes 24580 | tf_op jit(solution)/shard_map/while
  250.6 249.5 %reduce-scatter.19.cloned.1.call-start = ((), (), s32[]{:S(2)}) async-start(), calls=%async_computation.19 | async-start | bytes 6225920 | tf_op jit(solution)/shard_map/while/body/eval_jaxpr/reduce_scatter | solution.py:234
  254.4 113.5 %copy-start.10 = (pred[608,608]{0,1:T(8,128)(4,1)}, pred[608,608]{0,1:T(8,128)(4,1)S(1)}, u32[]{:S(2)}) copy-start(pred[608,608]{0,1:T(8,128)(4,1)S(1)} %slice.564) | copy-start | bytes 1108996 | tf_op jit(solution)/shard_map/while
  255.4 138.4 %copy-start.8 = (pred[608,1216]{0,1:T(8,128)(4,1)}, pred[608,1216]{0,1:T(8,128)(4,1)S(1)}, u32[]{:S(2)}) copy-start(pred[608,1216]{0,1:T(8,128)(4,1)S(1)} %slice.563) | copy-start | bytes 2217988 | tf_op jit(solution)/shard_map/while
  256.0 105.1 %copy-start.20 = (f32[1216,32]{0,1:T(8,128)}, f32[1216,32]{0,1:T(8,128)S(1)}, u32[]{:S(2)}) copy-start(f32[1216,32]{0,1:T(8,128)S(1)} %get-tuple-element.887) | copy-start | bytes 466948 | tf_op jit(solution)/shard_map/while
  256.1 105.1 %copy-start.22 = (f32[1216,32]{0,1:T(8,128)}, f32[1216,32]{0,1:T(8,128)S(1)}, u32[]{:S(2)}) copy-start(f32[1216,32]{0,1:T(8,128)S(1)} %get-tuple-element.886) | copy-start | bytes 466948 | tf_op jit(solution)/shard_map/while
  412.0 88.1 %copy-start.5 = (bf16[2,1,304,2048]{3,2,1,0:T(8,128)(2,1)S(1)}, bf16[2,1,304,2048]{3,2,1,0:T(8,128)(2,1)}, u32[]{:S(2)}) copy-start(bf16[2,1,304,2048]{3,2,1,0:T(8,128)(2,1)} %get-tuple-element.1020) | copy-start | bytes 7471108 | tf_op jit(solution)/shard_map/while
  412.1 187.3 %all-gather.22.cloned.1.call-start = ((), (), s32[]{:S(2)}) async-start(), calls=%async_computation.20 | async-start | bytes 6225920 | tf_op jit(solution)/shard_map/while/body/eval_jaxpr/all_gather | solution.py:244
  502.0 337.1 %copy-start.61 = (f32[304]{0:T(512)}, f32[304]{0:T(512)S(1)}, u32[]{:S(2)}) copy-start(f32[304]{0:T(512)S(1)} %add_rsqrt_fusion.5) | copy-start | bytes 3652 | tf_op jit(solution)/shard_map/while
  505.0 188.6 %all-gather.24.cloned.1.call-start = ((), (), s32[]{:S(2)}) async-start(), calls=%async_computation.21 | async-start | bytes 6225920 | tf_op jit(solution)/shard_map/while/body/eval_jaxpr/all_gather | solution.py:264
  507.7 327.9 %reduce-scatter.23.cloned.1.call-start = ((), (), s32[]{:S(2)}) async-start(), calls=%async_computation.23 | async-start | bytes 6225920 | tf_op jit(solution)/shard_map/while/body/eval_jaxpr/reduce_scatter | solution.py:273
  747.5 189.8 %all-gather.26.cloned.1.call-start = ((), (), s32[]{:S(2)}) async-start(), calls=%async_computation.24 | async-start | bytes 6225920 | tf_op jit(solution)/shard_map/while/body/eval_jaxpr/all_gather | solution.py:284
  842.9 231.4 %reduce-scatter.21.cloned.1.call-start = ((), (), s32[]{:S(2)}) async-start(), calls=%async_computation.22 | async-start | bytes 6225920 | tf_op jit(solution)/shard_map/while/body/eval_jaxpr/reduce_scatter | solution.py:253
  843.0 112.5 %copy-start.43 = (f32[1,8,608]{2,1,0:T(8,128)}, f32[1,8,608]{2,1,0:T(8,128)S(1)}, u32[]{:S(2)}) copy-start(f32[1,8,608]{2,1,0:T(8,128)S(1)} %log_add_fusion.5) | copy-start | bytes 58372 | tf_op jit(solution)/shard_map/while
  859.0 273.6 %reduce-scatter.25.cloned.1.call-start = ((), (), s32[]{:S(2)}) async-start(), calls=%async_computation.25 | async-start | bytes 6225920 | tf_op jit(solution)/shard_map/while/body/eval_jaxpr/reduce_scatter | solution.py:306
  859.1 78.3 %copy-start.83 = (bf16[512,2048]{1,0:T(8,128)(2,1)S(1)}, bf16[512,2048]{1,0:T(8,128)(2,1)}, u32[]{:S(2)}) copy-start(bf16[512,2048]{1,0:T(8,128)(2,1)} %get-tuple-element.973) | copy-start | bytes 6291460 | tf_op jit(solution)/shard_map/while
  969.2 42.4 %slice-start.6 = ((s8[6225920]{0:T(1024)(128)(4,1)}), s8[2031616]{0:T(1024)(128)(4,1)S(1)}, s32[]{:S(2)}) async-start(s8[6225920]{0:T(1024)(128)(4,1)} %bitcast.547), calls=%async_computation.32 | async-start | bytes 4063232 | tf_op jit(solution)/shard_map/while
  1090.6 44.3 %copy-start.64 = (f32[2048]{0:T(1024)S(1)}, f32[2048]{0:T(1024)}, u32[]{:S(2)}) copy-start(f32[2048]{0:T(1024)} %get-tuple-element.917) | copy-start | bytes 24580 | tf_op jit(solution)/shard_map/while
  1090.6 62.3 %copy-start.67 = (f32[2,2048]{1,0:T(2,128)S(1)}, f32[2,2048]{1,0:T(2,128)}, u32[]{:S(2)}) copy-start(f32[2,2048]{1,0:T(2,128)} %get-tuple-element.947) | copy-start | bytes 49156 | tf_op jit(solution)/shard_map/while
  1090.6 62.4 %copy-start.40 = (f32[1,2048]{1,0:T(1,128)S(1)}, f32[1,2048]{1,0:T(1,128)}, u32[]{:S(2)}) copy-start(f32[1,2048]{1,0:T(1,128)} %copy-done.39) | copy-start | bytes 24580 | tf_op jit(solution)/shard_map/while
  1090.6 62.4 %copy-start.62 = (f32[304]{0:T(512)S(1)}, f32[304]{0:T(512)}, u32[]{:S(2)}) copy-start(f32[304]{0:T(512)} %copy-done.61) | copy-start | bytes 3652 | tf_op jit(solution)/shard_map/while
  1090.6 62.4 %copy-start.74 = (f32[304]{0:T(512)S(1)}, f32[304]{0:T(512)}, u32[]{:S(2)}) copy-start(f32[304]{0:T(512)} %copy-done.73) | copy-start | bytes 3652 | tf_op jit(solution)/shard_map/while
  1159.1 94.9 %all-gather.20.cloned.1.call-start = ((), (), s32[]{:S(2)}) async-start(), calls=%async_computation.18 | async-start | bytes 6225920 | tf_op jit(solution)/shard_map/while/body/eval_jaxpr/all_gather | solution.py:218
  1160.4 98.7 %copy-start.47 = (f32[1,2048]{1,0:T(1,128)}, f32[1,2048]{1,0:T(1,128)S(1)}, u32[]{:S(2)}) copy-start(f32[1,2048]{1,0:T(1,128)S(1)} %get-tuple-element.884) | copy-start | bytes 24580 | tf_op jit(solution)/shard_map/while
  1160.4 588.3 %copy-start.39 = (f32[1,2048]{1,0:T(1,128)}, f32[1,2048]{1,0:T(1,128)S(1)}, u32[]{:S(2)}) copy-start(f32[1,2048]{1,0:T(1,128)S(1)} %get-tuple-element.882) | copy-start | bytes 24580 | tf_op jit(solution)/shard_map/while
  1161.8 247.9 %reduce-scatter.19.cloned.1.call-start = ((), (), s32[]{:S(2)}) async-start(), calls=%async_computation.19 | async-start | bytes 6225920 | tf_op jit(solution)/shard_map/while/body/eval_jaxpr/reduce_scatter | solution.py:234
  1165.6 111.6 %copy-start.10 = (pred[608,608]{0,1:T(8,128)(4,1)}, pred[608,608]{0,1:T(8,128)(4,1)S(1)}, u32[]{:S(2)}) copy-start(pred[608,608]{0,1:T(8,128)(4,1)S(1)} %slice.564) | copy-start | bytes 1108996 | tf_op jit(solution)/shard_map/while
  1166.6 136.7 %copy-start.8 = (pred[608,1216]{0,1:T(8,128)(4,1)}, pred[608,1216]{0,1:T(8,128)(4,1)S(1)}, u32[]{:S(2)}) copy-start(pred[608,1216]{0,1:T(8,128)(4,1)S(1)} %slice.563) | copy-start | bytes 2217988 | tf_op jit(solution)/shard_map/while
  1167.3 103.5 %copy-start.20 = (f32[1216,32]{0,1:T(8,128)}, f32[1216,32]{0,1:T(8,128)S(1)}, u32[]{:S(2)}) copy-start(f32[1216,32]{0,1:T(8,128)S(1)} %get-tuple-element.887) | copy-start | bytes 466948 | tf_op jit(solution)/shard_map/while
  1167.3 103.5 %copy-start.22 = (f32[1216,32]{0,1:T(8,128)}, f32[1216,32]{0,1:T(8,128)S(1)}, u32[]{:S(2)}) copy-start(f32[1216,32]{0,1:T(8,128)S(1)} %get-tuple-element.886) | copy-start | bytes 466948 | tf_op jit(solution)/shard_map/while
  1321.6 88.1 %copy-start.5 = (bf16[2,1,304,2048]{3,2,1,0:T(8,128)(2,1)S(1)}, bf16[2,1,304,2048]{3,2,1,0:T(8,128)(2,1)}, u32[]{:S(2)}) copy-start(bf16[2,1,304,2048]{3,2,1,0:T(8,128)(2,1)} %get-tuple-element.1020) | copy-start | bytes 7471108 | tf_op jit(solution)/shard_map/while
  1321.7 187.3 %all-gather.22.cloned.1.call-start = ((), (), s32[]{:S(2)}) async-start(), calls=%async_computation.20 | async-start | bytes 6225920 | tf_op jit(solution)/shard_map/while/body/eval_jaxpr/all_gather | solution.py:244
  1411.6 337.1 %copy-start.61 = (f32[304]{0:T(512)}, f32[304]{0:T(512)S(1)}, u32[]{:S(2)}) copy-start(f32[304]{0:T(512)S(1)} %add_rsqrt_fusion.5) | copy-start | bytes 3652 | tf_op jit(solution)/shard_map/while
  1414.6 188.5 %all-gather.24.cloned.1.call-start = ((), (), s32[]{:S(2)}) async-start(), calls=%async_computation.21 | async-start | bytes 6225920 | tf_op jit(solution)/shard_map/while/body/eval_jaxpr/all_gather | solution.py:264
  1417.2 327.8 %reduce-scatter.23.cloned.1.call-start = ((), (), s32[]{:S(2)}) async-start(), calls=%async_computation.23 | async-start | bytes 6225920 | tf_op jit(solution)/shard_map/while/body/eval_jaxpr/reduce_scatter | solution.py:273
  1657.0 189.8 %all-gather.26.cloned.1.call-start = ((), (), s32[]{:S(2)}) async-start(), calls=%async_computation.24 | async-start | bytes 6225920 | tf_op jit(solution)/shard_map/while/body/eval_jaxpr/all_gather | solution.py:284
  1752.5 236.0 %reduce-scatter.21.cloned.1.call-start = ((), (), s32[]{:S(2)}) async-start(), calls=%async_computation.22 | async-start | bytes 6225920 | tf_op jit(solution)/shard_map/while/body/eval_jaxpr/reduce_scatter | solution.py:253
  1752.6 112.5 %copy-start.43 = (f32[1,8,608]{2,1,0:T(8,128)}, f32[1,8,608]{2,1,0:T(8,128)S(1)}, u32[]{:S(2)}) copy-start(f32[1,8,608]{2,1,0:T(8,128)S(1)} %log_add_fusion.5) | copy-start | bytes 58372 | tf_op jit(solution)/shard_map/while
  1768.5 273.6 %reduce-scatter.25.cloned.1.call-start = ((), (), s32[]{:S(2)}) async-start(), calls=%async_computation.25 | async-start | bytes 6225920 | tf_op jit(solution)/shard_map/while/body/eval_jaxpr/reduce_scatter | solution.py:306
  1768.6 78.3 %copy-start.83 = (bf16[512,2048]{1,0:T(8,128)(2,1)S(1)}, bf16[512,2048]{1,0:T(8,128)(2,1)}, u32[]{:S(2)}) copy-start(bf16[512,2048]{1,0:T(8,128)(2,1)} %get-tuple-element.973) | copy-start | bytes 6291460 | tf_op jit(solution)/shard_map/while
  1878.7 42.4 %slice-start.6 = ((s8[6225920]{0:T(1024)(128)(4,1)}), s8[2031616]{0:T(1024)(128)(4,1)S(1)}, s32[]{:S(2)}) async-start(s8[6225920]{0:T(1024)(128)(4,1)} %bitcast.547), calls=%async_computation.32 | async-start | bytes 4063232 | tf_op jit(solution)/shard_map/while
  2004.8 57.6 %copy-start.67 = (f32[2,2048]{1,0:T(2,128)S(1)}, f32[2,2048]{1,0:T(2,128)}, u32[]{:S(2)}) copy-start(f32[2,2048]{1,0:T(2,128)} %get-tuple-element.947) | copy-start | bytes 49156 | tf_op jit(solution)/shard_map/while
  2004.8 57.7 %copy-start.40 = (f32[1,2048]{1,0:T(1,128)S(1)}, f32[1,2048]{1,0:T(1,128)}, u32[]{:S(2)}) copy-start(f32[1,2048]{1,0:T(1,128)} %copy-done.39) | copy-start | bytes 24580 | tf_op jit(solution)/shard_map/while
  2004.8 57.7 %copy-start.62 = (f32[304]{0:T(512)S(1)}, f32[304]{0:T(512)}, u32[]{:S(2)}) copy-start(f32[304]{0:T(512)} %copy-done.61) | copy-start | bytes 3652 | tf_op jit(solution)/shard_map/while
  2004.9 57.6 %copy-start.74 = (f32[304]{0:T(512)S(1)}, f32[304]{0:T(512)}, u32[]{:S(2)}) copy-start(f32[304]{0:T(512)} %copy-done.73) | copy-start | bytes 3652 | tf_op jit(solution)/shard_map/while
  2073.7 95.8 %reduce-scatter.17.cloned.1.call-start = ((), (), s32[]{:S(2)}) async-start(), calls=%async_computation.16 | async-start | bytes 589824
  2075.5 95.6 %reduce-scatter.11.cloned.1.call-start = ((), (), s32[]{:S(2)}) async-start(), calls=%async_computation.13 | async-start | bytes 2359296 | tf_op jit(solution)/shard_map/reduce_scatter | solution.py:346
  2079.4 121.1 %reduce-scatter.13.cloned.1.call-start = ((), (), s32[]{:S(2)}) async-start(), calls=%async_computation.14 | async-start | bytes 2359296 | tf_op jit(solution)/shard_map/reduce_scatter | solution.py:352
  2083.4 350.4 %all-reduce.7.cloned.1.call-start = ((), (), s32[]{:S(2)}) async-start(), calls=%async_computation.17 | async-start | bytes 35651584
  2146.8 361.7 %reduce-scatter.15.cloned.1.call-start = ((), (), s32[]{:S(2)}) async-start(), calls=%async_computation.15 | async-start | bytes 9437184 | tf_op jit(solution)/shard_map/reduce_scatter | solution.py:358
  2156.4 44.1 %copy-start.71 = (f32[512,256]{1,0:T(8,128)S(1)}, f32[512,256]{1,0:T(8,128)}, u32[]{:S(2)}) copy-start(f32[512,256]{1,0:T(8,128)} %param.46) | copy-start | bytes 1572868
  2156.4 44.1 %copy-start.72 = (f32[512,256]{1,0:T(8,128)S(1)}, f32[512,256]{1,0:T(8,128)}, u32[]{:S(2)}) copy-start(f32[512,256]{1,0:T(8,128)} %param.52) | copy-start | bytes 1572868
  2173.1 397.4 %copy-start.50 = (f32[256,512]{1,0:T(8,128)}, f32[256,512]{1,0:T(8,128)S(1)}, u32[]{:S(2)}) copy-start(f32[256,512]{1,0:T(8,128)S(1)} %get-tuple-element.690) | copy-start | bytes 1572868
  2173.1 397.4 %copy-start.51 = (f32[256,512]{1,0:T(8,128)}, f32[256,512]{1,0:T(8,128)S(1)}, u32[]{:S(2)}) copy-start(f32[256,512]{1,0:T(8,128)S(1)} %get-tuple-element.691) | copy-start | bytes 1572868
  2454.1 107.0 %copy-start.76 = (f32[2,256]{1,0:T(2,128)S(1)}, f32[2,256]{1,0:T(2,128)}, u32[]{:S(2)}) copy-start(f32[2,256]{1,0:T(2,128)} %param.43) | copy-start | bytes 6148
  2514.3 57.2 %copy-start.36 = (f32[2048,256]{1,0:T(8,128)}, f32[2048,256]{1,0:T(8,128)S(1)}, u32[]{:S(2)}) copy-start(f32[2048,256]{1,0:T(8,128)S(1)} %get-tuple-element.676) | copy-start | bytes 6291460
  (136 other events, 1101.9 us)
Sparse Core Ops, SparseCore 0:
  10.5 26.1 all-gather.9
  39.1 27.7 all-gather.11
  69.3 28.0 all-gather.13
  99.8 55.8 all-gather.17
  158.0 89.7 all-gather.15
  250.7 93.6 all-gather.19
  412.2 87.9 reduce-scatter.18
  505.1 94.2 all-gather.21
  601.5 92.0 all-gather.23
  747.6 87.8 reduce-scatter.22
  843.1 94.2 all-gather.25
  939.5 87.9 reduce-scatter.20
  1043.9 88.6 reduce-scatter.24
  1161.9 92.0 all-gather.19
  1321.8 87.8 reduce-scatter.18
  1414.7 94.2 all-gather.21
  1510.9 92.0 all-gather.23
  1657.1 87.9 reduce-scatter.22
  1752.6 94.2 all-gather.25
  1849.0 87.9 reduce-scatter.20
  1953.4 88.6 reduce-scatter.24
  2078.1 32.4 reduce-scatter.16
  2114.5 41.0 reduce-scatter.10
  2159.4 41.1 reduce-scatter.12
  2205.0 228.7 all-reduce.6
  2437.2 71.2 reduce-scatter.14
where the time goes:
time: 2590 us; the launch traced here: 2580 us
  waiting for transfers between devices  1550 us (60%)
  matrix products  553 us (21%)
  other arithmetic  218 us (8%)
  local copies, waits for them, and re-layouts  143 us (6%)
  blocking collectives  86 us (3%)
    unnamed x12, waiting for transfers between devices  231 us
    all_gather x2, waiting for transfers between devices, micro_step(): rows_two = lax.all_gather(normed_two, 'tensor', axis=0, tiled=True)  183 us
    reduce_scatter x2, waiting for transfers between devices, micro_step(): lax.psum_scatter(jnp.dot(mixed, full_output, preferred_element_type=jnp.f...  176 us
    reduce_scatter x2, waiting for transfers between devices, micro_step(): lax.psum_scatter(jnp.einsum('rcf,dcf->rd', gateup_grad, full_gateup, pref...  176 us
    all_gather x2, waiting for transfers between devices, micro_step(): rows_one = lax.all_gather(normed_one, 'tensor', axis=0, tiled=True)  175 us
    all_gather x2, waiting for transfers between devices, micro_step(): ffn_grad_all = lax.all_gather(ffn_grad, 'tensor', axis=0, tiled=True)  134 us
    all_gather x2, waiting for transfers between devices, micro_step(): attn_grad_all = lax.all_gather(attn_grad, 'tensor', axis=0, tiled=True)  118 us
    all_gather x1, waiting for transfers between devices, per_device(): lax.all_gather(rounded[3], 'dp', axis=0, tiled=True)  92.1 us
  transfers between devices with their start and end apart: 26, of which 22 were waited for; matrix products, arithmetic and copies ran while one was open for 22% of the time, Pallas kernels for 0%

commit v1 on v0

--- a/solution.py
+++ b/solution.py
@@ -7,7 +7,6 @@
 PROMPT = 1024
 CONTS = 3
 STEP = 3
-GROUP = 1216
 
 
 norm_eps = 1e-05
@@ -20,8 +19,8 @@
 masked_fill = -1e30
 
 
-def layout(lengths):
-    row_index = jnp.arange(GROUP, dtype=jnp.int32)
+def layout(lengths, group_rows):
+    row_index = jnp.arange(group_rows, dtype=jnp.int32)
     ends = jnp.cumsum(lengths)
     starts = ends - lengths
     within = row_index - PROMPT
@@ -163,6 +162,55 @@
     return lax.dot_general(
         left, right, (((1,), (1,)), ((), ())), preferred_element_type=jnp.float32
     )
+
+
+def line_gather(x, count):
+    place = lax.axis_index("tensor")
+    rows = x.shape[0]
+    out = jnp.zeros((count * rows,) + x.shape[1:], x.dtype)
+    from_left = x
+    from_right = x
+    received = []
+    for step in range(1, count):
+        from_left = lax.ppermute(
+            from_left, "tensor", [(i, i + 1) for i in range(step - 1, count - 1)]
+        )
+        from_right = lax.ppermute(
+            from_right, "tensor", [(i, i - 1) for i in range(1, count - step + 1)]
+        )
+        received.append((from_left, place - step, place - step >= 0))
+        received.append((from_right, place + step, place + step <= count - 1))
+    for piece, slot, valid in received:
+        out = lax.dynamic_update_slice_in_dim(out, piece, jnp.where(valid, slot, place) * rows, 0)
+    return lax.dynamic_update_slice_in_dim(out, x, place * rows, 0)
+
+
+def line_scatter(partial, count):
+    place = lax.axis_index("tensor")
+    rows = partial.shape[0] // count
+
+    def chunk(index):
+        return lax.dynamic_slice_in_dim(partial, jnp.clip(index, 0, count - 1) * rows, rows, 0)
+
+    to_right = None
+    to_left = None
+    for step in range(1, count):
+        send = chunk(place + count - step)
+        if to_right is not None:
+            send = send + to_right
+        to_right = lax.ppermute(
+            send.astype(jnp.bfloat16), "tensor", [(i, i + 1) for i in range(step)]
+        ).astype(jnp.float32)
+        send = chunk(place - count + step)
+        if to_left is not None:
+            send = send + to_left
+        to_left = lax.ppermute(
+            send.astype(jnp.bfloat16), "tensor", [(i, i - 1) for i in range(count - step, count)]
+        ).astype(jnp.float32)
+    total = chunk(place)
+    if to_right is not None:
+        total = total + to_right + to_left
+    return total
 
 
 def per_device(
@@ -203,21 +251,22 @@
     full_query, full_keyval, full_output, full_gateup, full_down, full_gains = gathered
     gain_values = full_gains.astype(jnp.float32)
     tensor_count = lax.axis_size("tensor")
-    block_rows = GROUP // 2
+    group_rows = tokens.shape[2] * tensor_count
+    block_rows = group_rows // 2
     keyval_heads = full_keyval.shape[1]
     query_heads = full_query.shape[1] // HD
     head_repeat = query_heads // keyval_heads
 
     def micro_step(token_rows, cot_rows, lengths):
-        visible, position = layout(lengths)
+        visible, position = layout(lengths, group_rows)
         cos_table, sin_table = rope_tables(position)
         start_rows = token_rows.astype(jnp.float32)
         scale_one = lax.rsqrt(jnp.mean(start_rows * start_rows, axis=1, keepdims=True) + norm_eps)
         hat_one = start_rows * scale_one
         normed_one = (hat_one * gain_values[0][None, :]).astype(jnp.bfloat16)
-        rows_one = lax.all_gather(normed_one, "tensor", axis=0, tiled=True)
+        rows_one = line_gather(normed_one, tensor_count)
         query_raw = jnp.dot(rows_one, full_query, preferred_element_type=jnp.float32).reshape(
-            GROUP, query_heads, HD
+            group_rows, query_heads, HD
         )
         keyval_raw = jnp.einsum(
             "rd,dhk->rhk", rows_one, full_keyval, preferred_element_type=jnp.float32
@@ -225,23 +274,20 @@
         queries = (
             rotate(query_raw, cos_table, sin_table)
             .astype(jnp.bfloat16)
-            .reshape(GROUP, keyval_heads, head_repeat, HD)
+            .reshape(group_rows, keyval_heads, head_repeat, HD)
         )
         key_rows = rotate(keyval_raw[:, :, :HD], cos_table, sin_table).astype(jnp.bfloat16)
         values = keyval_raw[:, :, HD:].astype(jnp.bfloat16)
         mixed_full, log_totals = attend(queries, key_rows, values, visible, block_rows)
-        mixed = mixed_full.astype(jnp.bfloat16).reshape(GROUP, query_heads * HD)
-        attn_branch = lax.psum_scatter(
-            jnp.dot(mixed, full_output, preferred_element_type=jnp.float32).astype(jnp.bfloat16),
-            "tensor",
-            scatter_dimension=0,
-            tiled=True,
-        ).astype(jnp.float32)
+        mixed = mixed_full.astype(jnp.bfloat16).reshape(group_rows, query_heads * HD)
+        attn_branch = line_scatter(
+            jnp.dot(mixed, full_output, preferred_element_type=jnp.float32), tensor_count
+        )
         middle = start_rows + branch_scale * attn_branch
         scale_two = lax.rsqrt(jnp.mean(middle * middle, axis=1, keepdims=True) + norm_eps)
         hat_two = middle * scale_two
         normed_two = (hat_two * gain_values[1][None, :]).astype(jnp.bfloat16)
-        rows_two = lax.all_gather(normed_two, "tensor", axis=0, tiled=True)
+        rows_two = line_gather(normed_two, tensor_count)
         gate_up = jnp.einsum(
             "rd,dcf->rcf", rows_two, full_gateup, preferred_element_type=jnp.float32
         )
@@ -250,18 +296,13 @@
         sigmoid_gate = jax.nn.sigmoid(gate_part)
         silu_gate = gate_part * sigmoid_gate
         hidden_state = (silu_gate * up_part).astype(jnp.bfloat16)
-        ffn_branch = lax.psum_scatter(
-            jnp.dot(hidden_state, full_down, preferred_element_type=jnp.float32).astype(
-                jnp.bfloat16
-            ),
-            "tensor",
-            scatter_dimension=0,
-            tiled=True,
-        ).astype(jnp.float32)
+        ffn_branch = line_scatter(
+            jnp.dot(hidden_state, full_down, preferred_element_type=jnp.float32), tensor_count
+        )
         layer_rows = (middle + branch_scale * ffn_branch).astype(jnp.bfloat16)
         upstream = cot_rows.astype(jnp.float32)
         ffn_grad = (branch_scale * upstream).astype(jnp.bfloat16)
-        ffn_grad_all = lax.all_gather(ffn_grad, "tensor", axis=0, tiled=True)
+        ffn_grad_all = line_gather(ffn_grad, tensor_count)
         grad_down = contract_rows(hidden_state, ffn_grad_all)
         hidden_grad = contract_cols(ffn_grad_all, full_down)
         gate_grad = hidden_grad * up_part * sigmoid_gate * (1.0 + gate_part * (1.0 - sigmoid_gate))
@@ -270,31 +311,29 @@
         grad_gateup = jnp.einsum(
             "rd,rcf->dcf", rows_two, gateup_grad, preferred_element_type=jnp.float32
         )
-        normed_two_grad = lax.psum_scatter(
+        normed_two_grad = line_scatter(
             jnp.einsum(
                 "rcf,dcf->rd", gateup_grad, full_gateup, preferred_element_type=jnp.float32
-            ).astype(jnp.bfloat16),
-            "tensor",
-            scatter_dimension=0,
-            tiled=True,
-        ).astype(jnp.float32)
+            ),
+            tensor_count,
+        )
         middle_back, gain_two = norm_back(normed_two_grad, hat_two, scale_two, gain_values[1])
         middle_grad = upstream + middle_back
         attn_grad = (branch_scale * middle_grad).astype(jnp.bfloat16)
-        attn_grad_all = lax.all_gather(attn_grad, "tensor", axis=0, tiled=True)
+        attn_grad_all = line_gather(attn_grad, tensor_count)
         grad_output = contract_rows(mixed, attn_grad_all)
         mixed_grad = (
             contract_cols(attn_grad_all, full_output)
             .astype(jnp.bfloat16)
-            .reshape(GROUP, keyval_heads, head_repeat, HD)
+            .reshape(group_rows, keyval_heads, head_repeat, HD)
         )
         query_grad, key_grad, value_grad = attend_back(
             queries, key_rows, values, visible, log_totals, mixed_grad, block_rows
         )
         query_raw_grad = (
-            rotate_back(query_grad.reshape(GROUP, query_heads, HD), cos_table, sin_table)
+            rotate_back(query_grad.reshape(group_rows, query_heads, HD), cos_table, sin_table)
             .astype(jnp.bfloat16)
-            .reshape(GROUP, query_heads * HD)
+            .reshape(group_rows, query_heads * HD)
         )
         keyval_raw_grad = jnp.concatenate(
             [rotate_back(key_grad, cos_table, sin_table), value_grad], axis=2
@@ -303,63 +342,61 @@
         grad_keyval = jnp.einsum(
             "rd,rhk->dhk", rows_one, keyval_raw_grad, preferred_element_type=jnp.float32
         )
-        normed_one_grad = lax.psum_scatter(
-            (
-                contract_cols(query_raw_grad, full_query)
-                + jnp.einsum(
-                    "rhk,dhk->rd", keyval_raw_grad, full_keyval, preferred_element_type=jnp.float32
-                )
-            ).astype(jnp.bfloat16),
-            "tensor",
-            scatter_dimension=0,
-            tiled=True,
-        ).astype(jnp.float32)
+        normed_one_grad = line_scatter(
+            contract_cols(query_raw_grad, full_query)
+            + jnp.einsum(
+                "rhk,dhk->rd", keyval_raw_grad, full_keyval, preferred_element_type=jnp.float32
+            ),
+            tensor_count,
+        )
         start_back, gain_one = norm_back(normed_one_grad, hat_one, scale_one, gain_values[0])
         input_rows = middle_grad + start_back
-        gain_grad = lax.psum(jnp.stack([gain_one, gain_two]), "tensor")
+        gain_grad = jnp.stack([gain_one, gain_two])
         return (
             layer_rows,
             input_rows,
             (grad_query, grad_keyval, grad_output, grad_gateup, grad_down, gain_grad),
         )
 
-    totals_init = tuple((jnp.zeros(piece_full.shape, jnp.float32) for piece_full in gathered))
-
-    def run_micro(step_index, carry):
-        out_rows, grad_rows, totals = carry
-        token_rows = lax.dynamic_index_in_dim(tokens, step_index, 0, keepdims=False)[0]
-        cot_rows = lax.dynamic_index_in_dim(cotangent, step_index, 0, keepdims=False)[0]
-        lengths = lax.dynamic_index_in_dim(cont_lengths, step_index, 0, keepdims=False)[0]
-        layer_rows, input_rows, grads = micro_step(token_rows, cot_rows, lengths)
-        totals = tuple((old_sum + new_term for old_sum, new_term in zip(totals, grads)))
-        out_rows = lax.dynamic_update_index_in_dim(out_rows, layer_rows[None], step_index, 0)
-        grad_rows = lax.dynamic_update_index_in_dim(grad_rows, input_rows[None], step_index, 0)
-        return (out_rows, grad_rows, totals)
-
-    initial = (
-        jnp.zeros(tokens.shape, jnp.bfloat16),
-        jnp.zeros(tokens.shape, jnp.float32),
-        totals_init,
-    )
-    layer_output, input_grad, totals = lax.fori_loop(0, tokens.shape[0], run_micro, initial)
+    out_list = []
+    grad_list = []
+    totals = None
+    for step_index in range(tokens.shape[0]):
+        layer_rows, input_rows, grads = micro_step(
+            tokens[step_index, 0], cotangent[step_index, 0], cont_lengths[step_index, 0]
+        )
+        out_list.append(layer_rows)
+        grad_list.append(input_rows)
+        if totals is None:
+            totals = grads
+        else:
+            totals = tuple((old_sum + new_term for old_sum, new_term in zip(totals, grads)))
+    layer_output = jnp.stack(out_list)[:, None]
+    input_grad = jnp.stack(grad_list)[:, None]
+    width = totals[0].shape[0]
+    gain_total = lax.psum(totals[5], "tensor")
     summed = (
         lax.psum_scatter(
             totals[0].astype(jnp.bfloat16), "dp", scatter_dimension=0, tiled=True
         ).astype(jnp.float32),
         lax.psum_scatter(
-            totals[1].astype(jnp.bfloat16), "dp", scatter_dimension=0, tiled=True
-        ).astype(jnp.float32),
+            totals[1].reshape(width, -1).astype(jnp.bfloat16), "dp", scatter_dimension=0, tiled=True
+        )
+        .astype(jnp.float32)
+        .reshape(-1, *totals[1].shape[1:]),
         lax.psum_scatter(
             totals[2].astype(jnp.bfloat16), "dp", scatter_dimension=1, tiled=True
         ).astype(jnp.float32),
         lax.psum_scatter(
-            totals[3].astype(jnp.bfloat16), "dp", scatter_dimension=0, tiled=True
-        ).astype(jnp.float32),
+            totals[3].reshape(width, -1).astype(jnp.bfloat16), "dp", scatter_dimension=0, tiled=True
+        )
+        .astype(jnp.float32)
+        .reshape(-1, *totals[3].shape[1:]),
         lax.psum_scatter(
             totals[4].astype(jnp.bfloat16), "dp", scatter_dimension=1, tiled=True
         ).astype(jnp.float32),
         lax.psum_scatter(
-            totals[5].astype(jnp.bfloat16), "dp", scatter_dimension=1, tiled=True
+            gain_total.astype(jnp.bfloat16), "dp", scatter_dimension=1, tiled=True
         ).astype(jnp.float32),
     )
     correction = 1.0 - moment_decay**STEP

time: 2590 us -> 2030 us (0.78)
  waiting for transfers between devices: 1550 us -> 682 us
  starting transfers between devices: 1.12 us -> 281 us
  other arithmetic: 218 us -> 259 us
  matrix products: 553 us -> 523 us
    ppermute x0 -> x96, waiting for transfers between devices: none -> 682 us  [the longest x24 289 us: line_gather(): lax.ppermute(from_right, 'tensor', [(i, i - 1) for i in range(1, count -...]
    all_gather x8 -> x0, waiting for transfers between devices: 610 us -> none  [the longest x2 183 us: micro_step(): rows_two = lax.all_gather(normed_two, 'tensor', axis=0, tiled=True)]
    reduce_scatter x8 -> x2, waiting for transfers between devices: 420 us -> 0.04 us  [the longest x1 0.02 us: per_device(): lax.psum_scatter(totals[1].reshape(width, -1).astype(jnp.bfloat16), 'dp',...]
    ppermute x0 -> x96, starting transfers between devices: none -> 279 us  [the longest x24 130 us: line_scatter(): lax.ppermute(send.astype(jnp.bfloat16), 'tensor', [(i, i + 1) for i in ra...]
    unnamed x12, waiting for transfers between devices: 231 us -> 0.18 us
    while x306 -> x0, local copies, waits for them, and re-layouts: 113 us -> none  [the longest x2 63.2 us: per_device(): lax.fori_loop(0, tokens.shape[0], run_micro, initial)]
    all_gather x1, waiting for transfers between devices: 92.1 us -> 0.01 us  [per_device(): lax.all_gather(rounded[3], 'dp', axis=0, tiled=True)]
    dynamic_update_slice x0 -> x54, local copies, waits for them, and re-layouts: none -> 62.9 us  [the longest x48 56.3 us: line_gather(): lax.dynamic_update_slice_in_dim(out, piece, jnp.where(valid, slot, place)...]
  transfers between devices with their start and end apart: 26 -> 107, of which waited for: 22 -> 49; matrix products, arithmetic and copies ran while one was open for 22% -> 35% of each run, Pallas kernels for 0% -> 0%
where the time goes in v1:
time: 2030 us; the launch traced here: 2010 us
  waiting for transfers between devices  682 us (34%)
  matrix products  523 us (26%)
  starting transfers between devices  281 us (14%)
  other arithmetic  259 us (13%)
  local copies, waits for them, and re-layouts  155 us (8%)
  blocking collectives  91.2 us (4%)
  between operations  21.1 us (1%)
    ppermute x24, waiting for transfers between devices, line_gather(): lax.ppermute(from_right, 'tensor', [(i, i - 1) for i in range(1, count -...  289 us
    ppermute x24, waiting for transfers between devices, line_scatter(): lax.ppermute(send.astype(jnp.bfloat16), 'tensor', [(i, i + 1) for i in ra...  209 us
    ppermute x24, starting transfers between devices, line_scatter(): lax.ppermute(send.astype(jnp.bfloat16), 'tensor', [(i, i + 1) for i in ra...  130 us
    ppermute x24, waiting for transfers between devices, line_gather(): lax.ppermute(from_left, 'tensor', [(i, i + 1) for i in range(step - 1, co...  101 us
    ppermute x24, starting transfers between devices, line_gather(): lax.ppermute(from_left, 'tensor', [(i, i + 1) for i in range(step - 1, co...  87.3 us
    ppermute x24, waiting for transfers between devices, line_scatter(): lax.ppermute(send.astype(jnp.bfloat16), 'tensor', [(i, i - 1) for i in ra...  82.7 us
    convert_element_type x24, other arithmetic, line_scatter(): send.astype(jnp.bfloat16)  67.7 us
    dot_general x6, matrix products, contract_cols(): lax.dot_general(left, right, (((1,), (1,)), ((), ())), preferred_element_...  63.1 us
  transfers between devices with their start and end apart: 107, of which 49 were waited for; matrix products, arithmetic and copies ran while one was open for 35% of the time, Pallas kernels for 0%

profile of v1, /device:TPU:0, one launch (start us, length us, event | category | flops | bytes accessed | tf_op | source)
XLA Modules:
  0.0 2012.0 jit_solution(2475740379531020903)
XLA Ops:
  15.1 10.4 all_gather.18
  50.1 10.3 collective-permute-done
  67.2 19.3 collective-permute-done.24
  122.3 23.6 %collective-permute-done.27 = bf16[304,2048]{1,0:T(8,128)(2,1)} collective-permute-done((bf16[304,2048]{1,0:T(8,128)(2,1)}, bf16[304,2048]{1,0:T(8,128)(2,1)}, u32[]{:S(2)}, u32[]{:S(2)}) %collective-permute-start.27) | collective-permute-done | bytes 1245216 | tf_op jit(solution)/shard_map/ppermute | solution.py:178
  156.5 16.0 collective-permute-done.5
  218.4 12.2 fusion.136
  301.8 12.3 fusion.135
  335.0 17.1 collective-permute-done.30
  385.7 19.7 collective-permute-done.31
  411.3 20.7 %collective-permute-done.72 = bf16[304,2048]{1,0:T(8,128)(2,1)} collective-permute-done((bf16[304,2048]{1,0:T(8,128)(2,1)}, bf16[304,2048]{1,0:T(8,128)(2,1)}, u32[]{:S(2)}, u32[]{:S(2)}) %collective-permute-start.72) | collective-permute-done | bytes 1245216 | tf_op jit(solution)/shard_map/ppermute | solution.py:175
  439.7 16.9 collective-permute-done.48
  465.0 13.5 collective-permute-start.8
  481.1 12.3 collective-permute-start.32
  504.1 12.1 collective-permute-done.51
  527.8 14.9 collective-permute-done.11
  544.1 25.5 %collective-permute-done.35 = bf16[304,2048]{1,0:T(8,128)(2,1)} collective-permute-done((bf16[304,2048]{1,0:T(8,128)(2,1)S(1)}, bf16[304,2048]{1,0:T(8,128)(2,1)}, u32[]{:S(2)}, u32[]{:S(2)}) %collective-permute-start.35) | collective-permute-done | bytes 1245216 | tf_op jit(solution)/shard_map/ppermute | solution.py:207
  577.4 10.3 collective-permute-start.36
  604.8 18.1 collective-permute-done.53
  625.3 24.2 %collective-permute-done.37 = bf16[304,2048]{1,0:T(8,128)(2,1)S(1)} collective-permute-done((bf16[304,2048]{1,0:T(8,128)(2,1)S(1)}, bf16[304,2048]{1,0:T(8,128)(2,1)S(1)}, u32[]{:S(2)}, u32[]{:S(2)}) %collective-permute-start.37) | collective-permute-done | bytes 1245216 | tf_op jit(solution)/shard_map/ppermute | solution.py:178
  651.5 24.6 %collective-permute-done.13 = bf16[304,2048]{1,0:T(8,128)(2,1)S(1)} collective-permute-done((bf16[304,2048]{1,0:T(8,128)(2,1)S(1)}, bf16[304,2048]{1,0:T(8,128)(2,1)S(1)}, u32[]{:S(2)}, u32[]{:S(2)}) %collective-permute-start.13) | collective-permute-done | bytes 1245216 | tf_op jit(solution)/shard_map/ppermute | solution.py:178
  686.7 16.1 collective-permute-done.39
  704.9 24.6 %collective-permute-done.15 = bf16[304,2048]{1,0:T(8,128)(2,1)S(1)} collective-permute-done((bf16[304,2048]{1,0:T(8,128)(2,1)S(1)}, bf16[304,2048]{1,0:T(8,128)(2,1)S(1)}, u32[]{:S(2)}, u32[]{:S(2)}) %collective-permute-start.15) | collective-permute-done | bytes 1245216 | tf_op jit(solution)/shard_map/ppermute | solution.py:178
  733.6 22.6 %collective-permute-done.41 = bf16[304,2048]{1,0:T(8,128)(2,1)S(1)} collective-permute-done((bf16[304,2048]{1,0:T(8,128)(2,1)S(1)}, bf16[304,2048]{1,0:T(8,128)(2,1)S(1)}, u32[]{:S(2)}, u32[]{:S(2)}) %collective-permute-start.41) | collective-permute-done | bytes 1245216 | tf_op jit(solution)/shard_map/ppermute | solution.py:178
  757.8 22.4 %collective-permute-done.17 = bf16[304,2048]{1,0:T(8,128)(2,1)S(1)} collective-permute-done((bf16[304,2048]{1,0:T(8,128)(2,1)S(1)}, bf16[304,2048]{1,0:T(8,128)(2,1)S(1)}, u32[]{:S(2)}, u32[]{:S(2)}) %collective-permute-start.17) | collective-permute-done | bytes 1245216 | tf_op jit(solution)/shard_map/ppermute | solution.py:178
  782.4 27.3 %fusion.56 = f32[1216,2,2048]{2,0,1:T(8,128)} fusion(bf16[2048,2,2048]{2,0,1:T(8,128)(2,1)} %all-gather.12.cloned.1.call-done, bf16[1216,2048]{1,0:T(8,128)(2,1)} %copy-done.61), kind=kOutput, calls=%fused_computation.100 | convolution fusion | flops 20401094656 | bytes 41680896 | tf_op jit(solution)/shard_map/rd,dcf->rcf/dot_general | solution.py:291
  809.7 25.6 %fusion.70 = (bf16[1216,1,2048]{2,0,1:T(8,128)(2,1)}, bf16[1216,1,2048]{2,0,1:T(8,128)(2,1)}, bf16[1216,2048]{1,0:T(8,128)(2,1)}) fusion(f32[1216,2,2048]{2,0,1:T(8,128)} %fusion.56, bf16[1216,2048]{1,0:T(8,128)(2,1)} %copy-done.60, bf16[2048,2048]{1,0:T(8,128)(2,1)} %all-gather.14.cloned.1.call-done), kind=kOutput, calls=%fused_computation.114 | convolution fusion | flops 10237902848 | bytes 48234496 | tf_op jit(solution)/shard_map/dot_general | solution.py:162
  835.3 24.9 %convolution_bitcast_fusion = f32[1216,2048]{1,0:T(8,128)S(1)} fusion(bf16[2048,2,2048]{2,0,1:T(8,128)(2,1)} %all-gather.12.cloned.1.call-done, bf16[1216,1,2048]{2,0,1:T(8,128)(2,1)} %get-tuple-element.302, bf16[1216,1,2048]{2,0,1:T(8,128)(2,1)} %get-tuple-element.301), kind=kOutput, calls=%fused_computation.80 | convolution fusion | flops 20406075392 | bytes 36700160 | tf_op jit(solution)/shard_map/rcf,dcf->rd/dot_general | solution.py:315
  865.1 27.3 %fusion.63 = f32[1216,2,2048]{2,0,1:T(8,128)} fusion(bf16[2048,2,2048]{2,0,1:T(8,128)(2,1)} %all-gather.12.cloned.1.call-done, bf16[1216,2048]{1,0:T(8,128)(2,1)} %constant_dynamic-update-slice_fusion.42), kind=kOutput, calls=%fused_computation.107 | convolution fusion | flops 20401094656 | bytes 41680896 | tf_op jit(solution)/shard_map/rd,dcf->rcf/dot_general | solution.py:291
  892.4 25.7 %fusion.69 = (bf16[1216,1,2048]{2,0,1:T(8,128)(2,1)}, bf16[1216,1,2048]{2,0,1:T(8,128)(2,1)}, bf16[1216,2048]{1,0:T(8,128)(2,1)}) fusion(f32[1216,2,2048]{2,0,1:T(8,128)} %fusion.63, bf16[1216,2048]{1,0:T(8,128)(2,1)} %copy-done.58, bf16[2048,2048]{1,0:T(8,128)(2,1)} %all-gather.14.cloned.1.call-done), kind=kOutput, calls=%fused_computation.113 | convolution fusion | flops 10237902848 | bytes 48234496 | tf_op jit(solution)/shard_map/dot_general | solution.py:162
  918.1 24.7 %convolution_bitcast_fusion.1 = f32[1216,2048]{1,0:T(8,128)S(1)} fusion(bf16[2048,2,2048]{2,0,1:T(8,128)(2,1)} %all-gather.12.cloned.1.call-done, bf16[1216,1,2048]{2,0,1:T(8,128)(2,1)} %get-tuple-element.304, bf16[1216,1,2048]{2,0,1:T(8,128)(2,1)} %get-tuple-element.303), kind=kOutput, calls=%fused_computation.81 | convolution fusion | flops 20406075392 | bytes 36700160 | tf_op jit(solution)/shard_map/rcf,dcf->rd/dot_general | solution.py:315
  948.0 14.6 fusion.233
  981.2 19.1 collective-permute-done.18
  1006.0 21.0 %collective-permute-done.79 = bf16[304,2048]{1,0:T(8,128)(2,1)} collective-permute-done((bf16[304,2048]{1,0:T(8,128)(2,1)S(1)}, bf16[304,2048]{1,0:T(8,128)(2,1)}, u32[]{:S(2)}, u32[]{:S(2)}) %collective-permute-start.79) | collective-permute-done | bytes 1245216 | tf_op jit(solution)/shard_map/ppermute | solution.py:201
  1031.6 22.1 %collective-permute-done.55 = bf16[304,2048]{1,0:T(8,128)(2,1)} collective-permute-done((bf16[304,2048]{1,0:T(8,128)(2,1)S(1)}, bf16[304,2048]{1,0:T(8,128)(2,1)}, u32[]{:S(2)}, u32[]{:S(2)}) %collective-permute-start.55) | collective-permute-done | bytes 1245216 | tf_op jit(solution)/shard_map/ppermute | solution.py:201
  1068.9 11.5 collective-permute-done.19
  1088.3 31.9 %collective-permute-start.20 = (bf16[304,2048]{1,0:T(8,128)(2,1)}, bf16[304,2048]{1,0:T(8,128)(2,1)}, u32[]{:S(2)}, u32[]{:S(2)}) collective-permute-start(bf16[304,2048]{1,0:T(8,128)(2,1)} %get-tuple-element.323), channel_id=1, source_target_pairs={{0,1},{1,2},{2,3},{4,5},{5,6},{6,7},{8,9},{9,10},{10,11},{12,13},{... | collective-permute-start | bytes 3735560 | tf_op jit(solution)/shard_map/ppermute | solution.py:201
  1123.0 10.9 collective-permute-done.56
  1169.3 31.6 %collective-permute-start.60 = (bf16[304,2048]{1,0:T(8,128)(2,1)S(1)}, bf16[304,2048]{1,0:T(8,128)(2,1)S(1)}, u32[]{:S(2)}, u32[]{:S(2)}) collective-permute-start(bf16[304,2048]{1,0:T(8,128)(2,1)S(1)} %get-tuple-element.348), channel_id=1, source_target_pairs={{0,1},{1,2},{2,3},{4,5},{5,6},{6,7},{8,9},{9,10},{10,11},{12,13},{... | collective-permute-start | bytes 3735560 | tf_op jit(solution)/shard_map/ppermute | solution.py:175
  1210.1 18.5 collective-permute-done.60
  1234.4 15.4 collective-permute-done.84
  1261.5 17.9 fusion.237
  1289.5 23.8 %collective-permute-done.87 = bf16[304,2048]{1,0:T(8,128)(2,1)} collective-permute-done((bf16[304,2048]{1,0:T(8,128)(2,1)S(1)}, bf16[304,2048]{1,0:T(8,128)(2,1)}, u32[]{:S(2)}, u32[]{:S(2)}) %collective-permute-start.87) | collective-permute-done | bytes 1245216 | tf_op jit(solution)/shard_map/ppermute | solution.py:178
  1317.9 21.9 %collective-permute-done.65 = bf16[304,2048]{1,0:T(8,128)(2,1)S(1)} collective-permute-done((bf16[304,2048]{1,0:T(8,128)(2,1)S(1)}, bf16[304,2048]{1,0:T(8,128)(2,1)S(1)}, u32[]{:S(2)}, u32[]{:S(2)}) %collective-permute-start.65) | collective-permute-done | bytes 1245216 | tf_op jit(solution)/shard_map/ppermute | solution.py:178
  1344.4 11.4 fusion.19
  1386.7 9.8 fusion.16
  1408.0 17.5 fusion.3
  1425.5 12.0 fusion.125
  1437.5 16.7 fusion.5
  1481.2 17.8 fusion
  1498.9 11.9 fusion.122
  1510.8 16.9 fusion.2
  1586.5 12.8 collective-permute-done.90
  1606.0 19.0 add_convert_fusion.1
  1632.1 9.5 collective-permute-done.91
  1664.6 28.4 %fusion.42 = f32[2048,2,2048]{0,2,1:T(8,128)} fusion(bf16[1216,1,2048]{2,0,1:T(8,128)(2,1)} %get-tuple-element.302, bf16[1216,1,2048]{2,0,1:T(8,128)(2,1)} %get-tuple-element.301, bf16[1216,2048]{1,0:T(8,128)(2,1)S(1)} %bitcast.621), kind=kOutput, calls=%fused_computation.84 | convolution fusion | flops 20421017600 | bytes 48496640 | tf_op jit(solution)/shard_map/rd,rcf->dcf/dot_general | solution.py:311
  1694.8 17.9 collective-permute-done.95
  1718.3 35.7 %psum.14 = bf16[2,2048]{1,0:T(2,128)(2,1)S(1)} all-reduce(f32[2,2048]{1,0:T(2,128)S(1)} %maximum_add_fusion), channel_id=1, replica_groups=mesh['dp'=8,'tensor'=4] {'tensor'}, use_global_device_ids=true, to_apply=%region_46.47 | all-reduce | flops 4096 | bytes 24576 | tf_op jit(solution)/shard_map/psum | solution.py:377
  1755.5 30.5 %add_convert_fusion = bf16[2048,2,2048]{0,2,1:T(8,128)(2,1)} fusion(f32[2048,2,2048]{0,2,1:T(8,128)} %fusion.42, bf16[1216,1,2048]{2,0,1:T(8,128)(2,1)} %get-tuple-element.304, bf16[1216,1,2048]{2,0,1:T(8,128)(2,1)} %get-tuple-element.303, bf16[1216,2048]{1,0:T(8,128)(2,1)} %constant_dynamic-update-slice_fusion.42), kind=kOutput, calls=%fused_computation | convolution fusion | flops 20437794816 | bytes 65273856 | tf_op jit(solution)/shard_map/rd,rcf->dcf/dot_general | solution.py:311
  1786.1 14.6 fusion.235
  1803.3 25.9 %collective-permute-done.42 = bf16[304,2048]{1,0:T(8,128)(2,1)S(1)} collective-permute-done((bf16[304,2048]{1,0:T(8,128)(2,1)S(1)}, bf16[304,2048]{1,0:T(8,128)(2,1)S(1)}, u32[]{:S(2)}, u32[]{:S(2)}) %collective-permute-start.42) | collective-permute-done | bytes 1245216 | tf_op jit(solution)/shard_map/ppermute | solution.py:201
  1834.2 14.3 collective-permute-done.43
  1893.4 10.2 collective-permute-done.47
  1919.3 18.3 multiply_reduce_fusion
  1942.7 45.1 %psum.15 = f32[2,7]{1,0:T(2,128)S(1)} all-reduce(f32[2,7]{1,0:T(2,128)S(1)} %pad_maximum_fusion.26), channel_id=1, replica_groups=mesh['dp'=8,'tensor'=4] {'dp','tensor'}, use_global_device_ids=true, to_apply=%region_49.50 | all-reduce | flops 14 | bytes 112 | tf_op jit(solution)/shard_map/psum | solution.py:425
  (828 shorter events, 759.2 us)
Async XLA Ops:
  7.2 168.9 %all-gather.6.cloned.1.call-start = ((), (), s32[]{:S(2)}) async-start(), calls=%async_computation.6 | async-start | bytes 1179648 | tf_op jit(solution)/shard_map/all_gather | solution.py:245
  9.1 173.8 %all-gather.8.cloned.1.call-start = ((), (), s32[]{:S(2)}) async-start(), calls=%async_computation.7 | async-start | bytes 2359296 | tf_op jit(solution)/shard_map/all_gather | solution.py:244
  11.7 225.9 %all-gather.10.cloned.1.call-start = ((), (), s32[]{:S(2)}) async-start(), calls=%async_computation.8 | async-start | bytes 2359296 | tf_op jit(solution)/shard_map/all_gather | solution.py:246
  14.4 768.0 %all-gather.12.cloned.1.call-start = ((), (), s32[]{:S(2)}) async-start(), calls=%async_computation.9 | async-start | bytes 18874368 | tf_op jit(solution)/shard_map/all_gather | solution.py:247
  34.7 51.8 %collective-permute-start.24 = (bf16[304,2048]{1,0:T(8,128)(2,1)}, bf16[304,2048]{1,0:T(8,128)(2,1)}, u32[]{:S(2)}, u32[]{:S(2)}) collective-permute-start(bf16[304,2048]{1,0:T(8,128)(2,1)} %get-tuple-element.350), channel_id=1, source_target_pairs={{0,1},{1,2},{2,3},{4,5},{5,6},{6,7},{8,9},{9,10},{10,11},{12,13},{... | collective-permute-start | bytes 3735560 | tf_op jit(solution)/shard_map/ppermute | solution.py:175
  40.4 52.2 %collective-permute-start.25 = (bf16[304,2048]{1,0:T(8,128)(2,1)}, bf16[304,2048]{1,0:T(8,128)(2,1)}, u32[]{:S(2)}, u32[]{:S(2)}) collective-permute-start(bf16[304,2048]{1,0:T(8,128)(2,1)} %get-tuple-element.350), channel_id=1, source_target_pairs={{1,0},{2,1},{3,2},{5,4},{6,5},{7,6},{9,8},{10,9},{11,10},{13,12},{... | collective-permute-start | bytes 3735560 | tf_op jit(solution)/shard_map/ppermute | solution.py:178
  45.2 764.4 %all-gather.14.cloned.1.call-start = ((), (), s32[]{:S(2)}) async-start(), calls=%async_computation.10 | async-start | bytes 9437184 | tf_op jit(solution)/shard_map/all_gather | solution.py:248
  65.9 53.4 %collective-permute-start.3 = (bf16[304,2048]{1,0:T(8,128)(2,1)}, bf16[304,2048]{1,0:T(8,128)(2,1)}, u32[]{:S(2)}, u32[]{:S(2)}) collective-permute-start(bf16[304,2048]{1,0:T(8,128)(2,1)} %collective-permute-done.1), channel_id=1, source_target_pairs={{1,0},{2,1},{5,4},{6,5},{9,8},{10,9},{13,12},{14,13},{17,16},{18,1... | collective-permute-start | bytes 3735560 | tf_op jit(solution)/shard_map/ppermute | solution.py:178
  92.6 53.4 %collective-permute-start.27 = (bf16[304,2048]{1,0:T(8,128)(2,1)}, bf16[304,2048]{1,0:T(8,128)(2,1)}, u32[]{:S(2)}, u32[]{:S(2)}) collective-permute-start(bf16[304,2048]{1,0:T(8,128)(2,1)} %collective-permute-done.25), channel_id=1, source_target_pairs={{1,0},{2,1},{5,4},{6,5},{9,8},{10,9},{13,12},{14,13},{17,16},{18,1... | collective-permute-start | bytes 3735560 | tf_op jit(solution)/shard_map/ppermute | solution.py:178
  119.3 53.3 %collective-permute-start.5 = (bf16[304,2048]{1,0:T(8,128)(2,1)}, bf16[304,2048]{1,0:T(8,128)(2,1)S(1)}, u32[]{:S(2)}, u32[]{:S(2)}) collective-permute-start(bf16[304,2048]{1,0:T(8,128)(2,1)} %collective-permute-done.3), channel_id=1, source_target_pairs={{1,0},{5,4},{9,8},{13,12},{17,16},{21,20},{25,24},{29,28}} | collective-permute-start | bytes 3735560 | tf_op jit(solution)/shard_map/ppermute | solution.py:178
  120.6 126.8 %collective-permute-start.28 = (bf16[304,2048]{1,0:T(8,128)(2,1)}, bf16[304,2048]{1,0:T(8,128)(2,1)}, u32[]{:S(2)}, u32[]{:S(2)}) collective-permute-start(bf16[304,2048]{1,0:T(8,128)(2,1)} %collective-permute-done.26), channel_id=1, source_target_pairs={{2,3},{6,7},{10,11},{14,15},{18,19},{22,23},{26,27},{30,31}} | collective-permute-start | bytes 3735560 | tf_op jit(solution)/shard_map/ppermute | solution.py:175
  145.9 104.0 %collective-permute-start.29 = (bf16[304,2048]{1,0:T(8,128)(2,1)}, bf16[304,2048]{1,0:T(8,128)(2,1)}, u32[]{:S(2)}, u32[]{:S(2)}) collective-permute-start(bf16[304,2048]{1,0:T(8,128)(2,1)} %collective-permute-done.27), channel_id=1, source_target_pairs={{1,0},{5,4},{9,8},{13,12},{17,16},{21,20},{25,24},{29,28}} | collective-permute-start | bytes 3735560 | tf_op jit(solution)/shard_map/ppermute | solution.py:178
  244.5 84.5 %collective-permute-start.6 = (bf16[304,2048]{1,0:T(8,128)(2,1)}, bf16[304,2048]{1,0:T(8,128)(2,1)}, u32[]{:S(2)}, u32[]{:S(2)}) collective-permute-start(bf16[304,2048]{1,0:T(8,128)(2,1)} %get-tuple-element.329), channel_id=1, source_target_pairs={{0,1},{4,5},{8,9},{12,13},{16,17},{20,21},{24,25},{28,29}} | collective-permute-start | bytes 3735560 | tf_op jit(solution)/shard_map/ppermute | solution.py:201
  363.0 69.1 %collective-permute-start.72 = (bf16[304,2048]{1,0:T(8,128)(2,1)}, bf16[304,2048]{1,0:T(8,128)(2,1)}, u32[]{:S(2)}, u32[]{:S(2)}) collective-permute-start(bf16[304,2048]{1,0:T(8,128)(2,1)} %get-tuple-element.356), channel_id=1, source_target_pairs={{0,1},{1,2},{2,3},{4,5},{5,6},{6,7},{8,9},{9,10},{10,11},{12,13},{... | collective-permute-start | bytes 3735560 | tf_op jit(solution)/shard_map/ppermute | solution.py:175
  365.3 72.6 %collective-permute-start.73 = (bf16[304,2048]{1,0:T(8,128)(2,1)}, bf16[304,2048]{1,0:T(8,128)(2,1)}, u32[]{:S(2)}, u32[]{:S(2)}) collective-permute-start(bf16[304,2048]{1,0:T(8,128)(2,1)} %get-tuple-element.356), channel_id=1, source_target_pairs={{1,0},{2,1},{3,2},{5,4},{6,5},{7,6},{9,8},{10,9},{11,10},{13,12},{... | collective-permute-start | bytes 3735560 | tf_op jit(solution)/shard_map/ppermute | solution.py:178
  366.6 89.9 %collective-permute-start.48 = (bf16[304,2048]{1,0:T(8,128)(2,1)}, bf16[304,2048]{1,0:T(8,128)(2,1)}, u32[]{:S(2)}, u32[]{:S(2)}) collective-permute-start(bf16[304,2048]{1,0:T(8,128)(2,1)} %get-tuple-element.357), channel_id=1, source_target_pairs={{0,1},{1,2},{2,3},{4,5},{5,6},{6,7},{8,9},{9,10},{10,11},{12,13},{... | collective-permute-start | bytes 3735560 | tf_op jit(solution)/shard_map/ppermute | solution.py:175
  378.7 79.1 %collective-permute-start.49 = (bf16[304,2048]{1,0:T(8,128)(2,1)}, bf16[304,2048]{1,0:T(8,128)(2,1)}, u32[]{:S(2)}, u32[]{:S(2)}) collective-permute-start(bf16[304,2048]{1,0:T(8,128)(2,1)} %get-tuple-element.357), channel_id=1, source_target_pairs={{1,0},{2,1},{3,2},{5,4},{6,5},{7,6},{9,8},{10,9},{11,10},{13,12},{... | collective-permute-start | bytes 3735560 | tf_op jit(solution)/shard_map/ppermute | solution.py:178
  405.4 55.7 %collective-permute-start.10 = (bf16[304,2048]{1,0:T(8,128)(2,1)}, bf16[304,2048]{1,0:T(8,128)(2,1)}, u32[]{:S(2)}, u32[]{:S(2)}) collective-permute-start(bf16[304,2048]{1,0:T(8,128)(2,1)} %get-tuple-element.328), channel_id=1, source_target_pairs={{2,1},{3,2},{6,5},{7,6},{10,9},{11,10},{14,13},{15,14},{18,17},{19... | collective-permute-start | bytes 3735560 | tf_op jit(solution)/shard_map/ppermute | solution.py:207
  435.8 1436.4 %reduce-scatter.11.cloned.1.call-start = ((), (), s32[]{:S(2)}) async-start(), calls=%async_computation.12 | async-start | bytes 1179648 | tf_op jit(solution)/shard_map/reduce_scatter | solution.py:382
  461.1 55.0 %collective-permute-start.51 = (bf16[304,2048]{1,0:T(8,128)(2,1)}, bf16[304,2048]{1,0:T(8,128)(2,1)}, u32[]{:S(2)}, u32[]{:S(2)}) collective-permute-start(bf16[304,2048]{1,0:T(8,128)(2,1)} %collective-permute-done.49), channel_id=1, source_target_pairs={{1,0},{2,1},{5,4},{6,5},{9,8},{10,9},{13,12},{14,13},{17,16},{18,1... | collective-permute-start | bytes 3735560 | tf_op jit(solution)/shard_map/ppermute | solution.py:178
  465.0 52.8 %collective-permute-start.8 = (bf16[304,2048]{1,0:T(8,128)(2,1)S(1)}, bf16[304,2048]{1,0:T(8,128)(2,1)S(1)}, u32[]{:S(2)}, u32[]{:S(2)}) collective-permute-start(bf16[304,2048]{1,0:T(8,128)(2,1)S(1)} %copy-done.102), channel_id=1, source_target_pairs={{0,1},{1,2},{2,3},{4,5},{5,6},{6,7},{8,9},{9,10},{10,11},{12,13},{... | collective-permute-start | bytes 3735560 | tf_op jit(solution)/shard_map/ppermute | solution.py:201
  494.8 74.8 %collective-permute-start.35 = (bf16[304,2048]{1,0:T(8,128)(2,1)S(1)}, bf16[304,2048]{1,0:T(8,128)(2,1)}, u32[]{:S(2)}, u32[]{:S(2)}) collective-permute-start(bf16[304,2048]{1,0:T(8,128)(2,1)S(1)} %add_convert_fusion.25), channel_id=1, source_target_pairs={{1,0},{2,1},{3,2},{5,4},{6,5},{7,6},{9,8},{10,9},{11,10},{13,12},{... | collective-permute-start | bytes 3735560 | tf_op jit(solution)/shard_map/ppermute | solution.py:207
  516.2 71.5 %collective-permute-start.76 = (bf16[304,2048]{1,0:T(8,128)(2,1)}, bf16[304,2048]{1,0:T(8,128)(2,1)}, u32[]{:S(2)}, u32[]{:S(2)}) collective-permute-start(bf16[304,2048]{1,0:T(8,128)(2,1)} %collective-permute-done.74), channel_id=1, source_target_pairs={{2,3},{6,7},{10,11},{14,15},{18,19},{22,23},{26,27},{30,31}} | collective-permute-start | bytes 3735560 | tf_op jit(solution)/shard_map/ppermute | solution.py:175
  517.9 78.3 %collective-permute-start.77 = (bf16[304,2048]{1,0:T(8,128)(2,1)}, bf16[304,2048]{1,0:T(8,128)(2,1)}, u32[]{:S(2)}, u32[]{:S(2)}) collective-permute-start(bf16[304,2048]{1,0:T(8,128)(2,1)} %collective-permute-done.75), channel_id=1, source_target_pairs={{1,0},{5,4},{9,8},{13,12},{17,16},{21,20},{25,24},{29,28}} | collective-permute-start | bytes 3735560 | tf_op jit(solution)/shard_map/ppermute | solution.py:178
  526.1 71.6 %collective-permute-start.52 = (bf16[304,2048]{1,0:T(8,128)(2,1)}, bf16[304,2048]{1,0:T(8,128)(2,1)}, u32[]{:S(2)}, u32[]{:S(2)}) collective-permute-start(bf16[304,2048]{1,0:T(8,128)(2,1)} %collective-permute-done.50), channel_id=1, source_target_pairs={{2,3},{6,7},{10,11},{14,15},{18,19},{22,23},{26,27},{30,31}} | collective-permute-start | bytes 3735560 | tf_op jit(solution)/shard_map/ppermute | solution.py:175
  542.7 80.2 %collective-permute-start.53 = (bf16[304,2048]{1,0:T(8,128)(2,1)}, bf16[304,2048]{1,0:T(8,128)(2,1)}, u32[]{:S(2)}, u32[]{:S(2)}) collective-permute-start(bf16[304,2048]{1,0:T(8,128)(2,1)} %collective-permute-done.51), channel_id=1, source_target_pairs={{1,0},{5,4},{9,8},{13,12},{17,16},{21,20},{25,24},{29,28}} | collective-permute-start | bytes 3735560 | tf_op jit(solution)/shard_map/ppermute | solution.py:178
  587.7 61.8 %collective-permute-start.37 = (bf16[304,2048]{1,0:T(8,128)(2,1)S(1)}, bf16[304,2048]{1,0:T(8,128)(2,1)S(1)}, u32[]{:S(2)}, u32[]{:S(2)}) collective-permute-start(bf16[304,2048]{1,0:T(8,128)(2,1)S(1)} %get-tuple-element.394), channel_id=1, source_target_pairs={{1,0},{2,1},{3,2},{5,4},{6,5},{7,6},{9,8},{10,9},{11,10},{13,12},{... | collective-permute-start | bytes 3735560 | tf_op jit(solution)/shard_map/ppermute | solution.py:178
  596.2 54.6 %collective-permute-start.12 = (bf16[304,2048]{1,0:T(8,128)(2,1)S(1)}, bf16[304,2048]{1,0:T(8,128)(2,1)S(1)}, u32[]{:S(2)}, u32[]{:S(2)}) collective-permute-start(bf16[304,2048]{1,0:T(8,128)(2,1)S(1)} %get-tuple-element.393), channel_id=1, source_target_pairs={{0,1},{1,2},{2,3},{4,5},{5,6},{6,7},{8,9},{9,10},{10,11},{12,13},{... | collective-permute-start | bytes 3735560 | tf_op jit(solution)/shard_map/ppermute | solution.py:175
  597.7 78.4 %collective-permute-start.13 = (bf16[304,2048]{1,0:T(8,128)(2,1)S(1)}, bf16[304,2048]{1,0:T(8,128)(2,1)S(1)}, u32[]{:S(2)}, u32[]{:S(2)}) collective-permute-start(bf16[304,2048]{1,0:T(8,128)(2,1)S(1)} %get-tuple-element.393), channel_id=1, source_target_pairs={{1,0},{2,1},{3,2},{5,4},{6,5},{7,6},{9,8},{10,9},{11,10},{13,12},{... | collective-permute-start | bytes 3735560 | tf_op jit(solution)/shard_map/ppermute | solution.py:178
  624.3 60.5 %collective-permute-start.38 = (bf16[304,2048]{1,0:T(8,128)(2,1)S(1)}, bf16[304,2048]{1,0:T(8,128)(2,1)S(1)}, u32[]{:S(2)}, u32[]{:S(2)}) collective-permute-start(bf16[304,2048]{1,0:T(8,128)(2,1)S(1)} %collective-permute-done.36), channel_id=1, source_target_pairs={{1,2},{2,3},{5,6},{6,7},{9,10},{10,11},{13,14},{14,15},{17,18},{18... | collective-permute-start | bytes 3735560 | tf_op jit(solution)/shard_map/ppermute | solution.py:175
  649.5 53.4 %collective-permute-start.39 = (bf16[304,2048]{1,0:T(8,128)(2,1)S(1)}, bf16[304,2048]{1,0:T(8,128)(2,1)S(1)}, u32[]{:S(2)}, u32[]{:S(2)}) collective-permute-start(bf16[304,2048]{1,0:T(8,128)(2,1)S(1)} %collective-permute-done.37), channel_id=1, source_target_pairs={{1,0},{2,1},{5,4},{6,5},{9,8},{10,9},{13,12},{14,13},{17,16},{18,1... | collective-permute-start | bytes 3735560 | tf_op jit(solution)/shard_map/ppermute | solution.py:178
  650.8 53.4 %collective-permute-start.14 = (bf16[304,2048]{1,0:T(8,128)(2,1)S(1)}, bf16[304,2048]{1,0:T(8,128)(2,1)S(1)}, u32[]{:S(2)}, u32[]{:S(2)}) collective-permute-start(bf16[304,2048]{1,0:T(8,128)(2,1)S(1)} %collective-permute-done.12), channel_id=1, source_target_pairs={{1,2},{2,3},{5,6},{6,7},{9,10},{10,11},{13,14},{14,15},{17,18},{18... | collective-permute-start | bytes 3735560 | tf_op jit(solution)/shard_map/ppermute | solution.py:175
  676.2 53.4 %collective-permute-start.15 = (bf16[304,2048]{1,0:T(8,128)(2,1)S(1)}, bf16[304,2048]{1,0:T(8,128)(2,1)S(1)}, u32[]{:S(2)}, u32[]{:S(2)}) collective-permute-start(bf16[304,2048]{1,0:T(8,128)(2,1)S(1)} %collective-permute-done.13), channel_id=1, source_target_pairs={{1,0},{2,1},{5,4},{6,5},{9,8},{10,9},{13,12},{14,13},{17,16},{18,1... | collective-permute-start | bytes 3735560 | tf_op jit(solution)/shard_map/ppermute | solution.py:178
  702.8 53.4 %collective-permute-start.41 = (bf16[304,2048]{1,0:T(8,128)(2,1)S(1)}, bf16[304,2048]{1,0:T(8,128)(2,1)S(1)}, u32[]{:S(2)}, u32[]{:S(2)}) collective-permute-start(bf16[304,2048]{1,0:T(8,128)(2,1)S(1)} %collective-permute-done.39), channel_id=1, source_target_pairs={{1,0},{5,4},{9,8},{13,12},{17,16},{21,20},{25,24},{29,28}} | collective-permute-start | bytes 3735560 | tf_op jit(solution)/shard_map/ppermute | solution.py:178
  704.1 52.4 %collective-permute-start.16 = (bf16[304,2048]{1,0:T(8,128)(2,1)S(1)}, bf16[304,2048]{1,0:T(8,128)(2,1)S(1)}, u32[]{:S(2)}, u32[]{:S(2)}) collective-permute-start(bf16[304,2048]{1,0:T(8,128)(2,1)S(1)} %collective-permute-done.14), channel_id=1, source_target_pairs={{2,3},{6,7},{10,11},{14,15},{18,19},{22,23},{26,27},{30,31}} | collective-permute-start | bytes 3735560 | tf_op jit(solution)/shard_map/ppermute | solution.py:175
  729.5 50.6 %collective-permute-start.17 = (bf16[304,2048]{1,0:T(8,128)(2,1)S(1)}, bf16[304,2048]{1,0:T(8,128)(2,1)S(1)}, u32[]{:S(2)}, u32[]{:S(2)}) collective-permute-start(bf16[304,2048]{1,0:T(8,128)(2,1)S(1)} %collective-permute-done.15), channel_id=1, source_target_pairs={{1,0},{5,4},{9,8},{13,12},{17,16},{21,20},{25,24},{29,28}} | collective-permute-start | bytes 3735560 | tf_op jit(solution)/shard_map/ppermute | solution.py:178
  862.5 103.1 %collective-permute-start.78 = (bf16[304,2048]{1,0:T(8,128)(2,1)}, bf16[304,2048]{1,0:T(8,128)(2,1)}, u32[]{:S(2)}, u32[]{:S(2)}) collective-permute-start(bf16[304,2048]{1,0:T(8,128)(2,1)} %get-tuple-element.313), channel_id=1, source_target_pairs={{0,1},{4,5},{8,9},{12,13},{16,17},{20,21},{24,25},{28,29}} | collective-permute-start | bytes 3735560 | tf_op jit(solution)/shard_map/ppermute | solution.py:201
  968.2 58.9 %collective-permute-start.79 = (bf16[304,2048]{1,0:T(8,128)(2,1)S(1)}, bf16[304,2048]{1,0:T(8,128)(2,1)}, u32[]{:S(2)}, u32[]{:S(2)}) collective-permute-start(bf16[304,2048]{1,0:T(8,128)(2,1)S(1)} %add_convert_fusion.11), channel_id=1, source_target_pairs={{0,1},{1,2},{4,5},{5,6},{8,9},{9,10},{12,13},{13,14},{16,17},{17,1... | collective-permute-start | bytes 3735560 | tf_op jit(solution)/shard_map/ppermute | solution.py:201
  970.5 61.1 %collective-permute-start.57 = (bf16[304,2048]{1,0:T(8,128)(2,1)S(1)}, bf16[304,2048]{1,0:T(8,128)(2,1)S(1)}, u32[]{:S(2)}, u32[]{:S(2)}) collective-permute-start(bf16[304,2048]{1,0:T(8,128)(2,1)S(1)} %get-tuple-element.322), channel_id=1, source_target_pairs={{3,2},{7,6},{11,10},{15,14},{19,18},{23,22},{27,26},{31,30}} | collective-permute-start | bytes 3735560 | tf_op jit(solution)/shard_map/ppermute | solution.py:207
  975.9 77.8 %collective-permute-start.55 = (bf16[304,2048]{1,0:T(8,128)(2,1)S(1)}, bf16[304,2048]{1,0:T(8,128)(2,1)}, u32[]{:S(2)}, u32[]{:S(2)}) collective-permute-start(bf16[304,2048]{1,0:T(8,128)(2,1)S(1)} %add_convert_fusion.19), channel_id=1, source_target_pairs={{0,1},{1,2},{4,5},{5,6},{8,9},{9,10},{12,13},{13,14},{16,17},{17,1... | collective-permute-start | bytes 3735560 | tf_op jit(solution)/shard_map/ppermute | solution.py:201
  1000.3 64.0 %collective-permute-start.21 = (bf16[304,2048]{1,0:T(8,128)(2,1)S(1)}, bf16[304,2048]{1,0:T(8,128)(2,1)S(1)}, u32[]{:S(2)}, u32[]{:S(2)}) collective-permute-start(bf16[304,2048]{1,0:T(8,128)(2,1)S(1)} %get-tuple-element.326), channel_id=1, source_target_pairs={{3,2},{7,6},{11,10},{15,14},{19,18},{23,22},{27,26},{31,30}} | collective-permute-start | bytes 3735560 | tf_op jit(solution)/shard_map/ppermute | solution.py:207
  1001.5 78.9 %collective-permute-start.19 = (bf16[304,2048]{1,0:T(8,128)(2,1)S(1)}, bf16[304,2048]{1,0:T(8,128)(2,1)S(1)}, u32[]{:S(2)}, u32[]{:S(2)}) collective-permute-start(bf16[304,2048]{1,0:T(8,128)(2,1)S(1)} %add_convert_fusion.33), channel_id=1, source_target_pairs={{0,1},{1,2},{4,5},{5,6},{8,9},{9,10},{12,13},{13,14},{16,17},{17,1... | collective-permute-start | bytes 3735560 | tf_op jit(solution)/shard_map/ppermute | solution.py:201
  1030.7 52.4 %collective-permute-start.82 = (bf16[304,2048]{1,0:T(8,128)(2,1)}, bf16[304,2048]{1,0:T(8,128)(2,1)S(1)}, u32[]{:S(2)}, u32[]{:S(2)}) collective-permute-start(bf16[304,2048]{1,0:T(8,128)(2,1)} %get-tuple-element.312), channel_id=1, source_target_pairs={{2,1},{3,2},{6,5},{7,6},{10,9},{11,10},{14,13},{15,14},{18,17},{19... | collective-permute-start | bytes 3735560 | tf_op jit(solution)/shard_map/ppermute | solution.py:207
  1059.2 62.4 %collective-permute-start.80 = (bf16[304,2048]{1,0:T(8,128)(2,1)}, bf16[304,2048]{1,0:T(8,128)(2,1)S(1)}, u32[]{:S(2)}, u32[]{:S(2)}) collective-permute-start(bf16[304,2048]{1,0:T(8,128)(2,1)} %get-tuple-element.311), channel_id=1, source_target_pairs={{0,1},{1,2},{2,3},{4,5},{5,6},{6,7},{8,9},{9,10},{10,11},{12,13},{... | collective-permute-start | bytes 3735560 | tf_op jit(solution)/shard_map/ppermute | solution.py:201
  1064.3 69.6 %collective-permute-start.56 = (bf16[304,2048]{1,0:T(8,128)(2,1)}, bf16[304,2048]{1,0:T(8,128)(2,1)S(1)}, u32[]{:S(2)}, u32[]{:S(2)}) collective-permute-start(bf16[304,2048]{1,0:T(8,128)(2,1)} %get-tuple-element.319), channel_id=1, source_target_pairs={{0,1},{1,2},{2,3},{4,5},{5,6},{6,7},{8,9},{9,10},{10,11},{12,13},{... | collective-permute-start | bytes 3735560 | tf_op jit(solution)/shard_map/ppermute | solution.py:201
  1083.4 50.4 %collective-permute-start.83 = (bf16[304,2048]{1,0:T(8,128)(2,1)S(1)}, bf16[304,2048]{1,0:T(8,128)(2,1)S(1)}, u32[]{:S(2)}, u32[]{:S(2)}) collective-permute-start(bf16[304,2048]{1,0:T(8,128)(2,1)S(1)} %add_convert_fusion.8), channel_id=1, source_target_pairs={{1,0},{2,1},{3,2},{5,4},{6,5},{7,6},{9,8},{10,9},{11,10},{13,12},{... | collective-permute-start | bytes 3735560 | tf_op jit(solution)/shard_map/ppermute | solution.py:207
  1086.9 56.5 %collective-permute-start.59 = (bf16[304,2048]{1,0:T(8,128)(2,1)S(1)}, bf16[304,2048]{1,0:T(8,128)(2,1)}, u32[]{:S(2)}, u32[]{:S(2)}) collective-permute-start(bf16[304,2048]{1,0:T(8,128)(2,1)S(1)} %add_convert_fusion.16), channel_id=1, source_target_pairs={{1,0},{2,1},{3,2},{5,4},{6,5},{7,6},{9,8},{10,9},{11,10},{13,12},{... | collective-permute-start | bytes 3735560 | tf_op jit(solution)/shard_map/ppermute | solution.py:207
  1088.3 68.9 %collective-permute-start.20 = (bf16[304,2048]{1,0:T(8,128)(2,1)}, bf16[304,2048]{1,0:T(8,128)(2,1)}, u32[]{:S(2)}, u32[]{:S(2)}) collective-permute-start(bf16[304,2048]{1,0:T(8,128)(2,1)} %get-tuple-element.323), channel_id=1, source_target_pairs={{0,1},{1,2},{2,3},{4,5},{5,6},{6,7},{8,9},{9,10},{10,11},{12,13},{... | collective-permute-start | bytes 3735560 | tf_op jit(solution)/shard_map/ppermute | solution.py:201
  1169.3 59.3 %collective-permute-start.60 = (bf16[304,2048]{1,0:T(8,128)(2,1)S(1)}, bf16[304,2048]{1,0:T(8,128)(2,1)S(1)}, u32[]{:S(2)}, u32[]{:S(2)}) collective-permute-start(bf16[304,2048]{1,0:T(8,128)(2,1)S(1)} %get-tuple-element.348), channel_id=1, source_target_pairs={{0,1},{1,2},{2,3},{4,5},{5,6},{6,7},{8,9},{9,10},{10,11},{12,13},{... | collective-permute-start | bytes 3735560 | tf_op jit(solution)/shard_map/ppermute | solution.py:175
  1206.9 52.9 %collective-permute-start.85 = (bf16[304,2048]{1,0:T(8,128)(2,1)S(1)}, bf16[304,2048]{1,0:T(8,128)(2,1)S(1)}, u32[]{:S(2)}, u32[]{:S(2)}) collective-permute-start(bf16[304,2048]{1,0:T(8,128)(2,1)S(1)} %get-tuple-element.347), channel_id=1, source_target_pairs={{1,0},{2,1},{3,2},{5,4},{6,5},{7,6},{9,8},{10,9},{11,10},{13,12},{... | collective-permute-start | bytes 3735560 | tf_op jit(solution)/shard_map/ppermute | solution.py:178
  1228.6 52.5 %collective-permute-start.62 = (bf16[304,2048]{1,0:T(8,128)(2,1)S(1)}, bf16[304,2048]{1,0:T(8,128)(2,1)S(1)}, u32[]{:S(2)}, u32[]{:S(2)}) collective-permute-start(bf16[304,2048]{1,0:T(8,128)(2,1)S(1)} %collective-permute-done.60), channel_id=1, source_target_pairs={{1,2},{2,3},{5,6},{6,7},{9,10},{10,11},{13,14},{14,15},{17,18},{18... | collective-permute-start | bytes 3735560 | tf_op jit(solution)/shard_map/ppermute | solution.py:175
  1233.1 53.4 %collective-permute-start.63 = (bf16[304,2048]{1,0:T(8,128)(2,1)S(1)}, bf16[304,2048]{1,0:T(8,128)(2,1)S(1)}, u32[]{:S(2)}, u32[]{:S(2)}) collective-permute-start(bf16[304,2048]{1,0:T(8,128)(2,1)S(1)} %collective-permute-done.61), channel_id=1, source_target_pairs={{1,0},{2,1},{5,4},{6,5},{9,8},{10,9},{13,12},{14,13},{17,16},{18,1... | collective-permute-start | bytes 3735560 | tf_op jit(solution)/shard_map/ppermute | solution.py:178
  1259.8 53.5 %collective-permute-start.87 = (bf16[304,2048]{1,0:T(8,128)(2,1)S(1)}, bf16[304,2048]{1,0:T(8,128)(2,1)}, u32[]{:S(2)}, u32[]{:S(2)}) collective-permute-start(bf16[304,2048]{1,0:T(8,128)(2,1)S(1)} %collective-permute-done.85), channel_id=1, source_target_pairs={{1,0},{2,1},{5,4},{6,5},{9,8},{10,9},{13,12},{14,13},{17,16},{18,1... | collective-permute-start | bytes 3735560 | tf_op jit(solution)/shard_map/ppermute | solution.py:178
  1286.5 53.4 %collective-permute-start.65 = (bf16[304,2048]{1,0:T(8,128)(2,1)S(1)}, bf16[304,2048]{1,0:T(8,128)(2,1)S(1)}, u32[]{:S(2)}, u32[]{:S(2)}) collective-permute-start(bf16[304,2048]{1,0:T(8,128)(2,1)S(1)} %collective-permute-done.63), channel_id=1, source_target_pairs={{1,0},{5,4},{9,8},{13,12},{17,16},{21,20},{25,24},{29,28}} | collective-permute-start | bytes 3735560 | tf_op jit(solution)/shard_map/ppermute | solution.py:178
  1287.8 78.6 %collective-permute-start.88 = (bf16[304,2048]{1,0:T(8,128)(2,1)}, bf16[304,2048]{1,0:T(8,128)(2,1)}, u32[]{:S(2)}, u32[]{:S(2)}) collective-permute-start(bf16[304,2048]{1,0:T(8,128)(2,1)} %collective-permute-done.86), channel_id=1, source_target_pairs={{2,3},{6,7},{10,11},{14,15},{18,19},{22,23},{26,27},{30,31}} | collective-permute-start | bytes 3735560 | tf_op jit(solution)/shard_map/ppermute | solution.py:175
  1313.3 60.4 %collective-permute-start.89 = (bf16[304,2048]{1,0:T(8,128)(2,1)}, bf16[304,2048]{1,0:T(8,128)(2,1)}, u32[]{:S(2)}, u32[]{:S(2)}) collective-permute-start(bf16[304,2048]{1,0:T(8,128)(2,1)} %collective-permute-done.87), channel_id=1, source_target_pairs={{1,0},{5,4},{9,8},{13,12},{17,16},{21,20},{25,24},{29,28}} | collective-permute-start | bytes 3735560 | tf_op jit(solution)/shard_map/ppermute | solution.py:178
  1474.8 105.8 %collective-permute-start.66 = (bf16[304,2048]{1,0:T(8,128)(2,1)}, bf16[304,2048]{1,0:T(8,128)(2,1)}, u32[]{:S(2)}, u32[]{:S(2)}) collective-permute-start(bf16[304,2048]{1,0:T(8,128)(2,1)} %get-tuple-element.317), channel_id=1, source_target_pairs={{0,1},{4,5},{8,9},{12,13},{16,17},{20,21},{24,25},{28,29}} | collective-permute-start | bytes 3735560 | tf_op jit(solution)/shard_map/ppermute | solution.py:201
  1477.3 147.8 %collective-permute-start.69 = (bf16[304,2048]{1,0:T(8,128)(2,1)}, bf16[304,2048]{1,0:T(8,128)(2,1)}, u32[]{:S(2)}, u32[]{:S(2)}) collective-permute-start(bf16[304,2048]{1,0:T(8,128)(2,1)} %get-tuple-element.318), channel_id=1, source_target_pairs={{3,2},{7,6},{11,10},{15,14},{19,18},{23,22},{27,26},{31,30}} | collective-permute-start | bytes 3735560 | tf_op jit(solution)/shard_map/ppermute | solution.py:207
  1547.7 328.6 %reduce-scatter.9.cloned.1.call-start = ((), (), s32[]{:S(2)}) async-start(), calls=%async_computation.11 | async-start | bytes 2359296 | tf_op jit(solution)/shard_map/reduce_scatter | solution.py:379
  1560.9 318.4 %reduce-scatter.13.cloned.1.call-start = ((), (), s32[]{:S(2)}) async-start(), calls=%async_computation.13 | async-start | bytes 2359296 | tf_op jit(solution)/shard_map/reduce_scatter | solution.py:387
  1571.4 60.7 %collective-permute-start.93 = (bf16[304,2048]{1,0:T(8,128)(2,1)}, bf16[304,2048]{1,0:T(8,128)(2,1)}, u32[]{:S(2)}, u32[]{:S(2)}) collective-permute-start(bf16[304,2048]{1,0:T(8,128)(2,1)} %get-tuple-element.310), channel_id=1, source_target_pairs={{3,2},{7,6},{11,10},{15,14},{19,18},{23,22},{27,26},{31,30}} | collective-permute-start | bytes 3735560 | tf_op jit(solution)/shard_map/ppermute | solution.py:207
  1580.6 302.5 %reduce-scatter.17.cloned.1.call-start = ((), (), s32[]{:S(2)}) async-start(), calls=%async_computation.15 | async-start | bytes 9437184 | tf_op jit(solution)/shard_map/reduce_scatter | solution.py:395
  1625.0 286.2 %reduce-scatter.19.cloned.1.call-start = ((), (), s32[]{:S(2)}) async-start(), calls=%async_computation.16 | async-start | bytes 589824
  1755.1 157.8 %reduce-scatter.15.cloned.1.call-start = ((), (), s32[]{:S(2)}) async-start(), calls=%async_computation.14 | async-start | bytes 18874368 | tf_op jit(solution)/shard_map/reduce_scatter | solution.py:390
  (242 other events, 4945.7 us)
Sparse Core Ops, SparseCore 0:
  10.5 26.0 all-gather.5
  39.1 27.7 all-gather.7
  69.4 28.0 all-gather.9
  99.8 89.7 all-gather.11
  435.9 56.6 all-gather.13
  1547.8 33.3 reduce-scatter.10
  1585.1 41.0 reduce-scatter.8
  1630.1 41.0 reduce-scatter.12
  1674.7 71.2 reduce-scatter.16
  1755.2 31.3 reduce-scatter.18
  1790.2 116.0 reduce-scatter.14

commit v2 on v1

--- a/solution.py
+++ b/solution.py
@@ -211,6 +211,37 @@
     if to_right is not None:
         total = total + to_right + to_left
     return total
+
+
+def line_all_to_all(x, count, split_axis, concat_axis):
+    place = lax.axis_index("tensor")
+    size = x.shape[split_axis] // count
+
+    def block(index):
+        return lax.dynamic_slice_in_dim(
+            x, jnp.clip(index, 0, count - 1) * size, size, split_axis
+        )
+
+    own = block(place)
+    width = own.shape[concat_axis]
+    shape = list(own.shape)
+    shape[concat_axis] = width * count
+    out = jnp.zeros(shape, x.dtype)
+    received = []
+    for step in range(1, count):
+        from_left = lax.ppermute(
+            block(place + step), "tensor", [(i, i + step) for i in range(count - step)]
+        )
+        from_right = lax.ppermute(
+            block(place - step), "tensor", [(i, i - step) for i in range(step, count)]
+        )
+        received.append((from_left, place - step, place - step >= 0))
+        received.append((from_right, place + step, place + step <= count - 1))
+    for piece, source, valid in received:
+        out = lax.dynamic_update_slice_in_dim(
+            out, piece, jnp.where(valid, source, place) * width, concat_axis
+        )
+    return lax.dynamic_update_slice_in_dim(out, own, place * width, concat_axis)
 
 
 def per_device(
@@ -241,9 +272,15 @@
     seconds = (query_square, keyval_square, output_square, gateup_square, down_square, gains_square)
     rounded = tuple((master.astype(jnp.bfloat16) for master in masters))
     gathered = (
-        lax.all_gather(rounded[0], "dp", axis=0, tiled=True),
-        lax.all_gather(rounded[1], "dp", axis=0, tiled=True),
-        lax.all_gather(rounded[2], "dp", axis=1, tiled=True),
+        lax.all_gather(
+            lax.all_gather(rounded[0], "tensor", axis=1, tiled=True), "dp", axis=0, tiled=True
+        ),
+        lax.all_gather(
+            lax.all_gather(rounded[1], "tensor", axis=1, tiled=True), "dp", axis=0, tiled=True
+        ),
+        lax.all_gather(
+            lax.all_gather(rounded[2], "tensor", axis=0, tiled=True), "dp", axis=1, tiled=True
+        ),
         lax.all_gather(rounded[3], "dp", axis=0, tiled=True),
         lax.all_gather(rounded[4], "dp", axis=1, tiled=True),
         lax.all_gather(rounded[5], "dp", axis=1, tiled=True),
@@ -253,36 +290,45 @@
     tensor_count = lax.axis_size("tensor")
     group_rows = tokens.shape[2] * tensor_count
     block_rows = group_rows // 2
-    keyval_heads = full_keyval.shape[1]
-    query_heads = full_query.shape[1] // HD
+    place = lax.axis_index("tensor")
+    rows = tokens.shape[2]
+    all_query_heads = full_query.shape[1] // HD
+    keyval_heads = full_keyval.shape[1] // tensor_count
+    query_heads = all_query_heads // tensor_count
     head_repeat = query_heads // keyval_heads
 
     def micro_step(token_rows, cot_rows, lengths):
         visible, position = layout(lengths, group_rows)
         cos_table, sin_table = rope_tables(position)
+        cos_own, sin_own = rope_tables(lax.dynamic_slice_in_dim(position, place * rows, rows))
         start_rows = token_rows.astype(jnp.float32)
         scale_one = lax.rsqrt(jnp.mean(start_rows * start_rows, axis=1, keepdims=True) + norm_eps)
         hat_one = start_rows * scale_one
         normed_one = (hat_one * gain_values[0][None, :]).astype(jnp.bfloat16)
-        rows_one = line_gather(normed_one, tensor_count)
-        query_raw = jnp.dot(rows_one, full_query, preferred_element_type=jnp.float32).reshape(
-            group_rows, query_heads, HD
+        query_raw = jnp.dot(normed_one, full_query, preferred_element_type=jnp.float32).reshape(
+            rows, all_query_heads, HD
         )
         keyval_raw = jnp.einsum(
-            "rd,dhk->rhk", rows_one, full_keyval, preferred_element_type=jnp.float32
-        )
-        queries = (
-            rotate(query_raw, cos_table, sin_table)
-            .astype(jnp.bfloat16)
-            .reshape(group_rows, keyval_heads, head_repeat, HD)
-        )
-        key_rows = rotate(keyval_raw[:, :, :HD], cos_table, sin_table).astype(jnp.bfloat16)
-        values = keyval_raw[:, :, HD:].astype(jnp.bfloat16)
+            "rd,dhk->rhk", normed_one, full_keyval, preferred_element_type=jnp.float32
+        )
+        queries_own = rotate(query_raw, cos_own, sin_own).astype(jnp.bfloat16)
+        keyval_own = jnp.concatenate(
+            [rotate(keyval_raw[:, :, :HD], cos_own, sin_own), keyval_raw[:, :, HD:]], axis=2
+        ).astype(jnp.bfloat16)
+        queries = line_all_to_all(queries_own, tensor_count, 1, 0).reshape(
+            group_rows, keyval_heads, head_repeat, HD
+        )
+        keyval_rows = line_all_to_all(keyval_own, tensor_count, 1, 0)
+        key_rows = keyval_rows[:, :, :HD]
+        values = keyval_rows[:, :, HD:]
         mixed_full, log_totals = attend(queries, key_rows, values, visible, block_rows)
-        mixed = mixed_full.astype(jnp.bfloat16).reshape(group_rows, query_heads * HD)
-        attn_branch = line_scatter(
-            jnp.dot(mixed, full_output, preferred_element_type=jnp.float32), tensor_count
-        )
+        mixed = line_all_to_all(
+            mixed_full.astype(jnp.bfloat16).reshape(group_rows, query_heads, HD),
+            tensor_count,
+            0,
+            1,
+        ).reshape(rows, all_query_heads * HD)
+        attn_branch = jnp.dot(mixed, full_output, preferred_element_type=jnp.float32)
         middle = start_rows + branch_scale * attn_branch
         scale_two = lax.rsqrt(jnp.mean(middle * middle, axis=1, keepdims=True) + norm_eps)
         hat_two = middle * scale_two
@@ -320,34 +366,39 @@
         middle_back, gain_two = norm_back(normed_two_grad, hat_two, scale_two, gain_values[1])
         middle_grad = upstream + middle_back
         attn_grad = (branch_scale * middle_grad).astype(jnp.bfloat16)
-        attn_grad_all = line_gather(attn_grad, tensor_count)
-        grad_output = contract_rows(mixed, attn_grad_all)
-        mixed_grad = (
-            contract_cols(attn_grad_all, full_output)
+        grad_output = contract_rows(mixed, attn_grad)
+        mixed_grad = line_all_to_all(
+            contract_cols(attn_grad, full_output)
             .astype(jnp.bfloat16)
-            .reshape(group_rows, keyval_heads, head_repeat, HD)
-        )
+            .reshape(rows, all_query_heads, HD),
+            tensor_count,
+            1,
+            0,
+        ).reshape(group_rows, keyval_heads, head_repeat, HD)
         query_grad, key_grad, value_grad = attend_back(
             queries, key_rows, values, visible, log_totals, mixed_grad, block_rows
         )
-        query_raw_grad = (
+        query_raw_grad = line_all_to_all(
             rotate_back(query_grad.reshape(group_rows, query_heads, HD), cos_table, sin_table)
-            .astype(jnp.bfloat16)
-            .reshape(group_rows, query_heads * HD)
-        )
-        keyval_raw_grad = jnp.concatenate(
-            [rotate_back(key_grad, cos_table, sin_table), value_grad], axis=2
-        ).astype(jnp.bfloat16)
-        grad_query = contract_rows(rows_one, query_raw_grad)
+            .astype(jnp.bfloat16),
+            tensor_count,
+            0,
+            1,
+        ).reshape(rows, all_query_heads * HD)
+        keyval_raw_grad = line_all_to_all(
+            jnp.concatenate(
+                [rotate_back(key_grad, cos_table, sin_table), value_grad], axis=2
+            ).astype(jnp.bfloat16),
+            tensor_count,
+            0,
+            1,
+        )
+        grad_query = contract_rows(normed_one, query_raw_grad)
         grad_keyval = jnp.einsum(
-            "rd,rhk->dhk", rows_one, keyval_raw_grad, preferred_element_type=jnp.float32
-        )
-        normed_one_grad = line_scatter(
-            contract_cols(query_raw_grad, full_query)
-            + jnp.einsum(
-                "rhk,dhk->rd", keyval_raw_grad, full_keyval, preferred_element_type=jnp.float32
-            ),
-            tensor_count,
+            "rd,rhk->dhk", normed_one, keyval_raw_grad, preferred_element_type=jnp.float32
+        )
+        normed_one_grad = contract_cols(query_raw_grad, full_query) + jnp.einsum(
+            "rhk,dhk->rd", keyval_raw_grad, full_keyval, preferred_element_type=jnp.float32
         )
         start_back, gain_one = norm_back(normed_one_grad, hat_one, scale_one, gain_values[0])
         input_rows = middle_grad + start_back
@@ -377,15 +428,33 @@
     gain_total = lax.psum(totals[5], "tensor")
     summed = (
         lax.psum_scatter(
-            totals[0].astype(jnp.bfloat16), "dp", scatter_dimension=0, tiled=True
+            lax.psum_scatter(
+                totals[0].astype(jnp.bfloat16), "dp", scatter_dimension=0, tiled=True
+            ),
+            "tensor",
+            scatter_dimension=1,
+            tiled=True,
         ).astype(jnp.float32),
         lax.psum_scatter(
-            totals[1].reshape(width, -1).astype(jnp.bfloat16), "dp", scatter_dimension=0, tiled=True
+            lax.psum_scatter(
+                totals[1].reshape(width, -1).astype(jnp.bfloat16),
+                "dp",
+                scatter_dimension=0,
+                tiled=True,
+            ),
+            "tensor",
+            scatter_dimension=1,
+            tiled=True,
         )
         .astype(jnp.float32)
-        .reshape(-1, *totals[1].shape[1:]),
+        .reshape(-1, keyval_heads, totals[1].shape[2]),
         lax.psum_scatter(
-            totals[2].astype(jnp.bfloat16), "dp", scatter_dimension=1, tiled=True
+            lax.psum_scatter(
+                totals[2].astype(jnp.bfloat16), "dp", scatter_dimension=1, tiled=True
+            ),
+            "tensor",
+            scatter_dimension=0,
+            tiled=True,
         ).astype(jnp.float32),
         lax.psum_scatter(
             totals[3].reshape(width, -1).astype(jnp.bfloat16), "dp", scatter_dimension=0, tiled=True

time: 2030 us -> 2330 us (1.15)
  local copies, waits for them, and re-layouts: 155 us -> 376 us
  starting transfers between devices: 281 us -> 442 us
  waiting for transfers between devices: 682 us -> 580 us
  matrix products: 523 us -> 570 us
    ppermute x0 -> x72, starting transfers between devices: none -> 319 us  [the longest x36 271 us: line_all_to_all(): lax.ppermute(block(place + step), 'tensor', [(i, i + step) for i in range...]
    dynamic_update_slice x0 -> x80, local copies, waits for them, and re-layouts: none -> 199 us  [the longest x72 174 us: line_all_to_all(): lax.dynamic_update_slice_in_dim(out, piece, jnp.where(valid, source, plac...]
    ppermute x24 -> x12, waiting for transfers between devices: 289 us -> 112 us  [line_gather(): lax.ppermute(from_right, 'tensor', [(i, i - 1) for i in range(1, count -...]
    reduce_scatter x1, waiting for transfers between devices: 0.02 us -> 115 us  [per_device(): lax.psum_scatter(totals[3].reshape(width, -1).astype(jnp.bfloat16), 'dp',...]
    ppermute x24 -> x12, waiting for transfers between devices: 209 us -> 99.5 us  [line_scatter(): lax.ppermute(send.astype(jnp.bfloat16), 'tensor', [(i, i + 1) for i in ra...]
    ppermute x24 -> x12, starting transfers between devices: 130 us -> 58.7 us  [line_scatter(): lax.ppermute(send.astype(jnp.bfloat16), 'tensor', [(i, i + 1) for i in ra...]
    ppermute x24 -> x12, waiting for transfers between devices: 101 us -> 31.4 us  [line_gather(): lax.ppermute(from_left, 'tensor', [(i, i + 1) for i in range(step - 1, co...]
    reduce_scatter x0 -> x3, waiting for transfers between devices: none -> 67.4 us  [the longest x1 25.3 us: per_device(): lax.psum_scatter(lax.psum_scatter(totals[0].astype(jnp.bfloat16), 'dp', s...]
  transfers between devices with their start and end apart: 107 -> 136, of which waited for: 49 -> 34; matrix products, arithmetic and copies ran while one was open for 35% -> 40% of each run, Pallas kernels for 0% -> 0%
where the time goes in v2:
time: 2330 us; the launch traced here: 2320 us
  waiting for transfers between devices  580 us (25%)
  matrix products  570 us (24%)
  starting transfers between devices  442 us (19%)
  local copies, waits for them, and re-layouts  376 us (16%)
  other arithmetic  237 us (10%)
  blocking collectives  88.5 us (4%)
    ppermute x36, starting transfers between devices, line_all_to_all(): lax.ppermute(block(place + step), 'tensor', [(i, i + step) for i in range...  271 us
    dynamic_update_slice x72, local copies, waits for them, and re-layouts, line_all_to_all(): lax.dynamic_update_slice_in_dim(out, piece, jnp.where(valid, source, plac...  174 us
    reduce_scatter x1, waiting for transfers between devices, per_device(): lax.psum_scatter(totals[3].reshape(width, -1).astype(jnp.bfloat16), 'dp',...  115 us
    ppermute x12, waiting for transfers between devices, line_gather(): lax.ppermute(from_right, 'tensor', [(i, i - 1) for i in range(1, count -...  112 us
    ppermute x12, waiting for transfers between devices, line_scatter(): lax.ppermute(send.astype(jnp.bfloat16), 'tensor', [(i, i + 1) for i in ra...  99.5 us
    dot_general x6, matrix products, contract_rows(): lax.dot_general(left, right, (((0,), (0,)), ((), ())), preferred_element_...  82.1 us
    dot_general x6, matrix products, contract_cols(): lax.dot_general(left, right, (((1,), (1,)), ((), ())), preferred_element_...  72.2 us
    dot_general x2, matrix products, micro_step(): jnp.einsum('rd,rcf->dcf', rows_two, gateup_grad, preferred_element_type=j...  59.9 us
  transfers between devices with their start and end apart: 136, of which 34 were waited for; matrix products, arithmetic and copies ran while one was open for 40% of the time, Pallas kernels for 0%

profile of v2, /device:TPU:0, one launch (start us, length us, event | category | flops | bytes accessed | tf_op | source)
XLA Modules:
  0.0 2315.3 jit_solution(1959673655299337032)
XLA Ops:
  13.6 24.5 %all_gather.28 = bf16[256,8,128]{2,0,1:T(8,128)(2,1)} all-gather(bf16[256,2,128]{2,0,1:T(8,128)(2,1)S(1)} %copy.382), channel_id=1, replica_groups=mesh['dp'=8,'tensor'=4] {'tensor'}, dimensions={1}, use_global_device_ids=true | all-gather | bytes 655360 | tf_op jit(solution)/shard_map/all_gather | solution.py:279
  45.8 30.6 %all-gather.14.cloned.1.call-done = bf16[2048,256]{1,0:T(8,128)(2,1)} async-done(((bf16[512,256]{1,0:T(8,128)(2,1)}), bf16[2048,256]{1,0:T(8,128)(2,1)}) %all-gather.14.cloned.1.call-update) | async-done | bytes 1048592 | tf_op jit(solution)/shard_map/all_gather | solution.py:282
  103.7 9.2 all_gather.27
  181.6 20.0 collective-permute-done.93
  206.6 19.4 collective-permute-done.65
  236.9 29.6 %collective-permute-start.2 = (bf16[304,2,128]{2,0,1:T(8,128)(2,1)}, bf16[304,2,128]{2,0,1:T(8,128)(2,1)}, u32[]{:S(2)}, u32[]{:S(2)}) collective-permute-start(bf16[304,2,128]{2,0,1:T(8,128)(2,1)} %get-tuple-element.423), channel_id=1, source_target_pairs={{0,2},{1,3},{4,6},{5,7},{8,10},{9,11},{12,14},{13,15},{16,18},{17,... | collective-permute-start | bytes 466952 | tf_op jit(solution)/shard_map/ppermute | solution.py:232
  279.3 12.4 copy.284
  316.1 9.1 collective-permute-start.10
  423.8 12.6 fusion.132
  476.3 12.2 collective-permute-done.15
  523.0 11.9 collective-permute-done.34
  539.2 10.4 collective-permute-start.40
  613.4 21.4 collective-permute-done.19
  642.6 11.1 collective-permute-done.21
  675.0 27.3 %fusion.59 = f32[1216,2,2048]{2,0,1:T(8,128)} fusion(bf16[2048,2,2048]{2,0,1:T(8,128)(2,1)} %all-gather.18.cloned.1.call-done, bf16[1216,2048]{1,0:T(8,128)(2,1)} %constant_dynamic-update-slice_fusion.51), kind=kOutput, calls=%fused_computation.104 | convolution fusion | flops 20401094656 | bytes 41680896 | tf_op jit(solution)/shard_map/rd,dcf->rcf/dot_general | solution.py:337
  702.3 25.7 %fusion.61 = (bf16[1216,1,2048]{2,0,1:T(8,128)(2,1)}, bf16[1216,1,2048]{2,0,1:T(8,128)(2,1)}, bf16[1216,2048]{1,0:T(8,128)(2,1)}) fusion(f32[1216,2,2048]{2,0,1:T(8,128)} %fusion.59, bf16[1216,2048]{1,0:T(8,128)(2,1)} %get-tuple-element.333, bf16[2048,2048]{1,0:T(8,128)(2,1)} %all-gather.20.cloned.1.call-done), kind=kOutput, calls=%fused_computation.106 | convolution fusion | flops 10237902848 | bytes 48234496 | tf_op jit(solution)/shard_map/dot_general | solution.py:162
  728.0 24.7 %convolution_bitcast_fusion.1 = f32[1216,2048]{1,0:T(8,128)S(1)} fusion(bf16[2048,2,2048]{2,0,1:T(8,128)(2,1)} %all-gather.18.cloned.1.call-done, bf16[1216,1,2048]{2,0,1:T(8,128)(2,1)} %get-tuple-element.296, bf16[1216,1,2048]{2,0,1:T(8,128)(2,1)} %get-tuple-element.295), kind=kOutput, calls=%fused_computation.81 | convolution fusion | flops 20406075392 | bytes 36700160 | tf_op jit(solution)/shard_map/rcf,dcf->rd/dot_general | solution.py:361
  755.6 13.6 fusion.131
  780.9 17.3 collective-permute-done.67
  810.8 11.0 collective-permute-start.42
  840.8 12.7 collective-permute-done.45
  869.3 10.5 collective-permute-done.71
  893.1 24.3 %collective-permute-done.48 = bf16[304,2048]{1,0:T(8,128)(2,1)S(1)} collective-permute-done((bf16[304,2048]{1,0:T(8,128)(2,1)S(1)}, bf16[304,2048]{1,0:T(8,128)(2,1)S(1)}, u32[]{:S(2)}, u32[]{:S(2)}) %collective-permute-start.48) | collective-permute-done | bytes 1245216 | tf_op jit(solution)/shard_map/ppermute | solution.py:175
  923.7 12.5 fusion.263
  947.9 15.9 collective-permute-done.53
  964.0 27.8 %fusion.56 = f32[1216,2,2048]{2,0,1:T(8,128)} fusion(bf16[2048,2,2048]{2,0,1:T(8,128)(2,1)} %all-gather.18.cloned.1.call-done, bf16[1216,2048]{1,0:T(8,128)(2,1)S(1)} %constant_dynamic-update-slice_fusion.38), kind=kOutput, calls=%fused_computation.101 | convolution fusion | flops 20401094656 | bytes 41680896 | tf_op jit(solution)/shard_map/rd,dcf->rcf/dot_general | solution.py:337
  991.8 25.6 %fusion.62 = (bf16[1216,1,2048]{2,0,1:T(8,128)(2,1)}, bf16[1216,1,2048]{2,0,1:T(8,128)(2,1)}, bf16[1216,2048]{1,0:T(8,128)(2,1)}) fusion(f32[1216,2,2048]{2,0,1:T(8,128)} %fusion.56, bf16[1216,2048]{1,0:T(8,128)(2,1)} %get-tuple-element.334, bf16[2048,2048]{1,0:T(8,128)(2,1)} %all-gather.20.cloned.1.call-done), kind=kOutput, calls=%fused_computation.107 | convolution fusion | flops 10237902848 | bytes 48234496 | tf_op jit(solution)/shard_map/dot_general | solution.py:162
  1017.4 25.1 %convolution_bitcast_fusion = f32[1216,2048]{1,0:T(8,128)S(1)} fusion(bf16[2048,2,2048]{2,0,1:T(8,128)(2,1)} %all-gather.18.cloned.1.call-done, bf16[1216,1,2048]{2,0,1:T(8,128)(2,1)} %get-tuple-element.298, bf16[1216,1,2048]{2,0,1:T(8,128)(2,1)} %get-tuple-element.297), kind=kOutput, calls=%fused_computation.80 | convolution fusion | flops 20406075392 | bytes 36700160 | tf_op jit(solution)/shard_map/rcf,dcf->rd/dot_general | solution.py:361
  1047.3 15.8 fusion.264
  1087.2 13.6 collective-permute-done.54
  1122.1 19.8 collective-permute-done.25
  1146.8 21.7 collective-permute-done.55
  1192.1 19.5 collective-permute-start.56
  1226.0 15.7 collective-permute-done.59
  1261.2 18.8 collective-permute-start.102
  1282.6 18.8 collective-permute-start.104
  1343.2 9.9 collective-permute-start.74
  1366.5 9.5 collective-permute-start.76
  1388.2 10.1 fusion.16
  1455.2 9.7 fusion.19
  1464.9 17.9 fusion
  1482.8 11.9 fusion.118
  1494.6 9.6 fusion.18
  1507.1 16.9 fusion.2
  1555.5 16.9 fusion.3
  1572.3 11.5 fusion.121
  1583.9 9.6 fusion.21
  1596.2 17.0 fusion.5
  1653.3 8.9 collective-permute-start.88
  1706.3 14.1 fusion.156
  1720.4 10.9 add_convert_fusion.2
  1813.3 10.6 add_convert_fusion.3
  1824.0 18.4 fusion.265
  1859.4 15.5 psum.14
  1876.1 19.5 add_convert_fusion.1
  1897.0 29.2 %fusion.42 = f32[2048,2,2048]{0,2,1:T(8,128)} fusion(bf16[1216,1,2048]{2,0,1:T(8,128)(2,1)} %get-tuple-element.298, bf16[1216,1,2048]{2,0,1:T(8,128)(2,1)} %get-tuple-element.297, bf16[1216,2048]{1,0:T(8,128)(2,1)} %copy-done.62), kind=kOutput, calls=%fused_computation.85 | convolution fusion | flops 20421017600 | bytes 48496640 | tf_op jit(solution)/shard_map/rd,rcf->dcf/dot_general | solution.py:357
  1926.3 30.7 %add_convert_fusion = bf16[2048,2,2048]{0,2,1:T(8,128)(2,1)} fusion(f32[2048,2,2048]{0,2,1:T(8,128)} %fusion.42, bf16[1216,1,2048]{2,0,1:T(8,128)(2,1)} %get-tuple-element.296, bf16[1216,1,2048]{2,0,1:T(8,128)(2,1)} %get-tuple-element.295, bf16[1216,2048]{1,0:T(8,128)(2,1)} %constant_dynamic-update-slice_fusion.51), kind=kOutput, calls=%fused_computation | convolution fusion | flops 20437794816 | bytes 65273856 | tf_op jit(solution)/shard_map/rd,rcf->dcf/dot_general | solution.py:357
  1980.9 40.5 %reduce-scatter.26.cloned.1.call-done = bf16[2048,256]{1,0:T(8,128)(2,1)} async-done(((bf16[2048,2048]{1,0:T(8,128)(2,1)}), bf16[2048,256]{1,0:T(8,128)(2,1)}) %reduce-scatter.26.cloned.1.call-update) | async-done | bytes 1048592 | tf_op jit(solution)/shard_map/reduce_scatter | solution.py:464
  2028.0 17.6 reduce-scatter.18.cloned.1.call-done
  2048.7 24.6 %reduce-scatter.22.cloned.1.call-done = bf16[512,256]{1,0:T(8,128)(2,1)} async-done(((bf16[2048,256]{1,0:T(8,128)(2,1)}), bf16[512,256]{1,0:T(8,128)(2,1)}) %reduce-scatter.22.cloned.1.call-update) | async-done | bytes 262160 | tf_op jit(solution)/shard_map/reduce_scatter | solution.py:451
  2076.0 25.3 %reduce-scatter.14.cloned.1.call-done = bf16[256,512]{1,0:T(8,128)(2,1)} async-done(((bf16[256,2048]{1,0:T(8,128)(2,1)}), bf16[256,512]{1,0:T(8,128)(2,1)}) %reduce-scatter.14.cloned.1.call-update) | async-done | bytes 262160 | tf_op jit(solution)/shard_map/reduce_scatter | solution.py:430
  2104.1 115.0 %reduce-scatter.24.cloned.1.call-done = bf16[256,4096]{0,1:T(8,128)(2,1)} async-done(((bf16[2048,4096]{0,1:T(8,128)(2,1)}), bf16[256,4096]{0,1:T(8,128)(2,1)}) %reduce-scatter.24.cloned.1.call-update) | async-done | bytes 2097168 | tf_op jit(solution)/shard_map/reduce_scatter | solution.py:459
  2225.5 18.3 multiply_reduce_fusion
  2251.6 39.2 %psum.15 = f32[2,7]{1,0:T(2,128)S(1)} all-reduce(f32[2,7]{1,0:T(2,128)S(1)} %pad_maximum_fusion.12), channel_id=1, replica_groups=mesh['dp'=8,'tensor'=4] {'dp','tensor'}, use_global_device_ids=true, to_apply=%region_52.53 | all-reduce | flops 14 | bytes 112 | tf_op jit(solution)/shard_map/psum | solution.py:494
  (957 shorter events, 1052.3 us)
Async XLA Ops:
  9.9 66.6 %all-gather.14.cloned.1.call-start = ((), (), s32[]{:S(2)}) async-start(), calls=%async_computation.12 | async-start | bytes 1310720 | tf_op jit(solution)/shard_map/all_gather | solution.py:282
  12.5 214.6 %all-gather.8.cloned.1.call-start = ((), (), s32[]{:S(2)}) async-start(), calls=%async_computation.9 | async-start | bytes 4718592 | tf_op jit(solution)/shard_map/all_gather | solution.py:278
  38.1 241.2 %all-gather.12.cloned.1.call-start = ((), (), s32[]{:S(2)}) async-start(), calls=%async_computation.11 | async-start | bytes 9437184 | tf_op jit(solution)/shard_map/all_gather | solution.py:275
  45.8 449.7 %all-gather.16.cloned.1.call-start = ((), (), s32[]{:S(2)}) async-start(), calls=%async_computation.13 | async-start | bytes 9437184 | tf_op jit(solution)/shard_map/all_gather | solution.py:281
  76.5 598.5 %all-gather.18.cloned.1.call-start = ((), (), s32[]{:S(2)}) async-start(), calls=%async_computation.14 | async-start | bytes 18874368 | tf_op jit(solution)/shard_map/all_gather | solution.py:284
  82.4 619.9 %all-gather.20.cloned.1.call-start = ((), (), s32[]{:S(2)}) async-start(), calls=%async_computation.15 | async-start | bytes 9437184 | tf_op jit(solution)/shard_map/all_gather | solution.py:285
  89.1 43.3 %collective-permute-start.61 = (bf16[304,2048]{1,0:T(8,128)(2,1)}, bf16[304,2048]{1,0:T(8,128)(2,1)}, u32[]{:S(2)}, u32[]{:S(2)}) collective-permute-start(bf16[304,2048]{1,0:T(8,128)(2,1)} %get-tuple-element.335), channel_id=1, source_target_pairs={{1,0},{2,1},{3,2},{5,4},{6,5},{7,6},{9,8},{10,9},{11,10},{13,12},{... | collective-permute-start | bytes 3735560 | tf_op jit(solution)/shard_map/ppermute | solution.py:178
  90.4 50.4 %collective-permute-start.90 = (bf16[304,2048]{1,0:T(8,128)(2,1)}, bf16[304,2048]{1,0:T(8,128)(2,1)}, u32[]{:S(2)}, u32[]{:S(2)}) collective-permute-start(bf16[304,2048]{1,0:T(8,128)(2,1)} %get-tuple-element.336), channel_id=1, source_target_pairs={{0,1},{1,2},{2,3},{4,5},{5,6},{6,7},{8,9},{9,10},{10,11},{12,13},{... | collective-permute-start | bytes 3735560 | tf_op jit(solution)/shard_map/ppermute | solution.py:175
  96.0 52.2 %collective-permute-start.91 = (bf16[304,2048]{1,0:T(8,128)(2,1)}, bf16[304,2048]{1,0:T(8,128)(2,1)}, u32[]{:S(2)}, u32[]{:S(2)}) collective-permute-start(bf16[304,2048]{1,0:T(8,128)(2,1)} %get-tuple-element.336), channel_id=1, source_target_pairs={{1,0},{2,1},{3,2},{5,4},{6,5},{7,6},{9,8},{10,9},{11,10},{13,12},{... | collective-permute-start | bytes 3735560 | tf_op jit(solution)/shard_map/ppermute | solution.py:178
  99.5 1796.2 %reduce-scatter.16.cloned.1.call-start = ((), (), s32[]{:S(2)}) async-start(), calls=%async_computation.18 | async-start | bytes 4718592 | tf_op jit(solution)/shard_map/reduce_scatter | solution.py:439
  117.3 45.8 %collective-permute-start.62 = (bf16[304,2048]{1,0:T(8,128)(2,1)}, bf16[304,2048]{1,0:T(8,128)(2,1)}, u32[]{:S(2)}, u32[]{:S(2)}) collective-permute-start(bf16[304,2048]{1,0:T(8,128)(2,1)} %collective-permute-done.60), channel_id=1, source_target_pairs={{1,2},{2,3},{5,6},{6,7},{9,10},{10,11},{13,14},{14,15},{17,18},{18... | collective-permute-start | bytes 3735560 | tf_op jit(solution)/shard_map/ppermute | solution.py:175
  132.4 42.4 %collective-permute-start.63 = (bf16[304,2048]{1,0:T(8,128)(2,1)}, bf16[304,2048]{1,0:T(8,128)(2,1)S(1)}, u32[]{:S(2)}, u32[]{:S(2)}) collective-permute-start(bf16[304,2048]{1,0:T(8,128)(2,1)} %collective-permute-done.61), channel_id=1, source_target_pairs={{1,0},{2,1},{5,4},{6,5},{9,8},{10,9},{13,12},{14,13},{17,16},{18,1... | collective-permute-start | bytes 3735560 | tf_op jit(solution)/shard_map/ppermute | solution.py:178
  148.2 53.4 %collective-permute-start.93 = (bf16[304,2048]{1,0:T(8,128)(2,1)}, bf16[304,2048]{1,0:T(8,128)(2,1)}, u32[]{:S(2)}, u32[]{:S(2)}) collective-permute-start(bf16[304,2048]{1,0:T(8,128)(2,1)} %collective-permute-done.91), channel_id=1, source_target_pairs={{1,0},{2,1},{5,4},{6,5},{9,8},{10,9},{13,12},{14,13},{17,16},{18,1... | collective-permute-start | bytes 3735560 | tf_op jit(solution)/shard_map/ppermute | solution.py:178
  174.8 51.2 %collective-permute-start.65 = (bf16[304,2048]{1,0:T(8,128)(2,1)S(1)}, bf16[304,2048]{1,0:T(8,128)(2,1)S(1)}, u32[]{:S(2)}, u32[]{:S(2)}) collective-permute-start(bf16[304,2048]{1,0:T(8,128)(2,1)S(1)} %collective-permute-done.63), channel_id=1, source_target_pairs={{1,0},{5,4},{9,8},{13,12},{17,16},{21,20},{25,24},{29,28}} | collective-permute-start | bytes 3735560 | tf_op jit(solution)/shard_map/ppermute | solution.py:178
  233.2 67.4 %collective-permute-start = (bf16[304,2,128]{2,0,1:T(8,128)(2,1)}, bf16[304,2,128]{2,0,1:T(8,128)(2,1)}, u32[]{:S(2)}, u32[]{:S(2)}) collective-permute-start(bf16[304,2,128]{2,0,1:T(8,128)(2,1)} %get-tuple-element.425), channel_id=1, source_target_pairs={{0,1},{1,2},{2,3},{4,5},{5,6},{6,7},{8,9},{9,10},{10,11},{12,13},{... | collective-permute-start | bytes 466952 | tf_op jit(solution)/shard_map/ppermute | solution.py:232
  235.7 66.3 %collective-permute-start.1 = (bf16[304,2,128]{2,0,1:T(8,128)(2,1)}, bf16[304,2,128]{2,0,1:T(8,128)(2,1)}, u32[]{:S(2)}, u32[]{:S(2)}) collective-permute-start(bf16[304,2,128]{2,0,1:T(8,128)(2,1)} %get-tuple-element.424), channel_id=1, source_target_pairs={{1,0},{2,1},{3,2},{5,4},{6,5},{7,6},{9,8},{10,9},{11,10},{13,12},{... | collective-permute-start | bytes 466952 | tf_op jit(solution)/shard_map/ppermute | solution.py:235
  236.9 67.6 %collective-permute-start.2 = (bf16[304,2,128]{2,0,1:T(8,128)(2,1)}, bf16[304,2,128]{2,0,1:T(8,128)(2,1)}, u32[]{:S(2)}, u32[]{:S(2)}) collective-permute-start(bf16[304,2,128]{2,0,1:T(8,128)(2,1)} %get-tuple-element.423), channel_id=1, source_target_pairs={{0,2},{1,3},{4,6},{5,7},{8,10},{9,11},{12,14},{13,15},{16,18},{17,... | collective-permute-start | bytes 466952 | tf_op jit(solution)/shard_map/ppermute | solution.py:232
  267.8 47.0 %collective-permute-start.4 = (bf16[304,2,128]{2,0,1:T(8,128)(2,1)}, bf16[304,2,128]{2,0,1:T(8,128)(2,1)}, u32[]{:S(2)}, u32[]{:S(2)}) collective-permute-start(bf16[304,2,128]{2,0,1:T(8,128)(2,1)} %get-tuple-element.421), channel_id=1, source_target_pairs={{0,3},{4,7},{8,11},{12,15},{16,19},{20,23},{24,27},{28,31}} | collective-permute-start | bytes 466952 | tf_op jit(solution)/shard_map/ppermute | solution.py:232
  304.6 46.0 %collective-permute-start.7 = (bf16[304,8,64]{0,2,1:T(8,128)(2,1)}, bf16[304,8,64]{0,2,1:T(8,128)(2,1)}, u32[]{:S(2)}, u32[]{:S(2)}) collective-permute-start(bf16[304,8,64]{0,2,1:T(8,128)(2,1)} %get-tuple-element.355), channel_id=1, source_target_pairs={{1,0},{2,1},{3,2},{5,4},{6,5},{7,6},{9,8},{10,9},{11,10},{13,12},{... | collective-permute-start | bytes 933896 | tf_op jit(solution)/shard_map/ppermute | solution.py:235
  305.9 51.4 %collective-permute-start.8 = (bf16[304,8,64]{0,2,1:T(8,128)(2,1)}, bf16[304,8,64]{0,2,1:T(8,128)(2,1)}, u32[]{:S(2)}, u32[]{:S(2)}) collective-permute-start(bf16[304,8,64]{0,2,1:T(8,128)(2,1)} %get-tuple-element.356), channel_id=1, source_target_pairs={{0,2},{1,3},{4,6},{5,7},{8,10},{9,11},{12,14},{13,15},{16,18},{17,... | collective-permute-start | bytes 933896 | tf_op jit(solution)/shard_map/ppermute | solution.py:232
  314.8 53.6 %collective-permute-start.9 = (bf16[304,8,64]{0,2,1:T(8,128)(2,1)}, bf16[304,8,64]{0,2,1:T(8,128)(2,1)}, u32[]{:S(2)}, u32[]{:S(2)}) collective-permute-start(bf16[304,8,64]{0,2,1:T(8,128)(2,1)} %get-tuple-element.357), channel_id=1, source_target_pairs={{2,0},{3,1},{6,4},{7,5},{10,8},{11,9},{14,12},{15,13},{18,16},{19,... | collective-permute-start | bytes 933896 | tf_op jit(solution)/shard_map/ppermute | solution.py:235
  316.1 57.8 %collective-permute-start.10 = (bf16[304,8,64]{0,2,1:T(8,128)(2,1)}, bf16[304,8,64]{0,2,1:T(8,128)(2,1)}, u32[]{:S(2)}, u32[]{:S(2)}) collective-permute-start(bf16[304,8,64]{0,2,1:T(8,128)(2,1)} %get-tuple-element.358), channel_id=1, source_target_pairs={{0,3},{4,7},{8,11},{12,15},{16,19},{20,23},{24,27},{28,31}} | collective-permute-start | bytes 933896 | tf_op jit(solution)/shard_map/ppermute | solution.py:232
  325.2 53.5 %collective-permute-start.11 = (bf16[304,8,64]{0,2,1:T(8,128)(2,1)}, bf16[304,8,64]{0,2,1:T(8,128)(2,1)}, u32[]{:S(2)}, u32[]{:S(2)}) collective-permute-start(bf16[304,8,64]{0,2,1:T(8,128)(2,1)} %fusion.202), channel_id=1, source_target_pairs={{3,0},{7,4},{11,8},{15,12},{19,16},{23,20},{27,24},{31,28}} | collective-permute-start | bytes 933896 | tf_op jit(solution)/shard_map/ppermute | solution.py:235
  350.5 157.9 %collective-permute-start.95 = (bf16[304,2048]{1,0:T(8,128)(2,1)}, bf16[304,2048]{1,0:T(8,128)(2,1)}, u32[]{:S(2)}, u32[]{:S(2)}) collective-permute-start(bf16[304,2048]{1,0:T(8,128)(2,1)} %collective-permute-done.93), channel_id=1, source_target_pairs={{1,0},{5,4},{9,8},{13,12},{17,16},{21,20},{25,24},{29,28}} | collective-permute-start | bytes 3735560 | tf_op jit(solution)/shard_map/ppermute | solution.py:178
  357.3 153.8 %collective-permute-start.30 = (bf16[304,2,128]{2,1,0:T(2,128)(2,1)}, bf16[304,2,128]{2,1,0:T(2,128)(2,1)}, u32[]{:S(2)}, u32[]{:S(2)}) collective-permute-start(bf16[304,2,128]{2,1,0:T(2,128)(2,1)} %get-tuple-element.432), channel_id=1, source_target_pairs={{0,1},{1,2},{2,3},{4,5},{5,6},{6,7},{8,9},{9,10},{10,11},{12,13},{... | collective-permute-start | bytes 466952 | tf_op jit(solution)/shard_map/ppermute | solution.py:232
  502.7 102.0 %collective-permute-start.18 = (bf16[304,2048]{1,0:T(8,128)(2,1)}, bf16[304,2048]{1,0:T(8,128)(2,1)}, u32[]{:S(2)}, u32[]{:S(2)}) collective-permute-start(bf16[304,2048]{1,0:T(8,128)(2,1)} %multiply_convert_fusion.9), channel_id=1, source_target_pairs={{0,1},{1,2},{2,3},{4,5},{5,6},{6,7},{8,9},{9,10},{10,11},{12,13},{... | collective-permute-start | bytes 3735560 | tf_op jit(solution)/shard_map/ppermute | solution.py:175
  536.3 44.1 %collective-permute-start.39 = (bf16[304,8,64]{0,2,1:T(8,128)(2,1)}, bf16[304,8,64]{0,2,1:T(8,128)(2,1)}, u32[]{:S(2)}, u32[]{:S(2)}) collective-permute-start(bf16[304,8,64]{0,2,1:T(8,128)(2,1)} %get-tuple-element.363), channel_id=1, source_target_pairs={{2,0},{3,1},{6,4},{7,5},{10,8},{11,9},{14,12},{15,13},{18,16},{19,... | collective-permute-start | bytes 933896 | tf_op jit(solution)/shard_map/ppermute | solution.py:235
  539.2 47.9 %collective-permute-start.40 = (bf16[304,8,64]{0,2,1:T(8,128)(2,1)}, bf16[304,8,64]{0,2,1:T(8,128)(2,1)}, u32[]{:S(2)}, u32[]{:S(2)}) collective-permute-start(bf16[304,8,64]{0,2,1:T(8,128)(2,1)} %get-tuple-element.364), channel_id=1, source_target_pairs={{0,3},{4,7},{8,11},{12,15},{16,19},{20,23},{24,27},{28,31}} | collective-permute-start | bytes 933896 | tf_op jit(solution)/shard_map/ppermute | solution.py:232
  549.6 42.8 %collective-permute-start.41 = (bf16[304,8,64]{0,2,1:T(8,128)(2,1)}, bf16[304,8,64]{0,2,1:T(8,128)(2,1)}, u32[]{:S(2)}, u32[]{:S(2)}) collective-permute-start(bf16[304,8,64]{0,2,1:T(8,128)(2,1)} %fusion.195), channel_id=1, source_target_pairs={{3,0},{7,4},{11,8},{15,12},{19,16},{23,20},{27,24},{31,28}} | collective-permute-start | bytes 933896 | tf_op jit(solution)/shard_map/ppermute | solution.py:235
  802.3 52.7 %collective-permute-start.70 = (bf16[304,2048]{1,0:T(8,128)(2,1)S(1)}, bf16[304,2048]{1,0:T(8,128)(2,1)S(1)}, u32[]{:S(2)}, u32[]{:S(2)}) collective-permute-start(bf16[304,2048]{1,0:T(8,128)(2,1)S(1)} %get-tuple-element.302), channel_id=1, source_target_pairs={{2,1},{3,2},{6,5},{7,6},{10,9},{11,10},{14,13},{15,14},{18,17},{19... | collective-permute-start | bytes 3735560 | tf_op jit(solution)/shard_map/ppermute | solution.py:207
  939.3 143.8 %collective-permute-start.24 = (bf16[304,2048]{1,0:T(8,128)(2,1)}, bf16[304,2048]{1,0:T(8,128)(2,1)}, u32[]{:S(2)}, u32[]{:S(2)}) collective-permute-start(bf16[304,2048]{1,0:T(8,128)(2,1)} %get-tuple-element.311), channel_id=1, source_target_pairs={{0,1},{4,5},{8,9},{12,13},{16,17},{20,21},{24,25},{28,29}} | collective-permute-start | bytes 3735560 | tf_op jit(solution)/shard_map/ppermute | solution.py:201
  1084.8 57.0 %collective-permute-start.25 = (bf16[304,2048]{1,0:T(8,128)(2,1)S(1)}, bf16[304,2048]{1,0:T(8,128)(2,1)}, u32[]{:S(2)}, u32[]{:S(2)}) collective-permute-start(bf16[304,2048]{1,0:T(8,128)(2,1)S(1)} %add_convert_fusion.22), channel_id=1, source_target_pairs={{0,1},{1,2},{4,5},{5,6},{8,9},{9,10},{12,13},{13,14},{16,17},{17,1... | collective-permute-start | bytes 3735560 | tf_op jit(solution)/shard_map/ppermute | solution.py:201
  1100.8 46.0 %collective-permute-start.57 = (bf16[304,2048]{1,0:T(8,128)(2,1)}, bf16[304,2048]{1,0:T(8,128)(2,1)}, u32[]{:S(2)}, u32[]{:S(2)}) collective-permute-start(bf16[304,2048]{1,0:T(8,128)(2,1)} %get-tuple-element.316), channel_id=1, source_target_pairs={{3,2},{7,6},{11,10},{15,14},{19,18},{23,22},{27,26},{31,30}} | collective-permute-start | bytes 3735560 | tf_op jit(solution)/shard_map/ppermute | solution.py:207
  1103.0 65.5 %collective-permute-start.55 = (bf16[304,2048]{1,0:T(8,128)(2,1)S(1)}, bf16[304,2048]{1,0:T(8,128)(2,1)}, u32[]{:S(2)}, u32[]{:S(2)}) collective-permute-start(bf16[304,2048]{1,0:T(8,128)(2,1)S(1)} %add_convert_fusion.17), channel_id=1, source_target_pairs={{0,1},{1,2},{4,5},{5,6},{8,9},{9,10},{12,13},{13,14},{16,17},{17,1... | collective-permute-start | bytes 3735560 | tf_op jit(solution)/shard_map/ppermute | solution.py:201
  1120.9 64.2 %collective-permute-start.100 = (bf16[304,2048]{1,0:T(8,128)(2,1)}, bf16[304,2048]{1,0:T(8,128)(2,1)S(1)}, u32[]{:S(2)}, u32[]{:S(2)}) collective-permute-start(bf16[304,2048]{1,0:T(8,128)(2,1)} %get-tuple-element.306), channel_id=1, source_target_pairs={{2,1},{3,2},{6,5},{7,6},{10,9},{11,10},{14,13},{15,14},{18,17},{19... | collective-permute-start | bytes 3735560 | tf_op jit(solution)/shard_map/ppermute | solution.py:207
  1145.9 42.7 %collective-permute-start.28 = (bf16[304,2048]{1,0:T(8,128)(2,1)}, bf16[304,2048]{1,0:T(8,128)(2,1)S(1)}, u32[]{:S(2)}, u32[]{:S(2)}) collective-permute-start(bf16[304,2048]{1,0:T(8,128)(2,1)} %get-tuple-element.310), channel_id=1, source_target_pairs={{2,1},{3,2},{6,5},{7,6},{10,9},{11,10},{14,13},{15,14},{18,17},{19... | collective-permute-start | bytes 3735560 | tf_op jit(solution)/shard_map/ppermute | solution.py:207
  1176.4 44.7 %collective-permute-start.26 = (bf16[304,2048]{1,0:T(8,128)(2,1)}, bf16[304,2048]{1,0:T(8,128)(2,1)S(1)}, u32[]{:S(2)}, u32[]{:S(2)}) collective-permute-start(bf16[304,2048]{1,0:T(8,128)(2,1)} %get-tuple-element.309), channel_id=1, source_target_pairs={{0,1},{1,2},{2,3},{4,5},{5,6},{6,7},{8,9},{9,10},{10,11},{12,13},{... | collective-permute-start | bytes 3735560 | tf_op jit(solution)/shard_map/ppermute | solution.py:201
  1261.2 48.6 %collective-permute-start.102 = (bf16[304,8,64]{0,2,1:T(8,128)(2,1)S(1)}, bf16[304,8,64]{0,2,1:T(8,128)(2,1)S(1)}, u32[]{:S(2)}, u32[]{:S(2)}) collective-permute-start(bf16[304,8,64]{0,2,1:T(8,128)(2,1)S(1)} %get-tuple-element.352), channel_id=1, source_target_pairs={{0,1},{1,2},{2,3},{4,5},{5,6},{6,7},{8,9},{9,10},{10,11},{12,13},{... | collective-permute-start | bytes 933896 | tf_op jit(solution)/shard_map/ppermute | solution.py:232
  1281.3 46.6 %collective-permute-start.103 = (bf16[304,8,64]{0,2,1:T(8,128)(2,1)}, bf16[304,8,64]{0,2,1:T(8,128)(2,1)}, u32[]{:S(2)}, u32[]{:S(2)}) collective-permute-start(bf16[304,8,64]{0,2,1:T(8,128)(2,1)} %get-tuple-element.351), channel_id=1, source_target_pairs={{1,0},{2,1},{3,2},{5,4},{6,5},{7,6},{9,8},{10,9},{11,10},{13,12},{... | collective-permute-start | bytes 933896 | tf_op jit(solution)/shard_map/ppermute | solution.py:235
  1282.6 53.8 %collective-permute-start.104 = (bf16[304,8,64]{0,2,1:T(8,128)(2,1)}, bf16[304,8,64]{0,2,1:T(8,128)(2,1)}, u32[]{:S(2)}, u32[]{:S(2)}) collective-permute-start(bf16[304,8,64]{0,2,1:T(8,128)(2,1)} %get-tuple-element.350), channel_id=1, source_target_pairs={{0,2},{1,3},{4,6},{5,7},{8,10},{9,11},{12,14},{13,15},{16,18},{17,... | collective-permute-start | bytes 933896 | tf_op jit(solution)/shard_map/ppermute | solution.py:232
  1301.5 41.7 %collective-permute-start.105 = (bf16[304,8,64]{0,2,1:T(8,128)(2,1)}, bf16[304,8,64]{0,2,1:T(8,128)(2,1)}, u32[]{:S(2)}, u32[]{:S(2)}) collective-permute-start(bf16[304,8,64]{0,2,1:T(8,128)(2,1)} %get-tuple-element.349), channel_id=1, source_target_pairs={{2,0},{3,1},{6,4},{7,5},{10,8},{11,9},{14,12},{15,13},{18,16},{19,... | collective-permute-start | bytes 933896 | tf_op jit(solution)/shard_map/ppermute | solution.py:235
  1302.8 56.9 %collective-permute-start.106 = (bf16[304,8,64]{0,2,1:T(8,128)(2,1)}, bf16[304,8,64]{0,2,1:T(8,128)(2,1)}, u32[]{:S(2)}, u32[]{:S(2)}) collective-permute-start(bf16[304,8,64]{0,2,1:T(8,128)(2,1)} %get-tuple-element.348), channel_id=1, source_target_pairs={{0,3},{4,7},{8,11},{12,15},{16,19},{20,23},{24,27},{28,31}} | collective-permute-start | bytes 933896 | tf_op jit(solution)/shard_map/ppermute | solution.py:232
  1310.6 55.8 %collective-permute-start.107 = (bf16[304,8,64]{0,2,1:T(8,128)(2,1)}, bf16[304,8,64]{0,2,1:T(8,128)(2,1)}, u32[]{:S(2)}, u32[]{:S(2)}) collective-permute-start(bf16[304,8,64]{0,2,1:T(8,128)(2,1)} %get-tuple-element.347), channel_id=1, source_target_pairs={{3,0},{7,4},{11,8},{15,12},{19,16},{23,20},{27,24},{31,28}} | collective-permute-start | bytes 933896 | tf_op jit(solution)/shard_map/ppermute | solution.py:235
  1327.9 70.4 %collective-permute-start.72 = (bf16[304,8,64]{0,2,1:T(8,128)(2,1)}, bf16[304,8,64]{0,2,1:T(8,128)(2,1)}, u32[]{:S(2)}, u32[]{:S(2)}) collective-permute-start(bf16[304,8,64]{0,2,1:T(8,128)(2,1)} %get-tuple-element.345), channel_id=1, source_target_pairs={{0,1},{1,2},{2,3},{4,5},{5,6},{6,7},{8,9},{9,10},{10,11},{12,13},{... | collective-permute-start | bytes 933896 | tf_op jit(solution)/shard_map/ppermute | solution.py:232
  1336.5 75.6 %collective-permute-start.73 = (bf16[304,8,64]{0,2,1:T(8,128)(2,1)}, bf16[304,8,64]{0,2,1:T(8,128)(2,1)}, u32[]{:S(2)}, u32[]{:S(2)}) collective-permute-start(bf16[304,8,64]{0,2,1:T(8,128)(2,1)} %get-tuple-element.344), channel_id=1, source_target_pairs={{1,0},{2,1},{3,2},{5,4},{6,5},{7,6},{9,8},{10,9},{11,10},{13,12},{... | collective-permute-start | bytes 933896 | tf_op jit(solution)/shard_map/ppermute | solution.py:235
  1343.2 75.5 %collective-permute-start.74 = (bf16[304,8,64]{0,2,1:T(8,128)(2,1)}, bf16[304,8,64]{0,2,1:T(8,128)(2,1)}, u32[]{:S(2)}, u32[]{:S(2)}) collective-permute-start(bf16[304,8,64]{0,2,1:T(8,128)(2,1)} %get-tuple-element.343), channel_id=1, source_target_pairs={{0,2},{1,3},{4,6},{5,7},{8,10},{9,11},{12,14},{13,15},{16,18},{17,... | collective-permute-start | bytes 933896 | tf_op jit(solution)/shard_map/ppermute | solution.py:232
  1359.7 64.4 %collective-permute-start.75 = (bf16[304,8,64]{0,2,1:T(8,128)(2,1)S(1)}, bf16[304,8,64]{0,2,1:T(8,128)(2,1)}, u32[]{:S(2)}, u32[]{:S(2)}) collective-permute-start(bf16[304,8,64]{0,2,1:T(8,128)(2,1)S(1)} %copy-done.99), channel_id=1, source_target_pairs={{2,0},{3,1},{6,4},{7,5},{10,8},{11,9},{14,12},{15,13},{18,16},{19,... | collective-permute-start | bytes 933896 | tf_op jit(solution)/shard_map/ppermute | solution.py:235
  1366.5 64.2 %collective-permute-start.76 = (bf16[304,8,64]{0,2,1:T(8,128)(2,1)}, bf16[304,8,64]{0,2,1:T(8,128)(2,1)}, u32[]{:S(2)}, u32[]{:S(2)}) collective-permute-start(bf16[304,8,64]{0,2,1:T(8,128)(2,1)} %get-tuple-element.341), channel_id=1, source_target_pairs={{0,3},{4,7},{8,11},{12,15},{16,19},{20,23},{24,27},{28,31}} | collective-permute-start | bytes 933896 | tf_op jit(solution)/shard_map/ppermute | solution.py:232
  1532.0 89.0 %collective-permute-start.114 = (bf16[304,2,128]{0,2,1:T(8,128)(2,1)}, bf16[304,2,128]{0,2,1:T(8,128)(2,1)}, u32[]{:S(2)}, u32[]{:S(2)}) collective-permute-start(bf16[304,2,128]{0,2,1:T(8,128)(2,1)} %get-tuple-element.418), channel_id=1, source_target_pairs={{0,1},{1,2},{2,3},{4,5},{5,6},{6,7},{8,9},{9,10},{10,11},{12,13},{... | collective-permute-start | bytes 466952 | tf_op jit(solution)/shard_map/ppermute | solution.py:232
  1537.3 89.3 %collective-permute-start.115 = (bf16[304,2,128]{0,2,1:T(8,128)(2,1)}, bf16[304,2,128]{0,2,1:T(8,128)(2,1)}, u32[]{:S(2)}, u32[]{:S(2)}) collective-permute-start(bf16[304,2,128]{0,2,1:T(8,128)(2,1)} %get-tuple-element.417), channel_id=1, source_target_pairs={{1,0},{2,1},{3,2},{5,4},{6,5},{7,6},{9,8},{10,9},{11,10},{13,12},{... | collective-permute-start | bytes 466952 | tf_op jit(solution)/shard_map/ppermute | solution.py:235
  1538.6 93.4 %collective-permute-start.116 = (bf16[304,2,128]{0,2,1:T(8,128)(2,1)}, bf16[304,2,128]{0,2,1:T(8,128)(2,1)}, u32[]{:S(2)}, u32[]{:S(2)}) collective-permute-start(bf16[304,2,128]{0,2,1:T(8,128)(2,1)} %get-tuple-element.416), channel_id=1, source_target_pairs={{0,2},{1,3},{4,6},{5,7},{8,10},{9,11},{12,14},{13,15},{16,18},{17,... | collective-permute-start | bytes 466952 | tf_op jit(solution)/shard_map/ppermute | solution.py:232
  1545.2 91.4 %collective-permute-start.117 = (bf16[304,2,128]{0,2,1:T(8,128)(2,1)}, bf16[304,2,128]{0,2,1:T(8,128)(2,1)}, u32[]{:S(2)}, u32[]{:S(2)}) collective-permute-start(bf16[304,2,128]{0,2,1:T(8,128)(2,1)} %get-tuple-element.415), channel_id=1, source_target_pairs={{2,0},{3,1},{6,4},{7,5},{10,8},{11,9},{14,12},{15,13},{18,16},{19,... | collective-permute-start | bytes 466952 | tf_op jit(solution)/shard_map/ppermute | solution.py:235
  1546.5 102.2 %collective-permute-start.118 = (bf16[304,2,128]{0,2,1:T(8,128)(2,1)}, bf16[304,2,128]{0,2,1:T(8,128)(2,1)}, u32[]{:S(2)}, u32[]{:S(2)}) collective-permute-start(bf16[304,2,128]{0,2,1:T(8,128)(2,1)} %get-tuple-element.414), channel_id=1, source_target_pairs={{0,3},{4,7},{8,11},{12,15},{16,19},{20,23},{24,27},{28,31}} | collective-permute-start | bytes 466952 | tf_op jit(solution)/shard_map/ppermute | solution.py:232
  1626.7 47.3 %collective-permute-start.84 = (bf16[304,2,128]{0,2,1:T(8,128)(2,1)}, bf16[304,2,128]{0,2,1:T(8,128)(2,1)}, u32[]{:S(2)}, u32[]{:S(2)}) collective-permute-start(bf16[304,2,128]{0,2,1:T(8,128)(2,1)} %get-tuple-element.411), channel_id=1, source_target_pairs={{0,1},{1,2},{2,3},{4,5},{5,6},{6,7},{8,9},{9,10},{10,11},{12,13},{... | collective-permute-start | bytes 466952 | tf_op jit(solution)/shard_map/ppermute | solution.py:232
  1632.0 47.5 %collective-permute-start.85 = (bf16[304,2,128]{0,2,1:T(8,128)(2,1)}, bf16[304,2,128]{0,2,1:T(8,128)(2,1)}, u32[]{:S(2)}, u32[]{:S(2)}) collective-permute-start(bf16[304,2,128]{0,2,1:T(8,128)(2,1)} %get-tuple-element.410), channel_id=1, source_target_pairs={{1,0},{2,1},{3,2},{5,4},{6,5},{7,6},{9,8},{10,9},{11,10},{13,12},{... | collective-permute-start | bytes 466952 | tf_op jit(solution)/shard_map/ppermute | solution.py:235
  1636.6 46.2 %collective-permute-start.86 = (bf16[304,2,128]{0,2,1:T(8,128)(2,1)}, bf16[304,2,128]{0,2,1:T(8,128)(2,1)}, u32[]{:S(2)}, u32[]{:S(2)}) collective-permute-start(bf16[304,2,128]{0,2,1:T(8,128)(2,1)} %get-tuple-element.409), channel_id=1, source_target_pairs={{0,2},{1,3},{4,6},{5,7},{8,10},{9,11},{12,14},{13,15},{16,18},{17,... | collective-permute-start | bytes 466952 | tf_op jit(solution)/shard_map/ppermute | solution.py:232
  1705.8 190.7 %reduce-scatter.20.cloned.1.call-start = ((), (), s32[]{:S(2)}) async-start(), calls=%async_computation.20 | async-start | bytes 9437184 | tf_op jit(solution)/shard_map/reduce_scatter | solution.py:452
  1731.3 194.9 %reduce-scatter.12.cloned.1.call-start = ((), (), s32[]{:S(2)}) async-start(), calls=%async_computation.16 | async-start | bytes 9437184 | tf_op jit(solution)/shard_map/reduce_scatter | solution.py:431
  1823.9 155.2 %reduce-scatter.28.cloned.1.call-start = ((), (), s32[]{:S(2)}) async-start(), calls=%async_computation.24 | async-start | bytes 589824
  1876.0 145.4 %reduce-scatter.26.cloned.1.call-start = ((), (), s32[]{:S(2)}) async-start(), calls=%async_computation.23 | async-start | bytes 9437184 | tf_op jit(solution)/shard_map/reduce_scatter | solution.py:464
  1895.6 149.9 %reduce-scatter.18.cloned.1.call-start = ((), (), s32[]{:S(2)}) async-start(), calls=%async_computation.19 | async-start | bytes 655360 | tf_op jit(solution)/shard_map/reduce_scatter | solution.py:438
  1896.4 176.9 %reduce-scatter.22.cloned.1.call-start = ((), (), s32[]{:S(2)}) async-start(), calls=%async_computation.21 | async-start | bytes 1310720 | tf_op jit(solution)/shard_map/reduce_scatter | solution.py:451
  1896.9 204.3 %reduce-scatter.14.cloned.1.call-start = ((), (), s32[]{:S(2)}) async-start(), calls=%async_computation.17 | async-start | bytes 1310720 | tf_op jit(solution)/shard_map/reduce_scatter | solution.py:430
  1926.3 292.9 %reduce-scatter.24.cloned.1.call-start = ((), (), s32[]{:S(2)}) async-start(), calls=%async_computation.22 | async-start | bytes 18874368 | tf_op jit(solution)/shard_map/reduce_scatter | solution.py:459
  (257 other events, 7697.5 us)
Sparse Core Ops, SparseCore 0:
  10.1 35.5 all-gather.9
  47.9 28.5 all-gather.13
  78.3 35.9 all-gather.7
  116.1 54.2 all-gather.11
  172.1 55.8 all-gather.15
  230.3 89.7 all-gather.17
  322.6 55.9 all-gather.19
  1705.9 53.3 reduce-scatter.15
  1762.8 71.2 reduce-scatter.19
  1837.4 71.5 reduce-scatter.11
  1912.6 34.1 reduce-scatter.27
  1950.1 71.2 reduce-scatter.25
  2023.7 21.8 reduce-scatter.17
  2047.7 25.5 reduce-scatter.21
  2075.4 25.7 reduce-scatter.13
  2104.7 114.4 reduce-scatter.23

commit v3 on v2

--- a/solution.py
+++ b/solution.py
@@ -214,6 +214,10 @@
 
 
 def line_all_to_all(x, count, split_axis, concat_axis):
+    return lax.all_to_all(x, "tensor", split_axis, concat_axis, tiled=True)
+
+
+def shifted_all_to_all(x, count, split_axis, concat_axis):
     place = lax.axis_index("tensor")
     size = x.shape[split_axis] // count
 

time: 2330 us -> 2130 us (0.914)
  starting transfers between devices: 442 us -> 224 us
  local copies, waits for them, and re-layouts: 376 us -> 274 us
  waiting for transfers between devices: 580 us -> 682 us
    ppermute x72 -> x0, starting transfers between devices: 319 us -> none  [the longest x36 271 us: line_all_to_all(): lax.ppermute(block(place + step), 'tensor', [(i, i + step) for i in range...]
    dynamic_update_slice x80 -> x0, local copies, waits for them, and re-layouts: 199 us -> none  [the longest x72 174 us: line_all_to_all(): lax.dynamic_update_slice_in_dim(out, piece, jnp.where(valid, source, plac...]
    all_to_all x0 -> x12, waiting for transfers between devices: none -> 152 us  [line_all_to_all(): return lax.all_to_all(x, 'tensor', split_axis, concat_axis, tiled=True)]
    all_to_all x0 -> x12, starting transfers between devices: none -> 89.1 us  [line_all_to_all(): return lax.all_to_all(x, 'tensor', split_axis, concat_axis, tiled=True)]
    unnamed x375 -> x320, local copies, waits for them, and re-layouts: 28.1 us -> 82.3 us
    ppermute x72 -> x0, waiting for transfers between devices: 48.3 us -> none  [the longest x36 34.7 us: line_all_to_all(): lax.ppermute(block(place - step), 'tensor', [(i, i - step) for i in range...]
    ppermute x12, waiting for transfers between devices: 99.5 us -> 140 us  [line_scatter(): lax.ppermute(send.astype(jnp.bfloat16), 'tensor', [(i, i + 1) for i in ra...]
    all_to_all x0 -> x16, local copies, waits for them, and re-layouts: none -> 39.5 us  [line_all_to_all(): return lax.all_to_all(x, 'tensor', split_axis, concat_axis, tiled=True)]
  transfers between devices with their start and end apart: 136 -> 76, of which waited for: 34 -> 38; matrix products, arithmetic and copies ran while one was open for 40% -> 40% of each run, Pallas kernels for 0% -> 0%
where the time goes in v3:
time: 2130 us; the launch traced here: 2120 us
  waiting for transfers between devices  682 us (32%)
  matrix products  579 us (27%)
  local copies, waits for them, and re-layouts  274 us (13%)
  other arithmetic  252 us (12%)
  starting transfers between devices  224 us (11%)
  blocking collectives  90.1 us (4%)
    all_to_all x12, waiting for transfers between devices, line_all_to_all(): return lax.all_to_all(x, 'tensor', split_axis, concat_axis, tiled=True)  152 us
    ppermute x12, waiting for transfers between devices, line_scatter(): lax.ppermute(send.astype(jnp.bfloat16), 'tensor', [(i, i + 1) for i in ra...  140 us
    reduce_scatter x1, waiting for transfers between devices, per_device(): lax.psum_scatter(totals[3].reshape(width, -1).astype(jnp.bfloat16), 'dp',...  115 us
    ppermute x12, waiting for transfers between devices, line_gather(): lax.ppermute(from_right, 'tensor', [(i, i - 1) for i in range(1, count -...  96.5 us
    all_to_all x12, starting transfers between devices, line_all_to_all(): return lax.all_to_all(x, 'tensor', split_axis, concat_axis, tiled=True)  89.1 us
    unnamed x320, local copies, waits for them, and re-layouts  82.3 us
    dot_general x6, matrix products, contract_rows(): lax.dot_general(left, right, (((0,), (0,)), ((), ())), preferred_element_...  80.7 us
    dot_general x6, matrix products, contract_cols(): lax.dot_general(left, right, (((1,), (1,)), ((), ())), preferred_element_...  75.6 us
  transfers between devices with their start and end apart: 76, of which 38 were waited for; matrix products, arithmetic and copies ran while one was open for 40% of the time, Pallas kernels for 0%

profile of v3, /device:TPU:0, one launch (start us, length us, event | category | flops | bytes accessed | tf_op | source)
XLA Modules:
  0.0 2120.7 jit_solution(893939502299642259)
XLA Ops:
  13.6 24.5 %all_gather.28 = bf16[256,8,128]{2,0,1:T(8,128)(2,1)} all-gather(bf16[256,2,128]{2,0,1:T(8,128)(2,1)S(1)} %copy.451), channel_id=1, replica_groups=mesh['dp'=8,'tensor'=4] {'tensor'}, dimensions={1}, use_global_device_ids=true | all-gather | bytes 655360 | tf_op jit(solution)/shard_map/all_gather | solution.py:283
  45.8 30.6 %all-gather.14.cloned.1.call-done = bf16[2048,256]{1,0:T(8,128)(2,1)} async-done(((bf16[512,256]{1,0:T(8,128)(2,1)}), bf16[2048,256]{1,0:T(8,128)(2,1)}) %all-gather.14.cloned.1.call-update) | async-done | bytes 1048592 | tf_op jit(solution)/shard_map/all_gather | solution.py:286
  120.9 9.0 all_gather.27
  183.1 18.5 collective-permute-done.39
  216.6 12.4 copy.329
  238.0 24.8 %all-to-all-done = bf16[304,8,128]{2,0,1:T(8,128)(2,1)} async-done(((bf16[304,8,128]{2,0,1:T(8,128)(2,1)}), bf16[304,8,128]{2,0,1:T(8,128)(2,1)}, u32[]{:S(2)}, u32[]{:S(2)}) %all-to-all-start) | async-done | bytes 622624 | tf_op jit(solution)/shard_map/all_to_all | solution.py:217
  283.5 19.0 all-to-all-done.1
  332.1 13.1 fusion.134
  387.3 15.0 all-to-all-done.2
  470.6 13.5 collective-permute-done.1
  487.4 12.0 fusion.133
  502.7 11.4 collective-permute-done.3
  530.7 12.5 collective-permute-done.5
  545.7 27.5 %fusion.59 = f32[1216,2,2048]{2,0,1:T(8,128)} fusion(bf16[2048,2,2048]{2,0,1:T(8,128)(2,1)} %all-gather.18.cloned.1.call-done, bf16[1216,2048]{1,0:T(8,128)(2,1)} %constant_dynamic-update-slice_fusion.21), kind=kOutput, calls=%fused_computation.104 | convolution fusion | flops 20401094656 | bytes 41680896 | tf_op jit(solution)/shard_map/rd,dcf->rcf/dot_general | solution.py:341
  573.2 25.7 %fusion.61 = (bf16[1216,1,2048]{2,0,1:T(8,128)(2,1)}, bf16[1216,1,2048]{2,0,1:T(8,128)(2,1)}, bf16[1216,2048]{1,0:T(8,128)(2,1)}) fusion(f32[1216,2,2048]{2,0,1:T(8,128)} %fusion.59, bf16[1216,2048]{1,0:T(8,128)(2,1)} %get-tuple-element.356, bf16[2048,2048]{1,0:T(8,128)(2,1)} %all-gather.20.cloned.1.call-done), kind=kOutput, calls=%fused_computation.110 | convolution fusion | flops 10237902848 | bytes 48234496 | tf_op jit(solution)/shard_map/dot_general | solution.py:162
  598.9 24.9 %convolution_bitcast_fusion.1 = f32[1216,2048]{1,0:T(8,128)S(1)} fusion(bf16[2048,2,2048]{2,0,1:T(8,128)(2,1)} %all-gather.18.cloned.1.call-done, bf16[1216,1,2048]{2,0,1:T(8,128)(2,1)} %get-tuple-element.317, bf16[1216,1,2048]{2,0,1:T(8,128)(2,1)} %get-tuple-element.316), kind=kOutput, calls=%fused_computation.81 | convolution fusion | flops 20406075392 | bytes 36700160 | tf_op jit(solution)/shard_map/rcf,dcf->rd/dot_general | solution.py:365
  636.9 16.9 collective-permute-done.30
  667.0 17.3 collective-permute-done.31
  691.2 8.7 pad_maximum_fusion.9
  718.8 31.6 %all-to-all-done.5 = bf16[4,2,77824]{2,1,0:T(2,128)(2,1)} async-done(((bf16[4,2,77824]{2,1,0:T(2,128)(2,1)}), bf16[4,2,77824]{2,1,0:T(2,128)(2,1)}, u32[]{:S(2)}, u32[]{:S(2)}) %all-to-all-start.5) | async-done | bytes 1245216 | tf_op jit(solution)/shard_map/all_to_all | solution.py:217
  780.8 19.8 collective-permute-done.12
  808.3 13.0 fusion.228
  836.2 21.9 %collective-permute-done.17 = bf16[304,2048]{1,0:T(8,128)(2,1)S(1)} collective-permute-done((bf16[304,2048]{1,0:T(8,128)(2,1)S(1)}, bf16[304,2048]{1,0:T(8,128)(2,1)S(1)}, u32[]{:S(2)}, u32[]{:S(2)}) %collective-permute-start.17) | collective-permute-done | bytes 1245216 | tf_op jit(solution)/shard_map/ppermute | solution.py:178
  858.4 28.0 %fusion.56 = f32[1216,2,2048]{2,0,1:T(8,128)} fusion(bf16[2048,2,2048]{2,0,1:T(8,128)(2,1)} %all-gather.18.cloned.1.call-done, bf16[1216,2048]{1,0:T(8,128)(2,1)S(1)} %constant_dynamic-update-slice_fusion.14), kind=kOutput, calls=%fused_computation.101 | convolution fusion | flops 20401094656 | bytes 41680896 | tf_op jit(solution)/shard_map/rd,dcf->rcf/dot_general | solution.py:341
  886.4 25.6 %fusion.62 = (bf16[1216,1,2048]{2,0,1:T(8,128)(2,1)}, bf16[1216,1,2048]{2,0,1:T(8,128)(2,1)}, bf16[1216,2048]{1,0:T(8,128)(2,1)}) fusion(f32[1216,2,2048]{2,0,1:T(8,128)} %fusion.56, bf16[1216,2048]{1,0:T(8,128)(2,1)} %get-tuple-element.357, bf16[2048,2048]{1,0:T(8,128)(2,1)} %all-gather.20.cloned.1.call-done), kind=kOutput, calls=%fused_computation.111 | convolution fusion | flops 10237902848 | bytes 48234496 | tf_op jit(solution)/shard_map/dot_general | solution.py:162
  912.0 24.7 %convolution_bitcast_fusion = f32[1216,2048]{1,0:T(8,128)S(1)} fusion(bf16[2048,2,2048]{2,0,1:T(8,128)(2,1)} %all-gather.18.cloned.1.call-done, bf16[1216,1,2048]{2,0,1:T(8,128)(2,1)} %get-tuple-element.319, bf16[1216,1,2048]{2,0,1:T(8,128)(2,1)} %get-tuple-element.318), kind=kOutput, calls=%fused_computation.80 | convolution fusion | flops 20406075392 | bytes 36700160 | tf_op jit(solution)/shard_map/rcf,dcf->rd/dot_general | solution.py:365
  941.8 14.7 fusion.229
  980.1 14.2 collective-permute-done.18
  1000.9 20.0 collective-permute-done.43
  1027.1 20.5 collective-permute-done.7
  1051.7 14.7 collective-permute-done.19
  1085.3 23.5 %collective-permute-start.20 = (bf16[304,2048]{1,0:T(8,128)(2,1)}, bf16[304,2048]{1,0:T(8,128)(2,1)S(1)}, u32[]{:S(2)}, u32[]{:S(2)}) collective-permute-start(bf16[304,2048]{1,0:T(8,128)(2,1)} %get-tuple-element.338), channel_id=1, source_target_pairs={{0,1},{1,2},{2,3},{4,5},{5,6},{6,7},{8,9},{9,10},{10,11},{12,13},{... | collective-permute-start | bytes 3735560 | tf_op jit(solution)/shard_map/ppermute | solution.py:201
  1109.3 20.9 collective-permute-done.44
  1148.1 10.0 collective-permute-done.23
  1173.5 34.1 %all-to-all-start.9 = ((bf16[304,32,64]{0,2,1:T(8,128)(2,1)}), bf16[304,32,64]{0,2,1:T(8,128)(2,1)}, u32[]{:S(2)}, u32[]{:S(2)}) async-start(bf16[304,32,64]{0,2,1:T(8,128)(2,1)} %bitcast.748), calls=%async_computation.9 | async-start | bytes 3145728 | tf_op jit(solution)/shard_map/all_to_all | solution.py:217
  1219.4 17.4 all-to-all-done.9
  1253.5 10.3 fusion.16
  1263.8 10.1 all-to-all-done.6
  1281.5 9.8 fusion.19
  1301.0 21.3 %fusion = (f32[2,4,608]{2,1,0:T(4,128)S(1)}, f32[2,1216,608,4]{2,1,3,0:T(8,128)}) fusion(f32[2,1216,608,4]{2,1,3,0:T(8,128)} %copy-done.1, f32[2,4,608]{2,1,0:T(4,128)S(1)} %bitcast.794, pred[608,1216]{0,1:T(8,128)(4,1)S(1)} %copy-done.33, bf16[608,2,4,64]{0,3,2,1:T(8,128)(2,1)} %slice.449, bf16[1216,2,128]{2,0,1:T(8,128)(2,1)S(1)} %bitcast.733), kind=kOutput, calls=%fused_computation.3 | convolution fusion | flops 786640128 | bytes 49340416 | tf_op jit(solution)/shard_map/ikrd,jkd->krij/dot_general | solution.py:119
  1322.3 11.9 fusion.120
  1334.2 9.6 fusion.18
  1346.6 16.7 fusion.2
  1379.3 21.3 %fusion.3 = (f32[2,4,608]{2,1,0:T(4,128)S(1)}, f32[2,1216,608,4]{2,1,3,0:T(8,128)}) fusion(f32[2,1216,608,4]{2,1,3,0:T(8,128)} %copy-done, f32[2,4,608]{2,1,0:T(4,128)S(1)} %bitcast.788, pred[608,1216]{0,1:T(8,128)(4,1)S(1)} %copy-done.31, bf16[608,2,4,64]{0,3,2,1:T(8,128)(2,1)} %slice.440, bf16[1216,2,128]{2,0,1:T(8,128)(2,1)S(1)} %bitcast.724), kind=kOutput, calls=%fused_computation.8 | convolution fusion | flops 786640128 | bytes 49340416 | tf_op jit(solution)/shard_map/ikrd,jkd->krij/dot_general | solution.py:119
  1400.7 10.9 fusion.123
  1411.5 9.6 fusion.21
  1423.8 16.7 fusion.5
  1454.3 12.9 all-to-all-done.8
  1475.8 13.7 fusion.173
  1489.5 10.5 add_convert_fusion.2
  1598.0 16.1 all-to-all-done.7
  1633.4 10.5 add_convert_fusion.3
  1644.1 18.0 fusion.232
  1680.5 17.4 psum.14
  1699.0 19.7 add_convert_fusion.1
  1720.1 29.1 %fusion.42 = f32[2048,2,2048]{0,2,1:T(8,128)} fusion(bf16[1216,1,2048]{2,0,1:T(8,128)(2,1)} %get-tuple-element.319, bf16[1216,1,2048]{2,0,1:T(8,128)(2,1)} %get-tuple-element.318, bf16[1216,2048]{1,0:T(8,128)(2,1)} %copy-done.60), kind=kOutput, calls=%fused_computation.85 | convolution fusion | flops 20421017600 | bytes 48496640 | tf_op jit(solution)/shard_map/rd,rcf->dcf/dot_general | solution.py:361
  1749.3 34.1 %add_convert_fusion = bf16[2048,2,2048]{0,2,1:T(8,128)(2,1)} fusion(f32[2048,2,2048]{0,2,1:T(8,128)} %fusion.42, bf16[1216,1,2048]{2,0,1:T(8,128)(2,1)} %get-tuple-element.317, bf16[1216,1,2048]{2,0,1:T(8,128)(2,1)} %get-tuple-element.316, bf16[1216,2048]{1,0:T(8,128)(2,1)} %constant_dynamic-update-slice_fusion.21), kind=kOutput, calls=%fused_computation | convolution fusion | flops 20437794816 | bytes 65273856 | tf_op jit(solution)/shard_map/rd,rcf->dcf/dot_general | solution.py:361
  1806.1 20.9 reduce-scatter.26.cloned.1.call-done
  1833.5 17.6 reduce-scatter.18.cloned.1.call-done
  1854.3 24.6 %reduce-scatter.22.cloned.1.call-done = bf16[512,256]{1,0:T(8,128)(2,1)} async-done(((bf16[2048,256]{1,0:T(8,128)(2,1)}), bf16[512,256]{1,0:T(8,128)(2,1)}) %reduce-scatter.22.cloned.1.call-update) | async-done | bytes 262160 | tf_op jit(solution)/shard_map/reduce_scatter | solution.py:455
  1881.5 25.3 %reduce-scatter.14.cloned.1.call-done = bf16[256,512]{1,0:T(8,128)(2,1)} async-done(((bf16[256,2048]{1,0:T(8,128)(2,1)}), bf16[256,512]{1,0:T(8,128)(2,1)}) %reduce-scatter.14.cloned.1.call-update) | async-done | bytes 262160 | tf_op jit(solution)/shard_map/reduce_scatter | solution.py:434
  1909.7 115.1 %reduce-scatter.24.cloned.1.call-done = bf16[256,4096]{0,1:T(8,128)(2,1)} async-done(((bf16[2048,4096]{0,1:T(8,128)(2,1)}), bf16[256,4096]{0,1:T(8,128)(2,1)}) %reduce-scatter.24.cloned.1.call-update) | async-done | bytes 2097168 | tf_op jit(solution)/shard_map/reduce_scatter | solution.py:463
  2031.1 18.3 multiply_reduce_fusion
  2057.2 39.2 %psum.15 = f32[2,7]{1,0:T(2,128)S(1)} all-reduce(f32[2,7]{1,0:T(2,128)S(1)} %pad_maximum_fusion.18), channel_id=1, replica_groups=mesh['dp'=8,'tensor'=4] {'dp','tensor'}, use_global_device_ids=true, to_apply=%region_52.53 | all-reduce | flops 14 | bytes 112 | tf_op jit(solution)/shard_map/psum | solution.py:498
  (685 shorter events, 817.5 us)
Async XLA Ops:
  7.2 38.5 %all-gather.10.cloned.1.call-start = ((), (), s32[]{:S(2)}) async-start(), calls=%async_computation.22 | async-start | bytes 1310720 | tf_op jit(solution)/shard_map/all_gather | solution.py:280
  9.8 66.6 %all-gather.14.cloned.1.call-start = ((), (), s32[]{:S(2)}) async-start(), calls=%async_computation.24 | async-start | bytes 1310720 | tf_op jit(solution)/shard_map/all_gather | solution.py:286
  12.5 190.4 %all-gather.8.cloned.1.call-start = ((), (), s32[]{:S(2)}) async-start(), calls=%async_computation.21 | async-start | bytes 4718592 | tf_op jit(solution)/shard_map/all_gather | solution.py:282
  38.1 178.5 %all-gather.12.cloned.1.call-start = ((), (), s32[]{:S(2)}) async-start(), calls=%async_computation.23 | async-start | bytes 9437184 | tf_op jit(solution)/shard_map/all_gather | solution.py:279
  45.8 378.9 %all-gather.16.cloned.1.call-start = ((), (), s32[]{:S(2)}) async-start(), calls=%async_computation.25 | async-start | bytes 9437184 | tf_op jit(solution)/shard_map/all_gather | solution.py:285
  76.5 469.2 %all-gather.18.cloned.1.call-start = ((), (), s32[]{:S(2)}) async-start(), calls=%async_computation.26 | async-start | bytes 18874368 | tf_op jit(solution)/shard_map/all_gather | solution.py:288
  82.4 490.7 %all-gather.20.cloned.1.call-start = ((), (), s32[]{:S(2)}) async-start(), calls=%async_computation.27 | async-start | bytes 9437184 | tf_op jit(solution)/shard_map/all_gather | solution.py:289
  84.5 46.0 %collective-permute-start.24 = (bf16[304,2048]{1,0:T(8,128)(2,1)}, bf16[304,2048]{1,0:T(8,128)(2,1)}, u32[]{:S(2)}, u32[]{:S(2)}) collective-permute-start(bf16[304,2048]{1,0:T(8,128)(2,1)} %get-tuple-element.358), channel_id=1, source_target_pairs={{0,1},{1,2},{2,3},{4,5},{5,6},{6,7},{8,9},{9,10},{10,11},{12,13},{... | collective-permute-start | bytes 3735560 | tf_op jit(solution)/shard_map/ppermute | solution.py:175
  89.1 43.2 %collective-permute-start.25 = (bf16[304,2048]{1,0:T(8,128)(2,1)}, bf16[304,2048]{1,0:T(8,128)(2,1)}, u32[]{:S(2)}, u32[]{:S(2)}) collective-permute-start(bf16[304,2048]{1,0:T(8,128)(2,1)} %get-tuple-element.358), channel_id=1, source_target_pairs={{1,0},{2,1},{3,2},{5,4},{6,5},{7,6},{9,8},{10,9},{11,10},{13,12},{... | collective-permute-start | bytes 3735560 | tf_op jit(solution)/shard_map/ppermute | solution.py:178
  90.4 50.4 %collective-permute-start.36 = (bf16[304,2048]{1,0:T(8,128)(2,1)}, bf16[304,2048]{1,0:T(8,128)(2,1)}, u32[]{:S(2)}, u32[]{:S(2)}) collective-permute-start(bf16[304,2048]{1,0:T(8,128)(2,1)} %get-tuple-element.359), channel_id=1, source_target_pairs={{0,1},{1,2},{2,3},{4,5},{5,6},{6,7},{8,9},{9,10},{10,11},{12,13},{... | collective-permute-start | bytes 3735560 | tf_op jit(solution)/shard_map/ppermute | solution.py:175
  96.1 52.2 %collective-permute-start.37 = (bf16[304,2048]{1,0:T(8,128)(2,1)}, bf16[304,2048]{1,0:T(8,128)(2,1)}, u32[]{:S(2)}, u32[]{:S(2)}) collective-permute-start(bf16[304,2048]{1,0:T(8,128)(2,1)} %get-tuple-element.359), channel_id=1, source_target_pairs={{1,0},{2,1},{3,2},{5,4},{6,5},{7,6},{9,8},{10,9},{11,10},{13,12},{... | collective-permute-start | bytes 3735560 | tf_op jit(solution)/shard_map/ppermute | solution.py:178
  130.6 34.8 %collective-permute-start.26 = (bf16[304,2048]{1,0:T(8,128)(2,1)}, bf16[304,2048]{1,0:T(8,128)(2,1)}, u32[]{:S(2)}, u32[]{:S(2)}) collective-permute-start(bf16[304,2048]{1,0:T(8,128)(2,1)} %collective-permute-done.24), channel_id=1, source_target_pairs={{1,2},{2,3},{5,6},{6,7},{9,10},{10,11},{13,14},{14,15},{17,18},{18... | collective-permute-start | bytes 3735560 | tf_op jit(solution)/shard_map/ppermute | solution.py:175
  132.3 42.6 %collective-permute-start.27 = (bf16[304,2048]{1,0:T(8,128)(2,1)}, bf16[304,2048]{1,0:T(8,128)(2,1)}, u32[]{:S(2)}, u32[]{:S(2)}) collective-permute-start(bf16[304,2048]{1,0:T(8,128)(2,1)} %collective-permute-done.25), channel_id=1, source_target_pairs={{1,0},{2,1},{5,4},{6,5},{9,8},{10,9},{13,12},{14,13},{17,16},{18,1... | collective-permute-start | bytes 3735560 | tf_op jit(solution)/shard_map/ppermute | solution.py:178
  140.8 35.4 %collective-permute-start.38 = (bf16[304,2048]{1,0:T(8,128)(2,1)}, bf16[304,2048]{1,0:T(8,128)(2,1)}, u32[]{:S(2)}, u32[]{:S(2)}) collective-permute-start(bf16[304,2048]{1,0:T(8,128)(2,1)} %collective-permute-done.36), channel_id=1, source_target_pairs={{1,2},{2,3},{5,6},{6,7},{9,10},{10,11},{13,14},{14,15},{17,18},{18... | collective-permute-start | bytes 3735560 | tf_op jit(solution)/shard_map/ppermute | solution.py:175
  148.3 53.4 %collective-permute-start.39 = (bf16[304,2048]{1,0:T(8,128)(2,1)}, bf16[304,2048]{1,0:T(8,128)(2,1)}, u32[]{:S(2)}, u32[]{:S(2)}) collective-permute-start(bf16[304,2048]{1,0:T(8,128)(2,1)} %collective-permute-done.37), channel_id=1, source_target_pairs={{1,0},{2,1},{5,4},{6,5},{9,8},{10,9},{13,12},{14,13},{17,16},{18,1... | collective-permute-start | bytes 3735560 | tf_op jit(solution)/shard_map/ppermute | solution.py:178
  165.4 107.0 %collective-permute-start.28 = (bf16[304,2048]{1,0:T(8,128)(2,1)}, bf16[304,2048]{1,0:T(8,128)(2,1)}, u32[]{:S(2)}, u32[]{:S(2)}) collective-permute-start(bf16[304,2048]{1,0:T(8,128)(2,1)} %collective-permute-done.26), channel_id=1, source_target_pairs={{2,3},{6,7},{10,11},{14,15},{18,19},{22,23},{26,27},{30,31}} | collective-permute-start | bytes 3735560 | tf_op jit(solution)/shard_map/ppermute | solution.py:175
  175.0 198.2 %collective-permute-start.29 = (bf16[304,2048]{1,0:T(8,128)(2,1)}, bf16[304,2048]{1,0:T(8,128)(2,1)}, u32[]{:S(2)}, u32[]{:S(2)}) collective-permute-start(bf16[304,2048]{1,0:T(8,128)(2,1)} %collective-permute-done.27), channel_id=1, source_target_pairs={{1,0},{5,4},{9,8},{13,12},{17,16},{21,20},{25,24},{29,28}} | collective-permute-start | bytes 3735560 | tf_op jit(solution)/shard_map/ppermute | solution.py:178
  176.3 99.2 %collective-permute-start.40 = (bf16[304,2048]{1,0:T(8,128)(2,1)}, bf16[304,2048]{1,0:T(8,128)(2,1)}, u32[]{:S(2)}, u32[]{:S(2)}) collective-permute-start(bf16[304,2048]{1,0:T(8,128)(2,1)} %collective-permute-done.38), channel_id=1, source_target_pairs={{2,3},{6,7},{10,11},{14,15},{18,19},{22,23},{26,27},{30,31}} | collective-permute-start | bytes 3735560 | tf_op jit(solution)/shard_map/ppermute | solution.py:175
  201.6 174.1 %collective-permute-start.41 = (bf16[304,2048]{1,0:T(8,128)(2,1)}, bf16[304,2048]{1,0:T(8,128)(2,1)}, u32[]{:S(2)}, u32[]{:S(2)}) collective-permute-start(bf16[304,2048]{1,0:T(8,128)(2,1)} %collective-permute-done.39), channel_id=1, source_target_pairs={{1,0},{5,4},{9,8},{13,12},{17,16},{21,20},{25,24},{29,28}} | collective-permute-start | bytes 3735560 | tf_op jit(solution)/shard_map/ppermute | solution.py:178
  209.0 53.8 %all-to-all-start = ((bf16[304,8,128]{2,0,1:T(8,128)(2,1)}), bf16[304,8,128]{2,0,1:T(8,128)(2,1)}, u32[]{:S(2)}, u32[]{:S(2)}) async-start(bf16[304,8,128]{2,0,1:T(8,128)(2,1)} %pad_maximum_fusion.16), calls=%async_computation | async-start | bytes 1245184 | tf_op jit(solution)/shard_map/all_to_all | solution.py:217
  262.8 39.7 %all-to-all-start.1 = ((bf16[304,32,64]{0,2,1:T(8,128)(2,1)}), bf16[304,32,64]{0,2,1:T(8,128)(2,1)}, u32[]{:S(2)}, u32[]{:S(2)}) async-start(bf16[304,32,64]{0,2,1:T(8,128)(2,1)} %pad_maximum_fusion.12), calls=%async_computation.1 | async-start | bytes 3145728 | tf_op jit(solution)/shard_map/all_to_all | solution.py:217
  302.5 65.8 %all-to-all-start.3 = ((bf16[304,8,128]{2,0,1:T(8,128)(2,1)}), bf16[304,8,128]{2,0,1:T(8,128)(2,1)}, u32[]{:S(2)}, u32[]{:S(2)}) async-start(bf16[304,8,128]{2,0,1:T(8,128)(2,1)} %pad_maximum_fusion.17), calls=%async_computation.3 | async-start | bytes 1245184 | tf_op jit(solution)/shard_map/all_to_all | solution.py:217
  368.3 34.1 %all-to-all-start.2 = ((bf16[4,2,77824]{2,1,0:T(2,128)(2,1)}), bf16[4,2,77824]{2,1,0:T(2,128)(2,1)}, u32[]{:S(2)}, u32[]{:S(2)}) async-start(bf16[4,2,77824]{2,1,0:T(2,128)(2,1)} %reshape.919), calls=%async_computation.2 | async-start | bytes 2490368 | tf_op jit(solution)/shard_map/all_to_all | solution.py:217
  402.4 40.9 %all-to-all-start.4 = ((bf16[304,32,64]{0,2,1:T(8,128)(2,1)}), bf16[304,32,64]{0,2,1:T(8,128)(2,1)}, u32[]{:S(2)}, u32[]{:S(2)}) async-start(bf16[304,32,64]{0,2,1:T(8,128)(2,1)} %pad_maximum_fusion.13), calls=%async_computation.4 | async-start | bytes 3145728 | tf_op jit(solution)/shard_map/all_to_all | solution.py:217
  433.3 29.8 %collective-permute-start = (bf16[304,2048]{1,0:T(8,128)(2,1)}, bf16[304,2048]{1,0:T(8,128)(2,1)}, u32[]{:S(2)}, u32[]{:S(2)}) collective-permute-start(bf16[304,2048]{1,0:T(8,128)(2,1)} %multiply_convert_fusion.9), channel_id=1, source_target_pairs={{0,1},{1,2},{2,3},{4,5},{5,6},{6,7},{8,9},{9,10},{10,11},{12,13},{... | collective-permute-start | bytes 3735560 | tf_op jit(solution)/shard_map/ppermute | solution.py:175
  453.5 30.6 %collective-permute-start.1 = (bf16[304,2048]{1,0:T(8,128)(2,1)}, bf16[304,2048]{1,0:T(8,128)(2,1)}, u32[]{:S(2)}, u32[]{:S(2)}) collective-permute-start(bf16[304,2048]{1,0:T(8,128)(2,1)} %multiply_convert_fusion.9), channel_id=1, source_target_pairs={{1,0},{2,1},{3,2},{5,4},{6,5},{7,6},{9,8},{10,9},{11,10},{13,12},{... | collective-permute-start | bytes 3735560 | tf_op jit(solution)/shard_map/ppermute | solution.py:178
  484.1 30.0 %collective-permute-start.3 = (bf16[304,2048]{1,0:T(8,128)(2,1)}, bf16[304,2048]{1,0:T(8,128)(2,1)}, u32[]{:S(2)}, u32[]{:S(2)}) collective-permute-start(bf16[304,2048]{1,0:T(8,128)(2,1)} %collective-permute-done.1), channel_id=1, source_target_pairs={{1,0},{2,1},{5,4},{6,5},{9,8},{10,9},{13,12},{14,13},{17,16},{18,1... | collective-permute-start | bytes 3735560 | tf_op jit(solution)/shard_map/ppermute | solution.py:178
  485.7 42.4 %collective-permute-start.4 = (bf16[304,2048]{1,0:T(8,128)(2,1)}, bf16[304,2048]{1,0:T(8,128)(2,1)}, u32[]{:S(2)}, u32[]{:S(2)}) collective-permute-start(bf16[304,2048]{1,0:T(8,128)(2,1)} %collective-permute-done.2), channel_id=1, source_target_pairs={{2,3},{6,7},{10,11},{14,15},{18,19},{22,23},{26,27},{30,31}} | collective-permute-start | bytes 3735560 | tf_op jit(solution)/shard_map/ppermute | solution.py:175
  514.1 29.1 %collective-permute-start.5 = (bf16[304,2048]{1,0:T(8,128)(2,1)}, bf16[304,2048]{1,0:T(8,128)(2,1)S(1)}, u32[]{:S(2)}, u32[]{:S(2)}) collective-permute-start(bf16[304,2048]{1,0:T(8,128)(2,1)} %collective-permute-done.3), channel_id=1, source_target_pairs={{1,0},{5,4},{9,8},{13,12},{17,16},{21,20},{25,24},{29,28}} | collective-permute-start | bytes 3735560 | tf_op jit(solution)/shard_map/ppermute | solution.py:178
  634.7 32.3 %collective-permute-start.33 = (bf16[304,2048]{1,0:T(8,128)(2,1)}, bf16[304,2048]{1,0:T(8,128)(2,1)}, u32[]{:S(2)}, u32[]{:S(2)}) collective-permute-start(bf16[304,2048]{1,0:T(8,128)(2,1)} %get-tuple-element.329), channel_id=1, source_target_pairs={{3,2},{7,6},{11,10},{15,14},{19,18},{23,22},{27,26},{31,30}} | collective-permute-start | bytes 3735560 | tf_op jit(solution)/shard_map/ppermute | solution.py:207
  702.8 47.6 %all-to-all-start.5 = ((bf16[4,2,77824]{2,1,0:T(2,128)(2,1)}), bf16[4,2,77824]{2,1,0:T(2,128)(2,1)}, u32[]{:S(2)}, u32[]{:S(2)}) async-start(bf16[4,2,77824]{2,1,0:T(2,128)(2,1)} %reshape.917), calls=%async_computation.5 | async-start | bytes 2490368 | tf_op jit(solution)/shard_map/all_to_all | solution.py:217
  708.9 57.3 %collective-permute-start.32 = (bf16[304,2048]{1,0:T(8,128)(2,1)}, bf16[304,2048]{1,0:T(8,128)(2,1)}, u32[]{:S(2)}, u32[]{:S(2)}) collective-permute-start(bf16[304,2048]{1,0:T(8,128)(2,1)} %get-tuple-element.326), channel_id=1, source_target_pairs={{0,1},{1,2},{2,3},{4,5},{5,6},{6,7},{8,9},{9,10},{10,11},{12,13},{... | collective-permute-start | bytes 3735560 | tf_op jit(solution)/shard_map/ppermute | solution.py:201
  717.3 48.8 %collective-permute-start.35 = (bf16[304,2048]{1,0:T(8,128)(2,1)}, bf16[304,2048]{1,0:T(8,128)(2,1)}, u32[]{:S(2)}, u32[]{:S(2)}) collective-permute-start(bf16[304,2048]{1,0:T(8,128)(2,1)} %add_convert_fusion.11), channel_id=1, source_target_pairs={{1,0},{2,1},{3,2},{5,4},{6,5},{7,6},{9,8},{10,9},{11,10},{13,12},{... | collective-permute-start | bytes 3735560 | tf_op jit(solution)/shard_map/ppermute | solution.py:207
  772.6 27.9 %collective-permute-start.12 = (bf16[304,2048]{1,0:T(8,128)(2,1)S(1)}, bf16[304,2048]{1,0:T(8,128)(2,1)S(1)}, u32[]{:S(2)}, u32[]{:S(2)}) collective-permute-start(bf16[304,2048]{1,0:T(8,128)(2,1)S(1)} %get-tuple-element.388), channel_id=1, source_target_pairs={{0,1},{1,2},{2,3},{4,5},{5,6},{6,7},{8,9},{9,10},{10,11},{12,13},{... | collective-permute-start | bytes 3735560 | tf_op jit(solution)/shard_map/ppermute | solution.py:175
  824.4 151.6 %collective-permute-start.6 = (bf16[304,2048]{1,0:T(8,128)(2,1)}, bf16[304,2048]{1,0:T(8,128)(2,1)}, u32[]{:S(2)}, u32[]{:S(2)}) collective-permute-start(bf16[304,2048]{1,0:T(8,128)(2,1)} %get-tuple-element.336), channel_id=1, source_target_pairs={{0,1},{4,5},{8,9},{12,13},{16,17},{20,21},{24,25},{28,29}} | collective-permute-start | bytes 3735560 | tf_op jit(solution)/shard_map/ppermute | solution.py:201
  938.0 29.6 %collective-permute-start.42 = (bf16[304,2048]{1,0:T(8,128)(2,1)S(1)}, bf16[304,2048]{1,0:T(8,128)(2,1)S(1)}, u32[]{:S(2)}, u32[]{:S(2)}) collective-permute-start(bf16[304,2048]{1,0:T(8,128)(2,1)S(1)} %get-tuple-element.332), channel_id=1, source_target_pairs={{0,1},{4,5},{8,9},{12,13},{16,17},{20,21},{24,25},{28,29}} | collective-permute-start | bytes 3735560 | tf_op jit(solution)/shard_map/ppermute | solution.py:201
  956.9 37.4 %collective-permute-start.18 = (bf16[304,2048]{1,0:T(8,128)(2,1)S(1)}, bf16[304,2048]{1,0:T(8,128)(2,1)S(1)}, u32[]{:S(2)}, u32[]{:S(2)}) collective-permute-start(bf16[304,2048]{1,0:T(8,128)(2,1)S(1)} %get-tuple-element.340), channel_id=1, source_target_pairs={{0,1},{4,5},{8,9},{12,13},{16,17},{20,21},{24,25},{28,29}} | collective-permute-start | bytes 3735560 | tf_op jit(solution)/shard_map/ppermute | solution.py:201
  958.4 37.1 %collective-permute-start.45 = (bf16[304,2048]{1,0:T(8,128)(2,1)}, bf16[304,2048]{1,0:T(8,128)(2,1)S(1)}, u32[]{:S(2)}, u32[]{:S(2)}) collective-permute-start(bf16[304,2048]{1,0:T(8,128)(2,1)} %get-tuple-element.333), channel_id=1, source_target_pairs={{3,2},{7,6},{11,10},{15,14},{19,18},{23,22},{27,26},{31,30}} | collective-permute-start | bytes 3735560 | tf_op jit(solution)/shard_map/ppermute | solution.py:207
  969.7 51.3 %collective-permute-start.43 = (bf16[304,2048]{1,0:T(8,128)(2,1)S(1)}, bf16[304,2048]{1,0:T(8,128)(2,1)}, u32[]{:S(2)}, u32[]{:S(2)}) collective-permute-start(bf16[304,2048]{1,0:T(8,128)(2,1)S(1)} %add_convert_fusion.10), channel_id=1, source_target_pairs={{0,1},{1,2},{4,5},{5,6},{8,9},{9,10},{12,13},{13,14},{16,17},{17,1... | collective-permute-start | bytes 3735560 | tf_op jit(solution)/shard_map/ppermute | solution.py:201
  975.2 51.9 %collective-permute-start.9 = (bf16[304,2048]{1,0:T(8,128)(2,1)S(1)}, bf16[304,2048]{1,0:T(8,128)(2,1)S(1)}, u32[]{:S(2)}, u32[]{:S(2)}) collective-permute-start(bf16[304,2048]{1,0:T(8,128)(2,1)S(1)} %copy-done.82), channel_id=1, source_target_pairs={{3,2},{7,6},{11,10},{15,14},{19,18},{23,22},{27,26},{31,30}} | collective-permute-start | bytes 3735560 | tf_op jit(solution)/shard_map/ppermute | solution.py:207
  977.7 69.9 %collective-permute-start.7 = (bf16[304,2048]{1,0:T(8,128)(2,1)S(1)}, bf16[304,2048]{1,0:T(8,128)(2,1)}, u32[]{:S(2)}, u32[]{:S(2)}) collective-permute-start(bf16[304,2048]{1,0:T(8,128)(2,1)S(1)} %add_convert_fusion.24), channel_id=1, source_target_pairs={{0,1},{1,2},{4,5},{5,6},{8,9},{9,10},{12,13},{13,14},{16,17},{17,1... | collective-permute-start | bytes 3735560 | tf_op jit(solution)/shard_map/ppermute | solution.py:201
  994.3 57.3 %collective-permute-start.21 = (bf16[304,2048]{1,0:T(8,128)(2,1)S(1)}, bf16[304,2048]{1,0:T(8,128)(2,1)S(1)}, u32[]{:S(2)}, u32[]{:S(2)}) collective-permute-start(bf16[304,2048]{1,0:T(8,128)(2,1)S(1)} %get-tuple-element.341), channel_id=1, source_target_pairs={{3,2},{7,6},{11,10},{15,14},{19,18},{23,22},{27,26},{31,30}} | collective-permute-start | bytes 3735560 | tf_op jit(solution)/shard_map/ppermute | solution.py:207
  995.5 70.9 %collective-permute-start.19 = (bf16[304,2048]{1,0:T(8,128)(2,1)S(1)}, bf16[304,2048]{1,0:T(8,128)(2,1)}, u32[]{:S(2)}, u32[]{:S(2)}) collective-permute-start(bf16[304,2048]{1,0:T(8,128)(2,1)S(1)} %add_convert_fusion.19), channel_id=1, source_target_pairs={{0,1},{1,2},{4,5},{5,6},{8,9},{9,10},{12,13},{13,14},{16,17},{17,1... | collective-permute-start | bytes 3735560 | tf_op jit(solution)/shard_map/ppermute | solution.py:201
  1026.2 54.0 %collective-permute-start.46 = (bf16[304,2048]{1,0:T(8,128)(2,1)}, bf16[304,2048]{1,0:T(8,128)(2,1)S(1)}, u32[]{:S(2)}, u32[]{:S(2)}) collective-permute-start(bf16[304,2048]{1,0:T(8,128)(2,1)} %get-tuple-element.331), channel_id=1, source_target_pairs={{2,1},{3,2},{6,5},{7,6},{10,9},{11,10},{14,13},{15,14},{18,17},{19... | collective-permute-start | bytes 3735560 | tf_op jit(solution)/shard_map/ppermute | solution.py:207
  1050.9 32.6 %collective-permute-start.10 = (bf16[304,2048]{1,0:T(8,128)(2,1)S(1)}, bf16[304,2048]{1,0:T(8,128)(2,1)S(1)}, u32[]{:S(2)}, u32[]{:S(2)}) collective-permute-start(bf16[304,2048]{1,0:T(8,128)(2,1)S(1)} %get-tuple-element.335), channel_id=1, source_target_pairs={{2,1},{3,2},{6,5},{7,6},{10,9},{11,10},{14,13},{15,14},{18,17},{19... | collective-permute-start | bytes 3735560 | tf_op jit(solution)/shard_map/ppermute | solution.py:207
  1070.4 66.1 %collective-permute-start.8 = (bf16[304,2048]{1,0:T(8,128)(2,1)}, bf16[304,2048]{1,0:T(8,128)(2,1)S(1)}, u32[]{:S(2)}, u32[]{:S(2)}) collective-permute-start(bf16[304,2048]{1,0:T(8,128)(2,1)} %get-tuple-element.334), channel_id=1, source_target_pairs={{0,1},{1,2},{2,3},{4,5},{5,6},{6,7},{8,9},{9,10},{10,11},{12,13},{... | collective-permute-start | bytes 3735560 | tf_op jit(solution)/shard_map/ppermute | solution.py:201
  1075.6 54.7 %collective-permute-start.44 = (bf16[304,2048]{1,0:T(8,128)(2,1)}, bf16[304,2048]{1,0:T(8,128)(2,1)S(1)}, u32[]{:S(2)}, u32[]{:S(2)}) collective-permute-start(bf16[304,2048]{1,0:T(8,128)(2,1)} %get-tuple-element.330), channel_id=1, source_target_pairs={{0,1},{1,2},{2,3},{4,5},{5,6},{6,7},{8,9},{9,10},{10,11},{12,13},{... | collective-permute-start | bytes 3735560 | tf_op jit(solution)/shard_map/ppermute | solution.py:201
  1082.3 49.3 %collective-permute-start.47 = (bf16[304,2048]{1,0:T(8,128)(2,1)S(1)}, bf16[304,2048]{1,0:T(8,128)(2,1)S(1)}, u32[]{:S(2)}, u32[]{:S(2)}) collective-permute-start(bf16[304,2048]{1,0:T(8,128)(2,1)S(1)} %add_convert_fusion.7), channel_id=1, source_target_pairs={{1,0},{2,1},{3,2},{5,4},{6,5},{7,6},{9,8},{10,9},{11,10},{13,12},{... | collective-permute-start | bytes 3735560 | tf_op jit(solution)/shard_map/ppermute | solution.py:207
  1084.0 57.1 %collective-permute-start.11 = (bf16[304,2048]{1,0:T(8,128)(2,1)S(1)}, bf16[304,2048]{1,0:T(8,128)(2,1)S(1)}, u32[]{:S(2)}, u32[]{:S(2)}) collective-permute-start(bf16[304,2048]{1,0:T(8,128)(2,1)S(1)} %add_convert_fusion.21), channel_id=1, source_target_pairs={{1,0},{2,1},{3,2},{5,4},{6,5},{7,6},{9,8},{10,9},{11,10},{13,12},{... | collective-permute-start | bytes 3735560 | tf_op jit(solution)/shard_map/ppermute | solution.py:207
  1085.3 62.8 %collective-permute-start.20 = (bf16[304,2048]{1,0:T(8,128)(2,1)}, bf16[304,2048]{1,0:T(8,128)(2,1)S(1)}, u32[]{:S(2)}, u32[]{:S(2)}) collective-permute-start(bf16[304,2048]{1,0:T(8,128)(2,1)} %get-tuple-element.338), channel_id=1, source_target_pairs={{0,1},{1,2},{2,3},{4,5},{5,6},{6,7},{8,9},{9,10},{10,11},{12,13},{... | collective-permute-start | bytes 3735560 | tf_op jit(solution)/shard_map/ppermute | solution.py:201
  1173.5 63.3 %all-to-all-start.9 = ((bf16[304,32,64]{0,2,1:T(8,128)(2,1)}), bf16[304,32,64]{0,2,1:T(8,128)(2,1)}, u32[]{:S(2)}, u32[]{:S(2)}) async-start(bf16[304,32,64]{0,2,1:T(8,128)(2,1)} %bitcast.748), calls=%async_computation.9 | async-start | bytes 3145728 | tf_op jit(solution)/shard_map/all_to_all | solution.py:217
  1236.8 37.1 %all-to-all-start.6 = ((bf16[304,32,64]{0,2,1:T(8,128)(2,1)}), bf16[304,32,64]{0,2,1:T(8,128)(2,1)}, u32[]{:S(2)}, u32[]{:S(2)}) async-start(bf16[304,32,64]{0,2,1:T(8,128)(2,1)} %bitcast.83), calls=%async_computation.6 | async-start | bytes 3145728 | tf_op jit(solution)/shard_map/all_to_all | solution.py:217
  1373.3 73.7 %all-to-all-start.11 = ((bf16[1216,2,128]{2,1,0:T(2,128)(2,1)}), bf16[1216,2,128]{2,1,0:T(2,128)(2,1)}, u32[]{:S(2)}, u32[]{:S(2)}) async-start(bf16[1216,2,128]{2,1,0:T(2,128)(2,1)} %copy.387), calls=%async_computation.11 | async-start | bytes 1245184 | tf_op jit(solution)/shard_map/all_to_all | solution.py:217
  1452.1 266.7 %reduce-scatter.16.cloned.1.call-start = ((), (), s32[]{:S(2)}) async-start(), calls=%async_computation.30 | async-start | bytes 4718592 | tf_op jit(solution)/shard_map/reduce_scatter | solution.py:443
  1475.8 243.7 %reduce-scatter.20.cloned.1.call-start = ((), (), s32[]{:S(2)}) async-start(), calls=%async_computation.32 | async-start | bytes 9437184 | tf_op jit(solution)/shard_map/reduce_scatter | solution.py:456
  1540.7 39.7 %all-to-all-start.10 = ((bf16[4,2,77824]{2,1,0:T(2,128)(2,1)}), bf16[4,2,77824]{2,1,0:T(2,128)(2,1)}, u32[]{:S(2)}, u32[]{:S(2)}) async-start(bf16[4,2,77824]{2,1,0:T(2,128)(2,1)} %reshape.921), calls=%async_computation.10 | async-start | bytes 2490368 | tf_op jit(solution)/shard_map/all_to_all | solution.py:217
  1580.4 33.7 %all-to-all-start.7 = ((bf16[4,2,77824]{2,1,0:T(2,128)(2,1)}), bf16[4,2,77824]{2,1,0:T(2,128)(2,1)}, u32[]{:S(2)}, u32[]{:S(2)}) async-start(bf16[4,2,77824]{2,1,0:T(2,128)(2,1)} %reshape.923), calls=%async_computation.7 | async-start | bytes 2490368 | tf_op jit(solution)/shard_map/all_to_all | solution.py:217
  1585.4 163.8 %reduce-scatter.12.cloned.1.call-start = ((), (), s32[]{:S(2)}) async-start(), calls=%async_computation.28 | async-start | bytes 9437184 | tf_op jit(solution)/shard_map/reduce_scatter | solution.py:435
  1644.0 160.4 %reduce-scatter.28.cloned.1.call-start = ((), (), s32[]{:S(2)}) async-start(), calls=%async_computation.36 | async-start | bytes 589824
  1698.9 128.1 %reduce-scatter.26.cloned.1.call-start = ((), (), s32[]{:S(2)}) async-start(), calls=%async_computation.35 | async-start | bytes 9437184 | tf_op jit(solution)/shard_map/reduce_scatter | solution.py:468
  1718.7 132.4 %reduce-scatter.18.cloned.1.call-start = ((), (), s32[]{:S(2)}) async-start(), calls=%async_computation.31 | async-start | bytes 655360 | tf_op jit(solution)/shard_map/reduce_scatter | solution.py:442
  1719.4 159.4 %reduce-scatter.22.cloned.1.call-start = ((), (), s32[]{:S(2)}) async-start(), calls=%async_computation.33 | async-start | bytes 1310720 | tf_op jit(solution)/shard_map/reduce_scatter | solution.py:455
  1720.0 186.8 %reduce-scatter.14.cloned.1.call-start = ((), (), s32[]{:S(2)}) async-start(), calls=%async_computation.29 | async-start | bytes 1310720 | tf_op jit(solution)/shard_map/reduce_scatter | solution.py:434
  1749.2 275.5 %reduce-scatter.24.cloned.1.call-start = ((), (), s32[]{:S(2)}) async-start(), calls=%async_computation.34 | async-start | bytes 18874368 | tf_op jit(solution)/shard_map/reduce_scatter | solution.py:463
  (164 other events, 4889.4 us)
Sparse Core Ops, SparseCore 0:
  10.1 35.5 all-gather.9
  47.9 28.5 all-gather.13
  78.4 35.9 all-gather.7
  116.1 54.2 all-gather.11
  172.1 55.8 all-gather.15
  230.3 89.7 all-gather.17
  322.5 55.8 all-gather.19
  1475.9 49.7 reduce-scatter.15
  1529.1 71.2 reduce-scatter.19
  1644.1 70.3 reduce-scatter.11
  1718.2 34.0 reduce-scatter.27
  1755.7 71.2 reduce-scatter.25
  1829.3 21.8 reduce-scatter.17
  1853.3 25.5 reduce-scatter.21
  1881.0 25.7 reduce-scatter.13
  1910.2 114.4 reduce-scatter.23

commit v4 on v1

--- a/solution.py
+++ b/solution.py
@@ -296,13 +296,18 @@
         sigmoid_gate = jax.nn.sigmoid(gate_part)
         silu_gate = gate_part * sigmoid_gate
         hidden_state = (silu_gate * up_part).astype(jnp.bfloat16)
-        ffn_branch = line_scatter(
-            jnp.dot(hidden_state, full_down, preferred_element_type=jnp.float32), tensor_count
-        )
+        ffn_branch = lax.psum_scatter(
+            jnp.dot(hidden_state, full_down, preferred_element_type=jnp.float32).astype(
+                jnp.bfloat16
+            ),
+            "tensor",
+            scatter_dimension=0,
+            tiled=True,
+        ).astype(jnp.float32)
         layer_rows = (middle + branch_scale * ffn_branch).astype(jnp.bfloat16)
         upstream = cot_rows.astype(jnp.float32)
         ffn_grad = (branch_scale * upstream).astype(jnp.bfloat16)
-        ffn_grad_all = line_gather(ffn_grad, tensor_count)
+        ffn_grad_all = lax.all_gather(ffn_grad, "tensor", axis=0, tiled=True)
         grad_down = contract_rows(hidden_state, ffn_grad_all)
         hidden_grad = contract_cols(ffn_grad_all, full_down)
         gate_grad = hidden_grad * up_part * sigmoid_gate * (1.0 + gate_part * (1.0 - sigmoid_gate))

time: 2030 us -> 2090 us (1.030)
  waiting for transfers between devices: 682 us -> 830 us
  starting transfers between devices: 281 us -> 193 us
    ppermute x24 -> x18, waiting for transfers between devices: 209 us -> 343 us  [line_scatter(): lax.ppermute(send.astype(jnp.bfloat16), 'tensor', [(i, i + 1) for i in ra...]
    reduce_scatter x1, waiting for transfers between devices: 0.02 us -> 70.3 us  [per_device(): lax.psum_scatter(totals[3].reshape(width, -1).astype(jnp.bfloat16), 'dp',...]
    ppermute x24 -> x18, starting transfers between devices: 130 us -> 66.8 us  [line_scatter(): lax.ppermute(send.astype(jnp.bfloat16), 'tensor', [(i, i + 1) for i in ra...]
    ppermute x24 -> x18, waiting for transfers between devices: 289 us -> 264 us  [line_gather(): lax.ppermute(from_right, 'tensor', [(i, i - 1) for i in range(1, count -...]
    convert_element_type x24 -> x18, other arithmetic: 67.7 us -> 46.3 us  [line_scatter(): send.astype(jnp.bfloat16)]
    ppermute x24 -> x18, waiting for transfers between devices: 101 us -> 83.9 us  [line_gather(): lax.ppermute(from_left, 'tensor', [(i, i + 1) for i in range(step - 1, co...]
    ppermute x24 -> x18, waiting for transfers between devices: 82.7 us -> 69 us  [line_scatter(): lax.ppermute(send.astype(jnp.bfloat16), 'tensor', [(i, i - 1) for i in ra...]
    ppermute x24 -> x18, starting transfers between devices: 87.3 us -> 79 us  [line_gather(): lax.ppermute(from_left, 'tensor', [(i, i + 1) for i in range(step - 1, co...]
  transfers between devices with their start and end apart: 107 -> 87, of which waited for: 49 -> 41; matrix products, arithmetic and copies ran while one was open for 35% -> 42% of each run, Pallas kernels for 0% -> 0%
where the time goes in v4:
time: 2090 us; the launch traced here: 2080 us
  waiting for transfers between devices  830 us (40%)
  matrix products  537 us (26%)
  other arithmetic  257 us (12%)
  starting transfers between devices  193 us (9%)
  local copies, waits for them, and re-layouts  168 us (8%)
  blocking collectives  70.5 us (3%)
  between operations  21.2 us (1%)
    ppermute x18, waiting for transfers between devices, line_scatter(): lax.ppermute(send.astype(jnp.bfloat16), 'tensor', [(i, i + 1) for i in ra...  343 us
    ppermute x18, waiting for transfers between devices, line_gather(): lax.ppermute(from_right, 'tensor', [(i, i - 1) for i in range(1, count -...  264 us
    ppermute x18, waiting for transfers between devices, line_gather(): lax.ppermute(from_left, 'tensor', [(i, i + 1) for i in range(step - 1, co...  83.9 us
    ppermute x18, starting transfers between devices, line_gather(): lax.ppermute(from_left, 'tensor', [(i, i + 1) for i in range(step - 1, co...  79 us
    reduce_scatter x1, waiting for transfers between devices, per_device(): lax.psum_scatter(totals[3].reshape(width, -1).astype(jnp.bfloat16), 'dp',...  70.3 us
    ppermute x18, waiting for transfers between devices, line_scatter(): lax.ppermute(send.astype(jnp.bfloat16), 'tensor', [(i, i - 1) for i in ra...  69 us
    ppermute x18, starting transfers between devices, line_scatter(): lax.ppermute(send.astype(jnp.bfloat16), 'tensor', [(i, i + 1) for i in ra...  66.8 us
    dynamic_update_slice x36, local copies, waits for them, and re-layouts, line_gather(): lax.dynamic_update_slice_in_dim(out, piece, jnp.where(valid, slot, place)...  64.3 us
  transfers between devices with their start and end apart: 87, of which 41 were waited for; matrix products, arithmetic and copies ran while one was open for 42% of the time, Pallas kernels for 0%

profile of v4, /device:TPU:0, one launch (start us, length us, event | category | flops | bytes accessed | tf_op | source)
XLA Modules:
  0.0 2077.0 jit_solution(4824459768735722369)
XLA Ops:
  24.9 10.5 all_gather.24
  58.7 11.7 collective-permute-done
  77.2 19.3 collective-permute-done.18
  132.3 23.7 %collective-permute-done.21 = bf16[304,2048]{1,0:T(8,128)(2,1)} collective-permute-done((bf16[304,2048]{1,0:T(8,128)(2,1)}, bf16[304,2048]{1,0:T(8,128)(2,1)}, u32[]{:S(2)}, u32[]{:S(2)}) %collective-permute-start.21) | collective-permute-done | bytes 1245216 | tf_op jit(solution)/shard_map/ppermute | solution.py:178
  168.4 14.1 collective-permute-done.5
  208.0 18.2 fusion.12
  226.2 12.4 fusion.136
  285.1 10.7 fusion.11
  320.3 12.2 fusion.135
  352.1 18.5 collective-permute-done.24
  378.6 18.7 collective-permute-done.7
  403.5 18.7 collective-permute-done.25
  447.0 13.1 collective-permute-done.8
  460.2 24.1 %collective-permute-done.26 = bf16[304,2048]{1,0:T(8,128)(2,1)} collective-permute-done((bf16[304,2048]{1,0:T(8,128)(2,1)}, bf16[304,2048]{1,0:T(8,128)(2,1)}, u32[]{:S(2)}, u32[]{:S(2)}) %collective-permute-start.26) | collective-permute-done | bytes 1245216 | tf_op jit(solution)/shard_map/ppermute | solution.py:201
  484.2 12.4 collective-permute-done.29
  504.3 19.8 collective-permute-start.30
  532.7 18.1 collective-permute-done.30
  557.6 17.6 collective-permute-done.12
  600.9 31.3 %collective-permute-done.33 = bf16[304,2048]{1,0:T(8,128)(2,1)} collective-permute-done((bf16[304,2048]{1,0:T(8,128)(2,1)}, bf16[304,2048]{1,0:T(8,128)(2,1)}, u32[]{:S(2)}, u32[]{:S(2)}) %collective-permute-start.33) | collective-permute-done | bytes 1245216 | tf_op jit(solution)/shard_map/ppermute | solution.py:178
  634.2 82.2 %collective-permute-done.15 = bf16[304,2048]{1,0:T(8,128)(2,1)} collective-permute-done((bf16[304,2048]{1,0:T(8,128)(2,1)}, bf16[304,2048]{1,0:T(8,128)(2,1)}, u32[]{:S(2)}, u32[]{:S(2)}) %collective-permute-start.15) | collective-permute-done | bytes 1245216 | tf_op jit(solution)/shard_map/ppermute | solution.py:178
  728.8 14.2 collective-permute-done.35
  746.5 20.7 collective-permute-done.17
  769.5 27.3 %fusion.56 = f32[1216,2,2048]{2,0,1:T(8,128)} fusion(bf16[2048,2,2048]{2,0,1:T(8,128)(2,1)} %all-gather.14.cloned.1.call-done, bf16[1216,2048]{1,0:T(8,128)(2,1)} %constant_dynamic-update-slice_fusion.14), kind=kOutput, calls=%fused_computation.102 | convolution fusion | flops 20401094656 | bytes 41680896 | tf_op jit(solution)/shard_map/rd,dcf->rcf/dot_general | solution.py:291
  796.9 25.6 %fusion.70 = (bf16[1216,1,2048]{2,0,1:T(8,128)(2,1)}, bf16[1216,1,2048]{2,0,1:T(8,128)(2,1)}, bf16[1216,2048]{1,0:T(8,128)(2,1)}) fusion(f32[1216,2,2048]{2,0,1:T(8,128)} %fusion.56, bf16[1216,2048]{1,0:T(8,128)(2,1)} %all-gather.20.cloned.1.call-done, bf16[2048,2048]{1,0:T(8,128)(2,1)} %all-gather.16.cloned.1.call-done), kind=kOutput, calls=%fused_computation.116 | convolution fusion | flops 10237902848 | bytes 48234496 | tf_op jit(solution)/shard_map/dot_general | solution.py:162
  822.5 24.7 %convolution_bitcast_fusion = f32[1216,2048]{1,0:T(8,128)S(1)} fusion(bf16[2048,2,2048]{2,0,1:T(8,128)(2,1)} %all-gather.14.cloned.1.call-done, bf16[1216,1,2048]{2,0,1:T(8,128)(2,1)} %get-tuple-element.302, bf16[1216,1,2048]{2,0,1:T(8,128)(2,1)} %get-tuple-element.301), kind=kOutput, calls=%fused_computation.80 | convolution fusion | flops 20406075392 | bytes 36700160 | tf_op jit(solution)/shard_map/rcf,dcf->rd/dot_general | solution.py:320
  855.2 27.3 %fusion.63 = f32[1216,2,2048]{2,0,1:T(8,128)} fusion(bf16[2048,2,2048]{2,0,1:T(8,128)(2,1)} %all-gather.14.cloned.1.call-done, bf16[1216,2048]{1,0:T(8,128)(2,1)} %constant_dynamic-update-slice_fusion.28), kind=kOutput, calls=%fused_computation.109 | convolution fusion | flops 20401094656 | bytes 41680896 | tf_op jit(solution)/shard_map/rd,dcf->rcf/dot_general | solution.py:291
  882.6 25.7 %fusion.69 = (bf16[1216,1,2048]{2,0,1:T(8,128)(2,1)}, bf16[1216,1,2048]{2,0,1:T(8,128)(2,1)}, bf16[1216,2048]{1,0:T(8,128)(2,1)}) fusion(f32[1216,2,2048]{2,0,1:T(8,128)} %fusion.63, bf16[1216,2048]{1,0:T(8,128)(2,1)} %all-gather.18.cloned.1.call-done, bf16[2048,2048]{1,0:T(8,128)(2,1)} %all-gather.16.cloned.1.call-done), kind=kOutput, calls=%fused_computation.115 | convolution fusion | flops 10237902848 | bytes 48234496 | tf_op jit(solution)/shard_map/dot_general | solution.py:162
  908.2 16.3 convolution_convert_fusion.1
  924.6 29.2 %convolution_bitcast_fusion.1 = f32[1216,2048]{1,0:T(8,128)} fusion(bf16[2048,2,2048]{2,0,1:T(8,128)(2,1)} %all-gather.14.cloned.1.call-done, bf16[1216,1,2048]{2,0,1:T(8,128)(2,1)} %get-tuple-element.304, bf16[1216,1,2048]{2,0,1:T(8,128)(2,1)} %get-tuple-element.303), kind=kOutput, calls=%fused_computation.81 | convolution fusion | flops 20406075392 | bytes 36700160 | tf_op jit(solution)/shard_map/rcf,dcf->rd/dot_general | solution.py:320
  963.9 48.8 %collective-permute-done.36 = bf16[304,2048]{1,0:T(8,128)(2,1)S(1)} collective-permute-done((bf16[304,2048]{1,0:T(8,128)(2,1)S(1)}, bf16[304,2048]{1,0:T(8,128)(2,1)S(1)}, u32[]{:S(2)}, u32[]{:S(2)}) %collective-permute-start.36) | collective-permute-done | bytes 1245216 | tf_op jit(solution)/shard_map/ppermute | solution.py:201
  1017.6 45.3 %collective-permute-done.55 = bf16[304,2048]{1,0:T(8,128)(2,1)} collective-permute-done((bf16[304,2048]{1,0:T(8,128)(2,1)S(1)}, bf16[304,2048]{1,0:T(8,128)(2,1)}, u32[]{:S(2)}, u32[]{:S(2)}) %collective-permute-start.55) | collective-permute-done | bytes 1245216 | tf_op jit(solution)/shard_map/ppermute | solution.py:201
  1066.0 22.2 %collective-permute-done.37 = bf16[304,2048]{1,0:T(8,128)(2,1)S(1)} collective-permute-done((bf16[304,2048]{1,0:T(8,128)(2,1)S(1)}, bf16[304,2048]{1,0:T(8,128)(2,1)S(1)}, u32[]{:S(2)}, u32[]{:S(2)}) %collective-permute-start.37) | collective-permute-done | bytes 1245216 | tf_op jit(solution)/shard_map/ppermute | solution.py:201
  1106.6 17.0 collective-permute-done.56
  1123.6 24.5 %collective-permute-done.38 = bf16[304,2048]{1,0:T(8,128)(2,1)} collective-permute-done((bf16[304,2048]{1,0:T(8,128)(2,1)S(1)}, bf16[304,2048]{1,0:T(8,128)(2,1)}, u32[]{:S(2)}, u32[]{:S(2)}) %collective-permute-start.38) | collective-permute-done | bytes 1245216 | tf_op jit(solution)/shard_map/ppermute | solution.py:201
  1148.1 10.0 collective-permute-done.41
  1171.6 21.2 %collective-permute-start.42 = (bf16[304,2048]{1,0:T(8,128)(2,1)S(1)}, bf16[304,2048]{1,0:T(8,128)(2,1)}, u32[]{:S(2)}, u32[]{:S(2)}) collective-permute-start(bf16[304,2048]{1,0:T(8,128)(2,1)S(1)} %get-tuple-element.340), channel_id=1, source_target_pairs={{0,1},{1,2},{2,3},{4,5},{5,6},{6,7},{8,9},{9,10},{10,11},{12,13},{... | collective-permute-start | bytes 3735560 | tf_op jit(solution)/shard_map/ppermute | solution.py:175
  1201.3 18.0 fusion.235
  1226.3 17.0 collective-permute-done.60
  1253.2 17.0 add_convert_fusion.1
  1281.3 23.8 %collective-permute-done.63 = bf16[304,2048]{1,0:T(8,128)(2,1)} collective-permute-done((bf16[304,2048]{1,0:T(8,128)(2,1)}, bf16[304,2048]{1,0:T(8,128)(2,1)}, u32[]{:S(2)}, u32[]{:S(2)}) %collective-permute-start.63) | collective-permute-done | bytes 1245216 | tf_op jit(solution)/shard_map/ppermute | solution.py:178
  1309.9 21.7 %collective-permute-done.47 = bf16[304,2048]{1,0:T(8,128)(2,1)S(1)} collective-permute-done((bf16[304,2048]{1,0:T(8,128)(2,1)S(1)}, bf16[304,2048]{1,0:T(8,128)(2,1)S(1)}, u32[]{:S(2)}, u32[]{:S(2)}) %collective-permute-start.47) | collective-permute-done | bytes 1245216 | tf_op jit(solution)/shard_map/ppermute | solution.py:178
  1335.8 7.5 fusion.143
  1343.3 9.8 fusion.19
  1364.5 21.3 %fusion.3 = (f32[2,4,608]{2,1,0:T(4,128)S(1)}, f32[2,1216,608,4]{2,1,3,0:T(8,128)}) fusion(f32[2,1216,608,4]{2,1,3,0:T(8,128)} %copy-done, f32[2,4,608]{2,1,0:T(4,128)S(1)} %bitcast.656, pred[608,1216]{0,1:T(8,128)(4,1)S(1)} %copy-done.16, bf16[608,2,4,64]{0,3,2,1:T(8,128)(2,1)S(1)} %bitcast.629, bf16[1216,2,128]{2,0,1:T(8,128)(2,1)S(1)} %copy-done.81), kind=kOutput, calls=%fused_computation.8 | convolution fusion | flops 786640128 | bytes 49340416 | tf_op jit(solution)/shard_map/ikrd,jkd->krij/dot_general | solution.py:119
  1385.8 11.0 fusion.125
  1396.8 16.8 fusion.5
  1445.2 11.3 fusion.16
  1467.6 18.1 fusion
  1485.7 17.0 fusion.2
  1512.5 8.5 fusion.118
  1523.9 11.1 fusion.122
  1577.6 15.7 collective-permute-done.66
  1606.0 14.1 collective-permute-done.49
  1626.6 13.1 collective-permute-done.67
  1646.0 14.0 convolution_convert_fusion
  1677.0 29.3 %fusion.42 = f32[2048,2,2048]{0,2,1:T(8,128)} fusion(bf16[1216,1,2048]{2,0,1:T(8,128)(2,1)} %get-tuple-element.302, bf16[1216,1,2048]{2,0,1:T(8,128)(2,1)} %get-tuple-element.301, bf16[1216,2048]{1,0:T(8,128)(2,1)} %constant_dynamic-update-slice_fusion.14), kind=kOutput, calls=%fused_computation.86 | convolution fusion | flops 20421017600 | bytes 48496640 | tf_op jit(solution)/shard_map/rd,rcf->dcf/dot_general | solution.py:316
  1709.9 45.9 %collective-permute-done.68 = bf16[304,2048]{1,0:T(8,128)(2,1)S(1)} collective-permute-done((bf16[304,2048]{1,0:T(8,128)(2,1)}, bf16[304,2048]{1,0:T(8,128)(2,1)S(1)}, u32[]{:S(2)}, u32[]{:S(2)}) %collective-permute-start.68) | collective-permute-done | bytes 1245216 | tf_op jit(solution)/shard_map/ppermute | solution.py:201
  1755.8 46.7 %collective-permute-done.71 = bf16[304,2048]{1,0:T(8,128)(2,1)S(1)} collective-permute-done((bf16[304,2048]{1,0:T(8,128)(2,1)S(1)}, bf16[304,2048]{1,0:T(8,128)(2,1)S(1)}, u32[]{:S(2)}, u32[]{:S(2)}) %collective-permute-start.71) | collective-permute-done | bytes 1245216 | tf_op jit(solution)/shard_map/ppermute | solution.py:207
  1808.5 20.8 psum.14
  1830.4 30.6 %add_convert_fusion = bf16[2048,2,2048]{0,2,1:T(8,128)(2,1)} fusion(f32[2048,2,2048]{0,2,1:T(8,128)} %fusion.42, bf16[1216,1,2048]{2,0,1:T(8,128)(2,1)} %get-tuple-element.304, bf16[1216,1,2048]{2,0,1:T(8,128)(2,1)} %get-tuple-element.303, bf16[1216,2048]{1,0:T(8,128)(2,1)} %constant_dynamic-update-slice_fusion.28), kind=kOutput, calls=%fused_computation | convolution fusion | flops 20437794816 | bytes 65273856 | tf_op jit(solution)/shard_map/rd,rcf->dcf/dot_general | solution.py:316
  1873.8 8.0 multiply_reduce_fusion.8
  1911.8 70.3 %reduce-scatter.21.cloned.1.call-done = bf16[256,4096]{0,1:T(8,128)(2,1)} async-done(((bf16[2048,4096]{0,1:T(8,128)(2,1)}), bf16[256,4096]{0,1:T(8,128)(2,1)}) %reduce-scatter.21.cloned.1.call-update) | async-done | bytes 2097168 | tf_op jit(solution)/shard_map/reduce_scatter | solution.py:395
  1988.5 18.5 multiply_reduce_fusion
  2013.1 39.2 %psum.15 = f32[2,7]{1,0:T(2,128)S(1)} all-reduce(f32[2,7]{1,0:T(2,128)S(1)} %pad_maximum_fusion.26), channel_id=1, replica_groups=mesh['dp'=8,'tensor'=4] {'dp','tensor'}, use_global_device_ids=true, to_apply=%region_51.52 | all-reduce | flops 14 | bytes 112 | tf_op jit(solution)/shard_map/psum | solution.py:430
  (734 shorter events, 652.9 us)
Async XLA Ops:
  7.2 178.9 %all-gather.8.cloned.1.call-start = ((), (), s32[]{:S(2)}) async-start(), calls=%async_computation.8 | async-start | bytes 1179648 | tf_op jit(solution)/shard_map/all_gather | solution.py:245
  8.9 184.4 %all-gather.10.cloned.1.call-start = ((), (), s32[]{:S(2)}) async-start(), calls=%async_computation.9 | async-start | bytes 2359296 | tf_op jit(solution)/shard_map/all_gather | solution.py:244
  11.7 237.5 %all-gather.12.cloned.1.call-start = ((), (), s32[]{:S(2)}) async-start(), calls=%async_computation.10 | async-start | bytes 2359296 | tf_op jit(solution)/shard_map/all_gather | solution.py:246
  14.3 755.2 %all-gather.14.cloned.1.call-start = ((), (), s32[]{:S(2)}) async-start(), calls=%async_computation.11 | async-start | bytes 18874368 | tf_op jit(solution)/shard_map/all_gather | solution.py:247
  20.2 776.7 %all-gather.20.cloned.1.call-start = ((), (), s32[]{:S(2)}) async-start(), calls=%async_computation.16 | async-start | bytes 6225920 | tf_op jit(solution)/shard_map/all_gather | solution.py:310
  24.2 772.6 %all-gather.16.cloned.1.call-start = ((), (), s32[]{:S(2)}) async-start(), calls=%async_computation.12 | async-start | bytes 9437184 | tf_op jit(solution)/shard_map/all_gather | solution.py:248
  44.7 51.8 %collective-permute-start.18 = (bf16[304,2048]{1,0:T(8,128)(2,1)}, bf16[304,2048]{1,0:T(8,128)(2,1)}, u32[]{:S(2)}, u32[]{:S(2)}) collective-permute-start(bf16[304,2048]{1,0:T(8,128)(2,1)} %get-tuple-element.342), channel_id=1, source_target_pairs={{0,1},{1,2},{2,3},{4,5},{5,6},{6,7},{8,9},{9,10},{10,11},{12,13},{... | collective-permute-start | bytes 3735560 | tf_op jit(solution)/shard_map/ppermute | solution.py:175
  50.4 52.2 %collective-permute-start.19 = (bf16[304,2048]{1,0:T(8,128)(2,1)}, bf16[304,2048]{1,0:T(8,128)(2,1)}, u32[]{:S(2)}, u32[]{:S(2)}) collective-permute-start(bf16[304,2048]{1,0:T(8,128)(2,1)} %get-tuple-element.342), channel_id=1, source_target_pairs={{1,0},{2,1},{3,2},{5,4},{6,5},{7,6},{9,8},{10,9},{11,10},{13,12},{... | collective-permute-start | bytes 3735560 | tf_op jit(solution)/shard_map/ppermute | solution.py:178
  53.9 828.7 %all-gather.18.cloned.1.call-start = ((), (), s32[]{:S(2)}) async-start(), calls=%async_computation.15 | async-start | bytes 6225920 | tf_op jit(solution)/shard_map/all_gather | solution.py:310
  70.4 53.2 %collective-permute-start.2 = (bf16[304,2048]{1,0:T(8,128)(2,1)}, bf16[304,2048]{1,0:T(8,128)(2,1)}, u32[]{:S(2)}, u32[]{:S(2)}) collective-permute-start(bf16[304,2048]{1,0:T(8,128)(2,1)} %collective-permute-done), channel_id=1, source_target_pairs={{1,2},{2,3},{5,6},{6,7},{9,10},{10,11},{13,14},{14,15},{17,18},{18... | collective-permute-start | bytes 3735560 | tf_op jit(solution)/shard_map/ppermute | solution.py:175
  75.9 53.4 %collective-permute-start.3 = (bf16[304,2048]{1,0:T(8,128)(2,1)}, bf16[304,2048]{1,0:T(8,128)(2,1)}, u32[]{:S(2)}, u32[]{:S(2)}) collective-permute-start(bf16[304,2048]{1,0:T(8,128)(2,1)} %collective-permute-done.1), channel_id=1, source_target_pairs={{1,0},{2,1},{5,4},{6,5},{9,8},{10,9},{13,12},{14,13},{17,16},{18,1... | collective-permute-start | bytes 3735560 | tf_op jit(solution)/shard_map/ppermute | solution.py:178
  102.6 53.4 %collective-permute-start.21 = (bf16[304,2048]{1,0:T(8,128)(2,1)}, bf16[304,2048]{1,0:T(8,128)(2,1)}, u32[]{:S(2)}, u32[]{:S(2)}) collective-permute-start(bf16[304,2048]{1,0:T(8,128)(2,1)} %collective-permute-done.19), channel_id=1, source_target_pairs={{1,0},{2,1},{5,4},{6,5},{9,8},{10,9},{13,12},{14,13},{17,16},{18,1... | collective-permute-start | bytes 3735560 | tf_op jit(solution)/shard_map/ppermute | solution.py:178
  129.2 53.3 %collective-permute-start.5 = (bf16[304,2048]{1,0:T(8,128)(2,1)}, bf16[304,2048]{1,0:T(8,128)(2,1)S(1)}, u32[]{:S(2)}, u32[]{:S(2)}) collective-permute-start(bf16[304,2048]{1,0:T(8,128)(2,1)} %collective-permute-done.3), channel_id=1, source_target_pairs={{1,0},{5,4},{9,8},{13,12},{17,16},{21,20},{25,24},{29,28}} | collective-permute-start | bytes 3735560 | tf_op jit(solution)/shard_map/ppermute | solution.py:178
  130.5 128.6 %collective-permute-start.22 = (bf16[304,2048]{1,0:T(8,128)(2,1)}, bf16[304,2048]{1,0:T(8,128)(2,1)}, u32[]{:S(2)}, u32[]{:S(2)}) collective-permute-start(bf16[304,2048]{1,0:T(8,128)(2,1)} %collective-permute-done.20), channel_id=1, source_target_pairs={{2,3},{6,7},{10,11},{14,15},{18,19},{22,23},{26,27},{30,31}} | collective-permute-start | bytes 3735560 | tf_op jit(solution)/shard_map/ppermute | solution.py:175
  155.9 105.8 %collective-permute-start.23 = (bf16[304,2048]{1,0:T(8,128)(2,1)}, bf16[304,2048]{1,0:T(8,128)(2,1)}, u32[]{:S(2)}, u32[]{:S(2)}) collective-permute-start(bf16[304,2048]{1,0:T(8,128)(2,1)} %collective-permute-done.21), channel_id=1, source_target_pairs={{1,0},{5,4},{9,8},{13,12},{17,16},{21,20},{25,24},{29,28}} | collective-permute-start | bytes 3735560 | tf_op jit(solution)/shard_map/ppermute | solution.py:178
  256.1 89.6 %collective-permute-start.6 = (bf16[304,2048]{1,0:T(8,128)(2,1)}, bf16[304,2048]{1,0:T(8,128)(2,1)}, u32[]{:S(2)}, u32[]{:S(2)}) collective-permute-start(bf16[304,2048]{1,0:T(8,128)(2,1)} %get-tuple-element.325), channel_id=1, source_target_pairs={{0,1},{4,5},{8,9},{12,13},{16,17},{20,21},{24,25},{28,29}} | collective-permute-start | bytes 3735560 | tf_op jit(solution)/shard_map/ppermute | solution.py:201
  348.1 49.2 %collective-permute-start.7 = (bf16[304,2048]{1,0:T(8,128)(2,1)S(1)}, bf16[304,2048]{1,0:T(8,128)(2,1)}, u32[]{:S(2)}, u32[]{:S(2)}) collective-permute-start(bf16[304,2048]{1,0:T(8,128)(2,1)S(1)} %add_convert_fusion.29), channel_id=1, source_target_pairs={{0,1},{1,2},{4,5},{5,6},{8,9},{9,10},{12,13},{13,14},{16,17},{17,1... | collective-permute-start | bytes 3735560 | tf_op jit(solution)/shard_map/ppermute | solution.py:201
  350.4 53.1 %collective-permute-start.27 = (bf16[304,2048]{1,0:T(8,128)(2,1)}, bf16[304,2048]{1,0:T(8,128)(2,1)}, u32[]{:S(2)}, u32[]{:S(2)}) collective-permute-start(bf16[304,2048]{1,0:T(8,128)(2,1)} %get-tuple-element.330), channel_id=1, source_target_pairs={{3,2},{7,6},{11,10},{15,14},{19,18},{23,22},{27,26},{31,30}} | collective-permute-start | bytes 3735560 | tf_op jit(solution)/shard_map/ppermute | solution.py:207
  373.1 49.1 %collective-permute-start.25 = (bf16[304,2048]{1,0:T(8,128)(2,1)S(1)}, bf16[304,2048]{1,0:T(8,128)(2,1)}, u32[]{:S(2)}, u32[]{:S(2)}) collective-permute-start(bf16[304,2048]{1,0:T(8,128)(2,1)S(1)} %add_convert_fusion.24), channel_id=1, source_target_pairs={{0,1},{1,2},{4,5},{5,6},{8,9},{9,10},{12,13},{13,14},{16,17},{17,1... | collective-permute-start | bytes 3735560 | tf_op jit(solution)/shard_map/ppermute | solution.py:201
  433.2 51.1 %collective-permute-start.26 = (bf16[304,2048]{1,0:T(8,128)(2,1)}, bf16[304,2048]{1,0:T(8,128)(2,1)}, u32[]{:S(2)}, u32[]{:S(2)}) collective-permute-start(bf16[304,2048]{1,0:T(8,128)(2,1)} %get-tuple-element.327), channel_id=1, source_target_pairs={{0,1},{1,2},{2,3},{4,5},{5,6},{6,7},{8,9},{9,10},{10,11},{12,13},{... | collective-permute-start | bytes 3735560 | tf_op jit(solution)/shard_map/ppermute | solution.py:201
  445.7 50.9 %collective-permute-start.29 = (bf16[304,2048]{1,0:T(8,128)(2,1)}, bf16[304,2048]{1,0:T(8,128)(2,1)}, u32[]{:S(2)}, u32[]{:S(2)}) collective-permute-start(bf16[304,2048]{1,0:T(8,128)(2,1)} %add_convert_fusion.21), channel_id=1, source_target_pairs={{1,0},{2,1},{3,2},{5,4},{6,5},{7,6},{9,8},{10,9},{11,10},{13,12},{... | collective-permute-start | bytes 3735560 | tf_op jit(solution)/shard_map/ppermute | solution.py:207
  504.3 46.5 %collective-permute-start.30 = (bf16[304,2048]{1,0:T(8,128)(2,1)S(1)}, bf16[304,2048]{1,0:T(8,128)(2,1)}, u32[]{:S(2)}, u32[]{:S(2)}) collective-permute-start(bf16[304,2048]{1,0:T(8,128)(2,1)S(1)} %get-tuple-element.384), channel_id=1, source_target_pairs={{0,1},{1,2},{2,3},{4,5},{5,6},{6,7},{8,9},{9,10},{10,11},{12,13},{... | collective-permute-start | bytes 3735560 | tf_op jit(solution)/shard_map/ppermute | solution.py:175
  525.4 49.8 %collective-permute-start.12 = (bf16[304,2048]{1,0:T(8,128)(2,1)S(1)}, bf16[304,2048]{1,0:T(8,128)(2,1)}, u32[]{:S(2)}, u32[]{:S(2)}) collective-permute-start(bf16[304,2048]{1,0:T(8,128)(2,1)S(1)} %get-tuple-element.383), channel_id=1, source_target_pairs={{0,1},{1,2},{2,3},{4,5},{5,6},{6,7},{8,9},{9,10},{10,11},{12,13},{... | collective-permute-start | bytes 3735560 | tf_op jit(solution)/shard_map/ppermute | solution.py:175
  531.4 51.6 %collective-permute-start.13 = (bf16[304,2048]{1,0:T(8,128)(2,1)S(1)}, bf16[304,2048]{1,0:T(8,128)(2,1)}, u32[]{:S(2)}, u32[]{:S(2)}) collective-permute-start(bf16[304,2048]{1,0:T(8,128)(2,1)S(1)} %get-tuple-element.383), channel_id=1, source_target_pairs={{1,0},{2,1},{3,2},{5,4},{6,5},{7,6},{9,8},{10,9},{11,10},{13,12},{... | collective-permute-start | bytes 3735560 | tf_op jit(solution)/shard_map/ppermute | solution.py:178
  550.8 46.9 %collective-permute-start.32 = (bf16[304,2048]{1,0:T(8,128)(2,1)}, bf16[304,2048]{1,0:T(8,128)(2,1)}, u32[]{:S(2)}, u32[]{:S(2)}) collective-permute-start(bf16[304,2048]{1,0:T(8,128)(2,1)} %collective-permute-done.30), channel_id=1, source_target_pairs={{1,2},{2,3},{5,6},{6,7},{9,10},{10,11},{13,14},{14,15},{17,18},{18... | collective-permute-start | bytes 3735560 | tf_op jit(solution)/shard_map/ppermute | solution.py:175
  556.4 75.8 %collective-permute-start.33 = (bf16[304,2048]{1,0:T(8,128)(2,1)}, bf16[304,2048]{1,0:T(8,128)(2,1)}, u32[]{:S(2)}, u32[]{:S(2)}) collective-permute-start(bf16[304,2048]{1,0:T(8,128)(2,1)} %collective-permute-done.31), channel_id=1, source_target_pairs={{1,0},{2,1},{5,4},{6,5},{9,8},{10,9},{13,12},{14,13},{17,16},{18,1... | collective-permute-start | bytes 3735560 | tf_op jit(solution)/shard_map/ppermute | solution.py:178
  575.3 58.2 %collective-permute-start.14 = (bf16[304,2048]{1,0:T(8,128)(2,1)}, bf16[304,2048]{1,0:T(8,128)(2,1)}, u32[]{:S(2)}, u32[]{:S(2)}) collective-permute-start(bf16[304,2048]{1,0:T(8,128)(2,1)} %collective-permute-done.12), channel_id=1, source_target_pairs={{1,2},{2,3},{5,6},{6,7},{9,10},{10,11},{13,14},{14,15},{17,18},{18... | collective-permute-start | bytes 3735560 | tf_op jit(solution)/shard_map/ppermute | solution.py:175
  583.0 133.4 %collective-permute-start.15 = (bf16[304,2048]{1,0:T(8,128)(2,1)}, bf16[304,2048]{1,0:T(8,128)(2,1)}, u32[]{:S(2)}, u32[]{:S(2)}) collective-permute-start(bf16[304,2048]{1,0:T(8,128)(2,1)} %collective-permute-done.13), channel_id=1, source_target_pairs={{1,0},{2,1},{5,4},{6,5},{9,8},{10,9},{13,12},{14,13},{17,16},{18,1... | collective-permute-start | bytes 3735560 | tf_op jit(solution)/shard_map/ppermute | solution.py:178
  584.3 581.2 %reduce-scatter.11.cloned.1.call-start = ((), (), s32[]{:S(2)}) async-start(), calls=%async_computation.13 | async-start | bytes 6225920 | tf_op jit(solution)/shard_map/reduce_scatter | solution.py:299
  597.7 129.9 %collective-permute-start.34 = (bf16[304,2048]{1,0:T(8,128)(2,1)}, bf16[304,2048]{1,0:T(8,128)(2,1)S(1)}, u32[]{:S(2)}, u32[]{:S(2)}) collective-permute-start(bf16[304,2048]{1,0:T(8,128)(2,1)} %collective-permute-done.32), channel_id=1, source_target_pairs={{2,3},{6,7},{10,11},{14,15},{18,19},{22,23},{26,27},{30,31}} | collective-permute-start | bytes 3735560 | tf_op jit(solution)/shard_map/ppermute | solution.py:175
  632.2 110.8 %collective-permute-start.35 = (bf16[304,2048]{1,0:T(8,128)(2,1)}, bf16[304,2048]{1,0:T(8,128)(2,1)S(1)}, u32[]{:S(2)}, u32[]{:S(2)}) collective-permute-start(bf16[304,2048]{1,0:T(8,128)(2,1)} %collective-permute-done.33), channel_id=1, source_target_pairs={{1,0},{5,4},{9,8},{13,12},{17,16},{21,20},{25,24},{29,28}} | collective-permute-start | bytes 3735560 | tf_op jit(solution)/shard_map/ppermute | solution.py:178
  633.5 111.8 %collective-permute-start.16 = (bf16[304,2048]{1,0:T(8,128)(2,1)}, bf16[304,2048]{1,0:T(8,128)(2,1)S(1)}, u32[]{:S(2)}, u32[]{:S(2)}) collective-permute-start(bf16[304,2048]{1,0:T(8,128)(2,1)} %collective-permute-done.14), channel_id=1, source_target_pairs={{2,3},{6,7},{10,11},{14,15},{18,19},{22,23},{26,27},{30,31}} | collective-permute-start | bytes 3735560 | tf_op jit(solution)/shard_map/ppermute | solution.py:175
  716.5 50.8 %collective-permute-start.17 = (bf16[304,2048]{1,0:T(8,128)(2,1)}, bf16[304,2048]{1,0:T(8,128)(2,1)S(1)}, u32[]{:S(2)}, u32[]{:S(2)}) collective-permute-start(bf16[304,2048]{1,0:T(8,128)(2,1)} %collective-permute-done.15), channel_id=1, source_target_pairs={{1,0},{5,4},{9,8},{13,12},{17,16},{21,20},{25,24},{29,28}} | collective-permute-start | bytes 3735560 | tf_op jit(solution)/shard_map/ppermute | solution.py:178
  852.6 106.5 %collective-permute-start.54 = (bf16[304,2048]{1,0:T(8,128)(2,1)}, bf16[304,2048]{1,0:T(8,128)(2,1)}, u32[]{:S(2)}, u32[]{:S(2)}) collective-permute-start(bf16[304,2048]{1,0:T(8,128)(2,1)} %get-tuple-element.313), channel_id=1, source_target_pairs={{0,1},{4,5},{8,9},{12,13},{16,17},{20,21},{24,25},{28,29}} | collective-permute-start | bytes 3735560 | tf_op jit(solution)/shard_map/ppermute | solution.py:201
  924.5 949.3 %reduce-scatter.23.cloned.1.call-start = ((), (), s32[]{:S(2)}) async-start(), calls=%async_computation.21 | async-start | bytes 9437184 | tf_op jit(solution)/shard_map/reduce_scatter | solution.py:400
  956.7 56.0 %collective-permute-start.36 = (bf16[304,2048]{1,0:T(8,128)(2,1)S(1)}, bf16[304,2048]{1,0:T(8,128)(2,1)S(1)}, u32[]{:S(2)}, u32[]{:S(2)}) collective-permute-start(bf16[304,2048]{1,0:T(8,128)(2,1)S(1)} %get-tuple-element.321), channel_id=1, source_target_pairs={{0,1},{4,5},{8,9},{12,13},{16,17},{20,21},{24,25},{28,29}} | collective-permute-start | bytes 3735560 | tf_op jit(solution)/shard_map/ppermute | solution.py:201
  958.4 59.2 %collective-permute-start.57 = (bf16[304,2048]{1,0:T(8,128)(2,1)S(1)}, bf16[304,2048]{1,0:T(8,128)(2,1)S(1)}, u32[]{:S(2)}, u32[]{:S(2)}) collective-permute-start(bf16[304,2048]{1,0:T(8,128)(2,1)S(1)} %copy-done.85), channel_id=1, source_target_pairs={{3,2},{7,6},{11,10},{15,14},{19,18},{23,22},{27,26},{31,30}} | collective-permute-start | bytes 3735560 | tf_op jit(solution)/shard_map/ppermute | solution.py:207
  960.8 102.0 %collective-permute-start.55 = (bf16[304,2048]{1,0:T(8,128)(2,1)S(1)}, bf16[304,2048]{1,0:T(8,128)(2,1)}, u32[]{:S(2)}, u32[]{:S(2)}) collective-permute-start(bf16[304,2048]{1,0:T(8,128)(2,1)S(1)} %add_convert_fusion.11), channel_id=1, source_target_pairs={{0,1},{1,2},{4,5},{5,6},{8,9},{9,10},{12,13},{13,14},{16,17},{17,1... | collective-permute-start | bytes 3735560 | tf_op jit(solution)/shard_map/ppermute | solution.py:201
  963.2 102.8 %collective-permute-start.39 = (bf16[304,2048]{1,0:T(8,128)(2,1)S(1)}, bf16[304,2048]{1,0:T(8,128)(2,1)S(1)}, u32[]{:S(2)}, u32[]{:S(2)}) collective-permute-start(bf16[304,2048]{1,0:T(8,128)(2,1)S(1)} %get-tuple-element.322), channel_id=1, source_target_pairs={{3,2},{7,6},{11,10},{15,14},{19,18},{23,22},{27,26},{31,30}} | collective-permute-start | bytes 3735560 | tf_op jit(solution)/shard_map/ppermute | solution.py:207
  1013.1 75.1 %collective-permute-start.37 = (bf16[304,2048]{1,0:T(8,128)(2,1)S(1)}, bf16[304,2048]{1,0:T(8,128)(2,1)S(1)}, u32[]{:S(2)}, u32[]{:S(2)}) collective-permute-start(bf16[304,2048]{1,0:T(8,128)(2,1)S(1)} %add_convert_fusion.19), channel_id=1, source_target_pairs={{0,1},{1,2},{4,5},{5,6},{8,9},{9,10},{12,13},{13,14},{16,17},{17,1... | collective-permute-start | bytes 3735560 | tf_op jit(solution)/shard_map/ppermute | solution.py:201
  1095.9 52.1 %collective-permute-start.38 = (bf16[304,2048]{1,0:T(8,128)(2,1)S(1)}, bf16[304,2048]{1,0:T(8,128)(2,1)}, u32[]{:S(2)}, u32[]{:S(2)}) collective-permute-start(bf16[304,2048]{1,0:T(8,128)(2,1)S(1)} %get-tuple-element.319), channel_id=1, source_target_pairs={{0,1},{1,2},{2,3},{4,5},{5,6},{6,7},{8,9},{9,10},{10,11},{12,13},{... | collective-permute-start | bytes 3735560 | tf_op jit(solution)/shard_map/ppermute | solution.py:201
  1102.0 46.1 %collective-permute-start.59 = (bf16[304,2048]{1,0:T(8,128)(2,1)S(1)}, bf16[304,2048]{1,0:T(8,128)(2,1)S(1)}, u32[]{:S(2)}, u32[]{:S(2)}) collective-permute-start(bf16[304,2048]{1,0:T(8,128)(2,1)S(1)} %add_convert_fusion.8), channel_id=1, source_target_pairs={{1,0},{2,1},{3,2},{5,4},{6,5},{7,6},{9,8},{10,9},{11,10},{13,12},{... | collective-permute-start | bytes 3735560 | tf_op jit(solution)/shard_map/ppermute | solution.py:207
  1103.9 54.1 %collective-permute-start.41 = (bf16[304,2048]{1,0:T(8,128)(2,1)S(1)}, bf16[304,2048]{1,0:T(8,128)(2,1)S(1)}, u32[]{:S(2)}, u32[]{:S(2)}) collective-permute-start(bf16[304,2048]{1,0:T(8,128)(2,1)S(1)} %add_convert_fusion.16), channel_id=1, source_target_pairs={{1,0},{2,1},{3,2},{5,4},{6,5},{7,6},{9,8},{10,9},{11,10},{13,12},{... | collective-permute-start | bytes 3735560 | tf_op jit(solution)/shard_map/ppermute | solution.py:207
  1171.6 47.9 %collective-permute-start.42 = (bf16[304,2048]{1,0:T(8,128)(2,1)S(1)}, bf16[304,2048]{1,0:T(8,128)(2,1)}, u32[]{:S(2)}, u32[]{:S(2)}) collective-permute-start(bf16[304,2048]{1,0:T(8,128)(2,1)S(1)} %get-tuple-element.340), channel_id=1, source_target_pairs={{0,1},{1,2},{2,3},{4,5},{5,6},{6,7},{8,9},{9,10},{10,11},{12,13},{... | collective-permute-start | bytes 3735560 | tf_op jit(solution)/shard_map/ppermute | solution.py:175
  1194.1 49.2 %collective-permute-start.60 = (bf16[304,2048]{1,0:T(8,128)(2,1)S(1)}, bf16[304,2048]{1,0:T(8,128)(2,1)}, u32[]{:S(2)}, u32[]{:S(2)}) collective-permute-start(bf16[304,2048]{1,0:T(8,128)(2,1)S(1)} %get-tuple-element.339), channel_id=1, source_target_pairs={{0,1},{1,2},{2,3},{4,5},{5,6},{6,7},{8,9},{9,10},{10,11},{12,13},{... | collective-permute-start | bytes 3735560 | tf_op jit(solution)/shard_map/ppermute | solution.py:175
  1200.0 51.7 %collective-permute-start.61 = (bf16[304,2048]{1,0:T(8,128)(2,1)S(1)}, bf16[304,2048]{1,0:T(8,128)(2,1)}, u32[]{:S(2)}, u32[]{:S(2)}) collective-permute-start(bf16[304,2048]{1,0:T(8,128)(2,1)S(1)} %get-tuple-element.339), channel_id=1, source_target_pairs={{1,0},{2,1},{3,2},{5,4},{6,5},{7,6},{9,8},{10,9},{11,10},{13,12},{... | collective-permute-start | bytes 3735560 | tf_op jit(solution)/shard_map/ppermute | solution.py:178
  1219.5 56.4 %collective-permute-start.44 = (bf16[304,2048]{1,0:T(8,128)(2,1)}, bf16[304,2048]{1,0:T(8,128)(2,1)S(1)}, u32[]{:S(2)}, u32[]{:S(2)}) collective-permute-start(bf16[304,2048]{1,0:T(8,128)(2,1)} %collective-permute-done.42), channel_id=1, source_target_pairs={{1,2},{2,3},{5,6},{6,7},{9,10},{10,11},{13,14},{14,15},{17,18},{18... | collective-permute-start | bytes 3735560 | tf_op jit(solution)/shard_map/ppermute | solution.py:175
  1225.0 53.3 %collective-permute-start.45 = (bf16[304,2048]{1,0:T(8,128)(2,1)}, bf16[304,2048]{1,0:T(8,128)(2,1)S(1)}, u32[]{:S(2)}, u32[]{:S(2)}) collective-permute-start(bf16[304,2048]{1,0:T(8,128)(2,1)} %collective-permute-done.43), channel_id=1, source_target_pairs={{1,0},{2,1},{5,4},{6,5},{9,8},{10,9},{13,12},{14,13},{17,16},{18,1... | collective-permute-start | bytes 3735560 | tf_op jit(solution)/shard_map/ppermute | solution.py:178
  1251.7 53.4 %collective-permute-start.63 = (bf16[304,2048]{1,0:T(8,128)(2,1)}, bf16[304,2048]{1,0:T(8,128)(2,1)}, u32[]{:S(2)}, u32[]{:S(2)}) collective-permute-start(bf16[304,2048]{1,0:T(8,128)(2,1)} %collective-permute-done.61), channel_id=1, source_target_pairs={{1,0},{2,1},{5,4},{6,5},{9,8},{10,9},{13,12},{14,13},{17,16},{18,1... | collective-permute-start | bytes 3735560 | tf_op jit(solution)/shard_map/ppermute | solution.py:178
  1270.3 611.6 %reduce-scatter.17.cloned.1.call-start = ((), (), s32[]{:S(2)}) async-start(), calls=%async_computation.18 | async-start | bytes 1179648 | tf_op jit(solution)/shard_map/reduce_scatter | solution.py:387
  1278.3 53.4 %collective-permute-start.47 = (bf16[304,2048]{1,0:T(8,128)(2,1)S(1)}, bf16[304,2048]{1,0:T(8,128)(2,1)S(1)}, u32[]{:S(2)}, u32[]{:S(2)}) collective-permute-start(bf16[304,2048]{1,0:T(8,128)(2,1)S(1)} %collective-permute-done.45), channel_id=1, source_target_pairs={{1,0},{5,4},{9,8},{13,12},{17,16},{21,20},{25,24},{29,28}} | collective-permute-start | bytes 3735560 | tf_op jit(solution)/shard_map/ppermute | solution.py:178
  1279.6 155.7 %collective-permute-start.64 = (bf16[304,2048]{1,0:T(8,128)(2,1)}, bf16[304,2048]{1,0:T(8,128)(2,1)}, u32[]{:S(2)}, u32[]{:S(2)}) collective-permute-start(bf16[304,2048]{1,0:T(8,128)(2,1)} %collective-permute-done.62), channel_id=1, source_target_pairs={{2,3},{6,7},{10,11},{14,15},{18,19},{22,23},{26,27},{30,31}} | collective-permute-start | bytes 3735560 | tf_op jit(solution)/shard_map/ppermute | solution.py:175
  1305.1 131.7 %collective-permute-start.65 = (bf16[304,2048]{1,0:T(8,128)(2,1)}, bf16[304,2048]{1,0:T(8,128)(2,1)}, u32[]{:S(2)}, u32[]{:S(2)}) collective-permute-start(bf16[304,2048]{1,0:T(8,128)(2,1)} %collective-permute-done.63), channel_id=1, source_target_pairs={{1,0},{5,4},{9,8},{13,12},{17,16},{21,20},{25,24},{29,28}} | collective-permute-start | bytes 3735560 | tf_op jit(solution)/shard_map/ppermute | solution.py:178
  1432.0 140.6 %collective-permute-start.48 = (bf16[304,2048]{1,0:T(8,128)(2,1)}, bf16[304,2048]{1,0:T(8,128)(2,1)}, u32[]{:S(2)}, u32[]{:S(2)}) collective-permute-start(bf16[304,2048]{1,0:T(8,128)(2,1)} %get-tuple-element.317), channel_id=1, source_target_pairs={{0,1},{4,5},{8,9},{12,13},{16,17},{20,21},{24,25},{28,29}} | collective-permute-start | bytes 3735560 | tf_op jit(solution)/shard_map/ppermute | solution.py:201
  1544.3 341.7 %reduce-scatter.15.cloned.1.call-start = ((), (), s32[]{:S(2)}) async-start(), calls=%async_computation.17 | async-start | bytes 2359296 | tf_op jit(solution)/shard_map/reduce_scatter | solution.py:384
  1556.3 332.9 %reduce-scatter.19.cloned.1.call-start = ((), (), s32[]{:S(2)}) async-start(), calls=%async_computation.19 | async-start | bytes 2359296 | tf_op jit(solution)/shard_map/reduce_scatter | solution.py:392
  1567.5 59.1 %collective-permute-start.69 = (bf16[304,2048]{1,0:T(8,128)(2,1)}, bf16[304,2048]{1,0:T(8,128)(2,1)}, u32[]{:S(2)}, u32[]{:S(2)}) collective-permute-start(bf16[304,2048]{1,0:T(8,128)(2,1)} %get-tuple-element.310), channel_id=1, source_target_pairs={{3,2},{7,6},{11,10},{15,14},{19,18},{23,22},{27,26},{31,30}} | collective-permute-start | bytes 3735560 | tf_op jit(solution)/shard_map/ppermute | solution.py:207
  1605.9 295.3 %reduce-scatter.13.cloned.1.call-start = ((), (), s32[]{:S(2)}) async-start(), calls=%async_computation.14 | async-start | bytes 6225920 | tf_op jit(solution)/shard_map/reduce_scatter | solution.py:299
  1660.1 250.1 %reduce-scatter.25.cloned.1.call-start = ((), (), s32[]{:S(2)}) async-start(), calls=%async_computation.22 | async-start | bytes 589824
  1660.1 49.8 %collective-permute-start.50 = (bf16[304,2048]{1,0:T(8,128)(2,1)}, bf16[304,2048]{1,0:T(8,128)(2,1)S(1)}, u32[]{:S(2)}, u32[]{:S(2)}) collective-permute-start(bf16[304,2048]{1,0:T(8,128)(2,1)} %get-tuple-element.315), channel_id=1, source_target_pairs={{0,1},{1,2},{2,3},{4,5},{5,6},{6,7},{8,9},{9,10},{10,11},{12,13},{... | collective-permute-start | bytes 3735560 | tf_op jit(solution)/shard_map/ppermute | solution.py:201
  1665.3 90.5 %collective-permute-start.68 = (bf16[304,2048]{1,0:T(8,128)(2,1)}, bf16[304,2048]{1,0:T(8,128)(2,1)S(1)}, u32[]{:S(2)}, u32[]{:S(2)}) collective-permute-start(bf16[304,2048]{1,0:T(8,128)(2,1)} %get-tuple-element.307), channel_id=1, source_target_pairs={{0,1},{1,2},{2,3},{4,5},{5,6},{6,7},{8,9},{9,10},{10,11},{12,13},{... | collective-permute-start | bytes 3735560 | tf_op jit(solution)/shard_map/ppermute | solution.py:201
  1671.8 84.0 %collective-permute-start.53 = (bf16[304,2048]{1,0:T(8,128)(2,1)S(1)}, bf16[304,2048]{1,0:T(8,128)(2,1)S(1)}, u32[]{:S(2)}, u32[]{:S(2)}) collective-permute-start(bf16[304,2048]{1,0:T(8,128)(2,1)S(1)} %add_convert_fusion.12), channel_id=1, source_target_pairs={{1,0},{2,1},{3,2},{5,4},{6,5},{7,6},{9,8},{10,9},{11,10},{13,12},{... | collective-permute-start | bytes 3735560 | tf_op jit(solution)/shard_map/ppermute | solution.py:207
  1675.3 127.2 %collective-permute-start.71 = (bf16[304,2048]{1,0:T(8,128)(2,1)S(1)}, bf16[304,2048]{1,0:T(8,128)(2,1)S(1)}, u32[]{:S(2)}, u32[]{:S(2)}) collective-permute-start(bf16[304,2048]{1,0:T(8,128)(2,1)S(1)} %add_convert_fusion.4), channel_id=1, source_target_pairs={{1,0},{2,1},{3,2},{5,4},{6,5},{7,6},{9,8},{10,9},{11,10},{13,12},{... | collective-permute-start | bytes 3735560 | tf_op jit(solution)/shard_map/ppermute | solution.py:207
  1830.3 151.8 %reduce-scatter.21.cloned.1.call-start = ((), (), s32[]{:S(2)}) async-start(), calls=%async_computation.20 | async-start | bytes 18874368 | tf_op jit(solution)/shard_map/reduce_scatter | solution.py:395
  (203 other events, 4183.7 us)
Sparse Core Ops, SparseCore 0:
  10.5 26.1 all-gather.7
  39.1 27.7 all-gather.9
  69.4 28.0 all-gather.11
  99.8 89.7 all-gather.13
  191.6 113.7 all-gather.19
  307.1 57.4 all-gather.15
  584.5 131.6 all-gather.17
  924.6 140.6 reduce-scatter.10
  1270.4 72.0 reduce-scatter.22
  1544.4 34.0 reduce-scatter.16
  1582.4 41.1 reduce-scatter.14
  1626.6 41.0 reduce-scatter.18
  1670.7 129.5 reduce-scatter.12
  1830.5 32.1 reduce-scatter.24
  1866.1 115.9 reduce-scatter.20

commit v5 on v1

--- a/solution.py
+++ b/solution.py
@@ -264,7 +264,7 @@
         scale_one = lax.rsqrt(jnp.mean(start_rows * start_rows, axis=1, keepdims=True) + norm_eps)
         hat_one = start_rows * scale_one
         normed_one = (hat_one * gain_values[0][None, :]).astype(jnp.bfloat16)
-        rows_one = line_gather(normed_one, tensor_count)
+        rows_one = yield ("gather", normed_one)
         query_raw = jnp.dot(rows_one, full_query, preferred_element_type=jnp.float32).reshape(
             group_rows, query_heads, HD
         )
@@ -280,14 +280,14 @@
         values = keyval_raw[:, :, HD:].astype(jnp.bfloat16)
         mixed_full, log_totals = attend(queries, key_rows, values, visible, block_rows)
         mixed = mixed_full.astype(jnp.bfloat16).reshape(group_rows, query_heads * HD)
-        attn_branch = line_scatter(
-            jnp.dot(mixed, full_output, preferred_element_type=jnp.float32), tensor_count
+        attn_branch = yield (
+            "scatter", jnp.dot(mixed, full_output, preferred_element_type=jnp.float32)
         )
         middle = start_rows + branch_scale * attn_branch
         scale_two = lax.rsqrt(jnp.mean(middle * middle, axis=1, keepdims=True) + norm_eps)
         hat_two = middle * scale_two
         normed_two = (hat_two * gain_values[1][None, :]).astype(jnp.bfloat16)
-        rows_two = line_gather(normed_two, tensor_count)
+        rows_two = yield ("gather", normed_two)
         gate_up = jnp.einsum(
             "rd,dcf->rcf", rows_two, full_gateup, preferred_element_type=jnp.float32
         )
@@ -296,13 +296,13 @@
         sigmoid_gate = jax.nn.sigmoid(gate_part)
         silu_gate = gate_part * sigmoid_gate
         hidden_state = (silu_gate * up_part).astype(jnp.bfloat16)
-        ffn_branch = line_scatter(
-            jnp.dot(hidden_state, full_down, preferred_element_type=jnp.float32), tensor_count
-        )
-        layer_rows = (middle + branch_scale * ffn_branch).astype(jnp.bfloat16)
         upstream = cot_rows.astype(jnp.float32)
         ffn_grad = (branch_scale * upstream).astype(jnp.bfloat16)
-        ffn_grad_all = line_gather(ffn_grad, tensor_count)
+        ffn_grad_all = yield ("gather", ffn_grad)
+        ffn_branch = yield (
+            "scatter", jnp.dot(hidden_state, full_down, preferred_element_type=jnp.float32)
+        )
+        layer_rows = (middle + branch_scale * ffn_branch).astype(jnp.bfloat16)
         grad_down = contract_rows(hidden_state, ffn_grad_all)
         hidden_grad = contract_cols(ffn_grad_all, full_down)
         gate_grad = hidden_grad * up_part * sigmoid_gate * (1.0 + gate_part * (1.0 - sigmoid_gate))
@@ -311,16 +311,16 @@
         grad_gateup = jnp.einsum(
             "rd,rcf->dcf", rows_two, gateup_grad, preferred_element_type=jnp.float32
         )
-        normed_two_grad = line_scatter(
+        normed_two_grad = yield (
+            "scatter",
             jnp.einsum(
                 "rcf,dcf->rd", gateup_grad, full_gateup, preferred_element_type=jnp.float32
             ),
-            tensor_count,
         )
         middle_back, gain_two = norm_back(normed_two_grad, hat_two, scale_two, gain_values[1])
         middle_grad = upstream + middle_back
         attn_grad = (branch_scale * middle_grad).astype(jnp.bfloat16)
-        attn_grad_all = line_gather(attn_grad, tensor_count)
+        attn_grad_all = yield ("gather", attn_grad)
         grad_output = contract_rows(mixed, attn_grad_all)
         mixed_grad = (
             contract_cols(attn_grad_all, full_output)
@@ -342,12 +342,12 @@
         grad_keyval = jnp.einsum(
             "rd,rhk->dhk", rows_one, keyval_raw_grad, preferred_element_type=jnp.float32
         )
-        normed_one_grad = line_scatter(
+        normed_one_grad = yield (
+            "scatter",
             contract_cols(query_raw_grad, full_query)
             + jnp.einsum(
                 "rhk,dhk->rd", keyval_raw_grad, full_keyval, preferred_element_type=jnp.float32
             ),
-            tensor_count,
         )
         start_back, gain_one = norm_back(normed_one_grad, hat_one, scale_one, gain_values[0])
         input_rows = middle_grad + start_back
@@ -358,19 +358,33 @@
             (grad_query, grad_keyval, grad_output, grad_gateup, grad_down, gain_grad),
         )
 
-    out_list = []
-    grad_list = []
-    totals = None
-    for step_index in range(tokens.shape[0]):
-        layer_rows, input_rows, grads = micro_step(
-            tokens[step_index, 0], cotangent[step_index, 0], cont_lengths[step_index, 0]
-        )
-        out_list.append(layer_rows)
-        grad_list.append(input_rows)
-        if totals is None:
-            totals = grads
-        else:
-            totals = tuple((old_sum + new_term for old_sum, new_term in zip(totals, grads)))
+    streams = [
+        micro_step(tokens[index, 0], cotangent[index, 0], cont_lengths[index, 0])
+        for index in range(tokens.shape[0])
+    ]
+    requests = [next(stream) for stream in streams]
+    finished = [None] * len(streams)
+    previous = None
+    while any(result is None for result in finished):
+        for index, stream in enumerate(streams):
+            if finished[index] is not None:
+                continue
+            kind, value = requests[index]
+            if previous is not None:
+                previous, value = lax.optimization_barrier((previous, value))
+            if kind == "gather":
+                previous = line_gather(value, tensor_count)
+            else:
+                previous = line_scatter(value, tensor_count)
+            try:
+                requests[index] = stream.send(previous)
+            except StopIteration as stop:
+                finished[index] = stop.value
+    out_list = [result[0] for result in finished]
+    grad_list = [result[1] for result in finished]
+    totals = finished[0][2]
+    for result in finished[1:]:
+        totals = tuple((old_sum + new_term for old_sum, new_term in zip(totals, result[2])))
     layer_output = jnp.stack(out_list)[:, None]
     input_grad = jnp.stack(grad_list)[:, None]
     width = totals[0].shape[0]

time: 2030 us -> 2010 us (level)
  waiting for transfers between devices: 682 us -> 763 us
  starting transfers between devices: 281 us -> 229 us
  local copies, waits for them, and re-layouts: 155 us -> 126 us
  blocking collectives: 91.2 us -> 69.8 us
    ppermute x24, waiting for transfers between devices: 209 us -> 258 us  [line_scatter(): lax.ppermute(send.astype(jnp.bfloat16), 'tensor', [(i, i + 1) for i in ra...]
    ppermute x24, waiting for transfers between devices: 101 us -> 60.1 us  [line_gather(): lax.ppermute(from_left, 'tensor', [(i, i + 1) for i in range(step - 1, co...]
    ppermute x24, starting transfers between devices: 87.3 us -> 47.8 us  [line_gather(): lax.ppermute(from_left, 'tensor', [(i, i + 1) for i in range(step - 1, co...]
    ppermute x24, waiting for transfers between devices: 289 us -> 322 us  [line_gather(): lax.ppermute(from_right, 'tensor', [(i, i - 1) for i in range(1, count -...]
    convert_element_type x24, other arithmetic: 67.7 us -> 37.5 us  [line_scatter(): send.astype(jnp.bfloat16)]
    unnamed x12, waiting for transfers between devices: 0.18 us -> 25.6 us
    reduce_scatter x1, waiting for transfers between devices: 0.01 us -> 23.9 us  [per_device(): lax.psum_scatter(totals[2].astype(jnp.bfloat16), 'dp', scatter_dimension=...]
    unnamed x406 -> x396, local copies, waits for them, and re-layouts: 43.4 us -> 29.1 us
  transfers between devices with their start and end apart: 107 -> 107, of which waited for: 49 -> 47; matrix products, arithmetic and copies ran while one was open for 35% -> 42% of each run, Pallas kernels for 0% -> 0%
where the time goes in v5:
time: 2010 us; the launch traced here: 1990 us
  waiting for transfers between devices  763 us (38%)
  matrix products  543 us (27%)
  other arithmetic  242 us (12%)
  starting transfers between devices  229 us (11%)
  local copies, waits for them, and re-layouts  126 us (6%)
  blocking collectives  69.8 us (3%)
  between operations  21.3 us (1%)
    ppermute x24, waiting for transfers between devices, line_gather(): lax.ppermute(from_right, 'tensor', [(i, i - 1) for i in range(1, count -...  322 us
    ppermute x24, waiting for transfers between devices, line_scatter(): lax.ppermute(send.astype(jnp.bfloat16), 'tensor', [(i, i + 1) for i in ra...  258 us
    ppermute x24, starting transfers between devices, line_scatter(): lax.ppermute(send.astype(jnp.bfloat16), 'tensor', [(i, i + 1) for i in ra...  120 us
    ppermute x24, waiting for transfers between devices, line_scatter(): lax.ppermute(send.astype(jnp.bfloat16), 'tensor', [(i, i - 1) for i in ra...  72.4 us
    dot_general x6, matrix products, contract_cols(): lax.dot_general(left, right, (((1,), (1,)), ((), ())), preferred_element_...  65.8 us
    dot_general x4, matrix products, attend_back(): jnp.einsum('ikrd,jkd->krij', grad_block, values[:stop], preferred_element...  64 us
    dot_general x2, matrix products, micro_step(): jnp.einsum('rd,rcf->dcf', rows_two, gateup_grad, preferred_element_type=j...  61.2 us
    ppermute x24, waiting for transfers between devices, line_gather(): lax.ppermute(from_left, 'tensor', [(i, i + 1) for i in range(step - 1, co...  60.1 us
  transfers between devices with their start and end apart: 107, of which 47 were waited for; matrix products, arithmetic and copies ran while one was open for 42% of the time, Pallas kernels for 0%

profile of v5, /device:TPU:0, one launch (start us, length us, event | category | flops | bytes accessed | tf_op | source)
XLA Modules:
  0.0 1994.2 jit_solution(1930092159429925587)
XLA Ops:
  41.1 18.8 collective-permute-done
  76.6 19.4 collective-permute-done.3
  113.1 15.1 collective-permute-done.5
  167.0 13.0 fusion.136
  198.8 18.6 collective-permute-done.9
  225.3 23.2 %collective-permute-done.11 = bf16[304,2048]{1,0:T(8,128)(2,1)S(1)} collective-permute-done((bf16[304,2048]{1,0:T(8,128)(2,1)}, bf16[304,2048]{1,0:T(8,128)(2,1)S(1)}, u32[]{:S(2)}, u32[]{:S(2)}) %collective-permute-start.11) | collective-permute-done | bytes 1245216 | tf_op jit(solution)/shard_map/ppermute | solution.py:178
  291.6 13.8 fusion.135
  351.6 23.4 %collective-permute-done.17 = bf16[304,2048]{1,0:T(8,128)(2,1)S(1)} collective-permute-done((bf16[304,2048]{1,0:T(8,128)(2,1)S(1)}, bf16[304,2048]{1,0:T(8,128)(2,1)S(1)}, u32[]{:S(2)}, u32[]{:S(2)}) %collective-permute-start.17) | collective-permute-done | bytes 1245216 | tf_op jit(solution)/shard_map/ppermute | solution.py:207
  382.3 21.9 %collective-permute-done.18 = bf16[304,2048]{1,0:T(8,128)(2,1)S(1)} collective-permute-done((bf16[304,2048]{1,0:T(8,128)(2,1)S(1)}, bf16[304,2048]{1,0:T(8,128)(2,1)S(1)}, u32[]{:S(2)}, u32[]{:S(2)}) %collective-permute-start.18) | collective-permute-done | bytes 1245216 | tf_op jit(solution)/shard_map/ppermute | solution.py:201
  409.1 20.8 %collective-permute-done.19 = bf16[304,2048]{1,0:T(8,128)(2,1)S(1)} collective-permute-done((bf16[304,2048]{1,0:T(8,128)(2,1)S(1)}, bf16[304,2048]{1,0:T(8,128)(2,1)S(1)}, u32[]{:S(2)}, u32[]{:S(2)}) %collective-permute-start.19) | collective-permute-done | bytes 1245216 | tf_op jit(solution)/shard_map/ppermute | solution.py:201
  438.4 17.7 collective-permute-done.20
  456.1 21.7 %collective-permute-done.23 = bf16[304,2048]{1,0:T(8,128)(2,1)S(1)} collective-permute-done((bf16[304,2048]{1,0:T(8,128)(2,1)S(1)}, bf16[304,2048]{1,0:T(8,128)(2,1)S(1)}, u32[]{:S(2)}, u32[]{:S(2)}) %collective-permute-start.23) | collective-permute-done | bytes 1245216 | tf_op jit(solution)/shard_map/ppermute | solution.py:207
  489.8 15.1 collective-permute-done.24
  520.9 22.3 %collective-permute-done.27 = bf16[304,2048]{1,0:T(8,128)(2,1)} collective-permute-done((bf16[304,2048]{1,0:T(8,128)(2,1)}, bf16[304,2048]{1,0:T(8,128)(2,1)}, u32[]{:S(2)}, u32[]{:S(2)}) %collective-permute-start.27) | collective-permute-done | bytes 1245216 | tf_op jit(solution)/shard_map/ppermute | solution.py:178
  551.6 17.7 collective-permute-done.29
  572.6 13.0 collective-permute-done.30
  586.3 13.3 collective-permute-done.31
  602.3 27.8 %collective-permute-done.33 = bf16[304,2048]{1,0:T(8,128)(2,1)S(1)} collective-permute-done((bf16[304,2048]{1,0:T(8,128)(2,1)S(1)}, bf16[304,2048]{1,0:T(8,128)(2,1)S(1)}, u32[]{:S(2)}, u32[]{:S(2)}) %collective-permute-start.33) | collective-permute-done | bytes 1245216 | tf_op jit(solution)/shard_map/ppermute | solution.py:178
  632.8 26.5 %collective-permute-done.35 = bf16[304,2048]{1,0:T(8,128)(2,1)S(1)} collective-permute-done((bf16[304,2048]{1,0:T(8,128)(2,1)S(1)}, bf16[304,2048]{1,0:T(8,128)(2,1)S(1)}, u32[]{:S(2)}, u32[]{:S(2)}) %collective-permute-start.35) | collective-permute-done | bytes 1245216 | tf_op jit(solution)/shard_map/ppermute | solution.py:178
  662.4 13.0 collective-permute-done.36
  676.2 17.0 collective-permute-done.37
  695.2 28.6 %collective-permute-done.39 = bf16[304,2048]{1,0:T(8,128)(2,1)S(1)} collective-permute-done((bf16[304,2048]{1,0:T(8,128)(2,1)S(1)}, bf16[304,2048]{1,0:T(8,128)(2,1)S(1)}, u32[]{:S(2)}, u32[]{:S(2)}) %collective-permute-start.39) | collective-permute-done | bytes 1245216 | tf_op jit(solution)/shard_map/ppermute | solution.py:178
  733.6 21.0 %collective-permute-done.41 = bf16[304,2048]{1,0:T(8,128)(2,1)S(1)} collective-permute-done((bf16[304,2048]{1,0:T(8,128)(2,1)S(1)}, bf16[304,2048]{1,0:T(8,128)(2,1)S(1)}, u32[]{:S(2)}, u32[]{:S(2)}) %collective-permute-start.41) | collective-permute-done | bytes 1245216 | tf_op jit(solution)/shard_map/ppermute | solution.py:178
  759.7 27.3 %fusion.59 = f32[1216,2,2048]{2,0,1:T(8,128)} fusion(bf16[2048,2,2048]{2,0,1:T(8,128)(2,1)} %all-gather.12.cloned.1.call-done, bf16[1216,2048]{1,0:T(8,128)(2,1)} %copy-done.60), kind=kOutput, calls=%fused_computation.103 | convolution fusion | flops 20401094656 | bytes 41680896 | tf_op jit(solution)/shard_map/rd,dcf->rcf/dot_general | solution.py:291
  789.1 25.6 %fusion.69 = (bf16[1216,1,2048]{2,0,1:T(8,128)(2,1)}, bf16[1216,1,2048]{2,0,1:T(8,128)(2,1)}, bf16[1216,2048]{1,0:T(8,128)(2,1)}) fusion(f32[1216,2,2048]{2,0,1:T(8,128)} %fusion.59, bf16[1216,2048]{1,0:T(8,128)(2,1)} %constant_dynamic-update-slice_fusion.21, bf16[2048,2048]{1,0:T(8,128)(2,1)} %all-gather.14.cloned.1.call-done), kind=kOutput, calls=%fused_computation.113 | convolution fusion | flops 10237902848 | bytes 48234496 | tf_op jit(solution)/shard_map/dot_general | solution.py:162
  816.7 14.5 fusion.234
  841.8 13.3 collective-permute-done.47
  860.4 13.6 collective-permute-done.48
  878.9 25.9 %fusion.56 = f32[1216,2,2048]{2,0,1:T(8,128)} fusion(bf16[2048,2,2048]{2,0,1:T(8,128)(2,1)} %all-gather.12.cloned.1.call-done, bf16[1216,2048]{1,0:T(8,128)(2,1)S(1)} %bitcast.619), kind=kOutput, calls=%fused_computation.100 | convolution fusion | flops 20401094656 | bytes 41680896 | tf_op jit(solution)/shard_map/rd,dcf->rcf/dot_general | solution.py:291
  907.7 25.6 %fusion.70 = (bf16[1216,1,2048]{2,0,1:T(8,128)(2,1)}, bf16[1216,1,2048]{2,0,1:T(8,128)(2,1)}, bf16[1216,2048]{1,0:T(8,128)(2,1)}) fusion(f32[1216,2,2048]{2,0,1:T(8,128)} %fusion.56, bf16[1216,2048]{1,0:T(8,128)(2,1)} %copy-done.62, bf16[2048,2048]{1,0:T(8,128)(2,1)} %all-gather.14.cloned.1.call-done), kind=kOutput, calls=%fused_computation.114 | convolution fusion | flops 10237902848 | bytes 48234496 | tf_op jit(solution)/shard_map/dot_general | solution.py:162
  939.7 13.2 fusion.235
  972.7 22.4 %collective-permute-done.54 = bf16[304,2048]{1,0:T(8,128)(2,1)S(1)} collective-permute-done((bf16[304,2048]{1,0:T(8,128)(2,1)S(1)}, bf16[304,2048]{1,0:T(8,128)(2,1)S(1)}, u32[]{:S(2)}, u32[]{:S(2)}) %collective-permute-start.54) | collective-permute-done | bytes 1245216 | tf_op jit(solution)/shard_map/ppermute | solution.py:201
  999.9 24.1 %collective-permute-done.55 = bf16[304,2048]{1,0:T(8,128)(2,1)S(1)} collective-permute-done((bf16[304,2048]{1,0:T(8,128)(2,1)S(1)}, bf16[304,2048]{1,0:T(8,128)(2,1)S(1)}, u32[]{:S(2)}, u32[]{:S(2)}) %collective-permute-start.55) | collective-permute-done | bytes 1245216 | tf_op jit(solution)/shard_map/ppermute | solution.py:201
  1032.9 28.2 %convolution_bitcast_fusion.1 = f32[1216,2048]{1,0:T(8,128)} fusion(bf16[2048,2,2048]{2,0,1:T(8,128)(2,1)} %all-gather.12.cloned.1.call-done, bf16[1216,1,2048]{2,0,1:T(8,128)(2,1)} %get-tuple-element.339, bf16[1216,1,2048]{2,0,1:T(8,128)(2,1)} %get-tuple-element.338), kind=kOutput, calls=%fused_computation.81 | convolution fusion | flops 20406075392 | bytes 36700160 | tf_op jit(solution)/shard_map/rcf,dcf->rd/dot_general | solution.py:316
  1070.7 15.9 collective-permute-start.60
  1087.3 24.5 %collective-permute-done.60 = bf16[304,2048]{1,0:T(8,128)(2,1)S(1)} collective-permute-done((bf16[304,2048]{1,0:T(8,128)(2,1)S(1)}, bf16[304,2048]{1,0:T(8,128)(2,1)S(1)}, u32[]{:S(2)}, u32[]{:S(2)}) %collective-permute-start.60) | collective-permute-done | bytes 1245216 | tf_op jit(solution)/shard_map/ppermute | solution.py:201
  1116.7 14.3 collective-permute-done.61
  1139.6 28.1 %convolution_bitcast_fusion = f32[1216,2048]{1,0:T(8,128)} fusion(bf16[2048,2,2048]{2,0,1:T(8,128)(2,1)} %all-gather.12.cloned.1.call-done, bf16[1216,1,2048]{2,0,1:T(8,128)(2,1)} %get-tuple-element.337, bf16[1216,1,2048]{2,0,1:T(8,128)(2,1)} %get-tuple-element.336), kind=kOutput, calls=%fused_computation.80 | convolution fusion | flops 20406075392 | bytes 36700160 | tf_op jit(solution)/shard_map/rcf,dcf->rd/dot_general | solution.py:316
  1174.3 17.0 collective-permute-start.66
  1192.1 21.1 %collective-permute-done.66 = bf16[304,2048]{1,0:T(8,128)(2,1)S(1)} collective-permute-done((bf16[304,2048]{1,0:T(8,128)(2,1)S(1)}, bf16[304,2048]{1,0:T(8,128)(2,1)S(1)}, u32[]{:S(2)}, u32[]{:S(2)}) %collective-permute-start.66) | collective-permute-done | bytes 1245216 | tf_op jit(solution)/shard_map/ppermute | solution.py:201
  1218.1 14.3 collective-permute-done.67
  1249.6 16.3 fusion.237
  1265.9 19.0 collective-permute-done.71
  1294.8 16.9 add_convert_fusion.1
  1315.3 30.4 %fusion.42 = f32[2048,2,2048]{0,2,1:T(8,128)} fusion(bf16[1216,1,2048]{2,0,1:T(8,128)(2,1)} %get-tuple-element.337, bf16[1216,1,2048]{2,0,1:T(8,128)(2,1)} %get-tuple-element.336, bf16[1216,2048]{1,0:T(8,128)(2,1)} %copy-done.61), kind=kOutput, calls=%fused_computation.84 | convolution fusion | flops 20421017600 | bytes 48496640 | tf_op jit(solution)/shard_map/rd,rcf->dcf/dot_general | solution.py:311
  1348.7 30.8 %add_convert_fusion = bf16[2048,2,2048]{0,2,1:T(8,128)(2,1)} fusion(f32[2048,2,2048]{0,2,1:T(8,128)} %fusion.42, bf16[1216,1,2048]{2,0,1:T(8,128)(2,1)} %get-tuple-element.339, bf16[1216,1,2048]{2,0,1:T(8,128)(2,1)} %get-tuple-element.338, bf16[1216,2048]{1,0:T(8,128)(2,1)} %copy-done.60), kind=kOutput, calls=%fused_computation | convolution fusion | flops 20437794816 | bytes 65273856 | tf_op jit(solution)/shard_map/rd,rcf->dcf/dot_general | solution.py:311
  1387.6 15.3 collective-permute-done.77
  1428.9 21.8 %fusion.3 = (f32[2,4,608]{2,1,0:T(4,128)S(1)}, f32[2,1216,608,4]{2,1,3,0:T(8,128)}) fusion(f32[2,1216,608,4]{2,1,3,0:T(8,128)} %copy-done.1, f32[2,4,608]{2,1,0:T(4,128)S(1)} %bitcast.661, pred[608,1216]{0,1:T(8,128)(4,1)S(1)} %copy-done.20, bf16[608,2,4,64]{0,3,2,1:T(8,128)(2,1)S(1)} %bitcast.633, bf16[1216,2,128]{2,0,1:T(8,128)(2,1)S(1)} %copy-done.98), kind=kOutput, calls=%fused_computation.8 | convolution fusion | flops 786640128 | bytes 49340416 | tf_op jit(solution)/shard_map/ikrd,jkd->krij/dot_general | solution.py:119
  1450.7 11.7 fusion.125
  1474.9 18.7 fusion.5
  1514.1 12.2 collective-permute-done.81
  1531.8 13.3 collective-permute-done.83
  1557.0 11.2 fusion.16
  1578.1 21.1 %fusion = (f32[2,4,608]{2,1,0:T(4,128)S(1)}, f32[2,1216,608,4]{2,1,3,0:T(8,128)}) fusion(f32[2,1216,608,4]{2,1,3,0:T(8,128)} %copy-done, f32[2,4,608]{2,1,0:T(4,128)S(1)} %bitcast.655, pred[608,1216]{0,1:T(8,128)(4,1)S(1)} %copy-done.19, bf16[608,2,4,64]{0,3,2,1:T(8,128)(2,1)S(1)} %bitcast.631, bf16[1216,2,128]{2,0,1:T(8,128)(2,1)S(1)} %copy-done.96), kind=kOutput, calls=%fused_computation.3 | convolution fusion | flops 786640128 | bytes 49340416 | tf_op jit(solution)/shard_map/ikrd,jkd->krij/dot_general | solution.py:119
  1599.2 21.1 %fusion.2 = bf16[2,4,608,1216]{2,3,1,0:T(8,128)(2,1)} fusion(f32[2,1216,608,4]{2,1,3,0:T(8,128)} %get-tuple-element.448, f32[2,1216,608,4]{2,1,3,0:T(8,128)} %copy-done, f32[2,4,608]{2,1,0:T(4,128)S(1)} %get-tuple-element.447, f32[2,4,608]{2,1,0:T(4,128)S(1)} %bitcast.656, pred[608,1216]{0,1:T(8,128)(4,1)S(1)} %copy-done.19), kind=kLoop, calls=%fused_computation.5 | loop fusion | flops 35487744 | bytes 59924480 | tf_op jit(solution)/shard_map/convert_element_type | solution.py:123
  1651.7 11.2 fusion.122
  1662.9 11.9 collective-permute-done.85
  1702.3 10.7 collective-permute-done.86
  1735.9 11.5 collective-permute-done.90
  1804.4 17.7 multiply_reduce_fusion
  1828.5 23.9 %reduce-scatter.13.cloned.1.call-done = bf16[512,256]{1,0:T(8,128)(2,1)} async-done(((bf16[512,2048]{1,0:T(8,128)(2,1)}), bf16[512,256]{1,0:T(8,128)(2,1)}) %reduce-scatter.13.cloned.1.call-update) | async-done | bytes 262160 | tf_op jit(solution)/shard_map/reduce_scatter | solution.py:401
  1867.0 19.9 psum.14
  1894.7 25.5 %reduce-scatter.19.cloned.1.call-done = bf16[256,2]{1,0:T(8,128)(2,1)} async-done(((bf16[2048,2]{1,0:T(8,128)(2,1)}), bf16[256,2]{1,0:T(8,128)(2,1)}) %reduce-scatter.19.cloned.1.call-update) | async-done | bytes 1040
  1931.9 39.5 %psum.15 = f32[2,7]{1,0:T(2,128)S(1)} all-reduce(f32[2,7]{1,0:T(2,128)S(1)} %pad_maximum_fusion.26), channel_id=1, replica_groups=mesh['dp'=8,'tensor'=4] {'dp','tensor'}, use_global_device_ids=true, to_apply=%region_49.50 | all-reduce | flops 14 | bytes 112 | tf_op jit(solution)/shard_map/psum | solution.py:439
  (827 shorter events, 729.6 us)
Async XLA Ops:
  7.2 128.6 %all-gather.6.cloned.1.call-start = ((), (), s32[]{:S(2)}) async-start(), calls=%async_computation.6 | async-start | bytes 1179648 | tf_op jit(solution)/shard_map/all_gather | solution.py:245
  9.1 133.8 %all-gather.8.cloned.1.call-start = ((), (), s32[]{:S(2)}) async-start(), calls=%async_computation.7 | async-start | bytes 2359296 | tf_op jit(solution)/shard_map/all_gather | solution.py:244
  11.8 182.0 %all-gather.10.cloned.1.call-start = ((), (), s32[]{:S(2)}) async-start(), calls=%async_computation.8 | async-start | bytes 2359296 | tf_op jit(solution)/shard_map/all_gather | solution.py:246
  14.4 745.2 %all-gather.12.cloned.1.call-start = ((), (), s32[]{:S(2)}) async-start(), calls=%async_computation.9 | async-start | bytes 18874368 | tf_op jit(solution)/shard_map/all_gather | solution.py:247
  28.9 31.1 %collective-permute-start = (bf16[304,2048]{1,0:T(8,128)(2,1)}, bf16[304,2048]{1,0:T(8,128)(2,1)}, u32[]{:S(2)}, u32[]{:S(2)}) collective-permute-start(bf16[304,2048]{1,0:T(8,128)(2,1)} %get-tuple-element.385), channel_id=1, source_target_pairs={{0,1},{1,2},{2,3},{4,5},{5,6},{6,7},{8,9},{9,10},{10,11},{12,13},{... | collective-permute-start | bytes 3735560 | tf_op jit(solution)/shard_map/ppermute | solution.py:175
  33.5 31.5 %collective-permute-start.1 = (bf16[304,2048]{1,0:T(8,128)(2,1)}, bf16[304,2048]{1,0:T(8,128)(2,1)}, u32[]{:S(2)}, u32[]{:S(2)}) collective-permute-start(bf16[304,2048]{1,0:T(8,128)(2,1)} %get-tuple-element.385), channel_id=1, source_target_pairs={{1,0},{2,1},{3,2},{5,4},{6,5},{7,6},{9,8},{10,9},{11,10},{13,12},{... | collective-permute-start | bytes 3735560 | tf_op jit(solution)/shard_map/ppermute | solution.py:178
  38.4 750.7 %all-gather.14.cloned.1.call-start = ((), (), s32[]{:S(2)}) async-start(), calls=%async_computation.10 | async-start | bytes 9437184 | tf_op jit(solution)/shard_map/all_gather | solution.py:248
  65.1 30.9 %collective-permute-start.3 = (bf16[304,2048]{1,0:T(8,128)(2,1)}, bf16[304,2048]{1,0:T(8,128)(2,1)}, u32[]{:S(2)}, u32[]{:S(2)}) collective-permute-start(bf16[304,2048]{1,0:T(8,128)(2,1)} %collective-permute-done.1), channel_id=1, source_target_pairs={{1,0},{2,1},{5,4},{6,5},{9,8},{10,9},{13,12},{14,13},{17,16},{18,1... | collective-permute-start | bytes 3735560 | tf_op jit(solution)/shard_map/ppermute | solution.py:178
  68.5 41.9 %collective-permute-start.4 = (bf16[304,2048]{1,0:T(8,128)(2,1)}, bf16[304,2048]{1,0:T(8,128)(2,1)}, u32[]{:S(2)}, u32[]{:S(2)}) collective-permute-start(bf16[304,2048]{1,0:T(8,128)(2,1)} %collective-permute-done.2), channel_id=1, source_target_pairs={{2,3},{6,7},{10,11},{14,15},{18,19},{22,23},{26,27},{30,31}} | collective-permute-start | bytes 3735560 | tf_op jit(solution)/shard_map/ppermute | solution.py:175
  95.9 32.3 %collective-permute-start.5 = (bf16[304,2048]{1,0:T(8,128)(2,1)}, bf16[304,2048]{1,0:T(8,128)(2,1)S(1)}, u32[]{:S(2)}, u32[]{:S(2)}) collective-permute-start(bf16[304,2048]{1,0:T(8,128)(2,1)} %collective-permute-done.3), channel_id=1, source_target_pairs={{1,0},{5,4},{9,8},{13,12},{17,16},{21,20},{25,24},{29,28}} | collective-permute-start | bytes 3735560 | tf_op jit(solution)/shard_map/ppermute | solution.py:178
  131.8 53.1 %collective-permute-start.6 = (bf16[304,2048]{1,0:T(8,128)(2,1)}, bf16[304,2048]{1,0:T(8,128)(2,1)}, u32[]{:S(2)}, u32[]{:S(2)}) collective-permute-start(bf16[304,2048]{1,0:T(8,128)(2,1)} %get-tuple-element.164), channel_id=1, source_target_pairs={{0,1},{1,2},{2,3},{4,5},{5,6},{6,7},{8,9},{9,10},{10,11},{12,13},{... | collective-permute-start | bytes 3735560 | tf_op jit(solution)/shard_map/ppermute | solution.py:175
  134.4 51.3 %collective-permute-start.7 = (bf16[304,2048]{1,0:T(8,128)(2,1)}, bf16[304,2048]{1,0:T(8,128)(2,1)}, u32[]{:S(2)}, u32[]{:S(2)}) collective-permute-start(bf16[304,2048]{1,0:T(8,128)(2,1)} %get-tuple-element.164), channel_id=1, source_target_pairs={{1,0},{2,1},{3,2},{5,4},{6,5},{7,6},{9,8},{10,9},{11,10},{13,12},{... | collective-permute-start | bytes 3735560 | tf_op jit(solution)/shard_map/ppermute | solution.py:178
  185.7 31.7 %collective-permute-start.9 = (bf16[304,2048]{1,0:T(8,128)(2,1)}, bf16[304,2048]{1,0:T(8,128)(2,1)}, u32[]{:S(2)}, u32[]{:S(2)}) collective-permute-start(bf16[304,2048]{1,0:T(8,128)(2,1)} %collective-permute-done.7), channel_id=1, source_target_pairs={{1,0},{2,1},{5,4},{6,5},{9,8},{10,9},{13,12},{14,13},{17,16},{18,1... | collective-permute-start | bytes 3735560 | tf_op jit(solution)/shard_map/ppermute | solution.py:178
  191.9 31.9 %collective-permute-start.10 = (bf16[304,2048]{1,0:T(8,128)(2,1)S(1)}, bf16[304,2048]{1,0:T(8,128)(2,1)}, u32[]{:S(2)}, u32[]{:S(2)}) collective-permute-start(bf16[304,2048]{1,0:T(8,128)(2,1)S(1)} %collective-permute-done.8), channel_id=1, source_target_pairs={{2,3},{6,7},{10,11},{14,15},{18,19},{22,23},{26,27},{30,31}} | collective-permute-start | bytes 3735560 | tf_op jit(solution)/shard_map/ppermute | solution.py:175
  217.4 31.0 %collective-permute-start.11 = (bf16[304,2048]{1,0:T(8,128)(2,1)}, bf16[304,2048]{1,0:T(8,128)(2,1)S(1)}, u32[]{:S(2)}, u32[]{:S(2)}) collective-permute-start(bf16[304,2048]{1,0:T(8,128)(2,1)} %collective-permute-done.9), channel_id=1, source_target_pairs={{1,0},{5,4},{9,8},{13,12},{17,16},{21,20},{25,24},{29,28}} | collective-permute-start | bytes 3735560 | tf_op jit(solution)/shard_map/ppermute | solution.py:178
  251.9 35.4 %collective-permute-start.12 = (bf16[304,2048]{1,0:T(8,128)(2,1)}, bf16[304,2048]{1,0:T(8,128)(2,1)}, u32[]{:S(2)}, u32[]{:S(2)}) collective-permute-start(bf16[304,2048]{1,0:T(8,128)(2,1)} %get-tuple-element.372), channel_id=1, source_target_pairs={{0,1},{4,5},{8,9},{12,13},{16,17},{20,21},{24,25},{28,29}} | collective-permute-start | bytes 3735560 | tf_op jit(solution)/shard_map/ppermute | solution.py:201
  254.5 50.9 %collective-permute-start.15 = (bf16[304,2048]{1,0:T(8,128)(2,1)}, bf16[304,2048]{1,0:T(8,128)(2,1)}, u32[]{:S(2)}, u32[]{:S(2)}) collective-permute-start(bf16[304,2048]{1,0:T(8,128)(2,1)} %get-tuple-element.373), channel_id=1, source_target_pairs={{3,2},{7,6},{11,10},{15,14},{19,18},{23,22},{27,26},{31,30}} | collective-permute-start | bytes 3735560 | tf_op jit(solution)/shard_map/ppermute | solution.py:207
  330.8 44.1 %collective-permute-start.17 = (bf16[304,2048]{1,0:T(8,128)(2,1)S(1)}, bf16[304,2048]{1,0:T(8,128)(2,1)S(1)}, u32[]{:S(2)}, u32[]{:S(2)}) collective-permute-start(bf16[304,2048]{1,0:T(8,128)(2,1)S(1)} %add_convert_fusion.34), channel_id=1, source_target_pairs={{1,0},{2,1},{3,2},{5,4},{6,5},{7,6},{9,8},{10,9},{11,10},{13,12},{... | collective-permute-start | bytes 3735560 | tf_op jit(solution)/shard_map/ppermute | solution.py:207
  437.1 40.7 %collective-permute-start.23 = (bf16[304,2048]{1,0:T(8,128)(2,1)S(1)}, bf16[304,2048]{1,0:T(8,128)(2,1)S(1)}, u32[]{:S(2)}, u32[]{:S(2)}) collective-permute-start(bf16[304,2048]{1,0:T(8,128)(2,1)S(1)} %add_convert_fusion.30), channel_id=1, source_target_pairs={{1,0},{2,1},{3,2},{5,4},{6,5},{7,6},{9,8},{10,9},{11,10},{13,12},{... | collective-permute-start | bytes 3735560 | tf_op jit(solution)/shard_map/ppermute | solution.py:207
  517.0 33.0 %collective-permute-start.28 = (bf16[304,2048]{1,0:T(8,128)(2,1)}, bf16[304,2048]{1,0:T(8,128)(2,1)}, u32[]{:S(2)}, u32[]{:S(2)}) collective-permute-start(bf16[304,2048]{1,0:T(8,128)(2,1)} %collective-permute-done.26), channel_id=1, source_target_pairs={{2,3},{6,7},{10,11},{14,15},{18,19},{22,23},{26,27},{30,31}} | collective-permute-start | bytes 3735560 | tf_op jit(solution)/shard_map/ppermute | solution.py:175
  520.9 1248.7 %reduce-scatter.17.cloned.1.call-start = ((), (), s32[]{:S(2)}) async-start(), calls=%async_computation.15 | async-start | bytes 9437184 | tf_op jit(solution)/shard_map/reduce_scatter | solution.py:409
  571.3 28.3 %collective-permute-start.31 = (bf16[304,2048]{1,0:T(8,128)(2,1)S(1)}, bf16[304,2048]{1,0:T(8,128)(2,1)S(1)}, u32[]{:S(2)}, u32[]{:S(2)}) collective-permute-start(bf16[304,2048]{1,0:T(8,128)(2,1)S(1)} %get-tuple-element.168), channel_id=1, source_target_pairs={{1,0},{2,1},{3,2},{5,4},{6,5},{7,6},{9,8},{10,9},{11,10},{13,12},{... | collective-permute-start | bytes 3735560 | tf_op jit(solution)/shard_map/ppermute | solution.py:178
  599.6 30.4 %collective-permute-start.33 = (bf16[304,2048]{1,0:T(8,128)(2,1)S(1)}, bf16[304,2048]{1,0:T(8,128)(2,1)S(1)}, u32[]{:S(2)}, u32[]{:S(2)}) collective-permute-start(bf16[304,2048]{1,0:T(8,128)(2,1)S(1)} %collective-permute-done.31), channel_id=1, source_target_pairs={{1,0},{2,1},{5,4},{6,5},{9,8},{10,9},{13,12},{14,13},{17,16},{18,1... | collective-permute-start | bytes 3735560 | tf_op jit(solution)/shard_map/ppermute | solution.py:178
  600.9 31.7 %collective-permute-start.34 = (bf16[304,2048]{1,0:T(8,128)(2,1)S(1)}, bf16[304,2048]{1,0:T(8,128)(2,1)S(1)}, u32[]{:S(2)}, u32[]{:S(2)}) collective-permute-start(bf16[304,2048]{1,0:T(8,128)(2,1)S(1)} %collective-permute-done.32), channel_id=1, source_target_pairs={{2,3},{6,7},{10,11},{14,15},{18,19},{22,23},{26,27},{30,31}} | collective-permute-start | bytes 3735560 | tf_op jit(solution)/shard_map/ppermute | solution.py:175
  630.0 29.2 %collective-permute-start.35 = (bf16[304,2048]{1,0:T(8,128)(2,1)S(1)}, bf16[304,2048]{1,0:T(8,128)(2,1)S(1)}, u32[]{:S(2)}, u32[]{:S(2)}) collective-permute-start(bf16[304,2048]{1,0:T(8,128)(2,1)S(1)} %collective-permute-done.33), channel_id=1, source_target_pairs={{1,0},{5,4},{9,8},{13,12},{17,16},{21,20},{25,24},{29,28}} | collective-permute-start | bytes 3735560 | tf_op jit(solution)/shard_map/ppermute | solution.py:178
  661.1 32.0 %collective-permute-start.37 = (bf16[304,2048]{1,0:T(8,128)(2,1)S(1)}, bf16[304,2048]{1,0:T(8,128)(2,1)S(1)}, u32[]{:S(2)}, u32[]{:S(2)}) collective-permute-start(bf16[304,2048]{1,0:T(8,128)(2,1)S(1)} %get-tuple-element.169), channel_id=1, source_target_pairs={{1,0},{2,1},{3,2},{5,4},{6,5},{7,6},{9,8},{10,9},{11,10},{13,12},{... | collective-permute-start | bytes 3735560 | tf_op jit(solution)/shard_map/ppermute | solution.py:178
  693.2 30.7 %collective-permute-start.39 = (bf16[304,2048]{1,0:T(8,128)(2,1)S(1)}, bf16[304,2048]{1,0:T(8,128)(2,1)S(1)}, u32[]{:S(2)}, u32[]{:S(2)}) collective-permute-start(bf16[304,2048]{1,0:T(8,128)(2,1)S(1)} %collective-permute-done.37), channel_id=1, source_target_pairs={{1,0},{2,1},{5,4},{6,5},{9,8},{10,9},{13,12},{14,13},{17,16},{18,1... | collective-permute-start | bytes 3735560 | tf_op jit(solution)/shard_map/ppermute | solution.py:178
  694.5 38.0 %collective-permute-start.40 = (bf16[304,2048]{1,0:T(8,128)(2,1)S(1)}, bf16[304,2048]{1,0:T(8,128)(2,1)S(1)}, u32[]{:S(2)}, u32[]{:S(2)}) collective-permute-start(bf16[304,2048]{1,0:T(8,128)(2,1)S(1)} %collective-permute-done.38), channel_id=1, source_target_pairs={{2,3},{6,7},{10,11},{14,15},{18,19},{22,23},{26,27},{30,31}} | collective-permute-start | bytes 3735560 | tf_op jit(solution)/shard_map/ppermute | solution.py:175
  723.8 30.8 %collective-permute-start.41 = (bf16[304,2048]{1,0:T(8,128)(2,1)S(1)}, bf16[304,2048]{1,0:T(8,128)(2,1)S(1)}, u32[]{:S(2)}, u32[]{:S(2)}) collective-permute-start(bf16[304,2048]{1,0:T(8,128)(2,1)S(1)} %collective-permute-done.39), channel_id=1, source_target_pairs={{1,0},{5,4},{9,8},{13,12},{17,16},{21,20},{25,24},{29,28}} | collective-permute-start | bytes 3735560 | tf_op jit(solution)/shard_map/ppermute | solution.py:178
  756.9 30.1 %collective-permute-start.42 = (bf16[304,2048]{1,0:T(8,128)(2,1)S(1)}, bf16[304,2048]{1,0:T(8,128)(2,1)S(1)}, u32[]{:S(2)}, u32[]{:S(2)}) collective-permute-start(bf16[304,2048]{1,0:T(8,128)(2,1)S(1)} %get-tuple-element.170), channel_id=1, source_target_pairs={{0,1},{1,2},{2,3},{4,5},{5,6},{6,7},{8,9},{9,10},{10,11},{12,13},{... | collective-permute-start | bytes 3735560 | tf_op jit(solution)/shard_map/ppermute | solution.py:175
  758.4 56.3 %collective-permute-start.43 = (bf16[304,2048]{1,0:T(8,128)(2,1)S(1)}, bf16[304,2048]{1,0:T(8,128)(2,1)}, u32[]{:S(2)}, u32[]{:S(2)}) collective-permute-start(bf16[304,2048]{1,0:T(8,128)(2,1)S(1)} %get-tuple-element.170), channel_id=1, source_target_pairs={{1,0},{2,1},{3,2},{5,4},{6,5},{7,6},{9,8},{10,9},{11,10},{13,12},{... | collective-permute-start | bytes 3735560 | tf_op jit(solution)/shard_map/ppermute | solution.py:178
  787.0 29.0 %collective-permute-start.44 = (bf16[304,2048]{1,0:T(8,128)(2,1)S(1)}, bf16[304,2048]{1,0:T(8,128)(2,1)}, u32[]{:S(2)}, u32[]{:S(2)}) collective-permute-start(bf16[304,2048]{1,0:T(8,128)(2,1)S(1)} %collective-permute-done.42), channel_id=1, source_target_pairs={{1,2},{2,3},{5,6},{6,7},{9,10},{10,11},{13,14},{14,15},{17,18},{18... | collective-permute-start | bytes 3735560 | tf_op jit(solution)/shard_map/ppermute | solution.py:175
  859.6 45.1 %collective-permute-start.51 = (bf16[304,2048]{1,0:T(8,128)(2,1)S(1)}, bf16[304,2048]{1,0:T(8,128)(2,1)S(1)}, u32[]{:S(2)}, u32[]{:S(2)}) collective-permute-start(bf16[304,2048]{1,0:T(8,128)(2,1)S(1)} %get-tuple-element.365), channel_id=1, source_target_pairs={{3,2},{7,6},{11,10},{15,14},{19,18},{23,22},{27,26},{31,30}} | collective-permute-start | bytes 3735560 | tf_op jit(solution)/shard_map/ppermute | solution.py:207
  874.4 30.4 %collective-permute-start.49 = (bf16[304,2048]{1,0:T(8,128)(2,1)S(1)}, bf16[304,2048]{1,0:T(8,128)(2,1)S(1)}, u32[]{:S(2)}, u32[]{:S(2)}) collective-permute-start(bf16[304,2048]{1,0:T(8,128)(2,1)S(1)} %add_convert_fusion.29), channel_id=1, source_target_pairs={{0,1},{1,2},{4,5},{5,6},{8,9},{9,10},{12,13},{13,14},{16,17},{17,1... | collective-permute-start | bytes 3735560 | tf_op jit(solution)/shard_map/ppermute | solution.py:201
  906.7 29.3 %collective-permute-start.52 = (bf16[304,2048]{1,0:T(8,128)(2,1)}, bf16[304,2048]{1,0:T(8,128)(2,1)S(1)}, u32[]{:S(2)}, u32[]{:S(2)}) collective-permute-start(bf16[304,2048]{1,0:T(8,128)(2,1)} %get-tuple-element.363), channel_id=1, source_target_pairs={{2,1},{3,2},{6,5},{7,6},{10,9},{11,10},{14,13},{15,14},{18,17},{19... | collective-permute-start | bytes 3735560 | tf_op jit(solution)/shard_map/ppermute | solution.py:207
  933.3 30.2 %collective-permute-start.50 = (bf16[304,2048]{1,0:T(8,128)(2,1)S(1)}, bf16[304,2048]{1,0:T(8,128)(2,1)S(1)}, u32[]{:S(2)}, u32[]{:S(2)}) collective-permute-start(bf16[304,2048]{1,0:T(8,128)(2,1)S(1)} %get-tuple-element.362), channel_id=1, source_target_pairs={{0,1},{1,2},{2,3},{4,5},{5,6},{6,7},{8,9},{9,10},{10,11},{12,13},{... | collective-permute-start | bytes 3735560 | tf_op jit(solution)/shard_map/ppermute | solution.py:201
  971.9 28.0 %collective-permute-start.57 = (bf16[304,2048]{1,0:T(8,128)(2,1)S(1)}, bf16[304,2048]{1,0:T(8,128)(2,1)S(1)}, u32[]{:S(2)}, u32[]{:S(2)}) collective-permute-start(bf16[304,2048]{1,0:T(8,128)(2,1)S(1)} %get-tuple-element.361), channel_id=1, source_target_pairs={{3,2},{7,6},{11,10},{15,14},{19,18},{23,22},{27,26},{31,30}} | collective-permute-start | bytes 3735560 | tf_op jit(solution)/shard_map/ppermute | solution.py:207
  995.5 28.6 %collective-permute-start.55 = (bf16[304,2048]{1,0:T(8,128)(2,1)S(1)}, bf16[304,2048]{1,0:T(8,128)(2,1)S(1)}, u32[]{:S(2)}, u32[]{:S(2)}) collective-permute-start(bf16[304,2048]{1,0:T(8,128)(2,1)S(1)} %add_convert_fusion.24), channel_id=1, source_target_pairs={{0,1},{1,2},{4,5},{5,6},{8,9},{9,10},{12,13},{13,14},{16,17},{17,1... | collective-permute-start | bytes 3735560 | tf_op jit(solution)/shard_map/ppermute | solution.py:201
  1025.7 35.5 %collective-permute-start.56 = (bf16[304,2048]{1,0:T(8,128)(2,1)S(1)}, bf16[304,2048]{1,0:T(8,128)(2,1)S(1)}, u32[]{:S(2)}, u32[]{:S(2)}) collective-permute-start(bf16[304,2048]{1,0:T(8,128)(2,1)S(1)} %get-tuple-element.358), channel_id=1, source_target_pairs={{0,1},{1,2},{2,3},{4,5},{5,6},{6,7},{8,9},{9,10},{10,11},{12,13},{... | collective-permute-start | bytes 3735560 | tf_op jit(solution)/shard_map/ppermute | solution.py:201
  1031.2 32.6 %collective-permute-start.59 = (bf16[304,2048]{1,0:T(8,128)(2,1)S(1)}, bf16[304,2048]{1,0:T(8,128)(2,1)S(1)}, u32[]{:S(2)}, u32[]{:S(2)}) collective-permute-start(bf16[304,2048]{1,0:T(8,128)(2,1)S(1)} %add_convert_fusion.21), channel_id=1, source_target_pairs={{1,0},{2,1},{3,2},{5,4},{6,5},{7,6},{9,8},{10,9},{11,10},{13,12},{... | collective-permute-start | bytes 3735560 | tf_op jit(solution)/shard_map/ppermute | solution.py:207
  1070.7 41.2 %collective-permute-start.60 = (bf16[304,2048]{1,0:T(8,128)(2,1)S(1)}, bf16[304,2048]{1,0:T(8,128)(2,1)S(1)}, u32[]{:S(2)}, u32[]{:S(2)}) collective-permute-start(bf16[304,2048]{1,0:T(8,128)(2,1)S(1)} %get-tuple-element.356), channel_id=1, source_target_pairs={{0,1},{4,5},{8,9},{12,13},{16,17},{20,21},{24,25},{28,29}} | collective-permute-start | bytes 3735560 | tf_op jit(solution)/shard_map/ppermute | solution.py:201
  1086.5 30.2 %collective-permute-start.63 = (bf16[304,2048]{1,0:T(8,128)(2,1)S(1)}, bf16[304,2048]{1,0:T(8,128)(2,1)S(1)}, u32[]{:S(2)}, u32[]{:S(2)}) collective-permute-start(bf16[304,2048]{1,0:T(8,128)(2,1)S(1)} %get-tuple-element.357), channel_id=1, source_target_pairs={{3,2},{7,6},{11,10},{15,14},{19,18},{23,22},{27,26},{31,30}} | collective-permute-start | bytes 3735560 | tf_op jit(solution)/shard_map/ppermute | solution.py:207
  1132.7 35.1 %collective-permute-start.62 = (bf16[304,2048]{1,0:T(8,128)(2,1)S(1)}, bf16[304,2048]{1,0:T(8,128)(2,1)S(1)}, u32[]{:S(2)}, u32[]{:S(2)}) collective-permute-start(bf16[304,2048]{1,0:T(8,128)(2,1)S(1)} %get-tuple-element.354), channel_id=1, source_target_pairs={{0,1},{1,2},{2,3},{4,5},{5,6},{6,7},{8,9},{9,10},{10,11},{12,13},{... | collective-permute-start | bytes 3735560 | tf_op jit(solution)/shard_map/ppermute | solution.py:201
  1138.1 32.3 %collective-permute-start.65 = (bf16[304,2048]{1,0:T(8,128)(2,1)S(1)}, bf16[304,2048]{1,0:T(8,128)(2,1)S(1)}, u32[]{:S(2)}, u32[]{:S(2)}) collective-permute-start(bf16[304,2048]{1,0:T(8,128)(2,1)S(1)} %add_convert_fusion.16), channel_id=1, source_target_pairs={{1,0},{2,1},{3,2},{5,4},{6,5},{7,6},{9,8},{10,9},{11,10},{13,12},{... | collective-permute-start | bytes 3735560 | tf_op jit(solution)/shard_map/ppermute | solution.py:207
  1174.3 38.9 %collective-permute-start.66 = (bf16[304,2048]{1,0:T(8,128)(2,1)S(1)}, bf16[304,2048]{1,0:T(8,128)(2,1)S(1)}, u32[]{:S(2)}, u32[]{:S(2)}) collective-permute-start(bf16[304,2048]{1,0:T(8,128)(2,1)S(1)} %get-tuple-element.352), channel_id=1, source_target_pairs={{0,1},{4,5},{8,9},{12,13},{16,17},{20,21},{24,25},{28,29}} | collective-permute-start | bytes 3735560 | tf_op jit(solution)/shard_map/ppermute | solution.py:201
  1248.1 36.8 %collective-permute-start.71 = (bf16[304,2048]{1,0:T(8,128)(2,1)S(1)}, bf16[304,2048]{1,0:T(8,128)(2,1)S(1)}, u32[]{:S(2)}, u32[]{:S(2)}) collective-permute-start(bf16[304,2048]{1,0:T(8,128)(2,1)S(1)} %add_convert_fusion.12), channel_id=1, source_target_pairs={{1,0},{2,1},{3,2},{5,4},{6,5},{7,6},{9,8},{10,9},{11,10},{13,12},{... | collective-permute-start | bytes 3735560 | tf_op jit(solution)/shard_map/ppermute | solution.py:207
  1311.7 464.6 %reduce-scatter.15.cloned.1.call-start = ((), (), s32[]{:S(2)}) async-start(), calls=%async_computation.14 | async-start | bytes 18874368 | tf_op jit(solution)/shard_map/reduce_scatter | solution.py:404
  1311.8 33.9 %collective-permute-start.73 = (bf16[304,2048]{1,0:T(8,128)(2,1)S(1)}, bf16[304,2048]{1,0:T(8,128)(2,1)}, u32[]{:S(2)}, u32[]{:S(2)}) collective-permute-start(bf16[304,2048]{1,0:T(8,128)(2,1)S(1)} %get-tuple-element.175), channel_id=1, source_target_pairs={{1,0},{2,1},{3,2},{5,4},{6,5},{7,6},{9,8},{10,9},{11,10},{13,12},{... | collective-permute-start | bytes 3735560 | tf_op jit(solution)/shard_map/ppermute | solution.py:178
  1313.1 33.9 %collective-permute-start.74 = (bf16[304,2048]{1,0:T(8,128)(2,1)S(1)}, bf16[304,2048]{1,0:T(8,128)(2,1)}, u32[]{:S(2)}, u32[]{:S(2)}) collective-permute-start(bf16[304,2048]{1,0:T(8,128)(2,1)S(1)} %collective-permute-done.72), channel_id=1, source_target_pairs={{1,2},{2,3},{5,6},{6,7},{9,10},{10,11},{13,14},{14,15},{17,18},{18... | collective-permute-start | bytes 3735560 | tf_op jit(solution)/shard_map/ppermute | solution.py:175
  1345.7 33.9 %collective-permute-start.75 = (bf16[304,2048]{1,0:T(8,128)(2,1)}, bf16[304,2048]{1,0:T(8,128)(2,1)}, u32[]{:S(2)}, u32[]{:S(2)}) collective-permute-start(bf16[304,2048]{1,0:T(8,128)(2,1)} %collective-permute-done.73), channel_id=1, source_target_pairs={{1,0},{2,1},{5,4},{6,5},{9,8},{10,9},{13,12},{14,13},{17,16},{18,1... | collective-permute-start | bytes 3735560 | tf_op jit(solution)/shard_map/ppermute | solution.py:178
  1347.0 39.2 %collective-permute-start.76 = (bf16[304,2048]{1,0:T(8,128)(2,1)}, bf16[304,2048]{1,0:T(8,128)(2,1)}, u32[]{:S(2)}, u32[]{:S(2)}) collective-permute-start(bf16[304,2048]{1,0:T(8,128)(2,1)} %collective-permute-done.74), channel_id=1, source_target_pairs={{2,3},{6,7},{10,11},{14,15},{18,19},{22,23},{26,27},{30,31}} | collective-permute-start | bytes 3735560 | tf_op jit(solution)/shard_map/ppermute | solution.py:175
  1379.5 442.5 %reduce-scatter.11.cloned.1.call-start = ((), (), s32[]{:S(2)}) async-start(), calls=%async_computation.12 | async-start | bytes 1179648 | tf_op jit(solution)/shard_map/reduce_scatter | solution.py:396
  1403.3 101.8 %collective-permute-start.78 = (bf16[304,2048]{1,0:T(8,128)(2,1)}, bf16[304,2048]{1,0:T(8,128)(2,1)}, u32[]{:S(2)}, u32[]{:S(2)}) collective-permute-start(bf16[304,2048]{1,0:T(8,128)(2,1)} %get-tuple-element.176), channel_id=1, source_target_pairs={{0,1},{1,2},{2,3},{4,5},{5,6},{6,7},{8,9},{9,10},{10,11},{12,13},{... | collective-permute-start | bytes 3735560 | tf_op jit(solution)/shard_map/ppermute | solution.py:175
  1405.9 100.0 %collective-permute-start.79 = (bf16[304,2048]{1,0:T(8,128)(2,1)}, bf16[304,2048]{1,0:T(8,128)(2,1)}, u32[]{:S(2)}, u32[]{:S(2)}) collective-permute-start(bf16[304,2048]{1,0:T(8,128)(2,1)} %get-tuple-element.176), channel_id=1, source_target_pairs={{1,0},{2,1},{3,2},{5,4},{6,5},{7,6},{9,8},{10,9},{11,10},{13,12},{... | collective-permute-start | bytes 3735560 | tf_op jit(solution)/shard_map/ppermute | solution.py:178
  1548.6 96.9 %collective-permute-start.84 = (bf16[304,2048]{1,0:T(8,128)(2,1)}, bf16[304,2048]{1,0:T(8,128)(2,1)}, u32[]{:S(2)}, u32[]{:S(2)}) collective-permute-start(bf16[304,2048]{1,0:T(8,128)(2,1)} %get-tuple-element.348), channel_id=1, source_target_pairs={{0,1},{4,5},{8,9},{12,13},{16,17},{20,21},{24,25},{28,29}} | collective-permute-start | bytes 3735560 | tf_op jit(solution)/shard_map/ppermute | solution.py:201
  1551.2 111.7 %collective-permute-start.87 = (bf16[304,2048]{1,0:T(8,128)(2,1)}, bf16[304,2048]{1,0:T(8,128)(2,1)}, u32[]{:S(2)}, u32[]{:S(2)}) collective-permute-start(bf16[304,2048]{1,0:T(8,128)(2,1)} %get-tuple-element.349), channel_id=1, source_target_pairs={{3,2},{7,6},{11,10},{15,14},{19,18},{23,22},{27,26},{31,30}} | collective-permute-start | bytes 3735560 | tf_op jit(solution)/shard_map/ppermute | solution.py:207
  1685.2 27.9 %collective-permute-start.86 = (bf16[304,2048]{1,0:T(8,128)(2,1)S(1)}, bf16[304,2048]{1,0:T(8,128)(2,1)S(1)}, u32[]{:S(2)}, u32[]{:S(2)}) collective-permute-start(bf16[304,2048]{1,0:T(8,128)(2,1)S(1)} %get-tuple-element.346), channel_id=1, source_target_pairs={{0,1},{1,2},{2,3},{4,5},{5,6},{6,7},{8,9},{9,10},{10,11},{12,13},{... | collective-permute-start | bytes 3735560 | tf_op jit(solution)/shard_map/ppermute | solution.py:201
  1729.1 96.2 %reduce-scatter.9.cloned.1.call-start = ((), (), s32[]{:S(2)}) async-start(), calls=%async_computation.11 | async-start | bytes 2359296 | tf_op jit(solution)/shard_map/reduce_scatter | solution.py:393
  1734.1 48.8 %collective-permute-start.93 = (bf16[304,2048]{1,0:T(8,128)(2,1)}, bf16[304,2048]{1,0:T(8,128)(2,1)}, u32[]{:S(2)}, u32[]{:S(2)}) collective-permute-start(bf16[304,2048]{1,0:T(8,128)(2,1)} %get-tuple-element.345), channel_id=1, source_target_pairs={{3,2},{7,6},{11,10},{15,14},{19,18},{23,22},{27,26},{31,30}} | collective-permute-start | bytes 3735560 | tf_op jit(solution)/shard_map/ppermute | solution.py:207
  1750.5 32.3 %collective-permute-start.91 = (bf16[304,2048]{1,0:T(8,128)(2,1)}, bf16[304,2048]{1,0:T(8,128)(2,1)}, u32[]{:S(2)}, u32[]{:S(2)}) collective-permute-start(bf16[304,2048]{1,0:T(8,128)(2,1)} %add_convert_fusion.7), channel_id=1, source_target_pairs={{0,1},{1,2},{4,5},{5,6},{8,9},{9,10},{12,13},{13,14},{16,17},{17,1... | collective-permute-start | bytes 3735560 | tf_op jit(solution)/shard_map/ppermute | solution.py:201
  1763.1 89.2 %reduce-scatter.13.cloned.1.call-start = ((), (), s32[]{:S(2)}) async-start(), calls=%async_computation.13 | async-start | bytes 2359296 | tf_op jit(solution)/shard_map/reduce_scatter | solution.py:401
  1796.7 123.5 %reduce-scatter.19.cloned.1.call-start = ((), (), s32[]{:S(2)}) async-start(), calls=%async_computation.16 | async-start | bytes 589824
  1796.7 58.9 %collective-permute-start.92 = (bf16[304,2048]{1,0:T(8,128)(2,1)}, bf16[304,2048]{1,0:T(8,128)(2,1)}, u32[]{:S(2)}, u32[]{:S(2)}) collective-permute-start(bf16[304,2048]{1,0:T(8,128)(2,1)} %get-tuple-element.342), channel_id=1, source_target_pairs={{0,1},{1,2},{2,3},{4,5},{5,6},{6,7},{8,9},{9,10},{10,11},{12,13},{... | collective-permute-start | bytes 3735560 | tf_op jit(solution)/shard_map/ppermute | solution.py:201
  1802.7 52.9 %collective-permute-start.95 = (bf16[304,2048]{1,0:T(8,128)(2,1)}, bf16[304,2048]{1,0:T(8,128)(2,1)}, u32[]{:S(2)}, u32[]{:S(2)}) collective-permute-start(bf16[304,2048]{1,0:T(8,128)(2,1)} %add_convert_fusion.4), channel_id=1, source_target_pairs={{1,0},{2,1},{3,2},{5,4},{6,5},{7,6},{9,8},{10,9},{11,10},{13,12},{... | collective-permute-start | bytes 3735560 | tf_op jit(solution)/shard_map/ppermute | solution.py:207
  (237 other events, 4147.3 us)
Sparse Core Ops, SparseCore 0:
  10.5 26.0 all-gather.5
  39.1 27.7 all-gather.7
  69.4 28.0 all-gather.9
  99.8 89.7 all-gather.11
  521.0 77.0 all-gather.13
  1311.8 68.5 reduce-scatter.16
  1384.0 118.4 reduce-scatter.14
  1729.2 33.2 reduce-scatter.10
  1766.4 41.1 reduce-scatter.8
  1811.2 41.0 reduce-scatter.12
  1888.8 31.3 reduce-scatter.18

commit v6 on v5

--- a/solution.py
+++ b/solution.py
@@ -298,6 +298,7 @@
         hidden_state = (silu_gate * up_part).astype(jnp.bfloat16)
         upstream = cot_rows.astype(jnp.float32)
         ffn_grad = (branch_scale * upstream).astype(jnp.bfloat16)
+        ffn_grad, _ = lax.optimization_barrier((ffn_grad, hidden_state))
         ffn_grad_all = yield ("gather", ffn_grad)
         ffn_branch = yield (
             "scatter", jnp.dot(hidden_state, full_down, preferred_element_type=jnp.float32)

time: 2010 us -> 2030 us (level)
  local copies, waits for them, and re-layouts: 126 us -> 150 us
  other arithmetic: 242 us -> 264 us
    reduce_scatter x1, waiting for transfers between devices: 0.01 us -> 31.5 us  [per_device(): lax.psum_scatter(totals[0].astype(jnp.bfloat16), 'dp', scatter_dimension=...]
    reduce_scatter x1, waiting for transfers between devices: 23.9 us -> 0.01 us  [per_device(): lax.psum_scatter(totals[2].astype(jnp.bfloat16), 'dp', scatter_dimension=...]
    unnamed x396 -> x414, local copies, waits for them, and re-layouts: 29.1 us -> 41.4 us
  transfers between devices with their start and end apart: 107 -> 107, of which waited for: 47 -> 49; matrix products, arithmetic and copies ran while one was open for 42% -> 43% of each run, Pallas kernels for 0% -> 0%
where the time goes in v6:
time: 2030 us; the launch traced here: 2020 us
  waiting for transfers between devices  758 us (37%)
  matrix products  535 us (26%)
  other arithmetic  264 us (13%)
  starting transfers between devices  222 us (11%)
  local copies, waits for them, and re-layouts  150 us (7%)
  blocking collectives  69.9 us (3%)
  between operations  21.3 us (1%)
    ppermute x24, waiting for transfers between devices, line_gather(): lax.ppermute(from_right, 'tensor', [(i, i - 1) for i in range(1, count -...  319 us
    ppermute x24, waiting for transfers between devices, line_scatter(): lax.ppermute(send.astype(jnp.bfloat16), 'tensor', [(i, i + 1) for i in ra...  264 us
    ppermute x24, starting transfers between devices, line_scatter(): lax.ppermute(send.astype(jnp.bfloat16), 'tensor', [(i, i + 1) for i in ra...  110 us
    ppermute x24, waiting for transfers between devices, line_gather(): lax.ppermute(from_left, 'tensor', [(i, i + 1) for i in range(step - 1, co...  71 us
    dot_general x6, matrix products, contract_cols(): lax.dot_general(left, right, (((1,), (1,)), ((), ())), preferred_element_...  65 us
    dot_general x4, matrix products, attend_back(): jnp.einsum('ikrd,jkd->krij', grad_block, values[:stop], preferred_element...  61.7 us
    dot_general x2, matrix products, micro_step(): jnp.einsum('rd,rcf->dcf', rows_two, gateup_grad, preferred_element_type=j...  59.9 us
    dot_general x6, matrix products, contract_rows(): lax.dot_general(left, right, (((0,), (0,)), ((), ())), preferred_element_...  58.7 us
  transfers between devices with their start and end apart: 107, of which 49 were waited for; matrix products, arithmetic and copies ran while one was open for 43% of the time, Pallas kernels for 0%

profile of v6, /device:TPU:0, one launch (start us, length us, event | category | flops | bytes accessed | tf_op | source)
XLA Modules:
  0.0 2020.0 jit_solution(14736584718815583129)
XLA Ops:
  40.1 19.8 collective-permute-done
  76.3 19.5 collective-permute-done.3
  111.5 16.5 collective-permute-done.5
  167.3 13.1 fusion.136
  199.1 18.9 collective-permute-done.9
  225.8 23.0 %collective-permute-done.11 = bf16[304,2048]{1,0:T(8,128)(2,1)S(1)} collective-permute-done((bf16[304,2048]{1,0:T(8,128)(2,1)}, bf16[304,2048]{1,0:T(8,128)(2,1)S(1)}, u32[]{:S(2)}, u32[]{:S(2)}) %collective-permute-start.11) | collective-permute-done | bytes 1245216 | tf_op jit(solution)/shard_map/ppermute | solution.py:178
  294.4 13.8 fusion.135
  352.5 22.4 %collective-permute-done.17 = bf16[304,2048]{1,0:T(8,128)(2,1)S(1)} collective-permute-done((bf16[304,2048]{1,0:T(8,128)(2,1)S(1)}, bf16[304,2048]{1,0:T(8,128)(2,1)S(1)}, u32[]{:S(2)}, u32[]{:S(2)}) %collective-permute-start.17) | collective-permute-done | bytes 1245216 | tf_op jit(solution)/shard_map/ppermute | solution.py:207
  382.3 21.9 %collective-permute-done.18 = bf16[304,2048]{1,0:T(8,128)(2,1)S(1)} collective-permute-done((bf16[304,2048]{1,0:T(8,128)(2,1)S(1)}, bf16[304,2048]{1,0:T(8,128)(2,1)S(1)}, u32[]{:S(2)}, u32[]{:S(2)}) %collective-permute-start.18) | collective-permute-done | bytes 1245216 | tf_op jit(solution)/shard_map/ppermute | solution.py:201
  409.1 20.8 %collective-permute-done.19 = bf16[304,2048]{1,0:T(8,128)(2,1)S(1)} collective-permute-done((bf16[304,2048]{1,0:T(8,128)(2,1)S(1)}, bf16[304,2048]{1,0:T(8,128)(2,1)S(1)}, u32[]{:S(2)}, u32[]{:S(2)}) %collective-permute-start.19) | collective-permute-done | bytes 1245216 | tf_op jit(solution)/shard_map/ppermute | solution.py:201
  438.3 16.7 collective-permute-done.20
  455.0 22.6 %collective-permute-done.23 = bf16[304,2048]{1,0:T(8,128)(2,1)S(1)} collective-permute-done((bf16[304,2048]{1,0:T(8,128)(2,1)S(1)}, bf16[304,2048]{1,0:T(8,128)(2,1)S(1)}, u32[]{:S(2)}, u32[]{:S(2)}) %collective-permute-start.23) | collective-permute-done | bytes 1245216 | tf_op jit(solution)/shard_map/ppermute | solution.py:207
  489.7 13.0 collective-permute-done.24
  503.5 12.6 collective-permute-done.25
  518.1 26.7 %collective-permute-done.27 = bf16[304,2048]{1,0:T(8,128)(2,1)S(1)} collective-permute-done((bf16[304,2048]{1,0:T(8,128)(2,1)S(1)}, bf16[304,2048]{1,0:T(8,128)(2,1)S(1)}, u32[]{:S(2)}, u32[]{:S(2)}) %collective-permute-start.27) | collective-permute-done | bytes 1245216 | tf_op jit(solution)/shard_map/ppermute | solution.py:178
  547.9 23.7 %collective-permute-done.29 = bf16[304,2048]{1,0:T(8,128)(2,1)S(1)} collective-permute-done((bf16[304,2048]{1,0:T(8,128)(2,1)S(1)}, bf16[304,2048]{1,0:T(8,128)(2,1)S(1)}, u32[]{:S(2)}, u32[]{:S(2)}) %collective-permute-start.29) | collective-permute-done | bytes 1245216 | tf_op jit(solution)/shard_map/ppermute | solution.py:178
  576.0 12.1 collective-permute-done.30
  590.0 17.2 collective-permute-done.31
  613.4 26.2 %collective-permute-done.33 = bf16[304,2048]{1,0:T(8,128)(2,1)} collective-permute-done((bf16[304,2048]{1,0:T(8,128)(2,1)}, bf16[304,2048]{1,0:T(8,128)(2,1)}, u32[]{:S(2)}, u32[]{:S(2)}) %collective-permute-start.33) | collective-permute-done | bytes 1245216 | tf_op jit(solution)/shard_map/ppermute | solution.py:178
  660.9 25.4 %fusion.59 = f32[1216,2,2048]{2,0,1:T(8,128)S(1)} fusion(bf16[2048,2,2048]{2,0,1:T(8,128)(2,1)} %all-gather.12.cloned.1.call-done, bf16[1216,2048]{1,0:T(8,128)(2,1)} %copy-done.60), kind=kOutput, calls=%fused_computation.103 | convolution fusion | flops 20401094656 | bytes 41680896 | tf_op jit(solution)/shard_map/rd,dcf->rcf/dot_general | solution.py:291
  697.8 13.0 collective-permute-done.36
  712.0 25.4 %fusion.56 = f32[1216,2,2048]{2,0,1:T(8,128)S(1)} fusion(bf16[2048,2,2048]{2,0,1:T(8,128)(2,1)} %all-gather.12.cloned.1.call-done, bf16[1216,2048]{1,0:T(8,128)(2,1)} %constant_dynamic-update-slice_fusion.28), kind=kOutput, calls=%fused_computation.100 | convolution fusion | flops 20401094656 | bytes 41680896 | tf_op jit(solution)/shard_map/rd,dcf->rcf/dot_general | solution.py:291
  745.6 29.4 %collective-permute-done.39 = bf16[304,2048]{1,0:T(8,128)(2,1)S(1)} collective-permute-done((bf16[304,2048]{1,0:T(8,128)(2,1)S(1)}, bf16[304,2048]{1,0:T(8,128)(2,1)S(1)}, u32[]{:S(2)}, u32[]{:S(2)}) %collective-permute-start.39) | collective-permute-done | bytes 1245216 | tf_op jit(solution)/shard_map/ppermute | solution.py:178
  785.0 17.3 collective-permute-done.41
  807.6 13.0 collective-permute-done.42
  822.3 10.8 collective-permute-done.43
  836.2 14.5 fusion.234
  860.3 11.7 collective-permute-done.47
  876.9 23.2 %collective-permute-done.48 = bf16[304,2048]{1,0:T(8,128)(2,1)S(1)} collective-permute-done((bf16[304,2048]{1,0:T(8,128)(2,1)S(1)}, bf16[304,2048]{1,0:T(8,128)(2,1)S(1)}, u32[]{:S(2)}, u32[]{:S(2)}) %collective-permute-start.48) | collective-permute-done | bytes 1245216 | tf_op jit(solution)/shard_map/ppermute | solution.py:201
  905.3 14.3 collective-permute-done.49
  929.1 13.0 fusion.235
  942.1 11.0 collective-permute-done.50
  963.1 12.1 collective-permute-start.54
  976.0 13.6 collective-permute-done.54
  994.5 20.5 %collective-permute-done.55 = bf16[304,2048]{1,0:T(8,128)(2,1)S(1)} collective-permute-done((bf16[304,2048]{1,0:T(8,128)(2,1)S(1)}, bf16[304,2048]{1,0:T(8,128)(2,1)S(1)}, u32[]{:S(2)}, u32[]{:S(2)}) %collective-permute-start.55) | collective-permute-done | bytes 1245216 | tf_op jit(solution)/shard_map/ppermute | solution.py:201
  1017.9 23.9 %fusion.69 = (bf16[1216,1,2048]{2,0,1:T(8,128)(2,1)}, bf16[1216,1,2048]{2,0,1:T(8,128)(2,1)}) fusion(f32[1216,2,2048]{2,0,1:T(8,128)} %copy-done.35, bf16[1216,2048]{1,0:T(8,128)(2,1)} %constant_dynamic-update-slice_fusion.21, bf16[2048,2048]{1,0:T(8,128)(2,1)} %all-gather.14.cloned.1.call-done), kind=kOutput, calls=%fused_computation.113 | convolution fusion | flops 10232922112 | bytes 43253760 | tf_op jit(solution)/shard_map/dot_general | solution.py:162
  1052.2 24.6 %convolution_bitcast_fusion.1 = f32[1216,2048]{1,0:T(8,128)S(1)} fusion(bf16[2048,2,2048]{2,0,1:T(8,128)(2,1)} %all-gather.12.cloned.1.call-done, bf16[1216,1,2048]{2,0,1:T(8,128)(2,1)} %get-tuple-element.343, bf16[1216,1,2048]{2,0,1:T(8,128)(2,1)} %get-tuple-element.342), kind=kOutput, calls=%fused_computation.81 | convolution fusion | flops 20406075392 | bytes 36700160 | tf_op jit(solution)/shard_map/rcf,dcf->rd/dot_general | solution.py:317
  1090.8 13.2 collective-permute-done.60
  1108.9 19.0 collective-permute-done.61
  1132.0 23.9 %fusion.70 = (bf16[1216,1,2048]{2,0,1:T(8,128)(2,1)}, bf16[1216,1,2048]{2,0,1:T(8,128)(2,1)}) fusion(f32[1216,2,2048]{2,0,1:T(8,128)} %copy-done.34, bf16[1216,2048]{1,0:T(8,128)(2,1)} %copy-done.61, bf16[2048,2048]{1,0:T(8,128)(2,1)} %all-gather.14.cloned.1.call-done), kind=kOutput, calls=%fused_computation.114 | convolution fusion | flops 10232922112 | bytes 43253760 | tf_op jit(solution)/shard_map/dot_general | solution.py:162
  1163.9 28.2 %convolution_bitcast_fusion = f32[1216,2048]{1,0:T(8,128)} fusion(bf16[2048,2,2048]{2,0,1:T(8,128)(2,1)} %all-gather.12.cloned.1.call-done, bf16[1216,1,2048]{2,0,1:T(8,128)(2,1)} %get-tuple-element.341, bf16[1216,1,2048]{2,0,1:T(8,128)(2,1)} %get-tuple-element.340), kind=kOutput, calls=%fused_computation.80 | convolution fusion | flops 20406075392 | bytes 36700160 | tf_op jit(solution)/shard_map/rcf,dcf->rd/dot_general | solution.py:317
  1203.3 14.7 collective-permute-done.66
  1223.4 23.5 %collective-permute-done.67 = bf16[304,2048]{1,0:T(8,128)(2,1)S(1)} collective-permute-done((bf16[304,2048]{1,0:T(8,128)(2,1)S(1)}, bf16[304,2048]{1,0:T(8,128)(2,1)S(1)}, u32[]{:S(2)}, u32[]{:S(2)}) %collective-permute-start.67) | collective-permute-done | bytes 1245216 | tf_op jit(solution)/shard_map/ppermute | solution.py:201
  1263.2 17.8 fusion.237
  1298.8 19.0 add_convert_fusion.1
  1320.9 29.2 %fusion.42 = f32[2048,2,2048]{0,2,1:T(8,128)} fusion(bf16[1216,1,2048]{2,0,1:T(8,128)(2,1)} %get-tuple-element.341, bf16[1216,1,2048]{2,0,1:T(8,128)(2,1)} %get-tuple-element.340, bf16[1216,2048]{1,0:T(8,128)(2,1)} %constant_dynamic-update-slice_fusion.28), kind=kOutput, calls=%fused_computation.84 | convolution fusion | flops 20421017600 | bytes 48496640 | tf_op jit(solution)/shard_map/rd,rcf->dcf/dot_general | solution.py:312
  1353.2 30.6 %add_convert_fusion = bf16[2048,2,2048]{0,2,1:T(8,128)(2,1)} fusion(f32[2048,2,2048]{0,2,1:T(8,128)} %fusion.42, bf16[1216,1,2048]{2,0,1:T(8,128)(2,1)} %get-tuple-element.343, bf16[1216,1,2048]{2,0,1:T(8,128)(2,1)} %get-tuple-element.342, bf16[1216,2048]{1,0:T(8,128)(2,1)} %copy-done.60), kind=kOutput, calls=%fused_computation | convolution fusion | flops 20437794816 | bytes 65273856 | tf_op jit(solution)/shard_map/rd,rcf->dcf/dot_general | solution.py:312
  1392.7 27.8 %collective-permute-done.77 = bf16[304,2048]{1,0:T(8,128)(2,1)S(1)} collective-permute-done((bf16[304,2048]{1,0:T(8,128)(2,1)}, bf16[304,2048]{1,0:T(8,128)(2,1)S(1)}, u32[]{:S(2)}, u32[]{:S(2)}) %collective-permute-start.77) | collective-permute-done | bytes 1245216 | tf_op jit(solution)/shard_map/ppermute | solution.py:178
  1448.5 22.0 %fusion.3 = (f32[2,4,608]{2,1,0:T(4,128)S(1)}, f32[2,1216,608,4]{2,1,3,0:T(8,128)}) fusion(f32[2,1216,608,4]{2,1,3,0:T(8,128)} %copy-done.1, f32[2,4,608]{2,1,0:T(4,128)S(1)} %bitcast.662, pred[608,1216]{0,1:T(8,128)(4,1)S(1)} %copy-done.20, bf16[608,2,4,64]{0,3,2,1:T(8,128)(2,1)S(1)} %bitcast.633, bf16[1216,2,128]{2,0,1:T(8,128)(2,1)S(1)} %copy-done.105), kind=kOutput, calls=%fused_computation.8 | convolution fusion | flops 786640128 | bytes 49340416 | tf_op jit(solution)/shard_map/ikrd,jkd->krij/dot_general | solution.py:119
  1470.5 17.2 fusion.5
  1491.1 10.8 fusion.21
  1512.8 11.3 fusion.125
  1538.7 14.4 collective-permute-done.81
  1558.6 13.3 collective-permute-done.83
  1586.5 11.2 fusion.16
  1608.6 18.1 fusion
  1626.7 17.2 fusion.2
  1671.3 14.1 collective-permute-done.85
  1691.2 12.4 fusion.122
  1826.6 17.7 multiply_reduce_fusion
  1850.0 31.5 %reduce-scatter.9.cloned.1.call-done = bf16[256,512]{1,0:T(8,128)(2,1)} async-done(((bf16[2048,512]{1,0:T(8,128)(2,1)}), bf16[256,512]{1,0:T(8,128)(2,1)}) %reduce-scatter.9.cloned.1.call-update) | async-done | bytes 262160 | tf_op jit(solution)/shard_map/reduce_scatter | solution.py:394
  1893.1 19.9 psum.14
  1926.5 19.9 reduce-scatter.19.cloned.1.call-done
  1956.9 39.5 %psum.15 = f32[2,7]{1,0:T(2,128)S(1)} all-reduce(f32[2,7]{1,0:T(2,128)S(1)} %pad_maximum_fusion.26), channel_id=1, replica_groups=mesh['dp'=8,'tensor'=4] {'dp','tensor'}, use_global_device_ids=true, to_apply=%region_49.50 | all-reduce | flops 14 | bytes 112 | tf_op jit(solution)/shard_map/psum | solution.py:440
  (846 shorter events, 784.1 us)
Async XLA Ops:
  7.2 128.5 %all-gather.6.cloned.1.call-start = ((), (), s32[]{:S(2)}) async-start(), calls=%async_computation.6 | async-start | bytes 1179648 | tf_op jit(solution)/shard_map/all_gather | solution.py:245
  9.1 133.6 %all-gather.8.cloned.1.call-start = ((), (), s32[]{:S(2)}) async-start(), calls=%async_computation.7 | async-start | bytes 2359296 | tf_op jit(solution)/shard_map/all_gather | solution.py:244
  11.7 182.4 %all-gather.10.cloned.1.call-start = ((), (), s32[]{:S(2)}) async-start(), calls=%async_computation.8 | async-start | bytes 2359296 | tf_op jit(solution)/shard_map/all_gather | solution.py:246
  14.3 646.6 %all-gather.12.cloned.1.call-start = ((), (), s32[]{:S(2)}) async-start(), calls=%async_computation.9 | async-start | bytes 18874368 | tf_op jit(solution)/shard_map/all_gather | solution.py:247
  28.7 31.1 %collective-permute-start = (bf16[304,2048]{1,0:T(8,128)(2,1)}, bf16[304,2048]{1,0:T(8,128)(2,1)S(1)}, u32[]{:S(2)}, u32[]{:S(2)}) collective-permute-start(bf16[304,2048]{1,0:T(8,128)(2,1)} %get-tuple-element.387), channel_id=1, source_target_pairs={{0,1},{1,2},{2,3},{4,5},{5,6},{6,7},{8,9},{9,10},{10,11},{12,13},{... | collective-permute-start | bytes 3735560 | tf_op jit(solution)/shard_map/ppermute | solution.py:175
  32.5 31.6 %collective-permute-start.1 = (bf16[304,2048]{1,0:T(8,128)(2,1)}, bf16[304,2048]{1,0:T(8,128)(2,1)}, u32[]{:S(2)}, u32[]{:S(2)}) collective-permute-start(bf16[304,2048]{1,0:T(8,128)(2,1)} %get-tuple-element.387), channel_id=1, source_target_pairs={{1,0},{2,1},{3,2},{5,4},{6,5},{7,6},{9,8},{10,9},{11,10},{13,12},{... | collective-permute-start | bytes 3735560 | tf_op jit(solution)/shard_map/ppermute | solution.py:178
  37.3 798.9 %all-gather.14.cloned.1.call-start = ((), (), s32[]{:S(2)}) async-start(), calls=%async_computation.10 | async-start | bytes 9437184 | tf_op jit(solution)/shard_map/all_gather | solution.py:248
  64.0 31.9 %collective-permute-start.3 = (bf16[304,2048]{1,0:T(8,128)(2,1)}, bf16[304,2048]{1,0:T(8,128)(2,1)}, u32[]{:S(2)}, u32[]{:S(2)}) collective-permute-start(bf16[304,2048]{1,0:T(8,128)(2,1)} %collective-permute-done.1), channel_id=1, source_target_pairs={{1,0},{2,1},{5,4},{6,5},{9,8},{10,9},{13,12},{14,13},{17,16},{18,1... | collective-permute-start | bytes 3735560 | tf_op jit(solution)/shard_map/ppermute | solution.py:178
  68.3 40.6 %collective-permute-start.4 = (bf16[304,2048]{1,0:T(8,128)(2,1)}, bf16[304,2048]{1,0:T(8,128)(2,1)}, u32[]{:S(2)}, u32[]{:S(2)}) collective-permute-start(bf16[304,2048]{1,0:T(8,128)(2,1)} %collective-permute-done.2), channel_id=1, source_target_pairs={{2,3},{6,7},{10,11},{14,15},{18,19},{22,23},{26,27},{30,31}} | collective-permute-start | bytes 3735560 | tf_op jit(solution)/shard_map/ppermute | solution.py:175
  95.9 32.1 %collective-permute-start.5 = (bf16[304,2048]{1,0:T(8,128)(2,1)}, bf16[304,2048]{1,0:T(8,128)(2,1)S(1)}, u32[]{:S(2)}, u32[]{:S(2)}) collective-permute-start(bf16[304,2048]{1,0:T(8,128)(2,1)} %collective-permute-done.3), channel_id=1, source_target_pairs={{1,0},{5,4},{9,8},{13,12},{17,16},{21,20},{25,24},{29,28}} | collective-permute-start | bytes 3735560 | tf_op jit(solution)/shard_map/ppermute | solution.py:178
  131.6 53.7 %collective-permute-start.6 = (bf16[304,2048]{1,0:T(8,128)(2,1)}, bf16[304,2048]{1,0:T(8,128)(2,1)}, u32[]{:S(2)}, u32[]{:S(2)}) collective-permute-start(bf16[304,2048]{1,0:T(8,128)(2,1)} %get-tuple-element.166), channel_id=1, source_target_pairs={{0,1},{1,2},{2,3},{4,5},{5,6},{6,7},{8,9},{9,10},{10,11},{12,13},{... | collective-permute-start | bytes 3735560 | tf_op jit(solution)/shard_map/ppermute | solution.py:175
  134.2 51.9 %collective-permute-start.7 = (bf16[304,2048]{1,0:T(8,128)(2,1)}, bf16[304,2048]{1,0:T(8,128)(2,1)}, u32[]{:S(2)}, u32[]{:S(2)}) collective-permute-start(bf16[304,2048]{1,0:T(8,128)(2,1)} %get-tuple-element.166), channel_id=1, source_target_pairs={{1,0},{2,1},{3,2},{5,4},{6,5},{7,6},{9,8},{10,9},{11,10},{13,12},{... | collective-permute-start | bytes 3735560 | tf_op jit(solution)/shard_map/ppermute | solution.py:178
  186.1 31.9 %collective-permute-start.9 = (bf16[304,2048]{1,0:T(8,128)(2,1)}, bf16[304,2048]{1,0:T(8,128)(2,1)}, u32[]{:S(2)}, u32[]{:S(2)}) collective-permute-start(bf16[304,2048]{1,0:T(8,128)(2,1)} %collective-permute-done.7), channel_id=1, source_target_pairs={{1,0},{2,1},{5,4},{6,5},{9,8},{10,9},{13,12},{14,13},{17,16},{18,1... | collective-permute-start | bytes 3735560 | tf_op jit(solution)/shard_map/ppermute | solution.py:178
  192.2 32.1 %collective-permute-start.10 = (bf16[304,2048]{1,0:T(8,128)(2,1)S(1)}, bf16[304,2048]{1,0:T(8,128)(2,1)}, u32[]{:S(2)}, u32[]{:S(2)}) collective-permute-start(bf16[304,2048]{1,0:T(8,128)(2,1)S(1)} %collective-permute-done.8), channel_id=1, source_target_pairs={{2,3},{6,7},{10,11},{14,15},{18,19},{22,23},{26,27},{30,31}} | collective-permute-start | bytes 3735560 | tf_op jit(solution)/shard_map/ppermute | solution.py:175
  218.0 30.8 %collective-permute-start.11 = (bf16[304,2048]{1,0:T(8,128)(2,1)}, bf16[304,2048]{1,0:T(8,128)(2,1)S(1)}, u32[]{:S(2)}, u32[]{:S(2)}) collective-permute-start(bf16[304,2048]{1,0:T(8,128)(2,1)} %collective-permute-done.9), channel_id=1, source_target_pairs={{1,0},{5,4},{9,8},{13,12},{17,16},{21,20},{25,24},{29,28}} | collective-permute-start | bytes 3735560 | tf_op jit(solution)/shard_map/ppermute | solution.py:178
  264.0 44.2 %collective-permute-start.15 = (bf16[304,2048]{1,0:T(8,128)(2,1)}, bf16[304,2048]{1,0:T(8,128)(2,1)}, u32[]{:S(2)}, u32[]{:S(2)}) collective-permute-start(bf16[304,2048]{1,0:T(8,128)(2,1)} %get-tuple-element.375), channel_id=1, source_target_pairs={{3,2},{7,6},{11,10},{15,14},{19,18},{23,22},{27,26},{31,30}} | collective-permute-start | bytes 3735560 | tf_op jit(solution)/shard_map/ppermute | solution.py:207
  325.6 26.9 %collective-permute-start.14 = (bf16[304,2048]{1,0:T(8,128)(2,1)S(1)}, bf16[304,2048]{1,0:T(8,128)(2,1)S(1)}, u32[]{:S(2)}, u32[]{:S(2)}) collective-permute-start(bf16[304,2048]{1,0:T(8,128)(2,1)S(1)} %get-tuple-element.372), channel_id=1, source_target_pairs={{0,1},{1,2},{2,3},{4,5},{5,6},{6,7},{8,9},{9,10},{10,11},{12,13},{... | collective-permute-start | bytes 3735560 | tf_op jit(solution)/shard_map/ppermute | solution.py:201
  332.7 42.2 %collective-permute-start.17 = (bf16[304,2048]{1,0:T(8,128)(2,1)S(1)}, bf16[304,2048]{1,0:T(8,128)(2,1)S(1)}, u32[]{:S(2)}, u32[]{:S(2)}) collective-permute-start(bf16[304,2048]{1,0:T(8,128)(2,1)S(1)} %add_convert_fusion.34), channel_id=1, source_target_pairs={{1,0},{2,1},{3,2},{5,4},{6,5},{7,6},{9,8},{10,9},{11,10},{13,12},{... | collective-permute-start | bytes 3735560 | tf_op jit(solution)/shard_map/ppermute | solution.py:207
  381.5 27.5 %collective-permute-start.21 = (bf16[304,2048]{1,0:T(8,128)(2,1)S(1)}, bf16[304,2048]{1,0:T(8,128)(2,1)S(1)}, u32[]{:S(2)}, u32[]{:S(2)}) collective-permute-start(bf16[304,2048]{1,0:T(8,128)(2,1)S(1)} %get-tuple-element.371), channel_id=1, source_target_pairs={{3,2},{7,6},{11,10},{15,14},{19,18},{23,22},{27,26},{31,30}} | collective-permute-start | bytes 3735560 | tf_op jit(solution)/shard_map/ppermute | solution.py:207
  437.0 40.6 %collective-permute-start.23 = (bf16[304,2048]{1,0:T(8,128)(2,1)S(1)}, bf16[304,2048]{1,0:T(8,128)(2,1)S(1)}, u32[]{:S(2)}, u32[]{:S(2)}) collective-permute-start(bf16[304,2048]{1,0:T(8,128)(2,1)S(1)} %add_convert_fusion.30), channel_id=1, source_target_pairs={{1,0},{2,1},{3,2},{5,4},{6,5},{7,6},{9,8},{10,9},{11,10},{13,12},{... | collective-permute-start | bytes 3735560 | tf_op jit(solution)/shard_map/ppermute | solution.py:207
  488.4 27.6 %collective-permute-start.25 = (bf16[304,2048]{1,0:T(8,128)(2,1)S(1)}, bf16[304,2048]{1,0:T(8,128)(2,1)S(1)}, u32[]{:S(2)}, u32[]{:S(2)}) collective-permute-start(bf16[304,2048]{1,0:T(8,128)(2,1)S(1)} %get-tuple-element.169), channel_id=1, source_target_pairs={{1,0},{2,1},{3,2},{5,4},{6,5},{7,6},{9,8},{10,9},{11,10},{13,12},{... | collective-permute-start | bytes 3735560 | tf_op jit(solution)/shard_map/ppermute | solution.py:178
  516.1 28.8 %collective-permute-start.27 = (bf16[304,2048]{1,0:T(8,128)(2,1)S(1)}, bf16[304,2048]{1,0:T(8,128)(2,1)S(1)}, u32[]{:S(2)}, u32[]{:S(2)}) collective-permute-start(bf16[304,2048]{1,0:T(8,128)(2,1)S(1)} %collective-permute-done.25), channel_id=1, source_target_pairs={{1,0},{2,1},{5,4},{6,5},{9,8},{10,9},{13,12},{14,13},{17,16},{18,1... | collective-permute-start | bytes 3735560 | tf_op jit(solution)/shard_map/ppermute | solution.py:178
  517.4 30.3 %collective-permute-start.28 = (bf16[304,2048]{1,0:T(8,128)(2,1)S(1)}, bf16[304,2048]{1,0:T(8,128)(2,1)S(1)}, u32[]{:S(2)}, u32[]{:S(2)}) collective-permute-start(bf16[304,2048]{1,0:T(8,128)(2,1)S(1)} %collective-permute-done.26), channel_id=1, source_target_pairs={{2,3},{6,7},{10,11},{14,15},{18,19},{22,23},{26,27},{30,31}} | collective-permute-start | bytes 3735560 | tf_op jit(solution)/shard_map/ppermute | solution.py:175
  544.9 26.7 %collective-permute-start.29 = (bf16[304,2048]{1,0:T(8,128)(2,1)S(1)}, bf16[304,2048]{1,0:T(8,128)(2,1)S(1)}, u32[]{:S(2)}, u32[]{:S(2)}) collective-permute-start(bf16[304,2048]{1,0:T(8,128)(2,1)S(1)} %collective-permute-done.27), channel_id=1, source_target_pairs={{1,0},{5,4},{9,8},{13,12},{17,16},{21,20},{25,24},{29,28}} | collective-permute-start | bytes 3735560 | tf_op jit(solution)/shard_map/ppermute | solution.py:178
  574.8 32.4 %collective-permute-start.31 = (bf16[304,2048]{1,0:T(8,128)(2,1)S(1)}, bf16[304,2048]{1,0:T(8,128)(2,1)}, u32[]{:S(2)}, u32[]{:S(2)}) collective-permute-start(bf16[304,2048]{1,0:T(8,128)(2,1)S(1)} %get-tuple-element.170), channel_id=1, source_target_pairs={{1,0},{2,1},{3,2},{5,4},{6,5},{7,6},{9,8},{10,9},{11,10},{13,12},{... | collective-permute-start | bytes 3735560 | tf_op jit(solution)/shard_map/ppermute | solution.py:178
  607.2 32.4 %collective-permute-start.33 = (bf16[304,2048]{1,0:T(8,128)(2,1)}, bf16[304,2048]{1,0:T(8,128)(2,1)}, u32[]{:S(2)}, u32[]{:S(2)}) collective-permute-start(bf16[304,2048]{1,0:T(8,128)(2,1)} %collective-permute-done.31), channel_id=1, source_target_pairs={{1,0},{2,1},{5,4},{6,5},{9,8},{10,9},{13,12},{14,13},{17,16},{18,1... | collective-permute-start | bytes 3735560 | tf_op jit(solution)/shard_map/ppermute | solution.py:178
  610.5 1178.2 %reduce-scatter.17.cloned.1.call-start = ((), (), s32[]{:S(2)}) async-start(), calls=%async_computation.15 | async-start | bytes 9437184 | tf_op jit(solution)/shard_map/reduce_scatter | solution.py:410
  610.6 43.2 %collective-permute-start.34 = (bf16[304,2048]{1,0:T(8,128)(2,1)}, bf16[304,2048]{1,0:T(8,128)(2,1)S(1)}, u32[]{:S(2)}, u32[]{:S(2)}) collective-permute-start(bf16[304,2048]{1,0:T(8,128)(2,1)} %collective-permute-done.32), channel_id=1, source_target_pairs={{2,3},{6,7},{10,11},{14,15},{18,19},{22,23},{26,27},{30,31}} | collective-permute-start | bytes 3735560 | tf_op jit(solution)/shard_map/ppermute | solution.py:175
  696.5 40.9 %collective-permute-start.37 = (bf16[304,2048]{1,0:T(8,128)(2,1)S(1)}, bf16[304,2048]{1,0:T(8,128)(2,1)S(1)}, u32[]{:S(2)}, u32[]{:S(2)}) collective-permute-start(bf16[304,2048]{1,0:T(8,128)(2,1)S(1)} %copy-done.67), channel_id=1, source_target_pairs={{1,0},{2,1},{3,2},{5,4},{6,5},{7,6},{9,8},{10,9},{11,10},{13,12},{... | collective-permute-start | bytes 3735560 | tf_op jit(solution)/shard_map/ppermute | solution.py:178
  710.8 27.9 %collective-permute-start.38 = (bf16[304,2048]{1,0:T(8,128)(2,1)S(1)}, bf16[304,2048]{1,0:T(8,128)(2,1)S(1)}, u32[]{:S(2)}, u32[]{:S(2)}) collective-permute-start(bf16[304,2048]{1,0:T(8,128)(2,1)S(1)} %collective-permute-done.36), channel_id=1, source_target_pairs={{1,2},{2,3},{5,6},{6,7},{9,10},{10,11},{13,14},{14,15},{17,18},{18... | collective-permute-start | bytes 3735560 | tf_op jit(solution)/shard_map/ppermute | solution.py:175
  737.4 37.6 %collective-permute-start.39 = (bf16[304,2048]{1,0:T(8,128)(2,1)S(1)}, bf16[304,2048]{1,0:T(8,128)(2,1)S(1)}, u32[]{:S(2)}, u32[]{:S(2)}) collective-permute-start(bf16[304,2048]{1,0:T(8,128)(2,1)S(1)} %collective-permute-done.37), channel_id=1, source_target_pairs={{1,0},{2,1},{5,4},{6,5},{9,8},{10,9},{13,12},{14,13},{17,16},{18,1... | collective-permute-start | bytes 3735560 | tf_op jit(solution)/shard_map/ppermute | solution.py:178
  738.7 45.2 %collective-permute-start.40 = (bf16[304,2048]{1,0:T(8,128)(2,1)S(1)}, bf16[304,2048]{1,0:T(8,128)(2,1)S(1)}, u32[]{:S(2)}, u32[]{:S(2)}) collective-permute-start(bf16[304,2048]{1,0:T(8,128)(2,1)S(1)} %collective-permute-done.38), channel_id=1, source_target_pairs={{2,3},{6,7},{10,11},{14,15},{18,19},{22,23},{26,27},{30,31}} | collective-permute-start | bytes 3735560 | tf_op jit(solution)/shard_map/ppermute | solution.py:175
  775.0 27.3 %collective-permute-start.41 = (bf16[304,2048]{1,0:T(8,128)(2,1)S(1)}, bf16[304,2048]{1,0:T(8,128)(2,1)S(1)}, u32[]{:S(2)}, u32[]{:S(2)}) collective-permute-start(bf16[304,2048]{1,0:T(8,128)(2,1)S(1)} %collective-permute-done.39), channel_id=1, source_target_pairs={{1,0},{5,4},{9,8},{13,12},{17,16},{21,20},{25,24},{29,28}} | collective-permute-start | bytes 3735560 | tf_op jit(solution)/shard_map/ppermute | solution.py:178
  806.3 26.9 %collective-permute-start.43 = (bf16[304,2048]{1,0:T(8,128)(2,1)S(1)}, bf16[304,2048]{1,0:T(8,128)(2,1)}, u32[]{:S(2)}, u32[]{:S(2)}) collective-permute-start(bf16[304,2048]{1,0:T(8,128)(2,1)S(1)} %copy-done.64), channel_id=1, source_target_pairs={{1,0},{2,1},{3,2},{5,4},{6,5},{7,6},{9,8},{10,9},{11,10},{13,12},{... | collective-permute-start | bytes 3735560 | tf_op jit(solution)/shard_map/ppermute | solution.py:178
  876.2 29.1 %collective-permute-start.51 = (bf16[304,2048]{1,0:T(8,128)(2,1)S(1)}, bf16[304,2048]{1,0:T(8,128)(2,1)S(1)}, u32[]{:S(2)}, u32[]{:S(2)}) collective-permute-start(bf16[304,2048]{1,0:T(8,128)(2,1)S(1)} %get-tuple-element.367), channel_id=1, source_target_pairs={{3,2},{7,6},{11,10},{15,14},{19,18},{23,22},{27,26},{31,30}} | collective-permute-start | bytes 3735560 | tf_op jit(solution)/shard_map/ppermute | solution.py:207
  921.2 31.9 %collective-permute-start.50 = (bf16[304,2048]{1,0:T(8,128)(2,1)S(1)}, bf16[304,2048]{1,0:T(8,128)(2,1)}, u32[]{:S(2)}, u32[]{:S(2)}) collective-permute-start(bf16[304,2048]{1,0:T(8,128)(2,1)S(1)} %get-tuple-element.364), channel_id=1, source_target_pairs={{0,1},{1,2},{2,3},{4,5},{5,6},{6,7},{8,9},{9,10},{10,11},{12,13},{... | collective-permute-start | bytes 3735560 | tf_op jit(solution)/shard_map/ppermute | solution.py:201
  927.6 31.5 %collective-permute-start.53 = (bf16[304,2048]{1,0:T(8,128)(2,1)S(1)}, bf16[304,2048]{1,0:T(8,128)(2,1)}, u32[]{:S(2)}, u32[]{:S(2)}) collective-permute-start(bf16[304,2048]{1,0:T(8,128)(2,1)S(1)} %add_convert_fusion.26), channel_id=1, source_target_pairs={{1,0},{2,1},{3,2},{5,4},{6,5},{7,6},{9,8},{10,9},{11,10},{13,12},{... | collective-permute-start | bytes 3735560 | tf_op jit(solution)/shard_map/ppermute | solution.py:207
  1017.0 30.8 %collective-permute-start.58 = (bf16[304,2048]{1,0:T(8,128)(2,1)S(1)}, bf16[304,2048]{1,0:T(8,128)(2,1)S(1)}, u32[]{:S(2)}, u32[]{:S(2)}) collective-permute-start(bf16[304,2048]{1,0:T(8,128)(2,1)S(1)} %get-tuple-element.361), channel_id=1, source_target_pairs={{2,1},{3,2},{6,5},{7,6},{10,9},{11,10},{14,13},{15,14},{18,17},{19... | collective-permute-start | bytes 3735560 | tf_op jit(solution)/shard_map/ppermute | solution.py:207
  1041.8 35.0 %collective-permute-start.56 = (bf16[304,2048]{1,0:T(8,128)(2,1)}, bf16[304,2048]{1,0:T(8,128)(2,1)}, u32[]{:S(2)}, u32[]{:S(2)}) collective-permute-start(bf16[304,2048]{1,0:T(8,128)(2,1)} %get-tuple-element.360), channel_id=1, source_target_pairs={{0,1},{1,2},{2,3},{4,5},{5,6},{6,7},{8,9},{9,10},{10,11},{12,13},{... | collective-permute-start | bytes 3735560 | tf_op jit(solution)/shard_map/ppermute | solution.py:201
  1130.3 29.6 %collective-permute-start.64 = (bf16[304,2048]{1,0:T(8,128)(2,1)}, bf16[304,2048]{1,0:T(8,128)(2,1)}, u32[]{:S(2)}, u32[]{:S(2)}) collective-permute-start(bf16[304,2048]{1,0:T(8,128)(2,1)} %get-tuple-element.357), channel_id=1, source_target_pairs={{2,1},{3,2},{6,5},{7,6},{10,9},{11,10},{14,13},{15,14},{18,17},{19... | collective-permute-start | bytes 3735560 | tf_op jit(solution)/shard_map/ppermute | solution.py:207
  1155.9 36.3 %collective-permute-start.62 = (bf16[304,2048]{1,0:T(8,128)(2,1)}, bf16[304,2048]{1,0:T(8,128)(2,1)S(1)}, u32[]{:S(2)}, u32[]{:S(2)}) collective-permute-start(bf16[304,2048]{1,0:T(8,128)(2,1)} %get-tuple-element.356), channel_id=1, source_target_pairs={{0,1},{1,2},{2,3},{4,5},{5,6},{6,7},{8,9},{9,10},{10,11},{12,13},{... | collective-permute-start | bytes 3735560 | tf_op jit(solution)/shard_map/ppermute | solution.py:201
  1162.4 29.8 %collective-permute-start.65 = (bf16[304,2048]{1,0:T(8,128)(2,1)S(1)}, bf16[304,2048]{1,0:T(8,128)(2,1)S(1)}, u32[]{:S(2)}, u32[]{:S(2)}) collective-permute-start(bf16[304,2048]{1,0:T(8,128)(2,1)S(1)} %add_convert_fusion.16), channel_id=1, source_target_pairs={{1,0},{2,1},{3,2},{5,4},{6,5},{7,6},{9,8},{10,9},{11,10},{13,12},{... | collective-permute-start | bytes 3735560 | tf_op jit(solution)/shard_map/ppermute | solution.py:207
  1218.3 28.6 %collective-permute-start.67 = (bf16[304,2048]{1,0:T(8,128)(2,1)S(1)}, bf16[304,2048]{1,0:T(8,128)(2,1)S(1)}, u32[]{:S(2)}, u32[]{:S(2)}) collective-permute-start(bf16[304,2048]{1,0:T(8,128)(2,1)S(1)} %add_convert_fusion.15), channel_id=1, source_target_pairs={{0,1},{1,2},{4,5},{5,6},{8,9},{9,10},{12,13},{13,14},{16,17},{17,1... | collective-permute-start | bytes 3735560 | tf_op jit(solution)/shard_map/ppermute | solution.py:201
  1256.6 30.0 %collective-permute-start.68 = (bf16[304,2048]{1,0:T(8,128)(2,1)S(1)}, bf16[304,2048]{1,0:T(8,128)(2,1)S(1)}, u32[]{:S(2)}, u32[]{:S(2)}) collective-permute-start(bf16[304,2048]{1,0:T(8,128)(2,1)S(1)} %get-tuple-element.352), channel_id=1, source_target_pairs={{0,1},{1,2},{2,3},{4,5},{5,6},{6,7},{8,9},{9,10},{10,11},{12,13},{... | collective-permute-start | bytes 3735560 | tf_op jit(solution)/shard_map/ppermute | solution.py:201
  1317.8 477.6 %reduce-scatter.15.cloned.1.call-start = ((), (), s32[]{:S(2)}) async-start(), calls=%async_computation.14 | async-start | bytes 18874368 | tf_op jit(solution)/shard_map/reduce_scatter | solution.py:405
  1317.8 32.3 %collective-permute-start.73 = (bf16[304,2048]{1,0:T(8,128)(2,1)}, bf16[304,2048]{1,0:T(8,128)(2,1)S(1)}, u32[]{:S(2)}, u32[]{:S(2)}) collective-permute-start(bf16[304,2048]{1,0:T(8,128)(2,1)} %get-tuple-element.179), channel_id=1, source_target_pairs={{1,0},{2,1},{3,2},{5,4},{6,5},{7,6},{9,8},{10,9},{11,10},{13,12},{... | collective-permute-start | bytes 3735560 | tf_op jit(solution)/shard_map/ppermute | solution.py:178
  1319.1 32.3 %collective-permute-start.74 = (bf16[304,2048]{1,0:T(8,128)(2,1)S(1)}, bf16[304,2048]{1,0:T(8,128)(2,1)}, u32[]{:S(2)}, u32[]{:S(2)}) collective-permute-start(bf16[304,2048]{1,0:T(8,128)(2,1)S(1)} %collective-permute-done.72), channel_id=1, source_target_pairs={{1,2},{2,3},{5,6},{6,7},{9,10},{10,11},{13,14},{14,15},{17,18},{18... | collective-permute-start | bytes 3735560 | tf_op jit(solution)/shard_map/ppermute | solution.py:175
  1350.1 36.0 %collective-permute-start.75 = (bf16[304,2048]{1,0:T(8,128)(2,1)S(1)}, bf16[304,2048]{1,0:T(8,128)(2,1)}, u32[]{:S(2)}, u32[]{:S(2)}) collective-permute-start(bf16[304,2048]{1,0:T(8,128)(2,1)S(1)} %collective-permute-done.73), channel_id=1, source_target_pairs={{1,0},{2,1},{5,4},{6,5},{9,8},{10,9},{13,12},{14,13},{17,16},{18,1... | collective-permute-start | bytes 3735560 | tf_op jit(solution)/shard_map/ppermute | solution.py:178
  1351.4 39.9 %collective-permute-start.76 = (bf16[304,2048]{1,0:T(8,128)(2,1)}, bf16[304,2048]{1,0:T(8,128)(2,1)}, u32[]{:S(2)}, u32[]{:S(2)}) collective-permute-start(bf16[304,2048]{1,0:T(8,128)(2,1)} %collective-permute-done.74), channel_id=1, source_target_pairs={{2,3},{6,7},{10,11},{14,15},{18,19},{22,23},{26,27},{30,31}} | collective-permute-start | bytes 3735560 | tf_op jit(solution)/shard_map/ppermute | solution.py:175
  1383.9 460.4 %reduce-scatter.11.cloned.1.call-start = ((), (), s32[]{:S(2)}) async-start(), calls=%async_computation.12 | async-start | bytes 1179648 | tf_op jit(solution)/shard_map/reduce_scatter | solution.py:397
  1386.1 34.4 %collective-permute-start.77 = (bf16[304,2048]{1,0:T(8,128)(2,1)}, bf16[304,2048]{1,0:T(8,128)(2,1)S(1)}, u32[]{:S(2)}, u32[]{:S(2)}) collective-permute-start(bf16[304,2048]{1,0:T(8,128)(2,1)} %collective-permute-done.75), channel_id=1, source_target_pairs={{1,0},{5,4},{9,8},{13,12},{17,16},{21,20},{25,24},{29,28}} | collective-permute-start | bytes 3735560 | tf_op jit(solution)/shard_map/ppermute | solution.py:178
  1422.4 104.6 %collective-permute-start.78 = (bf16[304,2048]{1,0:T(8,128)(2,1)}, bf16[304,2048]{1,0:T(8,128)(2,1)}, u32[]{:S(2)}, u32[]{:S(2)}) collective-permute-start(bf16[304,2048]{1,0:T(8,128)(2,1)} %get-tuple-element.180), channel_id=1, source_target_pairs={{0,1},{1,2},{2,3},{4,5},{5,6},{6,7},{8,9},{9,10},{10,11},{12,13},{... | collective-permute-start | bytes 3735560 | tf_op jit(solution)/shard_map/ppermute | solution.py:175
  1425.0 102.8 %collective-permute-start.79 = (bf16[304,2048]{1,0:T(8,128)(2,1)}, bf16[304,2048]{1,0:T(8,128)(2,1)}, u32[]{:S(2)}, u32[]{:S(2)}) collective-permute-start(bf16[304,2048]{1,0:T(8,128)(2,1)} %get-tuple-element.180), channel_id=1, source_target_pairs={{1,0},{2,1},{3,2},{5,4},{6,5},{7,6},{9,8},{10,9},{11,10},{13,12},{... | collective-permute-start | bytes 3735560 | tf_op jit(solution)/shard_map/ppermute | solution.py:178
  1531.0 27.4 %collective-permute-start.82 = (bf16[304,2048]{1,0:T(8,128)(2,1)S(1)}, bf16[304,2048]{1,0:T(8,128)(2,1)S(1)}, u32[]{:S(2)}, u32[]{:S(2)}) collective-permute-start(bf16[304,2048]{1,0:T(8,128)(2,1)S(1)} %collective-permute-done.80), channel_id=1, source_target_pairs={{2,3},{6,7},{10,11},{14,15},{18,19},{22,23},{26,27},{30,31}} | collective-permute-start | bytes 3735560 | tf_op jit(solution)/shard_map/ppermute | solution.py:175
  1582.2 79.8 %collective-permute-start.84 = (bf16[304,2048]{1,0:T(8,128)(2,1)}, bf16[304,2048]{1,0:T(8,128)(2,1)}, u32[]{:S(2)}, u32[]{:S(2)}) collective-permute-start(bf16[304,2048]{1,0:T(8,128)(2,1)} %get-tuple-element.350), channel_id=1, source_target_pairs={{0,1},{4,5},{8,9},{12,13},{16,17},{20,21},{24,25},{28,29}} | collective-permute-start | bytes 3735560 | tf_op jit(solution)/shard_map/ppermute | solution.py:201
  1584.7 86.5 %collective-permute-start.87 = (bf16[304,2048]{1,0:T(8,128)(2,1)}, bf16[304,2048]{1,0:T(8,128)(2,1)}, u32[]{:S(2)}, u32[]{:S(2)}) collective-permute-start(bf16[304,2048]{1,0:T(8,128)(2,1)} %get-tuple-element.351), channel_id=1, source_target_pairs={{3,2},{7,6},{11,10},{15,14},{19,18},{23,22},{27,26},{31,30}} | collective-permute-start | bytes 3735560 | tf_op jit(solution)/shard_map/ppermute | solution.py:207
  1703.6 29.8 %collective-permute-start.86 = (bf16[304,2048]{1,0:T(8,128)(2,1)}, bf16[304,2048]{1,0:T(8,128)(2,1)}, u32[]{:S(2)}, u32[]{:S(2)}) collective-permute-start(bf16[304,2048]{1,0:T(8,128)(2,1)} %get-tuple-element.348), channel_id=1, source_target_pairs={{0,1},{1,2},{2,3},{4,5},{5,6},{6,7},{8,9},{9,10},{10,11},{12,13},{... | collective-permute-start | bytes 3735560 | tf_op jit(solution)/shard_map/ppermute | solution.py:201
  1750.2 97.5 %reduce-scatter.13.cloned.1.call-start = ((), (), s32[]{:S(2)}) async-start(), calls=%async_computation.13 | async-start | bytes 2359296 | tf_op jit(solution)/shard_map/reduce_scatter | solution.py:402
  1755.5 46.4 %collective-permute-start.93 = (bf16[304,2048]{1,0:T(8,128)(2,1)}, bf16[304,2048]{1,0:T(8,128)(2,1)}, u32[]{:S(2)}, u32[]{:S(2)}) collective-permute-start(bf16[304,2048]{1,0:T(8,128)(2,1)} %get-tuple-element.347), channel_id=1, source_target_pairs={{3,2},{7,6},{11,10},{15,14},{19,18},{23,22},{27,26},{31,30}} | collective-permute-start | bytes 3735560 | tf_op jit(solution)/shard_map/ppermute | solution.py:207
  1768.6 33.2 %collective-permute-start.91 = (bf16[304,2048]{1,0:T(8,128)(2,1)}, bf16[304,2048]{1,0:T(8,128)(2,1)}, u32[]{:S(2)}, u32[]{:S(2)}) collective-permute-start(bf16[304,2048]{1,0:T(8,128)(2,1)} %add_convert_fusion.7), channel_id=1, source_target_pairs={{0,1},{1,2},{4,5},{5,6},{8,9},{9,10},{12,13},{13,14},{16,17},{17,1... | collective-permute-start | bytes 3735560 | tf_op jit(solution)/shard_map/ppermute | solution.py:201
  1780.9 100.7 %reduce-scatter.9.cloned.1.call-start = ((), (), s32[]{:S(2)}) async-start(), calls=%async_computation.11 | async-start | bytes 2359296 | tf_op jit(solution)/shard_map/reduce_scatter | solution.py:394
  1819.8 126.6 %reduce-scatter.19.cloned.1.call-start = ((), (), s32[]{:S(2)}) async-start(), calls=%async_computation.16 | async-start | bytes 589824
  1819.8 64.9 %collective-permute-start.92 = (bf16[304,2048]{1,0:T(8,128)(2,1)S(1)}, bf16[304,2048]{1,0:T(8,128)(2,1)}, u32[]{:S(2)}, u32[]{:S(2)}) collective-permute-start(bf16[304,2048]{1,0:T(8,128)(2,1)S(1)} %copy-done.109), channel_id=1, source_target_pairs={{0,1},{1,2},{2,3},{4,5},{5,6},{6,7},{8,9},{9,10},{10,11},{12,13},{... | collective-permute-start | bytes 3735560 | tf_op jit(solution)/shard_map/ppermute | solution.py:201
  1824.9 59.8 %collective-permute-start.95 = (bf16[304,2048]{1,0:T(8,128)(2,1)S(1)}, bf16[304,2048]{1,0:T(8,128)(2,1)}, u32[]{:S(2)}, u32[]{:S(2)}) collective-permute-start(bf16[304,2048]{1,0:T(8,128)(2,1)S(1)} %add_convert_fusion.4), channel_id=1, source_target_pairs={{1,0},{2,1},{3,2},{5,4},{6,5},{7,6},{9,8},{10,9},{11,10},{13,12},{... | collective-permute-start | bytes 3735560 | tf_op jit(solution)/shard_map/ppermute | solution.py:207
  (246 other events, 4180.2 us)
Sparse Core Ops, SparseCore 0:
  10.5 26.0 all-gather.5
  39.1 27.7 all-gather.7
  69.4 28.0 all-gather.9
  99.8 89.7 all-gather.11
  610.6 59.2 all-gather.13
  1317.9 74.6 reduce-scatter.16
  1396.2 115.9 reduce-scatter.14
  1750.3 41.8 reduce-scatter.10
  1795.5 41.1 reduce-scatter.12
  1840.4 41.1 reduce-scatter.8
  1915.0 31.3 reduce-scatter.18

commit v7 on v5

--- a/solution.py
+++ b/solution.py
@@ -241,9 +241,15 @@
     seconds = (query_square, keyval_square, output_square, gateup_square, down_square, gains_square)
     rounded = tuple((master.astype(jnp.bfloat16) for master in masters))
     gathered = (
-        lax.all_gather(rounded[0], "dp", axis=0, tiled=True),
-        lax.all_gather(rounded[1], "dp", axis=0, tiled=True),
-        lax.all_gather(rounded[2], "dp", axis=1, tiled=True),
+        lax.all_gather(
+            lax.all_gather(rounded[0], "tensor", axis=1, tiled=True), "dp", axis=0, tiled=True
+        ),
+        lax.all_gather(
+            lax.all_gather(rounded[1], "tensor", axis=1, tiled=True), "dp", axis=0, tiled=True
+        ),
+        lax.all_gather(
+            lax.all_gather(rounded[2], "tensor", axis=0, tiled=True), "dp", axis=1, tiled=True
+        ),
         lax.all_gather(rounded[3], "dp", axis=0, tiled=True),
         lax.all_gather(rounded[4], "dp", axis=1, tiled=True),
         lax.all_gather(rounded[5], "dp", axis=1, tiled=True),
@@ -253,36 +259,52 @@
     tensor_count = lax.axis_size("tensor")
     group_rows = tokens.shape[2] * tensor_count
     block_rows = group_rows // 2
-    keyval_heads = full_keyval.shape[1]
-    query_heads = full_query.shape[1] // HD
+    place = lax.axis_index("tensor")
+    rows = tokens.shape[2]
+    all_query_heads = full_query.shape[1] // HD
+    keyval_heads = full_keyval.shape[1] // tensor_count
+    query_heads = all_query_heads // tensor_count
     head_repeat = query_heads // keyval_heads
 
     def micro_step(token_rows, cot_rows, lengths):
         visible, position = layout(lengths, group_rows)
         cos_table, sin_table = rope_tables(position)
+        cos_own, sin_own = rope_tables(lax.dynamic_slice_in_dim(position, place * rows, rows))
         start_rows = token_rows.astype(jnp.float32)
         scale_one = lax.rsqrt(jnp.mean(start_rows * start_rows, axis=1, keepdims=True) + norm_eps)
         hat_one = start_rows * scale_one
         normed_one = (hat_one * gain_values[0][None, :]).astype(jnp.bfloat16)
-        rows_one = yield ("gather", normed_one)
-        query_raw = jnp.dot(rows_one, full_query, preferred_element_type=jnp.float32).reshape(
-            group_rows, query_heads, HD
+        query_raw = jnp.dot(normed_one, full_query, preferred_element_type=jnp.float32).reshape(
+            rows, all_query_heads, HD
         )
         keyval_raw = jnp.einsum(
-            "rd,dhk->rhk", rows_one, full_keyval, preferred_element_type=jnp.float32
-        )
-        queries = (
-            rotate(query_raw, cos_table, sin_table)
-            .astype(jnp.bfloat16)
-            .reshape(group_rows, keyval_heads, head_repeat, HD)
-        )
-        key_rows = rotate(keyval_raw[:, :, :HD], cos_table, sin_table).astype(jnp.bfloat16)
-        values = keyval_raw[:, :, HD:].astype(jnp.bfloat16)
+            "rd,dhk->rhk", normed_one, full_keyval, preferred_element_type=jnp.float32
+        )
+        queries_own = rotate(query_raw, cos_own, sin_own).astype(jnp.bfloat16)
+        keyval_own = jnp.concatenate(
+            [rotate(keyval_raw[:, :, :HD], cos_own, sin_own), keyval_raw[:, :, HD:]], axis=2
+        ).astype(jnp.bfloat16)
+        query_width = query_heads * HD
+        projected = yield (
+            "to_heads",
+            jnp.concatenate(
+                [
+                    queries_own.reshape(rows, tensor_count, query_width),
+                    keyval_own.reshape(rows, tensor_count, -1),
+                ],
+                axis=2,
+            ),
+        )
+        projected = projected.reshape(group_rows, -1)
+        queries = projected[:, :query_width].reshape(group_rows, keyval_heads, head_repeat, HD)
+        keyval_rows = projected[:, query_width:].reshape(group_rows, keyval_heads, 2 * HD)
+        key_rows = keyval_rows[:, :, :HD]
+        values = keyval_rows[:, :, HD:]
         mixed_full, log_totals = attend(queries, key_rows, values, visible, block_rows)
-        mixed = mixed_full.astype(jnp.bfloat16).reshape(group_rows, query_heads * HD)
-        attn_branch = yield (
-            "scatter", jnp.dot(mixed, full_output, preferred_element_type=jnp.float32)
-        )
+        mixed = yield (
+            "to_rows", mixed_full.astype(jnp.bfloat16).reshape(group_rows, query_width)
+        )
+        attn_branch = jnp.dot(mixed, full_output, preferred_element_type=jnp.float32)
         middle = start_rows + branch_scale * attn_branch
         scale_two = lax.rsqrt(jnp.mean(middle * middle, axis=1, keepdims=True) + norm_eps)
         hat_two = middle * scale_two
@@ -320,34 +342,42 @@
         middle_back, gain_two = norm_back(normed_two_grad, hat_two, scale_two, gain_values[1])
         middle_grad = upstream + middle_back
         attn_grad = (branch_scale * middle_grad).astype(jnp.bfloat16)
-        attn_grad_all = yield ("gather", attn_grad)
-        grad_output = contract_rows(mixed, attn_grad_all)
-        mixed_grad = (
-            contract_cols(attn_grad_all, full_output)
+        grad_output = contract_rows(mixed, attn_grad)
+        mixed_grad = yield (
+            "to_heads",
+            contract_cols(attn_grad, full_output)
             .astype(jnp.bfloat16)
-            .reshape(group_rows, keyval_heads, head_repeat, HD)
-        )
+            .reshape(rows, tensor_count, query_width),
+        )
+        mixed_grad = mixed_grad.reshape(group_rows, keyval_heads, head_repeat, HD)
         query_grad, key_grad, value_grad = attend_back(
             queries, key_rows, values, visible, log_totals, mixed_grad, block_rows
         )
-        query_raw_grad = (
-            rotate_back(query_grad.reshape(group_rows, query_heads, HD), cos_table, sin_table)
-            .astype(jnp.bfloat16)
-            .reshape(group_rows, query_heads * HD)
-        )
-        keyval_raw_grad = jnp.concatenate(
-            [rotate_back(key_grad, cos_table, sin_table), value_grad], axis=2
-        ).astype(jnp.bfloat16)
-        grad_query = contract_rows(rows_one, query_raw_grad)
+        raw_grads = yield (
+            "to_rows",
+            jnp.concatenate(
+                [
+                    rotate_back(
+                        query_grad.reshape(group_rows, query_heads, HD), cos_table, sin_table
+                    ).reshape(group_rows, query_width),
+                    jnp.concatenate(
+                        [rotate_back(key_grad, cos_table, sin_table), value_grad], axis=2
+                    ).reshape(group_rows, -1),
+                ],
+                axis=1,
+            ).astype(jnp.bfloat16),
+        )
+        raw_grads = raw_grads.reshape(rows, tensor_count, -1)
+        query_raw_grad = raw_grads[:, :, :query_width].reshape(rows, all_query_heads * HD)
+        keyval_raw_grad = raw_grads[:, :, query_width:].reshape(
+            rows, tensor_count * keyval_heads, 2 * HD
+        )
+        grad_query = contract_rows(normed_one, query_raw_grad)
         grad_keyval = jnp.einsum(
-            "rd,rhk->dhk", rows_one, keyval_raw_grad, preferred_element_type=jnp.float32
-        )
-        normed_one_grad = yield (
-            "scatter",
-            contract_cols(query_raw_grad, full_query)
-            + jnp.einsum(
-                "rhk,dhk->rd", keyval_raw_grad, full_keyval, preferred_element_type=jnp.float32
-            ),
+            "rd,rhk->dhk", normed_one, keyval_raw_grad, preferred_element_type=jnp.float32
+        )
+        normed_one_grad = contract_cols(query_raw_grad, full_query) + jnp.einsum(
+            "rhk,dhk->rd", keyval_raw_grad, full_keyval, preferred_element_type=jnp.float32
         )
         start_back, gain_one = norm_back(normed_one_grad, hat_one, scale_one, gain_values[0])
         input_rows = middle_grad + start_back
@@ -374,8 +404,12 @@
                 previous, value = lax.optimization_barrier((previous, value))
             if kind == "gather":
                 previous = line_gather(value, tensor_count)
+            elif kind == "scatter":
+                previous = line_scatter(value, tensor_count)
+            elif kind == "to_heads":
+                previous = lax.all_to_all(value, "tensor", 1, 0, tiled=True)
             else:
-                previous = line_scatter(value, tensor_count)
+                previous = lax.all_to_all(value, "tensor", 0, 1, tiled=True)
             try:
                 requests[index] = stream.send(previous)
             except StopIteration as stop:
@@ -389,26 +423,48 @@
     input_grad = jnp.stack(grad_list)[:, None]
     width = totals[0].shape[0]
     gain_total = lax.psum(totals[5], "tensor")
+    gateup_sum = (
+        lax.psum_scatter(
+            totals[3].reshape(width, -1).astype(jnp.bfloat16), "dp", scatter_dimension=0, tiled=True
+        )
+        .astype(jnp.float32)
+        .reshape(-1, *totals[3].shape[1:])
+    )
+    down_sum = lax.psum_scatter(
+        totals[4].astype(jnp.bfloat16), "dp", scatter_dimension=1, tiled=True
+    ).astype(jnp.float32)
+    query_low, keyval_low, output_low, _, _ = lax.optimization_barrier(
+        (
+            totals[0].astype(jnp.bfloat16),
+            totals[1].reshape(width, -1).astype(jnp.bfloat16),
+            totals[2].astype(jnp.bfloat16),
+            gateup_sum,
+            down_sum,
+        )
+    )
     summed = (
         lax.psum_scatter(
-            totals[0].astype(jnp.bfloat16), "dp", scatter_dimension=0, tiled=True
+            lax.psum_scatter(query_low, "dp", scatter_dimension=0, tiled=True),
+            "tensor",
+            scatter_dimension=1,
+            tiled=True,
         ).astype(jnp.float32),
         lax.psum_scatter(
-            totals[1].reshape(width, -1).astype(jnp.bfloat16), "dp", scatter_dimension=0, tiled=True
+            lax.psum_scatter(keyval_low, "dp", scatter_dimension=0, tiled=True),
+            "tensor",
+            scatter_dimension=1,
+            tiled=True,
         )
         .astype(jnp.float32)
-        .reshape(-1, *totals[1].shape[1:]),
+        .reshape(-1, keyval_heads, totals[1].shape[2]),
         lax.psum_scatter(
-            totals[2].astype(jnp.bfloat16), "dp", scatter_dimension=1, tiled=True
+            lax.psum_scatter(output_low, "dp", scatter_dimension=1, tiled=True),
+            "tensor",
+            scatter_dimension=0,
+            tiled=True,
         ).astype(jnp.float32),
-        lax.psum_scatter(
-            totals[3].reshape(width, -1).astype(jnp.bfloat16), "dp", scatter_dimension=0, tiled=True
-        )
-        .astype(jnp.float32)
-        .reshape(-1, *totals[3].shape[1:]),
-        lax.psum_scatter(
-            totals[4].astype(jnp.bfloat16), "dp", scatter_dimension=1, tiled=True
-        ).astype(jnp.float32),
+        gateup_sum,
+        down_sum,
         lax.psum_scatter(
             gain_total.astype(jnp.bfloat16), "dp", scatter_dimension=1, tiled=True
         ).astype(jnp.float32),

time: 2010 us -> 2030 us (level)
  starting transfers between devices: 229 us -> 163 us
  local copies, waits for them, and re-layouts: 126 us -> 186 us
  other arithmetic: 242 us -> 200 us
  matrix products: 543 us -> 575 us
  waiting for transfers between devices: 763 us -> 790 us
  blocking collectives: 69.8 us -> 91.4 us
    ppermute x24 -> x12, waiting for transfers between devices: 322 us -> 159 us  [line_gather(): lax.ppermute(from_right, 'tensor', [(i, i - 1) for i in range(1, count -...]
    reduce_scatter x3 -> x6, waiting for transfers between devices: 23.9 us -> 164 us  [the longest x1 73.1 us: per_device(): lax.psum_scatter(output_low, 'dp', scatter_dimension=1, tiled=True)]
    ppermute x24 -> x12, waiting for transfers between devices: 258 us -> 145 us  [line_scatter(): lax.ppermute(send.astype(jnp.bfloat16), 'tensor', [(i, i + 1) for i in ra...]
    all_gather x3 -> x5, waiting for transfers between devices: 0.06 us -> 102 us  [the longest x1 48.5 us: per_device(): lax.all_gather(lax.all_gather(rounded[0], 'tensor', axis=1, tiled=True),...]
    reduce_scatter x1, waiting for transfers between devices: 0.01 us -> 74.7 us  [per_device(): lax.psum_scatter(totals[4].astype(jnp.bfloat16), 'dp', scatter_dimension=...]
    ppermute x24 -> x12, waiting for transfers between devices: 72.4 us -> 18.6 us  [line_scatter(): lax.ppermute(send.astype(jnp.bfloat16), 'tensor', [(i, i - 1) for i in ra...]
    ppermute x24 -> x12, starting transfers between devices: 120 us -> 73.7 us  [line_scatter(): lax.ppermute(send.astype(jnp.bfloat16), 'tensor', [(i, i + 1) for i in ra...]
    all_to_all x0 -> x8, starting transfers between devices: none -> 45.1 us  [the longest x4 24.2 us: per_device(): previous = lax.all_to_all(value, 'tensor', 1, 0, tiled=True)]
  transfers between devices with their start and end apart: 107 -> 72, of which waited for: 47 -> 39; matrix products, arithmetic and copies ran while one was open for 42% -> 42% of each run, Pallas kernels for 0% -> 0%
where the time goes in v7:
time: 2030 us
  waiting for transfers between devices  790 us (39%)
  matrix products  575 us (28%)
  other arithmetic  200 us (10%)
  local copies, waits for them, and re-layouts  186 us (9%)
  starting transfers between devices  163 us (8%)
  blocking collectives  91.4 us (5%)
  between operations  20.4 us (1%)
    ppermute x12, waiting for transfers between devices, line_gather(): lax.ppermute(from_right, 'tensor', [(i, i - 1) for i in range(1, count -...  159 us
    ppermute x12, waiting for transfers between devices, line_scatter(): lax.ppermute(send.astype(jnp.bfloat16), 'tensor', [(i, i + 1) for i in ra...  145 us
    dot_general x6, matrix products, contract_cols(): lax.dot_general(left, right, (((1,), (1,)), ((), ())), preferred_element_...  78.4 us
    dot_general x6, matrix products, contract_rows(): lax.dot_general(left, right, (((0,), (0,)), ((), ())), preferred_element_...  76.5 us
    reduce_scatter x1, waiting for transfers between devices, per_device(): lax.psum_scatter(totals[4].astype(jnp.bfloat16), 'dp', scatter_dimension=...  74.7 us
    ppermute x12, starting transfers between devices, line_scatter(): lax.ppermute(send.astype(jnp.bfloat16), 'tensor', [(i, i + 1) for i in ra...  73.7 us
    reduce_scatter x1, waiting for transfers between devices, per_device(): lax.psum_scatter(output_low, 'dp', scatter_dimension=1, tiled=True)  73.1 us
    ppermute x12, waiting for transfers between devices, line_gather(): lax.ppermute(from_left, 'tensor', [(i, i + 1) for i in range(step - 1, co...  66 us
  transfers between devices with their start and end apart: 72, of which 39 were waited for; matrix products, arithmetic and copies ran while one was open for 42% of the time, Pallas kernels for 0%

profile of v7, /device:TPU:0, one launch (start us, length us, event | category | flops | bytes accessed | tf_op | source)
XLA Modules:
  0.0 2025.4 jit_solution(9457975343071523772)
XLA Ops:
  13.6 24.5 %all_gather.30 = bf16[256,8,128]{2,0,1:T(8,128)(2,1)} all-gather(bf16[256,2,128]{2,0,1:T(8,128)(2,1)S(1)} %copy.362), channel_id=1, replica_groups=mesh['dp'=8,'tensor'=4] {'tensor'}, dimensions={1}, use_global_device_ids=true | all-gather | bytes 655360 | tf_op jit(solution)/shard_map/all_gather | solution.py:248
  45.8 30.7 %all-gather.14.cloned.1.call-done = bf16[2048,256]{1,0:T(8,128)(2,1)} async-done(((bf16[512,256]{1,0:T(8,128)(2,1)}), bf16[2048,256]{1,0:T(8,128)(2,1)}) %all-gather.14.cloned.1.call-update) | async-done | bytes 1048592 | tf_op jit(solution)/shard_map/all_gather | solution.py:251
  86.5 9.6 all_gather.27
  99.3 15.1 all-gather.12.cloned.1.call-done
  122.0 48.5 %all-gather.10.cloned.1.call-done = bf16[2048,2048]{1,0:T(8,128)(2,1)} async-done(((bf16[256,2048]{1,0:T(8,128)(2,1)}), bf16[2048,2048]{1,0:T(8,128)(2,1)}) %all-gather.10.cloned.1.call-update) | async-done | bytes 8388624 | tf_op jit(solution)/shard_map/all_gather | solution.py:244
  170.4 12.4 copy.250
  234.9 10.7 all-to-all-done
  275.1 12.6 fusion.134
  331.4 12.4 fusion.133
  372.9 20.4 %all-to-all-done.3 = bf16[4,304,512]{2,1,0:T(8,128)(2,1)} async-done(((bf16[4,304,512]{2,1,0:T(8,128)(2,1)}), bf16[4,304,512]{2,1,0:T(8,128)(2,1)}, u32[]{:S(2)}, u32[]{:S(2)}) %all-to-all-start.3) | async-done | bytes 1245216 | tf_op jit(solution)/shard_map/all_to_all | solution.py:412
  405.6 24.8 %collective-permute-done = bf16[304,2048]{1,0:T(8,128)(2,1)S(1)} collective-permute-done((bf16[304,2048]{1,0:T(8,128)(2,1)S(1)}, bf16[304,2048]{1,0:T(8,128)(2,1)S(1)}, u32[]{:S(2)}, u32[]{:S(2)}) %collective-permute-start) | collective-permute-done | bytes 1245216 | tf_op jit(solution)/shard_map/ppermute | solution.py:175
  439.9 24.5 %collective-permute-done.3 = bf16[304,2048]{1,0:T(8,128)(2,1)} collective-permute-done((bf16[304,2048]{1,0:T(8,128)(2,1)}, bf16[304,2048]{1,0:T(8,128)(2,1)}, u32[]{:S(2)}, u32[]{:S(2)}) %collective-permute-start.3) | collective-permute-done | bytes 1245216 | tf_op jit(solution)/shard_map/ppermute | solution.py:178
  472.5 20.8 %collective-permute-done.5 = bf16[304,2048]{1,0:T(8,128)(2,1)S(1)} collective-permute-done((bf16[304,2048]{1,0:T(8,128)(2,1)}, bf16[304,2048]{1,0:T(8,128)(2,1)S(1)}, u32[]{:S(2)}, u32[]{:S(2)}) %collective-permute-start.5) | collective-permute-done | bytes 1245216 | tf_op jit(solution)/shard_map/ppermute | solution.py:178
  496.5 22.0 %collective-permute-done.6 = bf16[304,2048]{1,0:T(8,128)(2,1)S(1)} collective-permute-done((bf16[304,2048]{1,0:T(8,128)(2,1)S(1)}, bf16[304,2048]{1,0:T(8,128)(2,1)S(1)}, u32[]{:S(2)}, u32[]{:S(2)}) %collective-permute-start.6) | collective-permute-done | bytes 1245216 | tf_op jit(solution)/shard_map/ppermute | solution.py:175
  525.4 24.9 %collective-permute-done.9 = bf16[304,2048]{1,0:T(8,128)(2,1)S(1)} collective-permute-done((bf16[304,2048]{1,0:T(8,128)(2,1)S(1)}, bf16[304,2048]{1,0:T(8,128)(2,1)S(1)}, u32[]{:S(2)}, u32[]{:S(2)}) %collective-permute-start.9) | collective-permute-done | bytes 1245216 | tf_op jit(solution)/shard_map/ppermute | solution.py:178
  560.1 16.0 collective-permute-done.11
  581.1 19.2 collective-permute-done.12
  610.1 24.5 %collective-permute-done.15 = bf16[304,2048]{1,0:T(8,128)(2,1)} collective-permute-done((bf16[304,2048]{1,0:T(8,128)(2,1)}, bf16[304,2048]{1,0:T(8,128)(2,1)}, u32[]{:S(2)}, u32[]{:S(2)}) %collective-permute-start.15) | collective-permute-done | bytes 1245216 | tf_op jit(solution)/shard_map/ppermute | solution.py:178
  661.9 27.5 %fusion.59 = f32[1216,2,2048]{2,0,1:T(8,128)} fusion(bf16[2048,2,2048]{2,0,1:T(8,128)(2,1)} %all-gather.18.cloned.1.call-done, bf16[1216,2048]{1,0:T(8,128)(2,1)} %copy-done.55), kind=kOutput, calls=%fused_computation.104 | convolution fusion | flops 20401094656 | bytes 41680896 | tf_op jit(solution)/shard_map/rd,dcf->rcf/dot_general | solution.py:313
  692.5 25.7 %fusion.61 = (bf16[1216,1,2048]{2,0,1:T(8,128)(2,1)}, bf16[1216,1,2048]{2,0,1:T(8,128)(2,1)}, bf16[1216,2048]{1,0:T(8,128)(2,1)}) fusion(f32[1216,2,2048]{2,0,1:T(8,128)} %fusion.59, bf16[1216,2048]{1,0:T(8,128)(2,1)} %constant_dynamic-update-slice_fusion.7, bf16[2048,2048]{1,0:T(8,128)(2,1)} %all-gather.20.cloned.1.call-done), kind=kOutput, calls=%fused_computation.106 | convolution fusion | flops 10237902848 | bytes 48234496 | tf_op jit(solution)/shard_map/dot_general | solution.py:162
  720.2 14.7 fusion.230
  734.9 13.2 collective-permute-done.21
  753.5 16.4 collective-permute-done.23
  775.1 20.1 collective-permute-done.24
  802.1 27.3 %fusion.56 = f32[1216,2,2048]{2,0,1:T(8,128)} fusion(bf16[2048,2,2048]{2,0,1:T(8,128)(2,1)} %all-gather.18.cloned.1.call-done, bf16[1216,2048]{1,0:T(8,128)(2,1)} %constant_dynamic-update-slice_fusion.14), kind=kOutput, calls=%fused_computation.101 | convolution fusion | flops 20401094656 | bytes 41680896 | tf_op jit(solution)/shard_map/rd,dcf->rcf/dot_general | solution.py:313
  832.1 26.1 %fusion.62 = (bf16[1216,1,2048]{2,0,1:T(8,128)(2,1)}, bf16[1216,1,2048]{2,0,1:T(8,128)(2,1)}, bf16[1216,2048]{1,0:T(8,128)(2,1)}) fusion(f32[1216,2,2048]{2,0,1:T(8,128)} %fusion.56, bf16[1216,2048]{1,0:T(8,128)(2,1)} %copy-done.54, bf16[2048,2048]{1,0:T(8,128)(2,1)} %all-gather.20.cloned.1.call-done), kind=kOutput, calls=%fused_computation.107 | convolution fusion | flops 10237902848 | bytes 48234496 | tf_op jit(solution)/shard_map/dot_general | solution.py:162
  864.5 13.3 fusion.231
  891.2 24.9 %collective-permute-done.30 = bf16[304,2048]{1,0:T(8,128)(2,1)S(1)} collective-permute-done((bf16[304,2048]{1,0:T(8,128)(2,1)S(1)}, bf16[304,2048]{1,0:T(8,128)(2,1)S(1)}, u32[]{:S(2)}, u32[]{:S(2)}) %collective-permute-start.30) | collective-permute-done | bytes 1245216 | tf_op jit(solution)/shard_map/ppermute | solution.py:201
  921.0 25.0 %collective-permute-done.31 = bf16[304,2048]{1,0:T(8,128)(2,1)S(1)} collective-permute-done((bf16[304,2048]{1,0:T(8,128)(2,1)S(1)}, bf16[304,2048]{1,0:T(8,128)(2,1)S(1)}, u32[]{:S(2)}, u32[]{:S(2)}) %collective-permute-start.31) | collective-permute-done | bytes 1245216 | tf_op jit(solution)/shard_map/ppermute | solution.py:201
  954.4 28.5 %convolution_bitcast_fusion.1 = f32[1216,2048]{1,0:T(8,128)} fusion(bf16[2048,2,2048]{2,0,1:T(8,128)(2,1)} %all-gather.18.cloned.1.call-done, bf16[1216,1,2048]{2,0,1:T(8,128)(2,1)} %get-tuple-element.328, bf16[1216,1,2048]{2,0,1:T(8,128)(2,1)} %get-tuple-element.327), kind=kOutput, calls=%fused_computation.81 | convolution fusion | flops 20406075392 | bytes 36700160 | tf_op jit(solution)/shard_map/rcf,dcf->rd/dot_general | solution.py:338
  995.0 15.6 collective-permute-start.36
  1011.3 21.6 %collective-permute-done.36 = bf16[304,2048]{1,0:T(8,128)(2,1)S(1)} collective-permute-done((bf16[304,2048]{1,0:T(8,128)(2,1)S(1)}, bf16[304,2048]{1,0:T(8,128)(2,1)S(1)}, u32[]{:S(2)}, u32[]{:S(2)}) %collective-permute-start.36) | collective-permute-done | bytes 1245216 | tf_op jit(solution)/shard_map/ppermute | solution.py:201
  1037.8 14.3 collective-permute-done.37
  1060.5 28.5 %convolution_bitcast_fusion = f32[1216,2048]{1,0:T(8,128)} fusion(bf16[2048,2,2048]{2,0,1:T(8,128)(2,1)} %all-gather.18.cloned.1.call-done, bf16[1216,1,2048]{2,0,1:T(8,128)(2,1)} %get-tuple-element.326, bf16[1216,1,2048]{2,0,1:T(8,128)(2,1)} %get-tuple-element.325), kind=kOutput, calls=%fused_computation.80 | convolution fusion | flops 20406075392 | bytes 36700160 | tf_op jit(solution)/shard_map/rcf,dcf->rd/dot_general | solution.py:338
  1095.6 16.5 collective-permute-start.42
  1112.9 25.1 %collective-permute-done.42 = bf16[304,2048]{1,0:T(8,128)(2,1)S(1)} collective-permute-done((bf16[304,2048]{1,0:T(8,128)(2,1)S(1)}, bf16[304,2048]{1,0:T(8,128)(2,1)S(1)}, u32[]{:S(2)}, u32[]{:S(2)}) %collective-permute-start.42) | collective-permute-done | bytes 1245216 | tf_op jit(solution)/shard_map/ppermute | solution.py:201
  1143.1 14.3 collective-permute-done.43
  1169.2 29.2 %fusion.42 = f32[2048,2,2048]{0,2,1:T(8,128)} fusion(bf16[1216,1,2048]{2,0,1:T(8,128)(2,1)} %get-tuple-element.326, bf16[1216,1,2048]{2,0,1:T(8,128)(2,1)} %get-tuple-element.325, bf16[1216,2048]{1,0:T(8,128)(2,1)} %constant_dynamic-update-slice_fusion.14), kind=kOutput, calls=%fused_computation.85 | convolution fusion | flops 20421017600 | bytes 48496640 | tf_op jit(solution)/shard_map/rd,rcf->dcf/dot_general | solution.py:333
  1225.1 9.4 all-to-all-start.6
  1234.5 30.5 %add_convert_fusion = bf16[2048,2,2048]{0,2,1:T(8,128)(2,1)} fusion(f32[2048,2,2048]{0,2,1:T(8,128)} %fusion.42, bf16[1216,1,2048]{2,0,1:T(8,128)(2,1)} %get-tuple-element.328, bf16[1216,1,2048]{2,0,1:T(8,128)(2,1)} %get-tuple-element.327, bf16[1216,2048]{1,0:T(8,128)(2,1)} %copy-done.55), kind=kOutput, calls=%fused_computation | convolution fusion | flops 20437794816 | bytes 65273856 | tf_op jit(solution)/shard_map/rd,rcf->dcf/dot_general | solution.py:333
  1286.4 9.0 fusion.164
  1295.4 9.6 fusion.16
  1310.9 18.3 fusion
  1329.2 12.8 fusion.120
  1342.0 9.9 fusion.18
  1354.8 18.2 fusion.2
  1396.4 11.5 fusion.19
  1417.5 16.9 fusion.3
  1434.4 17.1 fusion.5
  1464.4 11.0 fusion.123
  1492.2 9.8 fusion.173
  1502.0 10.3 add_convert_fusion.2
  1541.1 10.3 add_convert_fusion.3
  1558.5 17.8 fusion.234
  1576.3 19.7 add_convert_fusion.1
  1613.3 18.7 psum.14
  1649.0 35.6 %reduce-scatter.16.cloned.1.call-done = bf16[256,2048]{1,0:T(8,128)(2,1)} async-done(((bf16[2048,2048]{1,0:T(8,128)(2,1)}), bf16[256,2048]{1,0:T(8,128)(2,1)}) %reduce-scatter.16.cloned.1.call-update) | async-done | bytes 1048592 | tf_op jit(solution)/shard_map/reduce_scatter | solution.py:447
  1684.7 74.7 %reduce-scatter.14.cloned.1.call-done = bf16[2048,256]{1,0:T(8,128)(2,1)} async-done(((bf16[2048,2048]{1,0:T(8,128)(2,1)}), bf16[2048,256]{1,0:T(8,128)(2,1)}) %reduce-scatter.14.cloned.1.call-update) | async-done | bytes 1048592 | tf_op jit(solution)/shard_map/reduce_scatter | solution.py:433
  1770.7 26.4 %reduce-scatter.28.cloned.1.call-done = bf16[256,2]{1,0:T(8,128)(2,1)} async-done(((bf16[2048,2]{1,0:T(8,128)(2,1)}), bf16[256,2]{1,0:T(8,128)(2,1)}) %reduce-scatter.28.cloned.1.call-update) | async-done | bytes 1040
  1798.7 73.1 %reduce-scatter.24.cloned.1.call-done = bf16[2048,256]{1,0:T(8,128)(2,1)} async-done(((bf16[2048,2048]{1,0:T(8,128)(2,1)}), bf16[2048,256]{1,0:T(8,128)(2,1)}) %reduce-scatter.24.cloned.1.call-update) | async-done | bytes 1048592 | tf_op jit(solution)/shard_map/reduce_scatter | solution.py:461
  1871.9 18.2 multiply_reduce_fusion
  1899.0 24.6 %reduce-scatter.18.cloned.1.call-done = bf16[256,512]{1,0:T(8,128)(2,1)} async-done(((bf16[256,2048]{1,0:T(8,128)(2,1)}), bf16[256,512]{1,0:T(8,128)(2,1)}) %reduce-scatter.18.cloned.1.call-update) | async-done | bytes 262160 | tf_op jit(solution)/shard_map/reduce_scatter | solution.py:446
  1926.6 24.9 %reduce-scatter.26.cloned.1.call-done = bf16[512,256]{1,0:T(8,128)(2,1)} async-done(((bf16[2048,256]{1,0:T(8,128)(2,1)}), bf16[512,256]{1,0:T(8,128)(2,1)}) %reduce-scatter.26.cloned.1.call-update) | async-done | bytes 262160 | tf_op jit(solution)/shard_map/reduce_scatter | solution.py:460
  1962.5 38.6 %psum.15 = f32[2,7]{1,0:T(2,128)S(1)} all-reduce(f32[2,7]{1,0:T(2,128)S(1)} %pad_maximum_fusion.22), channel_id=1, replica_groups=mesh['dp'=8,'tensor'=4] {'dp','tensor'}, use_global_device_ids=true, to_apply=%region_52.53 | all-reduce | flops 14 | bytes 112 | tf_op jit(solution)/shard_map/psum | solution.py:495
  (647 shorter events, 626.7 us)
Async XLA Ops:
  7.2 38.6 %all-gather.8.cloned.1.call-start = ((), (), s32[]{:S(2)}) async-start(), calls=%async_computation.17 | async-start | bytes 1310720 | tf_op jit(solution)/shard_map/all_gather | solution.py:245
  9.9 66.5 %all-gather.14.cloned.1.call-start = ((), (), s32[]{:S(2)}) async-start(), calls=%async_computation.20 | async-start | bytes 1310720 | tf_op jit(solution)/shard_map/all_gather | solution.py:251
  12.6 101.8 %all-gather.12.cloned.1.call-start = ((), (), s32[]{:S(2)}) async-start(), calls=%async_computation.19 | async-start | bytes 4718592 | tf_op jit(solution)/shard_map/all_gather | solution.py:247
  38.2 132.3 %all-gather.10.cloned.1.call-start = ((), (), s32[]{:S(2)}) async-start(), calls=%async_computation.18 | async-start | bytes 9437184 | tf_op jit(solution)/shard_map/all_gather | solution.py:244
  45.8 319.1 %all-gather.16.cloned.1.call-start = ((), (), s32[]{:S(2)}) async-start(), calls=%async_computation.21 | async-start | bytes 9437184 | tf_op jit(solution)/shard_map/all_gather | solution.py:250
  76.5 585.4 %all-gather.18.cloned.1.call-start = ((), (), s32[]{:S(2)}) async-start(), calls=%async_computation.22 | async-start | bytes 18874368 | tf_op jit(solution)/shard_map/all_gather | solution.py:253
  196.9 48.6 %all-to-all-start = ((bf16[304,4,768]{2,0,1:T(8,128)(2,1)}), bf16[304,4,768]{2,0,1:T(8,128)(2,1)}, u32[]{:S(2)}, u32[]{:S(2)}) async-start(bf16[304,4,768]{2,0,1:T(8,128)(2,1)} %pad_maximum_fusion.10), calls=%async_computation | async-start | bytes 3735552 | tf_op jit(solution)/shard_map/all_to_all | solution.py:410
  245.6 55.3 %all-to-all-start.2 = ((bf16[304,4,768]{2,0,1:T(8,128)(2,1)}), bf16[304,4,768]{2,0,1:T(8,128)(2,1)}, u32[]{:S(2)}, u32[]{:S(2)}) async-start(bf16[304,4,768]{2,0,1:T(8,128)(2,1)} %pad_maximum_fusion.11), calls=%async_computation.2 | async-start | bytes 3735552 | tf_op jit(solution)/shard_map/all_to_all | solution.py:410
  300.9 56.3 %all-to-all-start.1 = ((bf16[4,304,512]{2,1,0:T(8,128)(2,1)}), bf16[4,304,512]{2,1,0:T(8,128)(2,1)}, u32[]{:S(2)}, u32[]{:S(2)}) async-start(bf16[4,304,512]{2,1,0:T(8,128)(2,1)} %bitcast.33), calls=%async_computation.1 | async-start | bytes 2490368 | tf_op jit(solution)/shard_map/all_to_all | solution.py:412
  359.8 33.5 %all-to-all-start.3 = ((bf16[4,304,512]{2,1,0:T(8,128)(2,1)}), bf16[4,304,512]{2,1,0:T(8,128)(2,1)}, u32[]{:S(2)}, u32[]{:S(2)}) async-start(bf16[4,304,512]{2,1,0:T(8,128)(2,1)} %bitcast.731), calls=%async_computation.3 | async-start | bytes 2490368 | tf_op jit(solution)/shard_map/all_to_all | solution.py:412
  364.9 327.6 %all-gather.20.cloned.1.call-start = ((), (), s32[]{:S(2)}) async-start(), calls=%async_computation.23 | async-start | bytes 9437184 | tf_op jit(solution)/shard_map/all_gather | solution.py:254
  402.8 27.6 %collective-permute-start = (bf16[304,2048]{1,0:T(8,128)(2,1)S(1)}, bf16[304,2048]{1,0:T(8,128)(2,1)S(1)}, u32[]{:S(2)}, u32[]{:S(2)}) collective-permute-start(bf16[304,2048]{1,0:T(8,128)(2,1)S(1)} %get-tuple-element.163), channel_id=1, source_target_pairs={{0,1},{1,2},{2,3},{4,5},{5,6},{6,7},{8,9},{9,10},{10,11},{12,13},{... | collective-permute-start | bytes 3735560 | tf_op jit(solution)/shard_map/ppermute | solution.py:175
  404.3 30.4 %collective-permute-start.1 = (bf16[304,2048]{1,0:T(8,128)(2,1)S(1)}, bf16[304,2048]{1,0:T(8,128)(2,1)}, u32[]{:S(2)}, u32[]{:S(2)}) collective-permute-start(bf16[304,2048]{1,0:T(8,128)(2,1)S(1)} %get-tuple-element.163), channel_id=1, source_target_pairs={{1,0},{2,1},{3,2},{5,4},{6,5},{7,6},{9,8},{10,9},{11,10},{13,12},{... | collective-permute-start | bytes 3735560 | tf_op jit(solution)/shard_map/ppermute | solution.py:178
  434.7 29.7 %collective-permute-start.3 = (bf16[304,2048]{1,0:T(8,128)(2,1)}, bf16[304,2048]{1,0:T(8,128)(2,1)}, u32[]{:S(2)}, u32[]{:S(2)}) collective-permute-start(bf16[304,2048]{1,0:T(8,128)(2,1)} %collective-permute-done.1), channel_id=1, source_target_pairs={{1,0},{2,1},{5,4},{6,5},{9,8},{10,9},{13,12},{14,13},{17,16},{18,1... | collective-permute-start | bytes 3735560 | tf_op jit(solution)/shard_map/ppermute | solution.py:178
  436.0 34.9 %collective-permute-start.4 = (bf16[304,2048]{1,0:T(8,128)(2,1)}, bf16[304,2048]{1,0:T(8,128)(2,1)}, u32[]{:S(2)}, u32[]{:S(2)}) collective-permute-start(bf16[304,2048]{1,0:T(8,128)(2,1)} %collective-permute-done.2), channel_id=1, source_target_pairs={{2,3},{6,7},{10,11},{14,15},{18,19},{22,23},{26,27},{30,31}} | collective-permute-start | bytes 3735560 | tf_op jit(solution)/shard_map/ppermute | solution.py:175
  464.5 28.8 %collective-permute-start.5 = (bf16[304,2048]{1,0:T(8,128)(2,1)}, bf16[304,2048]{1,0:T(8,128)(2,1)S(1)}, u32[]{:S(2)}, u32[]{:S(2)}) collective-permute-start(bf16[304,2048]{1,0:T(8,128)(2,1)} %collective-permute-done.3), channel_id=1, source_target_pairs={{1,0},{5,4},{9,8},{13,12},{17,16},{21,20},{25,24},{29,28}} | collective-permute-start | bytes 3735560 | tf_op jit(solution)/shard_map/ppermute | solution.py:178
  493.6 24.9 %collective-permute-start.6 = (bf16[304,2048]{1,0:T(8,128)(2,1)S(1)}, bf16[304,2048]{1,0:T(8,128)(2,1)S(1)}, u32[]{:S(2)}, u32[]{:S(2)}) collective-permute-start(bf16[304,2048]{1,0:T(8,128)(2,1)S(1)} %get-tuple-element.164), channel_id=1, source_target_pairs={{0,1},{1,2},{2,3},{4,5},{5,6},{6,7},{8,9},{9,10},{10,11},{12,13},{... | collective-permute-start | bytes 3735560 | tf_op jit(solution)/shard_map/ppermute | solution.py:175
  495.2 27.6 %collective-permute-start.7 = (bf16[304,2048]{1,0:T(8,128)(2,1)S(1)}, bf16[304,2048]{1,0:T(8,128)(2,1)S(1)}, u32[]{:S(2)}, u32[]{:S(2)}) collective-permute-start(bf16[304,2048]{1,0:T(8,128)(2,1)S(1)} %get-tuple-element.164), channel_id=1, source_target_pairs={{1,0},{2,1},{3,2},{5,4},{6,5},{7,6},{9,8},{10,9},{11,10},{13,12},{... | collective-permute-start | bytes 3735560 | tf_op jit(solution)/shard_map/ppermute | solution.py:178
  522.8 27.5 %collective-permute-start.9 = (bf16[304,2048]{1,0:T(8,128)(2,1)S(1)}, bf16[304,2048]{1,0:T(8,128)(2,1)S(1)}, u32[]{:S(2)}, u32[]{:S(2)}) collective-permute-start(bf16[304,2048]{1,0:T(8,128)(2,1)S(1)} %collective-permute-done.7), channel_id=1, source_target_pairs={{1,0},{2,1},{5,4},{6,5},{9,8},{10,9},{13,12},{14,13},{17,16},{18,1... | collective-permute-start | bytes 3735560 | tf_op jit(solution)/shard_map/ppermute | solution.py:178
  524.0 34.9 %collective-permute-start.10 = (bf16[304,2048]{1,0:T(8,128)(2,1)S(1)}, bf16[304,2048]{1,0:T(8,128)(2,1)S(1)}, u32[]{:S(2)}, u32[]{:S(2)}) collective-permute-start(bf16[304,2048]{1,0:T(8,128)(2,1)S(1)} %collective-permute-done.8), channel_id=1, source_target_pairs={{2,3},{6,7},{10,11},{14,15},{18,19},{22,23},{26,27},{30,31}} | collective-permute-start | bytes 3735560 | tf_op jit(solution)/shard_map/ppermute | solution.py:175
  550.3 25.7 %collective-permute-start.11 = (bf16[304,2048]{1,0:T(8,128)(2,1)S(1)}, bf16[304,2048]{1,0:T(8,128)(2,1)S(1)}, u32[]{:S(2)}, u32[]{:S(2)}) collective-permute-start(bf16[304,2048]{1,0:T(8,128)(2,1)S(1)} %collective-permute-done.9), channel_id=1, source_target_pairs={{1,0},{5,4},{9,8},{13,12},{17,16},{21,20},{25,24},{29,28}} | collective-permute-start | bytes 3735560 | tf_op jit(solution)/shard_map/ppermute | solution.py:178
  578.3 22.1 %collective-permute-start.12 = (bf16[304,2048]{1,0:T(8,128)(2,1)S(1)}, bf16[304,2048]{1,0:T(8,128)(2,1)S(1)}, u32[]{:S(2)}, u32[]{:S(2)}) collective-permute-start(bf16[304,2048]{1,0:T(8,128)(2,1)S(1)} %get-tuple-element.165), channel_id=1, source_target_pairs={{0,1},{1,2},{2,3},{4,5},{5,6},{6,7},{8,9},{9,10},{10,11},{12,13},{... | collective-permute-start | bytes 3735560 | tf_op jit(solution)/shard_map/ppermute | solution.py:175
  579.8 27.3 %collective-permute-start.13 = (bf16[304,2048]{1,0:T(8,128)(2,1)S(1)}, bf16[304,2048]{1,0:T(8,128)(2,1)}, u32[]{:S(2)}, u32[]{:S(2)}) collective-permute-start(bf16[304,2048]{1,0:T(8,128)(2,1)S(1)} %get-tuple-element.165), channel_id=1, source_target_pairs={{1,0},{2,1},{3,2},{5,4},{6,5},{7,6},{9,8},{10,9},{11,10},{13,12},{... | collective-permute-start | bytes 3735560 | tf_op jit(solution)/shard_map/ppermute | solution.py:178
  607.1 27.5 %collective-permute-start.15 = (bf16[304,2048]{1,0:T(8,128)(2,1)}, bf16[304,2048]{1,0:T(8,128)(2,1)}, u32[]{:S(2)}, u32[]{:S(2)}) collective-permute-start(bf16[304,2048]{1,0:T(8,128)(2,1)} %collective-permute-done.13), channel_id=1, source_target_pairs={{1,0},{2,1},{5,4},{6,5},{9,8},{10,9},{13,12},{14,13},{17,16},{18,1... | collective-permute-start | bytes 3735560 | tf_op jit(solution)/shard_map/ppermute | solution.py:178
  608.4 39.0 %collective-permute-start.16 = (bf16[304,2048]{1,0:T(8,128)(2,1)}, bf16[304,2048]{1,0:T(8,128)(2,1)}, u32[]{:S(2)}, u32[]{:S(2)}) collective-permute-start(bf16[304,2048]{1,0:T(8,128)(2,1)} %collective-permute-done.14), channel_id=1, source_target_pairs={{2,3},{6,7},{10,11},{14,15},{18,19},{22,23},{26,27},{30,31}} | collective-permute-start | bytes 3735560 | tf_op jit(solution)/shard_map/ppermute | solution.py:175
  634.7 23.2 %collective-permute-start.17 = (bf16[304,2048]{1,0:T(8,128)(2,1)}, bf16[304,2048]{1,0:T(8,128)(2,1)S(1)}, u32[]{:S(2)}, u32[]{:S(2)}) collective-permute-start(bf16[304,2048]{1,0:T(8,128)(2,1)} %collective-permute-done.15), channel_id=1, source_target_pairs={{1,0},{5,4},{9,8},{13,12},{17,16},{21,20},{25,24},{29,28}} | collective-permute-start | bytes 3735560 | tf_op jit(solution)/shard_map/ppermute | solution.py:178
  660.2 30.5 %collective-permute-start.18 = (bf16[304,2048]{1,0:T(8,128)(2,1)S(1)}, bf16[304,2048]{1,0:T(8,128)(2,1)S(1)}, u32[]{:S(2)}, u32[]{:S(2)}) collective-permute-start(bf16[304,2048]{1,0:T(8,128)(2,1)S(1)} %get-tuple-element.166), channel_id=1, source_target_pairs={{0,1},{1,2},{2,3},{4,5},{5,6},{6,7},{8,9},{9,10},{10,11},{12,13},{... | collective-permute-start | bytes 3735560 | tf_op jit(solution)/shard_map/ppermute | solution.py:175
  689.4 28.7 %collective-permute-start.19 = (bf16[304,2048]{1,0:T(8,128)(2,1)S(1)}, bf16[304,2048]{1,0:T(8,128)(2,1)}, u32[]{:S(2)}, u32[]{:S(2)}) collective-permute-start(bf16[304,2048]{1,0:T(8,128)(2,1)S(1)} %get-tuple-element.166), channel_id=1, source_target_pairs={{1,0},{2,1},{3,2},{5,4},{6,5},{7,6},{9,8},{10,9},{11,10},{13,12},{... | collective-permute-start | bytes 3735560 | tf_op jit(solution)/shard_map/ppermute | solution.py:178
  690.7 28.7 %collective-permute-start.20 = (bf16[304,2048]{1,0:T(8,128)(2,1)S(1)}, bf16[304,2048]{1,0:T(8,128)(2,1)}, u32[]{:S(2)}, u32[]{:S(2)}) collective-permute-start(bf16[304,2048]{1,0:T(8,128)(2,1)S(1)} %collective-permute-done.18), channel_id=1, source_target_pairs={{1,2},{2,3},{5,6},{6,7},{9,10},{10,11},{13,14},{14,15},{17,18},{18... | collective-permute-start | bytes 3735560 | tf_op jit(solution)/shard_map/ppermute | solution.py:175
  718.1 30.1 %collective-permute-start.21 = (bf16[304,2048]{1,0:T(8,128)(2,1)}, bf16[304,2048]{1,0:T(8,128)(2,1)S(1)}, u32[]{:S(2)}, u32[]{:S(2)}) collective-permute-start(bf16[304,2048]{1,0:T(8,128)(2,1)} %collective-permute-done.19), channel_id=1, source_target_pairs={{1,0},{2,1},{5,4},{6,5},{9,8},{10,9},{13,12},{14,13},{17,16},{18,1... | collective-permute-start | bytes 3735560 | tf_op jit(solution)/shard_map/ppermute | solution.py:178
  719.4 33.9 %collective-permute-start.22 = (bf16[304,2048]{1,0:T(8,128)(2,1)}, bf16[304,2048]{1,0:T(8,128)(2,1)S(1)}, u32[]{:S(2)}, u32[]{:S(2)}) collective-permute-start(bf16[304,2048]{1,0:T(8,128)(2,1)} %collective-permute-done.20), channel_id=1, source_target_pairs={{2,3},{6,7},{10,11},{14,15},{18,19},{22,23},{26,27},{30,31}} | collective-permute-start | bytes 3735560 | tf_op jit(solution)/shard_map/ppermute | solution.py:175
  748.2 21.7 %collective-permute-start.23 = (bf16[304,2048]{1,0:T(8,128)(2,1)S(1)}, bf16[304,2048]{1,0:T(8,128)(2,1)S(1)}, u32[]{:S(2)}, u32[]{:S(2)}) collective-permute-start(bf16[304,2048]{1,0:T(8,128)(2,1)S(1)} %collective-permute-done.21), channel_id=1, source_target_pairs={{1,0},{5,4},{9,8},{13,12},{17,16},{21,20},{25,24},{29,28}} | collective-permute-start | bytes 3735560 | tf_op jit(solution)/shard_map/ppermute | solution.py:178
  772.8 22.4 %collective-permute-start.24 = (bf16[304,2048]{1,0:T(8,128)(2,1)}, bf16[304,2048]{1,0:T(8,128)(2,1)S(1)}, u32[]{:S(2)}, u32[]{:S(2)}) collective-permute-start(bf16[304,2048]{1,0:T(8,128)(2,1)} %get-tuple-element.345), channel_id=1, source_target_pairs={{0,1},{4,5},{8,9},{12,13},{16,17},{20,21},{24,25},{28,29}} | collective-permute-start | bytes 3735560 | tf_op jit(solution)/shard_map/ppermute | solution.py:201
  774.4 55.0 %collective-permute-start.27 = (bf16[304,2048]{1,0:T(8,128)(2,1)S(1)}, bf16[304,2048]{1,0:T(8,128)(2,1)S(1)}, u32[]{:S(2)}, u32[]{:S(2)}) collective-permute-start(bf16[304,2048]{1,0:T(8,128)(2,1)S(1)} %get-tuple-element.346), channel_id=1, source_target_pairs={{3,2},{7,6},{11,10},{15,14},{19,18},{23,22},{27,26},{31,30}} | collective-permute-start | bytes 3735560 | tf_op jit(solution)/shard_map/ppermute | solution.py:207
  797.5 31.9 %collective-permute-start.25 = (bf16[304,2048]{1,0:T(8,128)(2,1)S(1)}, bf16[304,2048]{1,0:T(8,128)(2,1)S(1)}, u32[]{:S(2)}, u32[]{:S(2)}) collective-permute-start(bf16[304,2048]{1,0:T(8,128)(2,1)S(1)} %add_convert_fusion.22), channel_id=1, source_target_pairs={{0,1},{1,2},{4,5},{5,6},{8,9},{9,10},{12,13},{13,14},{16,17},{17,1... | collective-permute-start | bytes 3735560 | tf_op jit(solution)/shard_map/ppermute | solution.py:201
  831.4 29.7 %collective-permute-start.28 = (bf16[304,2048]{1,0:T(8,128)(2,1)}, bf16[304,2048]{1,0:T(8,128)(2,1)S(1)}, u32[]{:S(2)}, u32[]{:S(2)}) collective-permute-start(bf16[304,2048]{1,0:T(8,128)(2,1)} %get-tuple-element.344), channel_id=1, source_target_pairs={{2,1},{3,2},{6,5},{7,6},{10,9},{11,10},{14,13},{15,14},{18,17},{19... | collective-permute-start | bytes 3735560 | tf_op jit(solution)/shard_map/ppermute | solution.py:207
  858.2 19.6 collective-permute-start.26
  863.2 19.4 collective-permute-start.29
  886.4 29.7 %collective-permute-start.30 = (bf16[304,2048]{1,0:T(8,128)(2,1)S(1)}, bf16[304,2048]{1,0:T(8,128)(2,1)S(1)}, u32[]{:S(2)}, u32[]{:S(2)}) collective-permute-start(bf16[304,2048]{1,0:T(8,128)(2,1)S(1)} %get-tuple-element.341), channel_id=1, source_target_pairs={{0,1},{4,5},{8,9},{12,13},{16,17},{20,21},{24,25},{28,29}} | collective-permute-start | bytes 3735560 | tf_op jit(solution)/shard_map/ppermute | solution.py:201
  890.4 30.5 %collective-permute-start.33 = (bf16[304,2048]{1,0:T(8,128)(2,1)S(1)}, bf16[304,2048]{1,0:T(8,128)(2,1)S(1)}, u32[]{:S(2)}, u32[]{:S(2)}) collective-permute-start(bf16[304,2048]{1,0:T(8,128)(2,1)S(1)} %get-tuple-element.342), channel_id=1, source_target_pairs={{3,2},{7,6},{11,10},{15,14},{19,18},{23,22},{27,26},{31,30}} | collective-permute-start | bytes 3735560 | tf_op jit(solution)/shard_map/ppermute | solution.py:207
  916.5 29.4 %collective-permute-start.31 = (bf16[304,2048]{1,0:T(8,128)(2,1)S(1)}, bf16[304,2048]{1,0:T(8,128)(2,1)S(1)}, u32[]{:S(2)}, u32[]{:S(2)}) collective-permute-start(bf16[304,2048]{1,0:T(8,128)(2,1)S(1)} %add_convert_fusion.17), channel_id=1, source_target_pairs={{0,1},{1,2},{4,5},{5,6},{8,9},{9,10},{12,13},{13,14},{16,17},{17,1... | collective-permute-start | bytes 3735560 | tf_op jit(solution)/shard_map/ppermute | solution.py:201
  947.6 35.2 %collective-permute-start.32 = (bf16[304,2048]{1,0:T(8,128)(2,1)S(1)}, bf16[304,2048]{1,0:T(8,128)(2,1)S(1)}, u32[]{:S(2)}, u32[]{:S(2)}) collective-permute-start(bf16[304,2048]{1,0:T(8,128)(2,1)S(1)} %get-tuple-element.339), channel_id=1, source_target_pairs={{0,1},{1,2},{2,3},{4,5},{5,6},{6,7},{8,9},{9,10},{10,11},{12,13},{... | collective-permute-start | bytes 3735560 | tf_op jit(solution)/shard_map/ppermute | solution.py:201
  953.1 35.0 %collective-permute-start.35 = (bf16[304,2048]{1,0:T(8,128)(2,1)S(1)}, bf16[304,2048]{1,0:T(8,128)(2,1)S(1)}, u32[]{:S(2)}, u32[]{:S(2)}) collective-permute-start(bf16[304,2048]{1,0:T(8,128)(2,1)S(1)} %add_convert_fusion.14), channel_id=1, source_target_pairs={{1,0},{2,1},{3,2},{5,4},{6,5},{7,6},{9,8},{10,9},{11,10},{13,12},{... | collective-permute-start | bytes 3735560 | tf_op jit(solution)/shard_map/ppermute | solution.py:207
  995.0 37.9 %collective-permute-start.36 = (bf16[304,2048]{1,0:T(8,128)(2,1)S(1)}, bf16[304,2048]{1,0:T(8,128)(2,1)S(1)}, u32[]{:S(2)}, u32[]{:S(2)}) collective-permute-start(bf16[304,2048]{1,0:T(8,128)(2,1)S(1)} %get-tuple-element.337), channel_id=1, source_target_pairs={{0,1},{4,5},{8,9},{12,13},{16,17},{20,21},{24,25},{28,29}} | collective-permute-start | bytes 3735560 | tf_op jit(solution)/shard_map/ppermute | solution.py:201
  1010.6 27.2 %collective-permute-start.39 = (bf16[304,2048]{1,0:T(8,128)(2,1)S(1)}, bf16[304,2048]{1,0:T(8,128)(2,1)S(1)}, u32[]{:S(2)}, u32[]{:S(2)}) collective-permute-start(bf16[304,2048]{1,0:T(8,128)(2,1)S(1)} %get-tuple-element.338), channel_id=1, source_target_pairs={{3,2},{7,6},{11,10},{15,14},{19,18},{23,22},{27,26},{31,30}} | collective-permute-start | bytes 3735560 | tf_op jit(solution)/shard_map/ppermute | solution.py:207
  1053.8 35.3 %collective-permute-start.38 = (bf16[304,2048]{1,0:T(8,128)(2,1)S(1)}, bf16[304,2048]{1,0:T(8,128)(2,1)S(1)}, u32[]{:S(2)}, u32[]{:S(2)}) collective-permute-start(bf16[304,2048]{1,0:T(8,128)(2,1)S(1)} %get-tuple-element.335), channel_id=1, source_target_pairs={{0,1},{1,2},{2,3},{4,5},{5,6},{6,7},{8,9},{9,10},{10,11},{12,13},{... | collective-permute-start | bytes 3735560 | tf_op jit(solution)/shard_map/ppermute | solution.py:201
  1059.2 32.3 %collective-permute-start.41 = (bf16[304,2048]{1,0:T(8,128)(2,1)S(1)}, bf16[304,2048]{1,0:T(8,128)(2,1)S(1)}, u32[]{:S(2)}, u32[]{:S(2)}) collective-permute-start(bf16[304,2048]{1,0:T(8,128)(2,1)S(1)} %add_convert_fusion.9), channel_id=1, source_target_pairs={{1,0},{2,1},{3,2},{5,4},{6,5},{7,6},{9,8},{10,9},{11,10},{13,12},{... | collective-permute-start | bytes 3735560 | tf_op jit(solution)/shard_map/ppermute | solution.py:207
  1095.6 42.4 %collective-permute-start.42 = (bf16[304,2048]{1,0:T(8,128)(2,1)S(1)}, bf16[304,2048]{1,0:T(8,128)(2,1)S(1)}, u32[]{:S(2)}, u32[]{:S(2)}) collective-permute-start(bf16[304,2048]{1,0:T(8,128)(2,1)S(1)} %get-tuple-element.333), channel_id=1, source_target_pairs={{0,1},{4,5},{8,9},{12,13},{16,17},{20,21},{24,25},{28,29}} | collective-permute-start | bytes 3735560 | tf_op jit(solution)/shard_map/ppermute | solution.py:201
  1112.1 31.0 %collective-permute-start.45 = (bf16[304,2048]{1,0:T(8,128)(2,1)S(1)}, bf16[304,2048]{1,0:T(8,128)(2,1)S(1)}, u32[]{:S(2)}, u32[]{:S(2)}) collective-permute-start(bf16[304,2048]{1,0:T(8,128)(2,1)S(1)} %get-tuple-element.334), channel_id=1, source_target_pairs={{3,2},{7,6},{11,10},{15,14},{19,18},{23,22},{27,26},{31,30}} | collective-permute-start | bytes 3735560 | tf_op jit(solution)/shard_map/ppermute | solution.py:207
  1162.5 36.0 %collective-permute-start.44 = (bf16[304,2048]{1,0:T(8,128)(2,1)S(1)}, bf16[304,2048]{1,0:T(8,128)(2,1)S(1)}, u32[]{:S(2)}, u32[]{:S(2)}) collective-permute-start(bf16[304,2048]{1,0:T(8,128)(2,1)S(1)} %get-tuple-element.331), channel_id=1, source_target_pairs={{0,1},{1,2},{2,3},{4,5},{5,6},{6,7},{8,9},{9,10},{10,11},{12,13},{... | collective-permute-start | bytes 3735560 | tf_op jit(solution)/shard_map/ppermute | solution.py:201
  1167.9 36.8 %collective-permute-start.47 = (bf16[304,2048]{1,0:T(8,128)(2,1)S(1)}, bf16[304,2048]{1,0:T(8,128)(2,1)S(1)}, u32[]{:S(2)}, u32[]{:S(2)}) collective-permute-start(bf16[304,2048]{1,0:T(8,128)(2,1)S(1)} %add_convert_fusion.5), channel_id=1, source_target_pairs={{1,0},{2,1},{3,2},{5,4},{6,5},{7,6},{9,8},{10,9},{11,10},{13,12},{... | collective-permute-start | bytes 3735560 | tf_op jit(solution)/shard_map/ppermute | solution.py:207
  1225.1 51.6 %all-to-all-start.6 = ((bf16[304,4,512]{2,0,1:T(8,128)(2,1)}), bf16[304,4,512]{2,0,1:T(8,128)(2,1)}, u32[]{:S(2)}, u32[]{:S(2)}) async-start(bf16[304,4,512]{2,0,1:T(8,128)(2,1)} %copy.292), calls=%async_computation.6 | async-start | bytes 2490368 | tf_op jit(solution)/shard_map/all_to_all | solution.py:410
  1234.5 317.0 %reduce-scatter.12.cloned.1.call-start = ((), (), s32[]{:S(2)}) async-start(), calls=%async_computation.24 | async-start | bytes 18874368 | tf_op jit(solution)/shard_map/reduce_scatter | solution.py:427
  1276.7 109.7 %all-to-all-start.4 = ((bf16[304,4,512]{2,0,1:T(8,128)(2,1)}), bf16[304,4,512]{2,0,1:T(8,128)(2,1)S(1)}, u32[]{:S(2)}, u32[]{:S(2)}) async-start(bf16[304,4,512]{2,0,1:T(8,128)(2,1)} %copy.279), calls=%async_computation.4 | async-start | bytes 2490368 | tf_op jit(solution)/shard_map/all_to_all | solution.py:410
  1386.5 100.5 %all-to-all-start.7 = ((bf16[4,304,768]{2,1,0:T(8,128)(2,1)}), bf16[4,304,768]{2,1,0:T(8,128)(2,1)}, u32[]{:S(2)}, u32[]{:S(2)}) async-start(bf16[4,304,768]{2,1,0:T(8,128)(2,1)} %bitcast.698), calls=%async_computation.7 | async-start | bytes 3735552 | tf_op jit(solution)/shard_map/all_to_all | solution.py:412
  1487.0 30.0 %all-to-all-start.5 = ((bf16[4,304,768]{2,1,0:T(8,128)(2,1)}), bf16[4,304,768]{2,1,0:T(8,128)(2,1)}, u32[]{:S(2)}, u32[]{:S(2)}) async-start(bf16[4,304,768]{2,1,0:T(8,128)(2,1)} %bitcast.699), calls=%async_computation.5 | async-start | bytes 3735552 | tf_op jit(solution)/shard_map/all_to_all | solution.py:412
  1492.2 141.7 %reduce-scatter.20.cloned.1.call-start = ((), (), s32[]{:S(2)}) async-start(), calls=%async_computation.28 | async-start | bytes 4718592 | tf_op jit(solution)/shard_map/reduce_scatter | solution.py:453
  1557.9 126.8 %reduce-scatter.16.cloned.1.call-start = ((), (), s32[]{:S(2)}) async-start(), calls=%async_computation.26 | async-start | bytes 9437184 | tf_op jit(solution)/shard_map/reduce_scatter | solution.py:447
  1558.5 201.0 %reduce-scatter.14.cloned.1.call-start = ((), (), s32[]{:S(2)}) async-start(), calls=%async_computation.25 | async-start | bytes 9437184 | tf_op jit(solution)/shard_map/reduce_scatter | solution.py:433
  1596.0 201.1 %reduce-scatter.28.cloned.1.call-start = ((), (), s32[]{:S(2)}) async-start(), calls=%async_computation.32 | async-start | bytes 589824
  1633.1 238.8 %reduce-scatter.24.cloned.1.call-start = ((), (), s32[]{:S(2)}) async-start(), calls=%async_computation.30 | async-start | bytes 9437184 | tf_op jit(solution)/shard_map/reduce_scatter | solution.py:461
  1633.9 262.0 %reduce-scatter.22.cloned.1.call-start = ((), (), s32[]{:S(2)}) async-start(), calls=%async_computation.29 | async-start | bytes 655360 | tf_op jit(solution)/shard_map/reduce_scatter | solution.py:452
  1634.4 289.2 %reduce-scatter.18.cloned.1.call-start = ((), (), s32[]{:S(2)}) async-start(), calls=%async_computation.27 | async-start | bytes 1310720 | tf_op jit(solution)/shard_map/reduce_scatter | solution.py:446
  1684.7 266.9 %reduce-scatter.26.cloned.1.call-start = ((), (), s32[]{:S(2)}) async-start(), calls=%async_computation.31 | async-start | bytes 1310720 | tf_op jit(solution)/shard_map/reduce_scatter | solution.py:460
  (145 other events, 2290.0 us)
Sparse Core Ops, SparseCore 0:
  10.1 35.5 all-gather.7
  47.9 28.5 all-gather.13
  78.4 35.9 all-gather.11
  116.2 54.2 all-gather.9
  172.2 55.8 all-gather.15
  230.4 89.7 all-gather.17
  440.0 80.6 all-gather.19
  1265.2 117.2 reduce-scatter.11
  1558.0 51.7 reduce-scatter.19
  1613.1 71.5 reduce-scatter.15
  1688.1 71.2 reduce-scatter.13
  1762.9 34.1 reduce-scatter.27
  1800.6 71.2 reduce-scatter.23
  1874.0 21.8 reduce-scatter.21
  1898.0 25.5 reduce-scatter.17
  1925.8 25.7 reduce-scatter.25

commit v8 on v7

--- a/solution.py
+++ b/solution.py
@@ -333,22 +333,28 @@
         grad_gateup = jnp.einsum(
             "rd,rcf->dcf", rows_two, gateup_grad, preferred_element_type=jnp.float32
         )
-        normed_two_grad = yield (
-            "scatter",
-            jnp.einsum(
-                "rcf,dcf->rd", gateup_grad, full_gateup, preferred_element_type=jnp.float32
-            ),
-        )
+        normed_two_partial, grad_gateup, grad_down = lax.optimization_barrier(
+            (
+                jnp.einsum(
+                    "rcf,dcf->rd", gateup_grad, full_gateup, preferred_element_type=jnp.float32
+                ),
+                grad_gateup,
+                grad_down,
+            )
+        )
+        normed_two_grad = yield ("scatter", normed_two_partial)
         middle_back, gain_two = norm_back(normed_two_grad, hat_two, scale_two, gain_values[1])
         middle_grad = upstream + middle_back
         attn_grad = (branch_scale * middle_grad).astype(jnp.bfloat16)
-        grad_output = contract_rows(mixed, attn_grad)
-        mixed_grad = yield (
-            "to_heads",
-            contract_cols(attn_grad, full_output)
-            .astype(jnp.bfloat16)
-            .reshape(rows, tensor_count, query_width),
-        )
+        mixed_grad_own, grad_output = lax.optimization_barrier(
+            (
+                contract_cols(attn_grad, full_output)
+                .astype(jnp.bfloat16)
+                .reshape(rows, tensor_count, query_width),
+                contract_rows(mixed, attn_grad),
+            )
+        )
+        mixed_grad = yield ("to_heads", mixed_grad_own)
         mixed_grad = mixed_grad.reshape(group_rows, keyval_heads, head_repeat, HD)
         query_grad, key_grad, value_grad = attend_back(
             queries, key_rows, values, visible, log_totals, mixed_grad, block_rows

time: 2030 us -> 2140 us (1.054)
  waiting for transfers between devices: 790 us -> 854 us
  other arithmetic: 200 us -> 259 us
  starting transfers between devices: 163 us -> 138 us
    convert_element_type x0 -> x3, other arithmetic: none -> 59.8 us  [the longest x1 27.6 us: per_device(): totals[3].reshape(width, -1).astype(jnp.bfloat16)]
    all_to_all x4, waiting for transfers between devices: 10.7 us -> 45.9 us  [per_device(): previous = lax.all_to_all(value, 'tensor', 1, 0, tiled=True)]
    reduce_scatter x1, waiting for transfers between devices: 35.6 us -> 66.9 us  [per_device(): lax.psum_scatter(query_low, 'dp', scatter_dimension=0, tiled=True)]
    ppermute x12, starting transfers between devices: 73.7 us -> 48.3 us  [line_scatter(): lax.ppermute(send.astype(jnp.bfloat16), 'tensor', [(i, i + 1) for i in ra...]
    convert_element_type x0 -> x1, local copies, waits for them, and re-layouts: none -> 22.5 us  [per_device(): totals[3].reshape(width, -1).astype(jnp.bfloat16)]
  transfers between devices with their start and end apart: 72 -> 72, of which waited for: 39 -> 38; matrix products, arithmetic and copies ran while one was open for 42% -> 44% of each run, Pallas kernels for 0% -> 0%
where the time goes in v8:
time: 2140 us; the launch traced here: 2130 us
  waiting for transfers between devices  854 us (40%)
  matrix products  572 us (27%)
  other arithmetic  259 us (12%)
  local copies, waits for them, and re-layouts  200 us (9%)
  starting transfers between devices  138 us (6%)
  blocking collectives  88.2 us (4%)
    ppermute x12, waiting for transfers between devices, line_gather(): lax.ppermute(from_right, 'tensor', [(i, i - 1) for i in range(1, count -...  160 us
    ppermute x12, waiting for transfers between devices, line_scatter(): lax.ppermute(send.astype(jnp.bfloat16), 'tensor', [(i, i + 1) for i in ra...  134 us
    dot_general x6, matrix products, contract_rows(): lax.dot_general(left, right, (((0,), (0,)), ((), ())), preferred_element_...  76.4 us
    dot_general x6, matrix products, contract_cols(): lax.dot_general(left, right, (((1,), (1,)), ((), ())), preferred_element_...  74.9 us
    reduce_scatter x1, waiting for transfers between devices, per_device(): lax.psum_scatter(totals[4].astype(jnp.bfloat16), 'dp', scatter_dimension=...  74.7 us
    reduce_scatter x1, waiting for transfers between devices, per_device(): lax.psum_scatter(query_low, 'dp', scatter_dimension=0, tiled=True)  66.9 us
    ppermute x12, waiting for transfers between devices, line_gather(): lax.ppermute(from_left, 'tensor', [(i, i + 1) for i in range(step - 1, co...  65.8 us
    dot_general x2, matrix products, micro_step(): jnp.einsum('rd,rcf->dcf', rows_two, gateup_grad, preferred_element_type=j...  56.6 us
  transfers between devices with their start and end apart: 72, of which 38 were waited for; matrix products, arithmetic and copies ran while one was open for 44% of the time, Pallas kernels for 0%

profile of v8, /device:TPU:0, one launch (start us, length us, event | category | flops | bytes accessed | tf_op | source)
XLA Modules:
  0.0 2131.7 jit_solution(3271274517461705405)
XLA Ops:
  13.7 24.5 %all_gather.30 = bf16[256,8,128]{2,0,1:T(8,128)(2,1)} all-gather(bf16[256,2,128]{2,0,1:T(8,128)(2,1)S(1)} %copy.368), channel_id=1, replica_groups=mesh['dp'=8,'tensor'=4] {'tensor'}, dimensions={1}, use_global_device_ids=true | all-gather | bytes 655360 | tf_op jit(solution)/shard_map/all_gather | solution.py:248
  46.0 30.6 %all-gather.14.cloned.1.call-done = bf16[2048,256]{1,0:T(8,128)(2,1)} async-done(((bf16[512,256]{1,0:T(8,128)(2,1)}), bf16[2048,256]{1,0:T(8,128)(2,1)}) %all-gather.14.cloned.1.call-update) | async-done | bytes 1048592 | tf_op jit(solution)/shard_map/all_gather | solution.py:251
  79.8 8.9 all_gather.27
  89.9 24.6 %all-gather.12.cloned.1.call-done = bf16[2048,8,128]{2,0,1:T(8,128)(2,1)} async-done(((bf16[256,8,128]{2,0,1:T(8,128)(2,1)}), bf16[2048,8,128]{2,0,1:T(8,128)(2,1)}) %all-gather.12.cloned.1.call-update) | async-done | bytes 4194320 | tf_op jit(solution)/shard_map/all_gather | solution.py:247
  122.1 48.5 %all-gather.10.cloned.1.call-done = bf16[2048,2048]{1,0:T(8,128)(2,1)} async-done(((bf16[256,2048]{1,0:T(8,128)(2,1)}), bf16[2048,2048]{1,0:T(8,128)(2,1)}) %all-gather.10.cloned.1.call-update) | async-done | bytes 8388624 | tf_op jit(solution)/shard_map/all_gather | solution.py:244
  170.5 12.4 copy.255
  220.0 25.9 %all-to-all-done.2 = bf16[304,4,768]{2,0,1:T(8,128)(2,1)} async-done(((bf16[304,4,768]{2,0,1:T(8,128)(2,1)}), bf16[304,4,768]{2,0,1:T(8,128)(2,1)}, u32[]{:S(2)}, u32[]{:S(2)}) %all-to-all-start.2) | async-done | bytes 1867808 | tf_op jit(solution)/shard_map/all_to_all | solution.py:416
  272.4 20.0 all-to-all-done
  332.7 12.4 fusion.135
  378.3 12.3 fusion.134
  416.4 20.9 all-to-all-done.3
  449.2 24.6 %collective-permute-done = bf16[304,2048]{1,0:T(8,128)(2,1)S(1)} collective-permute-done((bf16[304,2048]{1,0:T(8,128)(2,1)S(1)}, bf16[304,2048]{1,0:T(8,128)(2,1)S(1)}, u32[]{:S(2)}, u32[]{:S(2)}) %collective-permute-start) | collective-permute-done | bytes 1245216 | tf_op jit(solution)/shard_map/ppermute | solution.py:175
  483.5 24.5 %collective-permute-done.3 = bf16[304,2048]{1,0:T(8,128)(2,1)} collective-permute-done((bf16[304,2048]{1,0:T(8,128)(2,1)}, bf16[304,2048]{1,0:T(8,128)(2,1)}, u32[]{:S(2)}, u32[]{:S(2)}) %collective-permute-start.3) | collective-permute-done | bytes 1245216 | tf_op jit(solution)/shard_map/ppermute | solution.py:178
  516.1 20.7 collective-permute-done.5
  540.1 22.0 %collective-permute-done.6 = bf16[304,2048]{1,0:T(8,128)(2,1)S(1)} collective-permute-done((bf16[304,2048]{1,0:T(8,128)(2,1)S(1)}, bf16[304,2048]{1,0:T(8,128)(2,1)S(1)}, u32[]{:S(2)}, u32[]{:S(2)}) %collective-permute-start.6) | collective-permute-done | bytes 1245216 | tf_op jit(solution)/shard_map/ppermute | solution.py:175
  569.0 24.9 %collective-permute-done.9 = bf16[304,2048]{1,0:T(8,128)(2,1)S(1)} collective-permute-done((bf16[304,2048]{1,0:T(8,128)(2,1)S(1)}, bf16[304,2048]{1,0:T(8,128)(2,1)S(1)}, u32[]{:S(2)}, u32[]{:S(2)}) %collective-permute-start.9) | collective-permute-done | bytes 1245216 | tf_op jit(solution)/shard_map/ppermute | solution.py:178
  603.6 16.0 collective-permute-done.11
  624.7 19.2 collective-permute-done.12
  653.8 24.4 %collective-permute-done.15 = bf16[304,2048]{1,0:T(8,128)(2,1)} collective-permute-done((bf16[304,2048]{1,0:T(8,128)(2,1)}, bf16[304,2048]{1,0:T(8,128)(2,1)}, u32[]{:S(2)}, u32[]{:S(2)}) %collective-permute-start.15) | collective-permute-done | bytes 1245216 | tf_op jit(solution)/shard_map/ppermute | solution.py:178
  705.5 27.3 %fusion.60 = f32[1216,2,2048]{2,0,1:T(8,128)} fusion(bf16[2048,2,2048]{2,0,1:T(8,128)(2,1)} %all-gather.18.cloned.1.call-done, bf16[1216,2048]{1,0:T(8,128)(2,1)} %copy-done.51), kind=kOutput, calls=%fused_computation.105 | convolution fusion | flops 20401094656 | bytes 41680896 | tf_op jit(solution)/shard_map/rd,dcf->rcf/dot_general | solution.py:313
  736.3 25.7 %fusion.62 = (bf16[1216,1,2048]{2,0,1:T(8,128)(2,1)}, bf16[1216,1,2048]{2,0,1:T(8,128)(2,1)}, bf16[1216,2048]{1,0:T(8,128)(2,1)}) fusion(f32[1216,2,2048]{2,0,1:T(8,128)} %fusion.60, bf16[1216,2048]{1,0:T(8,128)(2,1)} %constant_dynamic-update-slice_fusion.7, bf16[2048,2048]{1,0:T(8,128)(2,1)} %all-gather.20.cloned.1.call-done), kind=kOutput, calls=%fused_computation.107 | convolution fusion | flops 10237902848 | bytes 48234496 | tf_op jit(solution)/shard_map/dot_general | solution.py:162
  764.0 14.5 fusion.232
  778.5 13.9 collective-permute-done.21
  797.9 16.7 collective-permute-done.23
  819.8 20.1 collective-permute-done.24
  846.8 27.3 %fusion.57 = f32[1216,2,2048]{2,0,1:T(8,128)} fusion(bf16[2048,2,2048]{2,0,1:T(8,128)(2,1)} %all-gather.18.cloned.1.call-done, bf16[1216,2048]{1,0:T(8,128)(2,1)} %constant_dynamic-update-slice_fusion.14), kind=kOutput, calls=%fused_computation.102 | convolution fusion | flops 20401094656 | bytes 41680896 | tf_op jit(solution)/shard_map/rd,dcf->rcf/dot_general | solution.py:313
  877.0 25.8 %fusion.63 = (bf16[1216,1,2048]{2,0,1:T(8,128)(2,1)}, bf16[1216,1,2048]{2,0,1:T(8,128)(2,1)}, bf16[1216,2048]{1,0:T(8,128)(2,1)}) fusion(f32[1216,2,2048]{2,0,1:T(8,128)} %fusion.57, bf16[1216,2048]{1,0:T(8,128)(2,1)} %copy-done.50, bf16[2048,2048]{1,0:T(8,128)(2,1)} %all-gather.20.cloned.1.call-done), kind=kOutput, calls=%fused_computation.108 | convolution fusion | flops 10237902848 | bytes 48234496 | tf_op jit(solution)/shard_map/dot_general | solution.py:162
  909.4 13.2 fusion.233
  936.0 25.1 %collective-permute-done.30 = bf16[304,2048]{1,0:T(8,128)(2,1)S(1)} collective-permute-done((bf16[304,2048]{1,0:T(8,128)(2,1)S(1)}, bf16[304,2048]{1,0:T(8,128)(2,1)S(1)}, u32[]{:S(2)}, u32[]{:S(2)}) %collective-permute-start.30) | collective-permute-done | bytes 1245216 | tf_op jit(solution)/shard_map/ppermute | solution.py:201
  966.4 27.8 %fusion.43 = f32[2048,2,2048]{2,0,1:T(8,128)} fusion(bf16[1216,1,2048]{2,0,1:T(8,128)(2,1)} %get-tuple-element.348, bf16[1216,1,2048]{2,0,1:T(8,128)(2,1)} %get-tuple-element.347, bf16[1216,2048]{1,0:T(8,128)(2,1)S(1)} %bitcast.735), kind=kOutput, calls=%fused_computation.86 | convolution fusion | flops 20421017600 | bytes 48496640 | tf_op jit(solution)/shard_map/rd,rcf->dcf/dot_general | solution.py:333
  995.9 28.2 %convolution_bitcast_fusion.1 = f32[1216,2048]{1,0:T(8,128)} fusion(bf16[2048,2,2048]{2,0,1:T(8,128)(2,1)} %all-gather.18.cloned.1.call-done, bf16[1216,1,2048]{2,0,1:T(8,128)(2,1)} %get-tuple-element.348, bf16[1216,1,2048]{2,0,1:T(8,128)(2,1)} %get-tuple-element.347), kind=kOutput, calls=%fused_computation.81 | convolution fusion | flops 20406075392 | bytes 36700160 | tf_op jit(solution)/shard_map/rcf,dcf->rd/dot_general | solution.py:338
  1029.6 18.6 fusion.234
  1057.9 26.1 %collective-permute-done.36 = bf16[304,2048]{1,0:T(8,128)(2,1)S(1)} collective-permute-done((bf16[304,2048]{1,0:T(8,128)(2,1)S(1)}, bf16[304,2048]{1,0:T(8,128)(2,1)S(1)}, u32[]{:S(2)}, u32[]{:S(2)}) %collective-permute-start.36) | collective-permute-done | bytes 1245216 | tf_op jit(solution)/shard_map/ppermute | solution.py:201
  1089.1 28.9 %fusion.42 = f32[2048,2,2048]{2,0,1:T(8,128)} fusion(bf16[1216,1,2048]{2,0,1:T(8,128)(2,1)} %get-tuple-element.346, bf16[1216,1,2048]{2,0,1:T(8,128)(2,1)S(1)} %bitcast.798, bf16[1216,2048]{1,0:T(8,128)(2,1)} %constant_dynamic-update-slice_fusion.14), kind=kOutput, calls=%fused_computation.85 | convolution fusion | flops 20421017600 | bytes 48496640 | tf_op jit(solution)/shard_map/rd,rcf->dcf/dot_general | solution.py:333
  1121.0 24.5 %convolution_bitcast_fusion = f32[1216,2048]{1,0:T(8,128)S(1)} fusion(bf16[2048,2,2048]{2,0,1:T(8,128)(2,1)} %all-gather.18.cloned.1.call-done, bf16[1216,1,2048]{2,0,1:T(8,128)(2,1)} %get-tuple-element.346, bf16[1216,1,2048]{2,0,1:T(8,128)(2,1)} %get-tuple-element.345), kind=kOutput, calls=%fused_computation.80 | convolution fusion | flops 20406075392 | bytes 36700160 | tf_op jit(solution)/shard_map/rcf,dcf->rd/dot_general | solution.py:338
  1151.9 17.8 fusion.235
  1180.5 26.8 %collective-permute-done.42 = bf16[304,2048]{1,0:T(8,128)(2,1)S(1)} collective-permute-done((bf16[304,2048]{1,0:T(8,128)(2,1)S(1)}, bf16[304,2048]{1,0:T(8,128)(2,1)S(1)}, u32[]{:S(2)}, u32[]{:S(2)}) %collective-permute-start.42) | collective-permute-done | bytes 1245216 | tf_op jit(solution)/shard_map/ppermute | solution.py:201
  1212.2 26.5 %collective-permute-done.43 = bf16[304,2048]{1,0:T(8,128)(2,1)S(1)} collective-permute-done((bf16[304,2048]{1,0:T(8,128)(2,1)S(1)}, bf16[304,2048]{1,0:T(8,128)(2,1)S(1)}, u32[]{:S(2)}, u32[]{:S(2)}) %collective-permute-start.43) | collective-permute-done | bytes 1245216 | tf_op jit(solution)/shard_map/ppermute | solution.py:201
  1251.0 9.0 collective-permute-done.44
  1260.0 24.8 %collective-permute-done.47 = bf16[304,2048]{1,0:T(8,128)(2,1)S(1)} collective-permute-done((bf16[304,2048]{1,0:T(8,128)(2,1)S(1)}, bf16[304,2048]{1,0:T(8,128)(2,1)S(1)}, u32[]{:S(2)}, u32[]{:S(2)}) %collective-permute-start.47) | collective-permute-done | bytes 1245216 | tf_op jit(solution)/shard_map/ppermute | solution.py:207
  1315.0 27.6 %add_convert_fusion = bf16[2048,2,2048]{2,0,1:T(8,128)(2,1)} fusion(f32[2048,2,2048]{2,0,1:T(8,128)} %fusion.43, f32[2048,2,2048]{2,0,1:T(8,128)} %fusion.42), kind=kLoop, calls=%fused_computation | loop fusion | flops 16777216 | bytes 83886080 | tf_op jit(solution)/shard_map/convert_element_type | solution.py:434
  1342.5 22.5 %copy.312 = bf16[2048,2,2048]{0,2,1:T(8,128)(2,1)} copy(bf16[2048,2,2048]{2,0,1:T(8,128)(2,1)} %add_convert_fusion) | data formatting | bytes 33554432 | tf_op jit(solution)/shard_map/convert_element_type | solution.py:434
  1376.2 12.6 fusion.174
  1406.5 9.9 fusion.16
  1418.1 10.4 fusion.18
  1431.3 17.4 fusion
  1448.7 17.9 fusion.2
  1475.9 11.9 fusion.121
  1515.2 11.3 fusion.19
  1536.0 16.9 fusion.3
  1553.0 17.1 fusion.5
  1582.9 11.0 fusion.124
  1610.6 15.2 add_convert_fusion.2
  1656.7 10.4 add_convert_fusion.3
  1667.8 17.1 add_convert_fusion.1
  1702.5 16.1 psum.14
  1736.1 55.0 %reduce-scatter.24.cloned.1.call-done = bf16[2048,256]{1,0:T(8,128)(2,1)} async-done(((bf16[2048,2048]{1,0:T(8,128)(2,1)}), bf16[2048,256]{1,0:T(8,128)(2,1)}) %reduce-scatter.24.cloned.1.call-update) | async-done | bytes 1048592 | tf_op jit(solution)/shard_map/reduce_scatter | solution.py:467
  1791.2 74.7 %reduce-scatter.14.cloned.1.call-done = bf16[2048,256]{1,0:T(8,128)(2,1)} async-done(((bf16[2048,2048]{1,0:T(8,128)(2,1)}), bf16[2048,256]{1,0:T(8,128)(2,1)}) %reduce-scatter.14.cloned.1.call-update) | async-done | bytes 1048592 | tf_op jit(solution)/shard_map/reduce_scatter | solution.py:439
  1877.2 26.4 %reduce-scatter.28.cloned.1.call-done = bf16[256,2]{1,0:T(8,128)(2,1)} async-done(((bf16[2048,2]{1,0:T(8,128)(2,1)}), bf16[256,2]{1,0:T(8,128)(2,1)}) %reduce-scatter.28.cloned.1.call-update) | async-done | bytes 1040
  1911.6 66.9 %reduce-scatter.16.cloned.1.call-done = bf16[256,2048]{1,0:T(8,128)(2,1)} async-done(((bf16[2048,2048]{1,0:T(8,128)(2,1)}), bf16[256,2048]{1,0:T(8,128)(2,1)}) %reduce-scatter.16.cloned.1.call-update) | async-done | bytes 1048592 | tf_op jit(solution)/shard_map/reduce_scatter | solution.py:453
  1978.6 18.2 multiply_reduce_fusion
  2005.7 24.6 %reduce-scatter.26.cloned.1.call-done = bf16[512,256]{1,0:T(8,128)(2,1)} async-done(((bf16[2048,256]{1,0:T(8,128)(2,1)}), bf16[512,256]{1,0:T(8,128)(2,1)}) %reduce-scatter.26.cloned.1.call-update) | async-done | bytes 262160 | tf_op jit(solution)/shard_map/reduce_scatter | solution.py:466
  2033.3 24.9 %reduce-scatter.18.cloned.1.call-done = bf16[256,512]{1,0:T(8,128)(2,1)} async-done(((bf16[256,2048]{1,0:T(8,128)(2,1)}), bf16[256,512]{1,0:T(8,128)(2,1)}) %reduce-scatter.18.cloned.1.call-update) | async-done | bytes 262160 | tf_op jit(solution)/shard_map/reduce_scatter | solution.py:452
  2069.2 38.6 %psum.15 = f32[2,7]{1,0:T(2,128)S(1)} all-reduce(f32[2,7]{1,0:T(2,128)S(1)} %pad_maximum_fusion.22), channel_id=1, replica_groups=mesh['dp'=8,'tensor'=4] {'dp','tensor'}, use_global_device_ids=true, to_apply=%region_52.53 | all-reduce | flops 14 | bytes 112 | tf_op jit(solution)/shard_map/psum | solution.py:501
  (666 shorter events, 650.3 us)
Async XLA Ops:
  7.2 38.7 %all-gather.8.cloned.1.call-start = ((), (), s32[]{:S(2)}) async-start(), calls=%async_computation.17 | async-start | bytes 1310720 | tf_op jit(solution)/shard_map/all_gather | solution.py:245
  9.9 66.7 %all-gather.14.cloned.1.call-start = ((), (), s32[]{:S(2)}) async-start(), calls=%async_computation.20 | async-start | bytes 1310720 | tf_op jit(solution)/shard_map/all_gather | solution.py:251
  12.6 101.9 %all-gather.12.cloned.1.call-start = ((), (), s32[]{:S(2)}) async-start(), calls=%async_computation.19 | async-start | bytes 4718592 | tf_op jit(solution)/shard_map/all_gather | solution.py:247
  38.3 132.2 %all-gather.10.cloned.1.call-start = ((), (), s32[]{:S(2)}) async-start(), calls=%async_computation.18 | async-start | bytes 9437184 | tf_op jit(solution)/shard_map/all_gather | solution.py:244
  45.9 362.4 %all-gather.16.cloned.1.call-start = ((), (), s32[]{:S(2)}) async-start(), calls=%async_computation.21 | async-start | bytes 9437184 | tf_op jit(solution)/shard_map/all_gather | solution.py:250
  197.0 48.9 %all-to-all-start.2 = ((bf16[304,4,768]{2,0,1:T(8,128)(2,1)}), bf16[304,4,768]{2,0,1:T(8,128)(2,1)}, u32[]{:S(2)}, u32[]{:S(2)}) async-start(bf16[304,4,768]{2,0,1:T(8,128)(2,1)} %pad_maximum_fusion.11), calls=%async_computation.2 | async-start | bytes 3735552 | tf_op jit(solution)/shard_map/all_to_all | solution.py:416
  245.9 46.5 %all-to-all-start = ((bf16[304,4,768]{2,0,1:T(8,128)(2,1)}), bf16[304,4,768]{2,0,1:T(8,128)(2,1)S(1)}, u32[]{:S(2)}, u32[]{:S(2)}) async-start(bf16[304,4,768]{2,0,1:T(8,128)(2,1)} %pad_maximum_fusion.10), calls=%async_computation | async-start | bytes 3735552 | tf_op jit(solution)/shard_map/all_to_all | solution.py:416
  249.6 455.9 %all-gather.18.cloned.1.call-start = ((), (), s32[]{:S(2)}) async-start(), calls=%async_computation.22 | async-start | bytes 18874368 | tf_op jit(solution)/shard_map/all_gather | solution.py:253
  346.5 54.1 %all-to-all-start.1 = ((bf16[4,304,512]{2,1,0:T(8,128)(2,1)}), bf16[4,304,512]{2,1,0:T(8,128)(2,1)}, u32[]{:S(2)}, u32[]{:S(2)}) async-start(bf16[4,304,512]{2,1,0:T(8,128)(2,1)} %bitcast.33), calls=%async_computation.1 | async-start | bytes 2490368 | tf_op jit(solution)/shard_map/all_to_all | solution.py:418
  403.3 34.1 %all-to-all-start.3 = ((bf16[4,304,512]{2,1,0:T(8,128)(2,1)}), bf16[4,304,512]{2,1,0:T(8,128)(2,1)}, u32[]{:S(2)}, u32[]{:S(2)}) async-start(bf16[4,304,512]{2,1,0:T(8,128)(2,1)} %bitcast.736), calls=%async_computation.3 | async-start | bytes 2490368 | tf_op jit(solution)/shard_map/all_to_all | solution.py:418
  408.3 327.9 %all-gather.20.cloned.1.call-start = ((), (), s32[]{:S(2)}) async-start(), calls=%async_computation.23 | async-start | bytes 9437184 | tf_op jit(solution)/shard_map/all_gather | solution.py:254
  446.2 27.6 %collective-permute-start = (bf16[304,2048]{1,0:T(8,128)(2,1)S(1)}, bf16[304,2048]{1,0:T(8,128)(2,1)S(1)}, u32[]{:S(2)}, u32[]{:S(2)}) collective-permute-start(bf16[304,2048]{1,0:T(8,128)(2,1)S(1)} %get-tuple-element.173), channel_id=1, source_target_pairs={{0,1},{1,2},{2,3},{4,5},{5,6},{6,7},{8,9},{9,10},{10,11},{12,13},{... | collective-permute-start | bytes 3735560 | tf_op jit(solution)/shard_map/ppermute | solution.py:175
  447.9 30.4 %collective-permute-start.1 = (bf16[304,2048]{1,0:T(8,128)(2,1)S(1)}, bf16[304,2048]{1,0:T(8,128)(2,1)}, u32[]{:S(2)}, u32[]{:S(2)}) collective-permute-start(bf16[304,2048]{1,0:T(8,128)(2,1)S(1)} %get-tuple-element.173), channel_id=1, source_target_pairs={{1,0},{2,1},{3,2},{5,4},{6,5},{7,6},{9,8},{10,9},{11,10},{13,12},{... | collective-permute-start | bytes 3735560 | tf_op jit(solution)/shard_map/ppermute | solution.py:178
  478.3 29.7 %collective-permute-start.3 = (bf16[304,2048]{1,0:T(8,128)(2,1)}, bf16[304,2048]{1,0:T(8,128)(2,1)}, u32[]{:S(2)}, u32[]{:S(2)}) collective-permute-start(bf16[304,2048]{1,0:T(8,128)(2,1)} %collective-permute-done.1), channel_id=1, source_target_pairs={{1,0},{2,1},{5,4},{6,5},{9,8},{10,9},{13,12},{14,13},{17,16},{18,1... | collective-permute-start | bytes 3735560 | tf_op jit(solution)/shard_map/ppermute | solution.py:178
  479.6 34.9 %collective-permute-start.4 = (bf16[304,2048]{1,0:T(8,128)(2,1)}, bf16[304,2048]{1,0:T(8,128)(2,1)}, u32[]{:S(2)}, u32[]{:S(2)}) collective-permute-start(bf16[304,2048]{1,0:T(8,128)(2,1)} %collective-permute-done.2), channel_id=1, source_target_pairs={{2,3},{6,7},{10,11},{14,15},{18,19},{22,23},{26,27},{30,31}} | collective-permute-start | bytes 3735560 | tf_op jit(solution)/shard_map/ppermute | solution.py:175
  508.0 28.8 %collective-permute-start.5 = (bf16[304,2048]{1,0:T(8,128)(2,1)}, bf16[304,2048]{1,0:T(8,128)(2,1)S(1)}, u32[]{:S(2)}, u32[]{:S(2)}) collective-permute-start(bf16[304,2048]{1,0:T(8,128)(2,1)} %collective-permute-done.3), channel_id=1, source_target_pairs={{1,0},{5,4},{9,8},{13,12},{17,16},{21,20},{25,24},{29,28}} | collective-permute-start | bytes 3735560 | tf_op jit(solution)/shard_map/ppermute | solution.py:178
  537.1 24.9 %collective-permute-start.6 = (bf16[304,2048]{1,0:T(8,128)(2,1)S(1)}, bf16[304,2048]{1,0:T(8,128)(2,1)S(1)}, u32[]{:S(2)}, u32[]{:S(2)}) collective-permute-start(bf16[304,2048]{1,0:T(8,128)(2,1)S(1)} %get-tuple-element.174), channel_id=1, source_target_pairs={{0,1},{1,2},{2,3},{4,5},{5,6},{6,7},{8,9},{9,10},{10,11},{12,13},{... | collective-permute-start | bytes 3735560 | tf_op jit(solution)/shard_map/ppermute | solution.py:175
  538.8 27.6 %collective-permute-start.7 = (bf16[304,2048]{1,0:T(8,128)(2,1)S(1)}, bf16[304,2048]{1,0:T(8,128)(2,1)S(1)}, u32[]{:S(2)}, u32[]{:S(2)}) collective-permute-start(bf16[304,2048]{1,0:T(8,128)(2,1)S(1)} %get-tuple-element.174), channel_id=1, source_target_pairs={{1,0},{2,1},{3,2},{5,4},{6,5},{7,6},{9,8},{10,9},{11,10},{13,12},{... | collective-permute-start | bytes 3735560 | tf_op jit(solution)/shard_map/ppermute | solution.py:178
  566.3 27.5 %collective-permute-start.9 = (bf16[304,2048]{1,0:T(8,128)(2,1)S(1)}, bf16[304,2048]{1,0:T(8,128)(2,1)S(1)}, u32[]{:S(2)}, u32[]{:S(2)}) collective-permute-start(bf16[304,2048]{1,0:T(8,128)(2,1)S(1)} %collective-permute-done.7), channel_id=1, source_target_pairs={{1,0},{2,1},{5,4},{6,5},{9,8},{10,9},{13,12},{14,13},{17,16},{18,1... | collective-permute-start | bytes 3735560 | tf_op jit(solution)/shard_map/ppermute | solution.py:178
  567.6 34.9 %collective-permute-start.10 = (bf16[304,2048]{1,0:T(8,128)(2,1)S(1)}, bf16[304,2048]{1,0:T(8,128)(2,1)S(1)}, u32[]{:S(2)}, u32[]{:S(2)}) collective-permute-start(bf16[304,2048]{1,0:T(8,128)(2,1)S(1)} %collective-permute-done.8), channel_id=1, source_target_pairs={{2,3},{6,7},{10,11},{14,15},{18,19},{22,23},{26,27},{30,31}} | collective-permute-start | bytes 3735560 | tf_op jit(solution)/shard_map/ppermute | solution.py:175
  593.9 25.7 %collective-permute-start.11 = (bf16[304,2048]{1,0:T(8,128)(2,1)S(1)}, bf16[304,2048]{1,0:T(8,128)(2,1)S(1)}, u32[]{:S(2)}, u32[]{:S(2)}) collective-permute-start(bf16[304,2048]{1,0:T(8,128)(2,1)S(1)} %collective-permute-done.9), channel_id=1, source_target_pairs={{1,0},{5,4},{9,8},{13,12},{17,16},{21,20},{25,24},{29,28}} | collective-permute-start | bytes 3735560 | tf_op jit(solution)/shard_map/ppermute | solution.py:178
  621.8 22.1 %collective-permute-start.12 = (bf16[304,2048]{1,0:T(8,128)(2,1)S(1)}, bf16[304,2048]{1,0:T(8,128)(2,1)S(1)}, u32[]{:S(2)}, u32[]{:S(2)}) collective-permute-start(bf16[304,2048]{1,0:T(8,128)(2,1)S(1)} %get-tuple-element.175), channel_id=1, source_target_pairs={{0,1},{1,2},{2,3},{4,5},{5,6},{6,7},{8,9},{9,10},{10,11},{12,13},{... | collective-permute-start | bytes 3735560 | tf_op jit(solution)/shard_map/ppermute | solution.py:175
  623.4 27.3 %collective-permute-start.13 = (bf16[304,2048]{1,0:T(8,128)(2,1)S(1)}, bf16[304,2048]{1,0:T(8,128)(2,1)}, u32[]{:S(2)}, u32[]{:S(2)}) collective-permute-start(bf16[304,2048]{1,0:T(8,128)(2,1)S(1)} %get-tuple-element.175), channel_id=1, source_target_pairs={{1,0},{2,1},{3,2},{5,4},{6,5},{7,6},{9,8},{10,9},{11,10},{13,12},{... | collective-permute-start | bytes 3735560 | tf_op jit(solution)/shard_map/ppermute | solution.py:178
  650.7 27.5 %collective-permute-start.15 = (bf16[304,2048]{1,0:T(8,128)(2,1)}, bf16[304,2048]{1,0:T(8,128)(2,1)}, u32[]{:S(2)}, u32[]{:S(2)}) collective-permute-start(bf16[304,2048]{1,0:T(8,128)(2,1)} %collective-permute-done.13), channel_id=1, source_target_pairs={{1,0},{2,1},{5,4},{6,5},{9,8},{10,9},{13,12},{14,13},{17,16},{18,1... | collective-permute-start | bytes 3735560 | tf_op jit(solution)/shard_map/ppermute | solution.py:178
  652.0 38.9 %collective-permute-start.16 = (bf16[304,2048]{1,0:T(8,128)(2,1)}, bf16[304,2048]{1,0:T(8,128)(2,1)}, u32[]{:S(2)}, u32[]{:S(2)}) collective-permute-start(bf16[304,2048]{1,0:T(8,128)(2,1)} %collective-permute-done.14), channel_id=1, source_target_pairs={{2,3},{6,7},{10,11},{14,15},{18,19},{22,23},{26,27},{30,31}} | collective-permute-start | bytes 3735560 | tf_op jit(solution)/shard_map/ppermute | solution.py:175
  678.3 23.2 %collective-permute-start.17 = (bf16[304,2048]{1,0:T(8,128)(2,1)}, bf16[304,2048]{1,0:T(8,128)(2,1)S(1)}, u32[]{:S(2)}, u32[]{:S(2)}) collective-permute-start(bf16[304,2048]{1,0:T(8,128)(2,1)} %collective-permute-done.15), channel_id=1, source_target_pairs={{1,0},{5,4},{9,8},{13,12},{17,16},{21,20},{25,24},{29,28}} | collective-permute-start | bytes 3735560 | tf_op jit(solution)/shard_map/ppermute | solution.py:178
  703.8 30.3 %collective-permute-start.18 = (bf16[304,2048]{1,0:T(8,128)(2,1)S(1)}, bf16[304,2048]{1,0:T(8,128)(2,1)S(1)}, u32[]{:S(2)}, u32[]{:S(2)}) collective-permute-start(bf16[304,2048]{1,0:T(8,128)(2,1)S(1)} %get-tuple-element.176), channel_id=1, source_target_pairs={{0,1},{1,2},{2,3},{4,5},{5,6},{6,7},{8,9},{9,10},{10,11},{12,13},{... | collective-permute-start | bytes 3735560 | tf_op jit(solution)/shard_map/ppermute | solution.py:175
  732.8 29.1 %collective-permute-start.19 = (bf16[304,2048]{1,0:T(8,128)(2,1)S(1)}, bf16[304,2048]{1,0:T(8,128)(2,1)}, u32[]{:S(2)}, u32[]{:S(2)}) collective-permute-start(bf16[304,2048]{1,0:T(8,128)(2,1)S(1)} %get-tuple-element.176), channel_id=1, source_target_pairs={{1,0},{2,1},{3,2},{5,4},{6,5},{7,6},{9,8},{10,9},{11,10},{13,12},{... | collective-permute-start | bytes 3735560 | tf_op jit(solution)/shard_map/ppermute | solution.py:178
  734.1 29.1 %collective-permute-start.20 = (bf16[304,2048]{1,0:T(8,128)(2,1)S(1)}, bf16[304,2048]{1,0:T(8,128)(2,1)}, u32[]{:S(2)}, u32[]{:S(2)}) collective-permute-start(bf16[304,2048]{1,0:T(8,128)(2,1)S(1)} %collective-permute-done.18), channel_id=1, source_target_pairs={{1,2},{2,3},{5,6},{6,7},{9,10},{10,11},{13,14},{14,15},{17,18},{18... | collective-permute-start | bytes 3735560 | tf_op jit(solution)/shard_map/ppermute | solution.py:175
  761.9 30.5 %collective-permute-start.21 = (bf16[304,2048]{1,0:T(8,128)(2,1)}, bf16[304,2048]{1,0:T(8,128)(2,1)S(1)}, u32[]{:S(2)}, u32[]{:S(2)}) collective-permute-start(bf16[304,2048]{1,0:T(8,128)(2,1)} %collective-permute-done.19), channel_id=1, source_target_pairs={{1,0},{2,1},{5,4},{6,5},{9,8},{10,9},{13,12},{14,13},{17,16},{18,1... | collective-permute-start | bytes 3735560 | tf_op jit(solution)/shard_map/ppermute | solution.py:178
  763.3 34.5 %collective-permute-start.22 = (bf16[304,2048]{1,0:T(8,128)(2,1)}, bf16[304,2048]{1,0:T(8,128)(2,1)S(1)}, u32[]{:S(2)}, u32[]{:S(2)}) collective-permute-start(bf16[304,2048]{1,0:T(8,128)(2,1)} %collective-permute-done.20), channel_id=1, source_target_pairs={{2,3},{6,7},{10,11},{14,15},{18,19},{22,23},{26,27},{30,31}} | collective-permute-start | bytes 3735560 | tf_op jit(solution)/shard_map/ppermute | solution.py:175
  792.5 22.1 %collective-permute-start.23 = (bf16[304,2048]{1,0:T(8,128)(2,1)S(1)}, bf16[304,2048]{1,0:T(8,128)(2,1)S(1)}, u32[]{:S(2)}, u32[]{:S(2)}) collective-permute-start(bf16[304,2048]{1,0:T(8,128)(2,1)S(1)} %collective-permute-done.21), channel_id=1, source_target_pairs={{1,0},{5,4},{9,8},{13,12},{17,16},{21,20},{25,24},{29,28}} | collective-permute-start | bytes 3735560 | tf_op jit(solution)/shard_map/ppermute | solution.py:178
  817.5 22.4 %collective-permute-start.24 = (bf16[304,2048]{1,0:T(8,128)(2,1)}, bf16[304,2048]{1,0:T(8,128)(2,1)S(1)}, u32[]{:S(2)}, u32[]{:S(2)}) collective-permute-start(bf16[304,2048]{1,0:T(8,128)(2,1)} %get-tuple-element.365), channel_id=1, source_target_pairs={{0,1},{4,5},{8,9},{12,13},{16,17},{20,21},{24,25},{28,29}} | collective-permute-start | bytes 3735560 | tf_op jit(solution)/shard_map/ppermute | solution.py:201
  819.1 55.0 %collective-permute-start.27 = (bf16[304,2048]{1,0:T(8,128)(2,1)S(1)}, bf16[304,2048]{1,0:T(8,128)(2,1)S(1)}, u32[]{:S(2)}, u32[]{:S(2)}) collective-permute-start(bf16[304,2048]{1,0:T(8,128)(2,1)S(1)} %get-tuple-element.366), channel_id=1, source_target_pairs={{3,2},{7,6},{11,10},{15,14},{19,18},{23,22},{27,26},{31,30}} | collective-permute-start | bytes 3735560 | tf_op jit(solution)/shard_map/ppermute | solution.py:207
  842.2 31.9 %collective-permute-start.25 = (bf16[304,2048]{1,0:T(8,128)(2,1)S(1)}, bf16[304,2048]{1,0:T(8,128)(2,1)S(1)}, u32[]{:S(2)}, u32[]{:S(2)}) collective-permute-start(bf16[304,2048]{1,0:T(8,128)(2,1)S(1)} %add_convert_fusion.22), channel_id=1, source_target_pairs={{0,1},{1,2},{4,5},{5,6},{8,9},{9,10},{12,13},{13,14},{16,17},{17,1... | collective-permute-start | bytes 3735560 | tf_op jit(solution)/shard_map/ppermute | solution.py:201
  876.1 29.7 %collective-permute-start.28 = (bf16[304,2048]{1,0:T(8,128)(2,1)}, bf16[304,2048]{1,0:T(8,128)(2,1)S(1)}, u32[]{:S(2)}, u32[]{:S(2)}) collective-permute-start(bf16[304,2048]{1,0:T(8,128)(2,1)} %get-tuple-element.364), channel_id=1, source_target_pairs={{2,1},{3,2},{6,5},{7,6},{10,9},{11,10},{14,13},{15,14},{18,17},{19... | collective-permute-start | bytes 3735560 | tf_op jit(solution)/shard_map/ppermute | solution.py:207
  931.3 29.8 %collective-permute-start.30 = (bf16[304,2048]{1,0:T(8,128)(2,1)S(1)}, bf16[304,2048]{1,0:T(8,128)(2,1)S(1)}, u32[]{:S(2)}, u32[]{:S(2)}) collective-permute-start(bf16[304,2048]{1,0:T(8,128)(2,1)S(1)} %get-tuple-element.361), channel_id=1, source_target_pairs={{0,1},{4,5},{8,9},{12,13},{16,17},{20,21},{24,25},{28,29}} | collective-permute-start | bytes 3735560 | tf_op jit(solution)/shard_map/ppermute | solution.py:201
  935.3 58.9 %collective-permute-start.33 = (bf16[304,2048]{1,0:T(8,128)(2,1)S(1)}, bf16[304,2048]{1,0:T(8,128)(2,1)S(1)}, u32[]{:S(2)}, u32[]{:S(2)}) collective-permute-start(bf16[304,2048]{1,0:T(8,128)(2,1)S(1)} %get-tuple-element.362), channel_id=1, source_target_pairs={{3,2},{7,6},{11,10},{15,14},{19,18},{23,22},{27,26},{31,30}} | collective-permute-start | bytes 3735560 | tf_op jit(solution)/shard_map/ppermute | solution.py:207
  961.5 32.7 %collective-permute-start.31 = (bf16[304,2048]{1,0:T(8,128)(2,1)S(1)}, bf16[304,2048]{1,0:T(8,128)(2,1)S(1)}, u32[]{:S(2)}, u32[]{:S(2)}) collective-permute-start(bf16[304,2048]{1,0:T(8,128)(2,1)S(1)} %add_convert_fusion.17), channel_id=1, source_target_pairs={{0,1},{1,2},{4,5},{5,6},{8,9},{9,10},{12,13},{13,14},{16,17},{17,1... | collective-permute-start | bytes 3735560 | tf_op jit(solution)/shard_map/ppermute | solution.py:201
  995.1 32.3 %collective-permute-start.34 = (bf16[304,2048]{1,0:T(8,128)(2,1)S(1)}, bf16[304,2048]{1,0:T(8,128)(2,1)S(1)}, u32[]{:S(2)}, u32[]{:S(2)}) collective-permute-start(bf16[304,2048]{1,0:T(8,128)(2,1)S(1)} %get-tuple-element.360), channel_id=1, source_target_pairs={{2,1},{3,2},{6,5},{7,6},{10,9},{11,10},{14,13},{15,14},{18,17},{19... | collective-permute-start | bytes 3735560 | tf_op jit(solution)/shard_map/ppermute | solution.py:207
  1024.0 24.2 %collective-permute-start.32 = (bf16[304,2048]{1,0:T(8,128)(2,1)S(1)}, bf16[304,2048]{1,0:T(8,128)(2,1)}, u32[]{:S(2)}, u32[]{:S(2)}) collective-permute-start(bf16[304,2048]{1,0:T(8,128)(2,1)S(1)} %get-tuple-element.359), channel_id=1, source_target_pairs={{0,1},{1,2},{2,3},{4,5},{5,6},{6,7},{8,9},{9,10},{10,11},{12,13},{... | collective-permute-start | bytes 3735560 | tf_op jit(solution)/shard_map/ppermute | solution.py:201
  1052.3 31.7 %collective-permute-start.36 = (bf16[304,2048]{1,0:T(8,128)(2,1)S(1)}, bf16[304,2048]{1,0:T(8,128)(2,1)S(1)}, u32[]{:S(2)}, u32[]{:S(2)}) collective-permute-start(bf16[304,2048]{1,0:T(8,128)(2,1)S(1)} %get-tuple-element.357), channel_id=1, source_target_pairs={{0,1},{4,5},{8,9},{12,13},{16,17},{20,21},{24,25},{28,29}} | collective-permute-start | bytes 3735560 | tf_op jit(solution)/shard_map/ppermute | solution.py:201
  1057.1 60.9 %collective-permute-start.39 = (bf16[304,2048]{1,0:T(8,128)(2,1)S(1)}, bf16[304,2048]{1,0:T(8,128)(2,1)S(1)}, u32[]{:S(2)}, u32[]{:S(2)}) collective-permute-start(bf16[304,2048]{1,0:T(8,128)(2,1)S(1)} %get-tuple-element.358), channel_id=1, source_target_pairs={{3,2},{7,6},{11,10},{15,14},{19,18},{23,22},{27,26},{31,30}} | collective-permute-start | bytes 3735560 | tf_op jit(solution)/shard_map/ppermute | solution.py:207
  1084.4 33.6 %collective-permute-start.37 = (bf16[304,2048]{1,0:T(8,128)(2,1)S(1)}, bf16[304,2048]{1,0:T(8,128)(2,1)S(1)}, u32[]{:S(2)}, u32[]{:S(2)}) collective-permute-start(bf16[304,2048]{1,0:T(8,128)(2,1)S(1)} %add_convert_fusion.12), channel_id=1, source_target_pairs={{0,1},{1,2},{4,5},{5,6},{8,9},{9,10},{12,13},{13,14},{16,17},{17,1... | collective-permute-start | bytes 3735560 | tf_op jit(solution)/shard_map/ppermute | solution.py:201
  1120.3 27.7 %collective-permute-start.40 = (bf16[304,2048]{1,0:T(8,128)(2,1)}, bf16[304,2048]{1,0:T(8,128)(2,1)S(1)}, u32[]{:S(2)}, u32[]{:S(2)}) collective-permute-start(bf16[304,2048]{1,0:T(8,128)(2,1)} %get-tuple-element.356), channel_id=1, source_target_pairs={{2,1},{3,2},{6,5},{7,6},{10,9},{11,10},{14,13},{15,14},{18,17},{19... | collective-permute-start | bytes 3735560 | tf_op jit(solution)/shard_map/ppermute | solution.py:207
  1145.5 24.3 %collective-permute-start.38 = (bf16[304,2048]{1,0:T(8,128)(2,1)}, bf16[304,2048]{1,0:T(8,128)(2,1)S(1)}, u32[]{:S(2)}, u32[]{:S(2)}) collective-permute-start(bf16[304,2048]{1,0:T(8,128)(2,1)} %get-tuple-element.355), channel_id=1, source_target_pairs={{0,1},{1,2},{2,3},{4,5},{5,6},{6,7},{8,9},{9,10},{10,11},{12,13},{... | collective-permute-start | bytes 3735560 | tf_op jit(solution)/shard_map/ppermute | solution.py:201
  1150.1 20.6 collective-permute-start.41
  1174.3 32.9 %collective-permute-start.42 = (bf16[304,2048]{1,0:T(8,128)(2,1)S(1)}, bf16[304,2048]{1,0:T(8,128)(2,1)S(1)}, u32[]{:S(2)}, u32[]{:S(2)}) collective-permute-start(bf16[304,2048]{1,0:T(8,128)(2,1)S(1)} %get-tuple-element.353), channel_id=1, source_target_pairs={{0,1},{4,5},{8,9},{12,13},{16,17},{20,21},{24,25},{28,29}} | collective-permute-start | bytes 3735560 | tf_op jit(solution)/shard_map/ppermute | solution.py:201
  1179.7 32.4 %collective-permute-start.45 = (bf16[304,2048]{1,0:T(8,128)(2,1)S(1)}, bf16[304,2048]{1,0:T(8,128)(2,1)S(1)}, u32[]{:S(2)}, u32[]{:S(2)}) collective-permute-start(bf16[304,2048]{1,0:T(8,128)(2,1)S(1)} %get-tuple-element.354), channel_id=1, source_target_pairs={{3,2},{7,6},{11,10},{15,14},{19,18},{23,22},{27,26},{31,30}} | collective-permute-start | bytes 3735560 | tf_op jit(solution)/shard_map/ppermute | solution.py:207
  1207.7 31.0 %collective-permute-start.43 = (bf16[304,2048]{1,0:T(8,128)(2,1)S(1)}, bf16[304,2048]{1,0:T(8,128)(2,1)S(1)}, u32[]{:S(2)}, u32[]{:S(2)}) collective-permute-start(bf16[304,2048]{1,0:T(8,128)(2,1)S(1)} %add_convert_fusion.8), channel_id=1, source_target_pairs={{0,1},{1,2},{4,5},{5,6},{8,9},{9,10},{12,13},{13,14},{16,17},{17,1... | collective-permute-start | bytes 3735560 | tf_op jit(solution)/shard_map/ppermute | solution.py:201
  1246.1 38.7 %collective-permute-start.47 = (bf16[304,2048]{1,0:T(8,128)(2,1)S(1)}, bf16[304,2048]{1,0:T(8,128)(2,1)S(1)}, u32[]{:S(2)}, u32[]{:S(2)}) collective-permute-start(bf16[304,2048]{1,0:T(8,128)(2,1)S(1)} %add_convert_fusion.5), channel_id=1, source_target_pairs={{1,0},{2,1},{3,2},{5,4},{6,5},{7,6},{9,8},{10,9},{11,10},{13,12},{... | collective-permute-start | bytes 3735560 | tf_op jit(solution)/shard_map/ppermute | solution.py:207
  1307.1 83.0 %all-to-all-start.6 = ((bf16[304,4,512]{2,0,1:T(8,128)(2,1)}), bf16[304,4,512]{2,0,1:T(8,128)(2,1)}, u32[]{:S(2)}, u32[]{:S(2)}) async-start(bf16[304,4,512]{2,0,1:T(8,128)(2,1)} %copy.297), calls=%async_computation.6 | async-start | bytes 2490368 | tf_op jit(solution)/shard_map/all_to_all | solution.py:416
  1314.8 352.4 %reduce-scatter.12.cloned.1.call-start = ((), (), s32[]{:S(2)}) async-start(), calls=%async_computation.24 | async-start | bytes 18874368 | tf_op jit(solution)/shard_map/reduce_scatter | solution.py:433
  1390.1 97.7 %all-to-all-start.4 = ((bf16[304,4,512]{2,0,1:T(8,128)(2,1)}), bf16[304,4,512]{2,0,1:T(8,128)(2,1)}, u32[]{:S(2)}, u32[]{:S(2)}) async-start(bf16[304,4,512]{2,0,1:T(8,128)(2,1)} %copy.284), calls=%async_computation.4 | async-start | bytes 2490368 | tf_op jit(solution)/shard_map/all_to_all | solution.py:416
  1509.5 96.0 %all-to-all-start.7 = ((bf16[4,304,768]{2,1,0:T(8,128)(2,1)}), bf16[4,304,768]{2,1,0:T(8,128)(2,1)}, u32[]{:S(2)}, u32[]{:S(2)}) async-start(bf16[4,304,768]{2,1,0:T(8,128)(2,1)} %bitcast.702), calls=%async_computation.7 | async-start | bytes 3735552 | tf_op jit(solution)/shard_map/all_to_all | solution.py:418
  1605.5 29.8 %all-to-all-start.5 = ((bf16[4,304,768]{2,1,0:T(8,128)(2,1)}), bf16[4,304,768]{2,1,0:T(8,128)(2,1)S(1)}, u32[]{:S(2)}, u32[]{:S(2)}) async-start(bf16[4,304,768]{2,1,0:T(8,128)(2,1)} %bitcast.703), calls=%async_computation.5 | async-start | bytes 3735552 | tf_op jit(solution)/shard_map/all_to_all | solution.py:418
  1610.6 109.9 %reduce-scatter.20.cloned.1.call-start = ((), (), s32[]{:S(2)}) async-start(), calls=%async_computation.28 | async-start | bytes 4718592 | tf_op jit(solution)/shard_map/reduce_scatter | solution.py:459
  1667.2 124.0 %reduce-scatter.24.cloned.1.call-start = ((), (), s32[]{:S(2)}) async-start(), calls=%async_computation.30 | async-start | bytes 9437184 | tf_op jit(solution)/shard_map/reduce_scatter | solution.py:467
  1667.8 198.2 %reduce-scatter.14.cloned.1.call-start = ((), (), s32[]{:S(2)}) async-start(), calls=%async_computation.25 | async-start | bytes 9437184 | tf_op jit(solution)/shard_map/reduce_scatter | solution.py:439
  1684.9 218.7 %reduce-scatter.28.cloned.1.call-start = ((), (), s32[]{:S(2)}) async-start(), calls=%async_computation.32 | async-start | bytes 589824
  1719.7 258.9 %reduce-scatter.16.cloned.1.call-start = ((), (), s32[]{:S(2)}) async-start(), calls=%async_computation.26 | async-start | bytes 9437184 | tf_op jit(solution)/shard_map/reduce_scatter | solution.py:453
  1720.4 282.1 %reduce-scatter.22.cloned.1.call-start = ((), (), s32[]{:S(2)}) async-start(), calls=%async_computation.29 | async-start | bytes 655360 | tf_op jit(solution)/shard_map/reduce_scatter | solution.py:458
  1721.0 309.3 %reduce-scatter.26.cloned.1.call-start = ((), (), s32[]{:S(2)}) async-start(), calls=%async_computation.31 | async-start | bytes 1310720 | tf_op jit(solution)/shard_map/reduce_scatter | solution.py:466
  1791.2 267.1 %reduce-scatter.18.cloned.1.call-start = ((), (), s32[]{:S(2)}) async-start(), calls=%async_computation.27 | async-start | bytes 1310720 | tf_op jit(solution)/shard_map/reduce_scatter | solution.py:452
  (151 other events, 2598.4 us)
Sparse Core Ops, SparseCore 0:
  10.1 35.7 all-gather.7
  48.0 28.5 all-gather.13
  78.5 35.9 all-gather.11
  116.2 54.2 all-gather.9
  172.3 55.8 all-gather.15
  255.5 90.2 all-gather.17
  483.6 80.2 all-gather.19
  1365.2 116.5 reduce-scatter.11
  1667.3 49.1 reduce-scatter.19
  1719.8 71.2 reduce-scatter.23
  1794.6 71.2 reduce-scatter.13
  1869.4 34.0 reduce-scatter.27
  1907.0 71.4 reduce-scatter.15
  1980.7 21.8 reduce-scatter.21
  2004.7 25.5 reduce-scatter.25
  2032.5 25.7 reduce-scatter.17

commit v9 on v7

--- a/solution.py
+++ b/solution.py
@@ -343,12 +343,16 @@
         middle_grad = upstream + middle_back
         attn_grad = (branch_scale * middle_grad).astype(jnp.bfloat16)
         grad_output = contract_rows(mixed, attn_grad)
-        mixed_grad = yield (
-            "to_heads",
-            contract_cols(attn_grad, full_output)
-            .astype(jnp.bfloat16)
-            .reshape(rows, tensor_count, query_width),
-        )
+        mixed_grad_own, grad_gateup, grad_down = lax.optimization_barrier(
+            (
+                contract_cols(attn_grad, full_output)
+                .astype(jnp.bfloat16)
+                .reshape(rows, tensor_count, query_width),
+                grad_gateup,
+                grad_down,
+            )
+        )
+        mixed_grad = yield ("to_heads", mixed_grad_own)
         mixed_grad = mixed_grad.reshape(group_rows, keyval_heads, head_repeat, HD)
         query_grad, key_grad, value_grad = attend_back(
             queries, key_rows, values, visible, log_totals, mixed_grad, block_rows

time: 2030 us -> 2060 us (1.015)
  other arithmetic: 200 us -> 247 us
  waiting for transfers between devices: 790 us -> 757 us
  local copies, waits for them, and re-layouts: 186 us -> 207 us
    convert_element_type x0 -> x2, other arithmetic: none -> 43 us  [the longest x1 27.5 us: per_device(): totals[3].reshape(width, -1).astype(jnp.bfloat16)]
    ppermute x12, waiting for transfers between devices: 145 us -> 105 us  [line_scatter(): lax.ppermute(send.astype(jnp.bfloat16), 'tensor', [(i, i + 1) for i in ra...]
    convert_element_type x0 -> x1, local copies, waits for them, and re-layouts: none -> 22.5 us  [per_device(): totals[3].reshape(width, -1).astype(jnp.bfloat16)]
  transfers between devices with their start and end apart: 72 -> 72, of which waited for: 39 -> 36; matrix products, arithmetic and copies ran while one was open for 42% -> 45% of each run, Pallas kernels for 0% -> 0%
where the time goes in v9:
time: 2060 us; the launch traced here: 2050 us
  waiting for transfers between devices  757 us (37%)
  matrix products  571 us (28%)
  other arithmetic  247 us (12%)
  local copies, waits for them, and re-layouts  207 us (10%)
  starting transfers between devices  155 us (8%)
  blocking collectives  91.4 us (4%)
    ppermute x12, waiting for transfers between devices, line_gather(): lax.ppermute(from_right, 'tensor', [(i, i - 1) for i in range(1, count -...  160 us
    ppermute x12, waiting for transfers between devices, line_scatter(): lax.ppermute(send.astype(jnp.bfloat16), 'tensor', [(i, i + 1) for i in ra...  105 us
    dot_general x6, matrix products, contract_cols(): lax.dot_general(left, right, (((1,), (1,)), ((), ())), preferred_element_...  78.4 us
    dot_general x6, matrix products, contract_rows(): lax.dot_general(left, right, (((0,), (0,)), ((), ())), preferred_element_...  73.2 us
    reduce_scatter x1, waiting for transfers between devices, per_device(): lax.psum_scatter(totals[4].astype(jnp.bfloat16), 'dp', scatter_dimension=...  73 us
    ppermute x12, starting transfers between devices, line_scatter(): lax.ppermute(send.astype(jnp.bfloat16), 'tensor', [(i, i + 1) for i in ra...  67.3 us
    ppermute x12, waiting for transfers between devices, line_gather(): lax.ppermute(from_left, 'tensor', [(i, i + 1) for i in range(step - 1, co...  66 us
    reduce_scatter x1, waiting for transfers between devices, per_device(): lax.psum_scatter(output_low, 'dp', scatter_dimension=1, tiled=True)  64.1 us
  transfers between devices with their start and end apart: 72, of which 36 were waited for; matrix products, arithmetic and copies ran while one was open for 45% of the time, Pallas kernels for 0%

profile of v9, /device:TPU:0, one launch (start us, length us, event | category | flops | bytes accessed | tf_op | source)
XLA Modules:
  0.0 2049.3 jit_solution(9931358451424187603)
XLA Ops:
  13.5 24.4 %all_gather.30 = bf16[256,8,128]{2,0,1:T(8,128)(2,1)} all-gather(bf16[256,2,128]{2,0,1:T(8,128)(2,1)S(1)} %copy.368), channel_id=1, replica_groups=mesh['dp'=8,'tensor'=4] {'tensor'}, dimensions={1}, use_global_device_ids=true | all-gather | bytes 655360 | tf_op jit(solution)/shard_map/all_gather | solution.py:248
  45.8 30.6 %all-gather.14.cloned.1.call-done = bf16[2048,256]{1,0:T(8,128)(2,1)} async-done(((bf16[512,256]{1,0:T(8,128)(2,1)}), bf16[2048,256]{1,0:T(8,128)(2,1)}) %all-gather.14.cloned.1.call-update) | async-done | bytes 1048592 | tf_op jit(solution)/shard_map/all_gather | solution.py:251
  86.5 9.3 all_gather.27
  99.0 15.4 all-gather.12.cloned.1.call-done
  121.9 48.5 %all-gather.10.cloned.1.call-done = bf16[2048,2048]{1,0:T(8,128)(2,1)} async-done(((bf16[256,2048]{1,0:T(8,128)(2,1)}), bf16[2048,2048]{1,0:T(8,128)(2,1)}) %all-gather.10.cloned.1.call-update) | async-done | bytes 8388624 | tf_op jit(solution)/shard_map/all_gather | solution.py:244
  170.4 12.3 copy.255
  234.9 10.7 all-to-all-done
  275.6 12.4 fusion.135
  331.7 12.6 fusion.134
  373.5 20.6 %all-to-all-done.3 = bf16[4,304,512]{2,1,0:T(8,128)(2,1)} async-done(((bf16[4,304,512]{2,1,0:T(8,128)(2,1)}), bf16[4,304,512]{2,1,0:T(8,128)(2,1)}, u32[]{:S(2)}, u32[]{:S(2)}) %all-to-all-start.3) | async-done | bytes 1245216 | tf_op jit(solution)/shard_map/all_to_all | solution.py:416
  406.0 24.8 %collective-permute-done = bf16[304,2048]{1,0:T(8,128)(2,1)S(1)} collective-permute-done((bf16[304,2048]{1,0:T(8,128)(2,1)S(1)}, bf16[304,2048]{1,0:T(8,128)(2,1)S(1)}, u32[]{:S(2)}, u32[]{:S(2)}) %collective-permute-start) | collective-permute-done | bytes 1245216 | tf_op jit(solution)/shard_map/ppermute | solution.py:175
  440.3 24.6 %collective-permute-done.3 = bf16[304,2048]{1,0:T(8,128)(2,1)} collective-permute-done((bf16[304,2048]{1,0:T(8,128)(2,1)}, bf16[304,2048]{1,0:T(8,128)(2,1)}, u32[]{:S(2)}, u32[]{:S(2)}) %collective-permute-start.3) | collective-permute-done | bytes 1245216 | tf_op jit(solution)/shard_map/ppermute | solution.py:178
  472.9 20.7 %collective-permute-done.5 = bf16[304,2048]{1,0:T(8,128)(2,1)S(1)} collective-permute-done((bf16[304,2048]{1,0:T(8,128)(2,1)}, bf16[304,2048]{1,0:T(8,128)(2,1)S(1)}, u32[]{:S(2)}, u32[]{:S(2)}) %collective-permute-start.5) | collective-permute-done | bytes 1245216 | tf_op jit(solution)/shard_map/ppermute | solution.py:178
  496.9 22.0 %collective-permute-done.6 = bf16[304,2048]{1,0:T(8,128)(2,1)S(1)} collective-permute-done((bf16[304,2048]{1,0:T(8,128)(2,1)S(1)}, bf16[304,2048]{1,0:T(8,128)(2,1)S(1)}, u32[]{:S(2)}, u32[]{:S(2)}) %collective-permute-start.6) | collective-permute-done | bytes 1245216 | tf_op jit(solution)/shard_map/ppermute | solution.py:175
  525.8 24.9 %collective-permute-done.9 = bf16[304,2048]{1,0:T(8,128)(2,1)S(1)} collective-permute-done((bf16[304,2048]{1,0:T(8,128)(2,1)S(1)}, bf16[304,2048]{1,0:T(8,128)(2,1)S(1)}, u32[]{:S(2)}, u32[]{:S(2)}) %collective-permute-start.9) | collective-permute-done | bytes 1245216 | tf_op jit(solution)/shard_map/ppermute | solution.py:178
  560.5 16.0 collective-permute-done.11
  581.5 19.2 collective-permute-done.12
  610.6 24.5 %collective-permute-done.15 = bf16[304,2048]{1,0:T(8,128)(2,1)} collective-permute-done((bf16[304,2048]{1,0:T(8,128)(2,1)}, bf16[304,2048]{1,0:T(8,128)(2,1)}, u32[]{:S(2)}, u32[]{:S(2)}) %collective-permute-start.15) | collective-permute-done | bytes 1245216 | tf_op jit(solution)/shard_map/ppermute | solution.py:178
  662.4 27.5 %fusion.60 = f32[1216,2,2048]{2,0,1:T(8,128)} fusion(bf16[2048,2,2048]{2,0,1:T(8,128)(2,1)} %all-gather.18.cloned.1.call-done, bf16[1216,2048]{1,0:T(8,128)(2,1)} %copy-done.54), kind=kOutput, calls=%fused_computation.105 | convolution fusion | flops 20401094656 | bytes 41680896 | tf_op jit(solution)/shard_map/rd,dcf->rcf/dot_general | solution.py:313
  693.0 25.6 %fusion.62 = (bf16[1216,1,2048]{2,0,1:T(8,128)(2,1)}, bf16[1216,1,2048]{2,0,1:T(8,128)(2,1)}, bf16[1216,2048]{1,0:T(8,128)(2,1)}) fusion(f32[1216,2,2048]{2,0,1:T(8,128)} %fusion.60, bf16[1216,2048]{1,0:T(8,128)(2,1)} %constant_dynamic-update-slice_fusion.7, bf16[2048,2048]{1,0:T(8,128)(2,1)} %all-gather.20.cloned.1.call-done), kind=kOutput, calls=%fused_computation.107 | convolution fusion | flops 10237902848 | bytes 48234496 | tf_op jit(solution)/shard_map/dot_general | solution.py:162
  720.6 14.9 fusion.231
  735.6 13.3 collective-permute-done.21
  754.2 16.7 collective-permute-done.23
  776.1 20.1 collective-permute-done.24
  803.1 27.3 %fusion.57 = f32[1216,2,2048]{2,0,1:T(8,128)} fusion(bf16[2048,2,2048]{2,0,1:T(8,128)(2,1)} %all-gather.18.cloned.1.call-done, bf16[1216,2048]{1,0:T(8,128)(2,1)} %constant_dynamic-update-slice_fusion.14), kind=kOutput, calls=%fused_computation.102 | convolution fusion | flops 20401094656 | bytes 41680896 | tf_op jit(solution)/shard_map/rd,dcf->rcf/dot_general | solution.py:313
  833.1 25.8 %fusion.63 = (bf16[1216,1,2048]{2,0,1:T(8,128)(2,1)}, bf16[1216,1,2048]{2,0,1:T(8,128)(2,1)}, bf16[1216,2048]{1,0:T(8,128)(2,1)}) fusion(f32[1216,2,2048]{2,0,1:T(8,128)} %fusion.57, bf16[1216,2048]{1,0:T(8,128)(2,1)} %copy-done.53, bf16[2048,2048]{1,0:T(8,128)(2,1)} %all-gather.20.cloned.1.call-done), kind=kOutput, calls=%fused_computation.108 | convolution fusion | flops 10237902848 | bytes 48234496 | tf_op jit(solution)/shard_map/dot_general | solution.py:162
  865.2 13.4 fusion.232
  891.9 24.9 %collective-permute-done.30 = bf16[304,2048]{1,0:T(8,128)(2,1)S(1)} collective-permute-done((bf16[304,2048]{1,0:T(8,128)(2,1)S(1)}, bf16[304,2048]{1,0:T(8,128)(2,1)S(1)}, u32[]{:S(2)}, u32[]{:S(2)}) %collective-permute-start.30) | collective-permute-done | bytes 1245216 | tf_op jit(solution)/shard_map/ppermute | solution.py:201
  921.7 25.0 %collective-permute-done.31 = bf16[304,2048]{1,0:T(8,128)(2,1)S(1)} collective-permute-done((bf16[304,2048]{1,0:T(8,128)(2,1)S(1)}, bf16[304,2048]{1,0:T(8,128)(2,1)S(1)}, u32[]{:S(2)}, u32[]{:S(2)}) %collective-permute-start.31) | collective-permute-done | bytes 1245216 | tf_op jit(solution)/shard_map/ppermute | solution.py:201
  955.2 28.8 %convolution_bitcast_fusion.1 = f32[1216,2048]{1,0:T(8,128)} fusion(bf16[2048,2,2048]{2,0,1:T(8,128)(2,1)} %all-gather.18.cloned.1.call-done, bf16[1216,1,2048]{2,0,1:T(8,128)(2,1)} %get-tuple-element.340, bf16[1216,1,2048]{2,0,1:T(8,128)(2,1)} %get-tuple-element.339), kind=kOutput, calls=%fused_computation.81 | convolution fusion | flops 20406075392 | bytes 36700160 | tf_op jit(solution)/shard_map/rcf,dcf->rd/dot_general | solution.py:338
  995.7 15.9 collective-permute-start.36
  1012.4 16.8 collective-permute-done.36
  1034.3 18.4 collective-permute-done.37
  1065.6 28.4 %convolution_bitcast_fusion = f32[1216,2048]{1,0:T(8,128)} fusion(bf16[2048,2,2048]{2,0,1:T(8,128)(2,1)} %all-gather.18.cloned.1.call-done, bf16[1216,1,2048]{2,0,1:T(8,128)(2,1)} %get-tuple-element.338, bf16[1216,1,2048]{2,0,1:T(8,128)(2,1)} %get-tuple-element.337), kind=kOutput, calls=%fused_computation.80 | convolution fusion | flops 20406075392 | bytes 36700160 | tf_op jit(solution)/shard_map/rcf,dcf->rd/dot_general | solution.py:338
  1101.3 13.6 collective-permute-start.42
  1114.9 27.8 %fusion.43 = f32[2048,2,2048]{2,0,1:T(8,128)} fusion(bf16[1216,1,2048]{2,0,1:T(8,128)(2,1)} %get-tuple-element.340, bf16[1216,1,2048]{2,0,1:T(8,128)(2,1)} %get-tuple-element.339, bf16[1216,2048]{1,0:T(8,128)(2,1)S(1)} %bitcast.733), kind=kOutput, calls=%fused_computation.86 | convolution fusion | flops 20421017600 | bytes 48496640 | tf_op jit(solution)/shard_map/rd,rcf->dcf/dot_general | solution.py:333
  1145.5 17.8 fusion.233
  1166.2 29.3 %fusion.42 = f32[2048,2,2048]{2,0,1:T(8,128)} fusion(bf16[1216,1,2048]{2,0,1:T(8,128)(2,1)} %get-tuple-element.338, bf16[1216,1,2048]{2,0,1:T(8,128)(2,1)} %get-tuple-element.337, bf16[1216,2048]{1,0:T(8,128)(2,1)} %constant_dynamic-update-slice_fusion.14), kind=kOutput, calls=%fused_computation.85 | convolution fusion | flops 20421017600 | bytes 48496640 | tf_op jit(solution)/shard_map/rd,rcf->dcf/dot_general | solution.py:333
  1201.7 16.4 fusion.235
  1255.7 27.5 %add_convert_fusion = bf16[2048,2,2048]{2,0,1:T(8,128)(2,1)} fusion(f32[2048,2,2048]{2,0,1:T(8,128)} %fusion.43, f32[2048,2,2048]{2,0,1:T(8,128)} %fusion.42), kind=kLoop, calls=%fused_computation | loop fusion | flops 16777216 | bytes 83886080 | tf_op jit(solution)/shard_map/convert_element_type | solution.py:432
  1283.2 22.5 %copy.312 = bf16[2048,2,2048]{0,2,1:T(8,128)(2,1)} copy(bf16[2048,2,2048]{2,0,1:T(8,128)(2,1)} %add_convert_fusion) | data formatting | bytes 33554432 | tf_op jit(solution)/shard_map/convert_element_type | solution.py:432
  1315.3 9.0 fusion.165
  1324.2 11.5 fusion.16
  1341.8 18.5 fusion
  1360.2 12.7 fusion.121
  1373.0 10.4 fusion.18
  1386.2 17.6 fusion.2
  1427.2 11.6 fusion.19
  1448.3 16.9 fusion.3
  1465.3 17.1 fusion.5
  1495.2 11.0 fusion.124
  1523.1 9.8 fusion.174
  1532.9 10.3 add_convert_fusion.2
  1571.7 10.4 add_convert_fusion.3
  1600.4 18.9 psum.14
  1620.4 15.5 add_convert_fusion.1
  1652.8 55.5 %reduce-scatter.16.cloned.1.call-done = bf16[256,2048]{1,0:T(8,128)(2,1)} async-done(((bf16[2048,2048]{1,0:T(8,128)(2,1)}), bf16[256,2048]{1,0:T(8,128)(2,1)}) %reduce-scatter.16.cloned.1.call-update) | async-done | bytes 1048592 | tf_op jit(solution)/shard_map/reduce_scatter | solution.py:451
  1714.5 31.6 %reduce-scatter.28.cloned.1.call-done = bf16[256,2]{1,0:T(8,128)(2,1)} async-done(((bf16[2048,2]{1,0:T(8,128)(2,1)}), bf16[256,2]{1,0:T(8,128)(2,1)}) %reduce-scatter.28.cloned.1.call-update) | async-done | bytes 1040
  1747.8 73.0 %reduce-scatter.14.cloned.1.call-done = bf16[2048,256]{1,0:T(8,128)(2,1)} async-done(((bf16[2048,2048]{1,0:T(8,128)(2,1)}), bf16[2048,256]{1,0:T(8,128)(2,1)}) %reduce-scatter.14.cloned.1.call-update) | async-done | bytes 1048592 | tf_op jit(solution)/shard_map/reduce_scatter | solution.py:437
  1831.5 64.1 %reduce-scatter.24.cloned.1.call-done = bf16[2048,256]{1,0:T(8,128)(2,1)} async-done(((bf16[2048,2048]{1,0:T(8,128)(2,1)}), bf16[2048,256]{1,0:T(8,128)(2,1)}) %reduce-scatter.24.cloned.1.call-update) | async-done | bytes 1048592 | tf_op jit(solution)/shard_map/reduce_scatter | solution.py:465
  1895.6 18.2 multiply_reduce_fusion
  1922.7 24.6 %reduce-scatter.18.cloned.1.call-done = bf16[256,512]{1,0:T(8,128)(2,1)} async-done(((bf16[256,2048]{1,0:T(8,128)(2,1)}), bf16[256,512]{1,0:T(8,128)(2,1)}) %reduce-scatter.18.cloned.1.call-update) | async-done | bytes 262160 | tf_op jit(solution)/shard_map/reduce_scatter | solution.py:450
  1950.3 25.0 %reduce-scatter.26.cloned.1.call-done = bf16[512,256]{1,0:T(8,128)(2,1)} async-done(((bf16[2048,256]{1,0:T(8,128)(2,1)}), bf16[512,256]{1,0:T(8,128)(2,1)}) %reduce-scatter.26.cloned.1.call-update) | async-done | bytes 262160 | tf_op jit(solution)/shard_map/reduce_scatter | solution.py:464
  1986.3 38.8 %psum.15 = f32[2,7]{1,0:T(2,128)S(1)} all-reduce(f32[2,7]{1,0:T(2,128)S(1)} %pad_maximum_fusion.22), channel_id=1, replica_groups=mesh['dp'=8,'tensor'=4] {'dp','tensor'}, use_global_device_ids=true, to_apply=%region_52.53 | all-reduce | flops 14 | bytes 112 | tf_op jit(solution)/shard_map/psum | solution.py:499
  (662 shorter events, 625.8 us)
Async XLA Ops:
  7.2 38.5 %all-gather.8.cloned.1.call-start = ((), (), s32[]{:S(2)}) async-start(), calls=%async_computation.17 | async-start | bytes 1310720 | tf_op jit(solution)/shard_map/all_gather | solution.py:245
  9.9 66.6 %all-gather.14.cloned.1.call-start = ((), (), s32[]{:S(2)}) async-start(), calls=%async_computation.20 | async-start | bytes 1310720 | tf_op jit(solution)/shard_map/all_gather | solution.py:251
  12.5 101.8 %all-gather.12.cloned.1.call-start = ((), (), s32[]{:S(2)}) async-start(), calls=%async_computation.19 | async-start | bytes 4718592 | tf_op jit(solution)/shard_map/all_gather | solution.py:247
  38.0 132.4 %all-gather.10.cloned.1.call-start = ((), (), s32[]{:S(2)}) async-start(), calls=%async_computation.18 | async-start | bytes 9437184 | tf_op jit(solution)/shard_map/all_gather | solution.py:244
  45.8 319.7 %all-gather.16.cloned.1.call-start = ((), (), s32[]{:S(2)}) async-start(), calls=%async_computation.21 | async-start | bytes 9437184 | tf_op jit(solution)/shard_map/all_gather | solution.py:250
  76.5 585.9 %all-gather.18.cloned.1.call-start = ((), (), s32[]{:S(2)}) async-start(), calls=%async_computation.22 | async-start | bytes 18874368 | tf_op jit(solution)/shard_map/all_gather | solution.py:253
  196.8 48.8 %all-to-all-start = ((bf16[304,4,768]{2,0,1:T(8,128)(2,1)}), bf16[304,4,768]{2,0,1:T(8,128)(2,1)}, u32[]{:S(2)}, u32[]{:S(2)}) async-start(bf16[304,4,768]{2,0,1:T(8,128)(2,1)} %pad_maximum_fusion.10), calls=%async_computation | async-start | bytes 3735552 | tf_op jit(solution)/shard_map/all_to_all | solution.py:414
  245.6 55.6 %all-to-all-start.2 = ((bf16[304,4,768]{2,0,1:T(8,128)(2,1)}), bf16[304,4,768]{2,0,1:T(8,128)(2,1)}, u32[]{:S(2)}, u32[]{:S(2)}) async-start(bf16[304,4,768]{2,0,1:T(8,128)(2,1)} %pad_maximum_fusion.11), calls=%async_computation.2 | async-start | bytes 3735552 | tf_op jit(solution)/shard_map/all_to_all | solution.py:414
  301.2 56.5 %all-to-all-start.1 = ((bf16[4,304,512]{2,1,0:T(8,128)(2,1)}), bf16[4,304,512]{2,1,0:T(8,128)(2,1)}, u32[]{:S(2)}, u32[]{:S(2)}) async-start(bf16[4,304,512]{2,1,0:T(8,128)(2,1)} %bitcast.33), calls=%async_computation.1 | async-start | bytes 2490368 | tf_op jit(solution)/shard_map/all_to_all | solution.py:416
  360.3 33.8 %all-to-all-start.3 = ((bf16[4,304,512]{2,1,0:T(8,128)(2,1)}), bf16[4,304,512]{2,1,0:T(8,128)(2,1)}, u32[]{:S(2)}, u32[]{:S(2)}) async-start(bf16[4,304,512]{2,1,0:T(8,128)(2,1)} %bitcast.735), calls=%async_computation.3 | async-start | bytes 2490368 | tf_op jit(solution)/shard_map/all_to_all | solution.py:416
  365.5 327.5 %all-gather.20.cloned.1.call-start = ((), (), s32[]{:S(2)}) async-start(), calls=%async_computation.23 | async-start | bytes 9437184 | tf_op jit(solution)/shard_map/all_gather | solution.py:254
  403.2 27.6 %collective-permute-start = (bf16[304,2048]{1,0:T(8,128)(2,1)S(1)}, bf16[304,2048]{1,0:T(8,128)(2,1)S(1)}, u32[]{:S(2)}, u32[]{:S(2)}) collective-permute-start(bf16[304,2048]{1,0:T(8,128)(2,1)S(1)} %get-tuple-element.169), channel_id=1, source_target_pairs={{0,1},{1,2},{2,3},{4,5},{5,6},{6,7},{8,9},{9,10},{10,11},{12,13},{... | collective-permute-start | bytes 3735560 | tf_op jit(solution)/shard_map/ppermute | solution.py:175
  404.7 30.4 %collective-permute-start.1 = (bf16[304,2048]{1,0:T(8,128)(2,1)S(1)}, bf16[304,2048]{1,0:T(8,128)(2,1)}, u32[]{:S(2)}, u32[]{:S(2)}) collective-permute-start(bf16[304,2048]{1,0:T(8,128)(2,1)S(1)} %get-tuple-element.169), channel_id=1, source_target_pairs={{1,0},{2,1},{3,2},{5,4},{6,5},{7,6},{9,8},{10,9},{11,10},{13,12},{... | collective-permute-start | bytes 3735560 | tf_op jit(solution)/shard_map/ppermute | solution.py:178
  435.1 29.7 %collective-permute-start.3 = (bf16[304,2048]{1,0:T(8,128)(2,1)}, bf16[304,2048]{1,0:T(8,128)(2,1)}, u32[]{:S(2)}, u32[]{:S(2)}) collective-permute-start(bf16[304,2048]{1,0:T(8,128)(2,1)} %collective-permute-done.1), channel_id=1, source_target_pairs={{1,0},{2,1},{5,4},{6,5},{9,8},{10,9},{13,12},{14,13},{17,16},{18,1... | collective-permute-start | bytes 3735560 | tf_op jit(solution)/shard_map/ppermute | solution.py:178
  436.4 34.9 %collective-permute-start.4 = (bf16[304,2048]{1,0:T(8,128)(2,1)}, bf16[304,2048]{1,0:T(8,128)(2,1)}, u32[]{:S(2)}, u32[]{:S(2)}) collective-permute-start(bf16[304,2048]{1,0:T(8,128)(2,1)} %collective-permute-done.2), channel_id=1, source_target_pairs={{2,3},{6,7},{10,11},{14,15},{18,19},{22,23},{26,27},{30,31}} | collective-permute-start | bytes 3735560 | tf_op jit(solution)/shard_map/ppermute | solution.py:175
  464.9 28.8 %collective-permute-start.5 = (bf16[304,2048]{1,0:T(8,128)(2,1)}, bf16[304,2048]{1,0:T(8,128)(2,1)S(1)}, u32[]{:S(2)}, u32[]{:S(2)}) collective-permute-start(bf16[304,2048]{1,0:T(8,128)(2,1)} %collective-permute-done.3), channel_id=1, source_target_pairs={{1,0},{5,4},{9,8},{13,12},{17,16},{21,20},{25,24},{29,28}} | collective-permute-start | bytes 3735560 | tf_op jit(solution)/shard_map/ppermute | solution.py:178
  494.0 24.9 %collective-permute-start.6 = (bf16[304,2048]{1,0:T(8,128)(2,1)S(1)}, bf16[304,2048]{1,0:T(8,128)(2,1)S(1)}, u32[]{:S(2)}, u32[]{:S(2)}) collective-permute-start(bf16[304,2048]{1,0:T(8,128)(2,1)S(1)} %get-tuple-element.170), channel_id=1, source_target_pairs={{0,1},{1,2},{2,3},{4,5},{5,6},{6,7},{8,9},{9,10},{10,11},{12,13},{... | collective-permute-start | bytes 3735560 | tf_op jit(solution)/shard_map/ppermute | solution.py:175
  495.6 27.6 %collective-permute-start.7 = (bf16[304,2048]{1,0:T(8,128)(2,1)S(1)}, bf16[304,2048]{1,0:T(8,128)(2,1)S(1)}, u32[]{:S(2)}, u32[]{:S(2)}) collective-permute-start(bf16[304,2048]{1,0:T(8,128)(2,1)S(1)} %get-tuple-element.170), channel_id=1, source_target_pairs={{1,0},{2,1},{3,2},{5,4},{6,5},{7,6},{9,8},{10,9},{11,10},{13,12},{... | collective-permute-start | bytes 3735560 | tf_op jit(solution)/shard_map/ppermute | solution.py:178
  523.1 27.5 %collective-permute-start.9 = (bf16[304,2048]{1,0:T(8,128)(2,1)S(1)}, bf16[304,2048]{1,0:T(8,128)(2,1)S(1)}, u32[]{:S(2)}, u32[]{:S(2)}) collective-permute-start(bf16[304,2048]{1,0:T(8,128)(2,1)S(1)} %collective-permute-done.7), channel_id=1, source_target_pairs={{1,0},{2,1},{5,4},{6,5},{9,8},{10,9},{13,12},{14,13},{17,16},{18,1... | collective-permute-start | bytes 3735560 | tf_op jit(solution)/shard_map/ppermute | solution.py:178
  524.4 34.9 %collective-permute-start.10 = (bf16[304,2048]{1,0:T(8,128)(2,1)S(1)}, bf16[304,2048]{1,0:T(8,128)(2,1)S(1)}, u32[]{:S(2)}, u32[]{:S(2)}) collective-permute-start(bf16[304,2048]{1,0:T(8,128)(2,1)S(1)} %collective-permute-done.8), channel_id=1, source_target_pairs={{2,3},{6,7},{10,11},{14,15},{18,19},{22,23},{26,27},{30,31}} | collective-permute-start | bytes 3735560 | tf_op jit(solution)/shard_map/ppermute | solution.py:175
  550.7 25.7 %collective-permute-start.11 = (bf16[304,2048]{1,0:T(8,128)(2,1)S(1)}, bf16[304,2048]{1,0:T(8,128)(2,1)S(1)}, u32[]{:S(2)}, u32[]{:S(2)}) collective-permute-start(bf16[304,2048]{1,0:T(8,128)(2,1)S(1)} %collective-permute-done.9), channel_id=1, source_target_pairs={{1,0},{5,4},{9,8},{13,12},{17,16},{21,20},{25,24},{29,28}} | collective-permute-start | bytes 3735560 | tf_op jit(solution)/shard_map/ppermute | solution.py:178
  578.6 22.1 %collective-permute-start.12 = (bf16[304,2048]{1,0:T(8,128)(2,1)S(1)}, bf16[304,2048]{1,0:T(8,128)(2,1)S(1)}, u32[]{:S(2)}, u32[]{:S(2)}) collective-permute-start(bf16[304,2048]{1,0:T(8,128)(2,1)S(1)} %get-tuple-element.171), channel_id=1, source_target_pairs={{0,1},{1,2},{2,3},{4,5},{5,6},{6,7},{8,9},{9,10},{10,11},{12,13},{... | collective-permute-start | bytes 3735560 | tf_op jit(solution)/shard_map/ppermute | solution.py:175
  580.2 27.3 %collective-permute-start.13 = (bf16[304,2048]{1,0:T(8,128)(2,1)S(1)}, bf16[304,2048]{1,0:T(8,128)(2,1)}, u32[]{:S(2)}, u32[]{:S(2)}) collective-permute-start(bf16[304,2048]{1,0:T(8,128)(2,1)S(1)} %get-tuple-element.171), channel_id=1, source_target_pairs={{1,0},{2,1},{3,2},{5,4},{6,5},{7,6},{9,8},{10,9},{11,10},{13,12},{... | collective-permute-start | bytes 3735560 | tf_op jit(solution)/shard_map/ppermute | solution.py:178
  607.5 27.5 %collective-permute-start.15 = (bf16[304,2048]{1,0:T(8,128)(2,1)}, bf16[304,2048]{1,0:T(8,128)(2,1)}, u32[]{:S(2)}, u32[]{:S(2)}) collective-permute-start(bf16[304,2048]{1,0:T(8,128)(2,1)} %collective-permute-done.13), channel_id=1, source_target_pairs={{1,0},{2,1},{5,4},{6,5},{9,8},{10,9},{13,12},{14,13},{17,16},{18,1... | collective-permute-start | bytes 3735560 | tf_op jit(solution)/shard_map/ppermute | solution.py:178
  608.8 39.0 %collective-permute-start.16 = (bf16[304,2048]{1,0:T(8,128)(2,1)}, bf16[304,2048]{1,0:T(8,128)(2,1)}, u32[]{:S(2)}, u32[]{:S(2)}) collective-permute-start(bf16[304,2048]{1,0:T(8,128)(2,1)} %collective-permute-done.14), channel_id=1, source_target_pairs={{2,3},{6,7},{10,11},{14,15},{18,19},{22,23},{26,27},{30,31}} | collective-permute-start | bytes 3735560 | tf_op jit(solution)/shard_map/ppermute | solution.py:175
  635.1 23.2 %collective-permute-start.17 = (bf16[304,2048]{1,0:T(8,128)(2,1)}, bf16[304,2048]{1,0:T(8,128)(2,1)S(1)}, u32[]{:S(2)}, u32[]{:S(2)}) collective-permute-start(bf16[304,2048]{1,0:T(8,128)(2,1)} %collective-permute-done.15), channel_id=1, source_target_pairs={{1,0},{5,4},{9,8},{13,12},{17,16},{21,20},{25,24},{29,28}} | collective-permute-start | bytes 3735560 | tf_op jit(solution)/shard_map/ppermute | solution.py:178
  660.6 30.6 %collective-permute-start.18 = (bf16[304,2048]{1,0:T(8,128)(2,1)S(1)}, bf16[304,2048]{1,0:T(8,128)(2,1)S(1)}, u32[]{:S(2)}, u32[]{:S(2)}) collective-permute-start(bf16[304,2048]{1,0:T(8,128)(2,1)S(1)} %get-tuple-element.172), channel_id=1, source_target_pairs={{0,1},{1,2},{2,3},{4,5},{5,6},{6,7},{8,9},{9,10},{10,11},{12,13},{... | collective-permute-start | bytes 3735560 | tf_op jit(solution)/shard_map/ppermute | solution.py:175
  689.9 28.7 %collective-permute-start.19 = (bf16[304,2048]{1,0:T(8,128)(2,1)S(1)}, bf16[304,2048]{1,0:T(8,128)(2,1)}, u32[]{:S(2)}, u32[]{:S(2)}) collective-permute-start(bf16[304,2048]{1,0:T(8,128)(2,1)S(1)} %get-tuple-element.172), channel_id=1, source_target_pairs={{1,0},{2,1},{3,2},{5,4},{6,5},{7,6},{9,8},{10,9},{11,10},{13,12},{... | collective-permute-start | bytes 3735560 | tf_op jit(solution)/shard_map/ppermute | solution.py:178
  691.2 28.7 %collective-permute-start.20 = (bf16[304,2048]{1,0:T(8,128)(2,1)S(1)}, bf16[304,2048]{1,0:T(8,128)(2,1)}, u32[]{:S(2)}, u32[]{:S(2)}) collective-permute-start(bf16[304,2048]{1,0:T(8,128)(2,1)S(1)} %collective-permute-done.18), channel_id=1, source_target_pairs={{1,2},{2,3},{5,6},{6,7},{9,10},{10,11},{13,14},{14,15},{17,18},{18... | collective-permute-start | bytes 3735560 | tf_op jit(solution)/shard_map/ppermute | solution.py:175
  718.6 30.3 %collective-permute-start.21 = (bf16[304,2048]{1,0:T(8,128)(2,1)}, bf16[304,2048]{1,0:T(8,128)(2,1)S(1)}, u32[]{:S(2)}, u32[]{:S(2)}) collective-permute-start(bf16[304,2048]{1,0:T(8,128)(2,1)} %collective-permute-done.19), channel_id=1, source_target_pairs={{1,0},{2,1},{5,4},{6,5},{9,8},{10,9},{13,12},{14,13},{17,16},{18,1... | collective-permute-start | bytes 3735560 | tf_op jit(solution)/shard_map/ppermute | solution.py:178
  719.9 34.1 %collective-permute-start.22 = (bf16[304,2048]{1,0:T(8,128)(2,1)}, bf16[304,2048]{1,0:T(8,128)(2,1)S(1)}, u32[]{:S(2)}, u32[]{:S(2)}) collective-permute-start(bf16[304,2048]{1,0:T(8,128)(2,1)} %collective-permute-done.20), channel_id=1, source_target_pairs={{2,3},{6,7},{10,11},{14,15},{18,19},{22,23},{26,27},{30,31}} | collective-permute-start | bytes 3735560 | tf_op jit(solution)/shard_map/ppermute | solution.py:175
  748.9 22.0 %collective-permute-start.23 = (bf16[304,2048]{1,0:T(8,128)(2,1)S(1)}, bf16[304,2048]{1,0:T(8,128)(2,1)S(1)}, u32[]{:S(2)}, u32[]{:S(2)}) collective-permute-start(bf16[304,2048]{1,0:T(8,128)(2,1)S(1)} %collective-permute-done.21), channel_id=1, source_target_pairs={{1,0},{5,4},{9,8},{13,12},{17,16},{21,20},{25,24},{29,28}} | collective-permute-start | bytes 3735560 | tf_op jit(solution)/shard_map/ppermute | solution.py:178
  773.8 22.4 %collective-permute-start.24 = (bf16[304,2048]{1,0:T(8,128)(2,1)}, bf16[304,2048]{1,0:T(8,128)(2,1)S(1)}, u32[]{:S(2)}, u32[]{:S(2)}) collective-permute-start(bf16[304,2048]{1,0:T(8,128)(2,1)} %get-tuple-element.357), channel_id=1, source_target_pairs={{0,1},{4,5},{8,9},{12,13},{16,17},{20,21},{24,25},{28,29}} | collective-permute-start | bytes 3735560 | tf_op jit(solution)/shard_map/ppermute | solution.py:201
  775.4 55.0 %collective-permute-start.27 = (bf16[304,2048]{1,0:T(8,128)(2,1)S(1)}, bf16[304,2048]{1,0:T(8,128)(2,1)S(1)}, u32[]{:S(2)}, u32[]{:S(2)}) collective-permute-start(bf16[304,2048]{1,0:T(8,128)(2,1)S(1)} %get-tuple-element.358), channel_id=1, source_target_pairs={{3,2},{7,6},{11,10},{15,14},{19,18},{23,22},{27,26},{31,30}} | collective-permute-start | bytes 3735560 | tf_op jit(solution)/shard_map/ppermute | solution.py:207
  798.5 31.9 %collective-permute-start.25 = (bf16[304,2048]{1,0:T(8,128)(2,1)S(1)}, bf16[304,2048]{1,0:T(8,128)(2,1)S(1)}, u32[]{:S(2)}, u32[]{:S(2)}) collective-permute-start(bf16[304,2048]{1,0:T(8,128)(2,1)S(1)} %add_convert_fusion.22), channel_id=1, source_target_pairs={{0,1},{1,2},{4,5},{5,6},{8,9},{9,10},{12,13},{13,14},{16,17},{17,1... | collective-permute-start | bytes 3735560 | tf_op jit(solution)/shard_map/ppermute | solution.py:201
  832.4 29.4 %collective-permute-start.28 = (bf16[304,2048]{1,0:T(8,128)(2,1)}, bf16[304,2048]{1,0:T(8,128)(2,1)S(1)}, u32[]{:S(2)}, u32[]{:S(2)}) collective-permute-start(bf16[304,2048]{1,0:T(8,128)(2,1)} %get-tuple-element.356), channel_id=1, source_target_pairs={{2,1},{3,2},{6,5},{7,6},{10,9},{11,10},{14,13},{15,14},{18,17},{19... | collective-permute-start | bytes 3735560 | tf_op jit(solution)/shard_map/ppermute | solution.py:207
  858.9 19.6 collective-permute-start.26
  887.2 29.7 %collective-permute-start.30 = (bf16[304,2048]{1,0:T(8,128)(2,1)S(1)}, bf16[304,2048]{1,0:T(8,128)(2,1)S(1)}, u32[]{:S(2)}, u32[]{:S(2)}) collective-permute-start(bf16[304,2048]{1,0:T(8,128)(2,1)S(1)} %get-tuple-element.353), channel_id=1, source_target_pairs={{0,1},{4,5},{8,9},{12,13},{16,17},{20,21},{24,25},{28,29}} | collective-permute-start | bytes 3735560 | tf_op jit(solution)/shard_map/ppermute | solution.py:201
  891.2 30.5 %collective-permute-start.33 = (bf16[304,2048]{1,0:T(8,128)(2,1)S(1)}, bf16[304,2048]{1,0:T(8,128)(2,1)S(1)}, u32[]{:S(2)}, u32[]{:S(2)}) collective-permute-start(bf16[304,2048]{1,0:T(8,128)(2,1)S(1)} %get-tuple-element.354), channel_id=1, source_target_pairs={{3,2},{7,6},{11,10},{15,14},{19,18},{23,22},{27,26},{31,30}} | collective-permute-start | bytes 3735560 | tf_op jit(solution)/shard_map/ppermute | solution.py:207
  917.3 29.5 %collective-permute-start.31 = (bf16[304,2048]{1,0:T(8,128)(2,1)S(1)}, bf16[304,2048]{1,0:T(8,128)(2,1)S(1)}, u32[]{:S(2)}, u32[]{:S(2)}) collective-permute-start(bf16[304,2048]{1,0:T(8,128)(2,1)S(1)} %add_convert_fusion.17), channel_id=1, source_target_pairs={{0,1},{1,2},{4,5},{5,6},{8,9},{9,10},{12,13},{13,14},{16,17},{17,1... | collective-permute-start | bytes 3735560 | tf_op jit(solution)/shard_map/ppermute | solution.py:201
  948.4 35.6 %collective-permute-start.32 = (bf16[304,2048]{1,0:T(8,128)(2,1)S(1)}, bf16[304,2048]{1,0:T(8,128)(2,1)S(1)}, u32[]{:S(2)}, u32[]{:S(2)}) collective-permute-start(bf16[304,2048]{1,0:T(8,128)(2,1)S(1)} %get-tuple-element.351), channel_id=1, source_target_pairs={{0,1},{1,2},{2,3},{4,5},{5,6},{6,7},{8,9},{9,10},{10,11},{12,13},{... | collective-permute-start | bytes 3735560 | tf_op jit(solution)/shard_map/ppermute | solution.py:201
  953.9 35.0 %collective-permute-start.35 = (bf16[304,2048]{1,0:T(8,128)(2,1)S(1)}, bf16[304,2048]{1,0:T(8,128)(2,1)S(1)}, u32[]{:S(2)}, u32[]{:S(2)}) collective-permute-start(bf16[304,2048]{1,0:T(8,128)(2,1)S(1)} %add_convert_fusion.14), channel_id=1, source_target_pairs={{1,0},{2,1},{3,2},{5,4},{6,5},{7,6},{9,8},{10,9},{11,10},{13,12},{... | collective-permute-start | bytes 3735560 | tf_op jit(solution)/shard_map/ppermute | solution.py:207
  995.7 33.4 %collective-permute-start.36 = (bf16[304,2048]{1,0:T(8,128)(2,1)S(1)}, bf16[304,2048]{1,0:T(8,128)(2,1)S(1)}, u32[]{:S(2)}, u32[]{:S(2)}) collective-permute-start(bf16[304,2048]{1,0:T(8,128)(2,1)S(1)} %get-tuple-element.349), channel_id=1, source_target_pairs={{0,1},{4,5},{8,9},{12,13},{16,17},{20,21},{24,25},{28,29}} | collective-permute-start | bytes 3735560 | tf_op jit(solution)/shard_map/ppermute | solution.py:201
  1011.6 22.6 %collective-permute-start.39 = (bf16[304,2048]{1,0:T(8,128)(2,1)S(1)}, bf16[304,2048]{1,0:T(8,128)(2,1)S(1)}, u32[]{:S(2)}, u32[]{:S(2)}) collective-permute-start(bf16[304,2048]{1,0:T(8,128)(2,1)S(1)} %get-tuple-element.350), channel_id=1, source_target_pairs={{3,2},{7,6},{11,10},{15,14},{19,18},{23,22},{27,26},{31,30}} | collective-permute-start | bytes 3735560 | tf_op jit(solution)/shard_map/ppermute | solution.py:207
  1029.6 23.0 %collective-permute-start.37 = (bf16[304,2048]{1,0:T(8,128)(2,1)S(1)}, bf16[304,2048]{1,0:T(8,128)(2,1)S(1)}, u32[]{:S(2)}, u32[]{:S(2)}) collective-permute-start(bf16[304,2048]{1,0:T(8,128)(2,1)S(1)} %add_convert_fusion.12), channel_id=1, source_target_pairs={{0,1},{1,2},{4,5},{5,6},{8,9},{9,10},{12,13},{13,14},{16,17},{17,1... | collective-permute-start | bytes 3735560 | tf_op jit(solution)/shard_map/ppermute | solution.py:201
  1058.9 35.1 %collective-permute-start.38 = (bf16[304,2048]{1,0:T(8,128)(2,1)S(1)}, bf16[304,2048]{1,0:T(8,128)(2,1)S(1)}, u32[]{:S(2)}, u32[]{:S(2)}) collective-permute-start(bf16[304,2048]{1,0:T(8,128)(2,1)S(1)} %get-tuple-element.347), channel_id=1, source_target_pairs={{0,1},{1,2},{2,3},{4,5},{5,6},{6,7},{8,9},{9,10},{10,11},{12,13},{... | collective-permute-start | bytes 3735560 | tf_op jit(solution)/shard_map/ppermute | solution.py:201
  1064.3 29.7 %collective-permute-start.41 = (bf16[304,2048]{1,0:T(8,128)(2,1)S(1)}, bf16[304,2048]{1,0:T(8,128)(2,1)}, u32[]{:S(2)}, u32[]{:S(2)}) collective-permute-start(bf16[304,2048]{1,0:T(8,128)(2,1)S(1)} %add_convert_fusion.9), channel_id=1, source_target_pairs={{1,0},{2,1},{3,2},{5,4},{6,5},{7,6},{9,8},{10,9},{11,10},{13,12},{... | collective-permute-start | bytes 3735560 | tf_op jit(solution)/shard_map/ppermute | solution.py:207
  1101.3 42.5 %collective-permute-start.42 = (bf16[304,2048]{1,0:T(8,128)(2,1)}, bf16[304,2048]{1,0:T(8,128)(2,1)S(1)}, u32[]{:S(2)}, u32[]{:S(2)}) collective-permute-start(bf16[304,2048]{1,0:T(8,128)(2,1)} %get-tuple-element.345), channel_id=1, source_target_pairs={{0,1},{4,5},{8,9},{12,13},{16,17},{20,21},{24,25},{28,29}} | collective-permute-start | bytes 3735560 | tf_op jit(solution)/shard_map/ppermute | solution.py:201
  1142.6 20.7 %collective-permute-start.45 = (bf16[304,2048]{1,0:T(8,128)(2,1)S(1)}, bf16[304,2048]{1,0:T(8,128)(2,1)S(1)}, u32[]{:S(2)}, u32[]{:S(2)}) collective-permute-start(bf16[304,2048]{1,0:T(8,128)(2,1)S(1)} %get-tuple-element.346), channel_id=1, source_target_pairs={{3,2},{7,6},{11,10},{15,14},{19,18},{23,22},{27,26},{31,30}} | collective-permute-start | bytes 3735560 | tf_op jit(solution)/shard_map/ppermute | solution.py:207
  1165.3 34.5 %collective-permute-start.46 = (bf16[304,2048]{1,0:T(8,128)(2,1)}, bf16[304,2048]{1,0:T(8,128)(2,1)S(1)}, u32[]{:S(2)}, u32[]{:S(2)}) collective-permute-start(bf16[304,2048]{1,0:T(8,128)(2,1)} %get-tuple-element.344), channel_id=1, source_target_pairs={{2,1},{3,2},{6,5},{7,6},{10,9},{11,10},{14,13},{15,14},{18,17},{19... | collective-permute-start | bytes 3735560 | tf_op jit(solution)/shard_map/ppermute | solution.py:207
  1195.4 22.7 %collective-permute-start.44 = (bf16[304,2048]{1,0:T(8,128)(2,1)S(1)}, bf16[304,2048]{1,0:T(8,128)(2,1)S(1)}, u32[]{:S(2)}, u32[]{:S(2)}) collective-permute-start(bf16[304,2048]{1,0:T(8,128)(2,1)S(1)} %get-tuple-element.343), channel_id=1, source_target_pairs={{0,1},{1,2},{2,3},{4,5},{5,6},{6,7},{8,9},{9,10},{10,11},{12,13},{... | collective-permute-start | bytes 3735560 | tf_op jit(solution)/shard_map/ppermute | solution.py:201
  1238.2 67.6 %all-to-all-start.6 = ((bf16[304,4,512]{2,0,1:T(8,128)(2,1)}), bf16[304,4,512]{2,0,1:T(8,128)(2,1)}, u32[]{:S(2)}, u32[]{:S(2)}) async-start(bf16[304,4,512]{2,0,1:T(8,128)(2,1)} %copy.297), calls=%async_computation.6 | async-start | bytes 2490368 | tf_op jit(solution)/shard_map/all_to_all | solution.py:414
  1243.7 338.4 %reduce-scatter.12.cloned.1.call-start = ((), (), s32[]{:S(2)}) async-start(), calls=%async_computation.24 | async-start | bytes 18874368 | tf_op jit(solution)/shard_map/reduce_scatter | solution.py:431
  1305.8 111.5 %all-to-all-start.4 = ((bf16[304,4,512]{2,0,1:T(8,128)(2,1)}), bf16[304,4,512]{2,0,1:T(8,128)(2,1)S(1)}, u32[]{:S(2)}, u32[]{:S(2)}) async-start(bf16[304,4,512]{2,0,1:T(8,128)(2,1)} %copy.284), calls=%async_computation.4 | async-start | bytes 2490368 | tf_op jit(solution)/shard_map/all_to_all | solution.py:414
  1417.3 100.5 %all-to-all-start.7 = ((bf16[4,304,768]{2,1,0:T(8,128)(2,1)}), bf16[4,304,768]{2,1,0:T(8,128)(2,1)}, u32[]{:S(2)}, u32[]{:S(2)}) async-start(bf16[4,304,768]{2,1,0:T(8,128)(2,1)} %bitcast.698), calls=%async_computation.7 | async-start | bytes 3735552 | tf_op jit(solution)/shard_map/all_to_all | solution.py:416
  1517.8 30.0 %all-to-all-start.5 = ((bf16[4,304,768]{2,1,0:T(8,128)(2,1)}), bf16[4,304,768]{2,1,0:T(8,128)(2,1)}, u32[]{:S(2)}, u32[]{:S(2)}) async-start(bf16[4,304,768]{2,1,0:T(8,128)(2,1)} %bitcast.699), calls=%async_computation.5 | async-start | bytes 3735552 | tf_op jit(solution)/shard_map/all_to_all | solution.py:416
  1523.0 113.8 %reduce-scatter.20.cloned.1.call-start = ((), (), s32[]{:S(2)}) async-start(), calls=%async_computation.28 | async-start | bytes 4718592 | tf_op jit(solution)/shard_map/reduce_scatter | solution.py:457
  1582.2 126.2 %reduce-scatter.16.cloned.1.call-start = ((), (), s32[]{:S(2)}) async-start(), calls=%async_computation.26 | async-start | bytes 9437184 | tf_op jit(solution)/shard_map/reduce_scatter | solution.py:451
  1582.7 163.4 %reduce-scatter.28.cloned.1.call-start = ((), (), s32[]{:S(2)}) async-start(), calls=%async_computation.32 | async-start | bytes 589824
  1620.3 200.4 %reduce-scatter.14.cloned.1.call-start = ((), (), s32[]{:S(2)}) async-start(), calls=%async_computation.25 | async-start | bytes 9437184 | tf_op jit(solution)/shard_map/reduce_scatter | solution.py:437
  1636.0 259.6 %reduce-scatter.24.cloned.1.call-start = ((), (), s32[]{:S(2)}) async-start(), calls=%async_computation.30 | async-start | bytes 9437184 | tf_op jit(solution)/shard_map/reduce_scatter | solution.py:465
  1636.7 282.8 %reduce-scatter.22.cloned.1.call-start = ((), (), s32[]{:S(2)}) async-start(), calls=%async_computation.29 | async-start | bytes 655360 | tf_op jit(solution)/shard_map/reduce_scatter | solution.py:456
  1637.3 310.0 %reduce-scatter.18.cloned.1.call-start = ((), (), s32[]{:S(2)}) async-start(), calls=%async_computation.27 | async-start | bytes 1310720 | tf_op jit(solution)/shard_map/reduce_scatter | solution.py:450
  1708.4 266.9 %reduce-scatter.26.cloned.1.call-start = ((), (), s32[]{:S(2)}) async-start(), calls=%async_computation.31 | async-start | bytes 1310720 | tf_op jit(solution)/shard_map/reduce_scatter | solution.py:464
  (150 other events, 2557.9 us)
Sparse Core Ops, SparseCore 0:
  10.1 35.5 all-gather.7
  47.9 28.5 all-gather.13
  78.3 35.9 all-gather.11
  116.1 54.2 all-gather.9
  172.1 55.8 all-gather.15
  230.3 89.7 all-gather.17
  440.3 80.4 all-gather.19
  1305.9 116.4 reduce-scatter.11
  1582.3 51.1 reduce-scatter.19
  1636.8 71.4 reduce-scatter.15
  1712.0 34.0 reduce-scatter.27
  1749.4 71.3 reduce-scatter.13
  1824.2 71.2 reduce-scatter.23
  1897.7 21.8 reduce-scatter.21
  1921.7 25.5 reduce-scatter.17
  1949.4 25.7 reduce-scatter.25

commit v10 on v5

--- a/solution.py
+++ b/solution.py
@@ -375,7 +375,9 @@
             if kind == "gather":
                 previous = line_gather(value, tensor_count)
             else:
-                previous = line_scatter(value, tensor_count)
+                previous = lax.psum_scatter(
+                    value.astype(jnp.bfloat16), "tensor", scatter_dimension=0, tiled=True
+                ).astype(jnp.float32)
             try:
                 requests[index] = stream.send(previous)
             except StopIteration as stop:

time: 2010 us -> 2230 us (1.11)
  waiting for transfers between devices: 763 us -> 1170 us
  starting transfers between devices: 229 us -> 73.4 us
  other arithmetic: 242 us -> 196 us
    reduce_scatter x0 -> x8, waiting for transfers between devices: none -> 502 us  [per_device(): lax.psum_scatter(value.astype(jnp.bfloat16), 'tensor', scatter_dimension=...]
    ppermute x48 -> x0, waiting for transfers between devices: 331 us -> none  [the longest x24 258 us: line_scatter(): lax.ppermute(send.astype(jnp.bfloat16), 'tensor', [(i, i + 1) for i in ra...]
    ppermute x48 -> x0, starting transfers between devices: 149 us -> none  [the longest x24 120 us: line_scatter(): lax.ppermute(send.astype(jnp.bfloat16), 'tensor', [(i, i + 1) for i in ra...]
    reduce_scatter x1, waiting for transfers between devices: 0.01 us -> 100 us  [per_device(): lax.psum_scatter(totals[3].reshape(width, -1).astype(jnp.bfloat16), 'dp',...]
    ppermute x24, waiting for transfers between devices: 322 us -> 412 us  [line_gather(): lax.ppermute(from_right, 'tensor', [(i, i - 1) for i in range(1, count -...]
    ppermute x24, waiting for transfers between devices: 60.1 us -> 126 us  [line_gather(): lax.ppermute(from_left, 'tensor', [(i, i + 1) for i in range(step - 1, co...]
    convert_element_type x24 -> x0, other arithmetic: 37.5 us -> none  [line_scatter(): send.astype(jnp.bfloat16)]
    reduce_scatter x1, waiting for transfers between devices: 23.9 us -> 0.01 us  [per_device(): lax.psum_scatter(totals[2].astype(jnp.bfloat16), 'dp', scatter_dimension=...]
  transfers between devices with their start and end apart: 107 -> 67, of which waited for: 47 -> 36; matrix products, arithmetic and copies ran while one was open for 42% -> 37% of each run, Pallas kernels for 0% -> 0%
where the time goes in v10:
time: 2230 us; the launch traced here: 2220 us
  waiting for transfers between devices  1170 us (52%)
  matrix products  564 us (25%)
  other arithmetic  196 us (9%)
  local copies, waits for them, and re-layouts  128 us (6%)
  starting transfers between devices  73.4 us (3%)
  blocking collectives  70.2 us (3%)
    reduce_scatter x8, waiting for transfers between devices, per_device(): lax.psum_scatter(value.astype(jnp.bfloat16), 'tensor', scatter_dimension=...  502 us
    ppermute x24, waiting for transfers between devices, line_gather(): lax.ppermute(from_right, 'tensor', [(i, i - 1) for i in range(1, count -...  412 us
    ppermute x24, waiting for transfers between devices, line_gather(): lax.ppermute(from_left, 'tensor', [(i, i + 1) for i in range(step - 1, co...  126 us
    reduce_scatter x1, waiting for transfers between devices, per_device(): lax.psum_scatter(totals[3].reshape(width, -1).astype(jnp.bfloat16), 'dp',...  100 us
    dot_general x6, matrix products, contract_cols(): lax.dot_general(left, right, (((1,), (1,)), ((), ())), preferred_element_...  67 us
    dot_general x2, matrix products, micro_step(): jnp.einsum('rd,rcf->dcf', rows_two, gateup_grad, preferred_element_type=j...  60.4 us
    dot_general x4, matrix products, attend_back(): jnp.einsum('ikrd,jkd->krij', grad_block, values[:stop], preferred_element...  60.3 us
    dot_general x6, matrix products, contract_rows(): lax.dot_general(left, right, (((0,), (0,)), ((), ())), preferred_element_...  57 us
  transfers between devices with their start and end apart: 67, of which 36 were waited for; matrix products, arithmetic and copies ran while one was open for 37% of the time, Pallas kernels for 0%

profile of v10, /device:TPU:0, one launch (start us, length us, event | category | flops | bytes accessed | tf_op | source)
XLA Modules:
  0.0 2224.0 jit_solution(13606755496050330969)
XLA Ops:
  13.3 10.4 all_gather.18
  36.4 23.1 %collective-permute-done = bf16[304,2048]{1,0:T(8,128)(2,1)} collective-permute-done((bf16[304,2048]{1,0:T(8,128)(2,1)}, bf16[304,2048]{1,0:T(8,128)(2,1)}, u32[]{:S(2)}, u32[]{:S(2)}) %collective-permute-start) | collective-permute-done | bytes 1245216 | tf_op jit(solution)/shard_map/ppermute | solution.py:175
  68.8 28.7 %collective-permute-done.3 = bf16[304,2048]{1,0:T(8,128)(2,1)S(1)} collective-permute-done((bf16[304,2048]{1,0:T(8,128)(2,1)}, bf16[304,2048]{1,0:T(8,128)(2,1)S(1)}, u32[]{:S(2)}, u32[]{:S(2)}) %collective-permute-start.3) | collective-permute-done | bytes 1245216 | tf_op jit(solution)/shard_map/ppermute | solution.py:178
  104.1 23.2 %collective-permute-done.5 = bf16[304,2048]{1,0:T(8,128)(2,1)S(1)} collective-permute-done((bf16[304,2048]{1,0:T(8,128)(2,1)S(1)}, bf16[304,2048]{1,0:T(8,128)(2,1)S(1)}, u32[]{:S(2)}, u32[]{:S(2)}) %collective-permute-start.5) | collective-permute-done | bytes 1245216 | tf_op jit(solution)/shard_map/ppermute | solution.py:178
  137.1 7.5 fusion.232
  144.6 10.8 collective-permute-done.6
  178.0 15.3 collective-permute-done.9
  201.3 19.4 collective-permute-done.11
  238.8 11.0 fusion.11
  256.7 7.6 fusion.133
  275.0 22.9 %fusion.135 = bf16[2,64,4,608]{3,1,2,0:T(8,128)(2,1)} fusion(f32[2,1216,608,4]{2,1,3,0:T(8,128)} %get-tuple-element.398, f32[2,4,608]{2,1,0:T(4,128)S(1)} %fusion.13, f32[2,4,608]{2,1,0:T(4,128)S(1)} %get-tuple-element.397, pred[608,1216]{0,1:T(8,128)(4,1)S(1)} %slice.468, bf16[1216,2,128]{2,0,1:T(8,128)(2,1)S(1)} %copy-done.77), kind=kOutput, calls=%fused_computation.210 | convolution fusion | flops 786956288 | bytes 25681920 | tf_op jit(solution)/shard_map/krij,jkd->ikrd/dot_general | solution.py:91
  333.9 12.3 fusion.136
  358.8 33.2 %reduce-scatter.19.cloned.1.call-done = bf16[304,2048]{1,0:T(8,128)(2,1)} async-done(((bf16[1216,2048]{1,0:T(8,128)(2,1)}), bf16[304,2048]{1,0:T(8,128)(2,1)}) %reduce-scatter.19.cloned.1.call-update) | async-done | bytes 1245200 | tf_op jit(solution)/shard_map/reduce_scatter | solution.py:378
  392.0 92.2 %reduce-scatter.17.cloned.1.call-done = bf16[304,2048]{1,0:T(8,128)(2,1)} async-done(((bf16[1216,2048]{1,0:T(8,128)(2,1)}), bf16[304,2048]{1,0:T(8,128)(2,1)}) %reduce-scatter.17.cloned.1.call-update) | async-done | bytes 1245200 | tf_op jit(solution)/shard_map/reduce_scatter | solution.py:378
  494.4 25.2 %collective-permute-done.12 = bf16[304,2048]{1,0:T(8,128)(2,1)S(1)} collective-permute-done((bf16[304,2048]{1,0:T(8,128)(2,1)S(1)}, bf16[304,2048]{1,0:T(8,128)(2,1)S(1)}, u32[]{:S(2)}, u32[]{:S(2)}) %collective-permute-start.12) | collective-permute-done | bytes 1245216 | tf_op jit(solution)/shard_map/ppermute | solution.py:175
  529.1 26.2 %collective-permute-done.15 = bf16[304,2048]{1,0:T(8,128)(2,1)} collective-permute-done((bf16[304,2048]{1,0:T(8,128)(2,1)S(1)}, bf16[304,2048]{1,0:T(8,128)(2,1)}, u32[]{:S(2)}, u32[]{:S(2)}) %collective-permute-start.15) | collective-permute-done | bytes 1245216 | tf_op jit(solution)/shard_map/ppermute | solution.py:178
  562.1 22.7 %collective-permute-done.17 = bf16[304,2048]{1,0:T(8,128)(2,1)S(1)} collective-permute-done((bf16[304,2048]{1,0:T(8,128)(2,1)}, bf16[304,2048]{1,0:T(8,128)(2,1)S(1)}, u32[]{:S(2)}, u32[]{:S(2)}) %collective-permute-start.17) | collective-permute-done | bytes 1245216 | tf_op jit(solution)/shard_map/ppermute | solution.py:178
  588.1 22.7 %collective-permute-done.18 = bf16[304,2048]{1,0:T(8,128)(2,1)S(1)} collective-permute-done((bf16[304,2048]{1,0:T(8,128)(2,1)S(1)}, bf16[304,2048]{1,0:T(8,128)(2,1)S(1)}, u32[]{:S(2)}, u32[]{:S(2)}) %collective-permute-start.18) | collective-permute-done | bytes 1245216 | tf_op jit(solution)/shard_map/ppermute | solution.py:175
  617.7 24.9 %collective-permute-done.21 = bf16[304,2048]{1,0:T(8,128)(2,1)S(1)} collective-permute-done((bf16[304,2048]{1,0:T(8,128)(2,1)S(1)}, bf16[304,2048]{1,0:T(8,128)(2,1)S(1)}, u32[]{:S(2)}, u32[]{:S(2)}) %collective-permute-start.21) | collective-permute-done | bytes 1245216 | tf_op jit(solution)/shard_map/ppermute | solution.py:178
  645.3 23.8 %collective-permute-done.23 = bf16[304,2048]{1,0:T(8,128)(2,1)S(1)} collective-permute-done((bf16[304,2048]{1,0:T(8,128)(2,1)S(1)}, bf16[304,2048]{1,0:T(8,128)(2,1)S(1)}, u32[]{:S(2)}, u32[]{:S(2)}) %collective-permute-start.23) | collective-permute-done | bytes 1245216 | tf_op jit(solution)/shard_map/ppermute | solution.py:178
  672.3 20.1 collective-permute-done.24
  700.6 25.5 %collective-permute-done.27 = bf16[304,2048]{1,0:T(8,128)(2,1)S(1)} collective-permute-done((bf16[304,2048]{1,0:T(8,128)(2,1)S(1)}, bf16[304,2048]{1,0:T(8,128)(2,1)S(1)}, u32[]{:S(2)}, u32[]{:S(2)}) %collective-permute-start.27) | collective-permute-done | bytes 1245216 | tf_op jit(solution)/shard_map/ppermute | solution.py:178
  735.9 14.1 collective-permute-done.29
  755.3 27.3 %fusion.59 = f32[1216,2,2048]{2,0,1:T(8,128)} fusion(bf16[2048,2,2048]{2,0,1:T(8,128)(2,1)} %all-gather.12.cloned.1.call-done, bf16[1216,2048]{1,0:T(8,128)(2,1)} %copy-done.42), kind=kOutput, calls=%fused_computation.103 | convolution fusion | flops 20401094656 | bytes 41680896 | tf_op jit(solution)/shard_map/rd,dcf->rcf/dot_general | solution.py:291
  782.6 25.6 %fusion.69 = (bf16[1216,1,2048]{2,0,1:T(8,128)(2,1)}, bf16[1216,1,2048]{2,0,1:T(8,128)(2,1)}, bf16[1216,2048]{1,0:T(8,128)(2,1)}) fusion(f32[1216,2,2048]{2,0,1:T(8,128)} %fusion.59, bf16[1216,2048]{1,0:T(8,128)(2,1)} %constant_dynamic-update-slice_fusion.21, bf16[2048,2048]{1,0:T(8,128)(2,1)} %all-gather.14.cloned.1.call-done), kind=kOutput, calls=%fused_computation.113 | convolution fusion | flops 10237902848 | bytes 48234496 | tf_op jit(solution)/shard_map/dot_general | solution.py:162
  810.1 27.8 %convolution_bitcast_fusion.1 = bf16[1216,2048]{1,0:T(8,128)(2,1)} fusion(bf16[2048,2,2048]{2,0,1:T(8,128)(2,1)} %all-gather.12.cloned.1.call-done, bf16[1216,1,2048]{2,0,1:T(8,128)(2,1)} %get-tuple-element.330, bf16[1216,1,2048]{2,0,1:T(8,128)(2,1)} %get-tuple-element.329), kind=kOutput, calls=%fused_computation.81 | convolution fusion | flops 20406075392 | bytes 31719424 | tf_op jit(solution)/shard_map/rcf,dcf->rd/dot_general | solution.py:316
  840.0 27.3 %fusion.56 = f32[1216,2,2048]{2,0,1:T(8,128)} fusion(bf16[2048,2,2048]{2,0,1:T(8,128)(2,1)} %all-gather.12.cloned.1.call-done, bf16[1216,2048]{1,0:T(8,128)(2,1)} %copy-done.43), kind=kOutput, calls=%fused_computation.100 | convolution fusion | flops 20401094656 | bytes 41680896 | tf_op jit(solution)/shard_map/rd,dcf->rcf/dot_general | solution.py:291
  867.4 68.1 %collective-permute-done.33 = bf16[304,2048]{1,0:T(8,128)(2,1)S(1)} collective-permute-done((bf16[304,2048]{1,0:T(8,128)(2,1)}, bf16[304,2048]{1,0:T(8,128)(2,1)S(1)}, u32[]{:S(2)}, u32[]{:S(2)}) %collective-permute-start.33) | collective-permute-done | bytes 1245216 | tf_op jit(solution)/shard_map/ppermute | solution.py:178
  948.3 21.3 collective-permute-done.35
  972.0 26.0 %fusion.70 = (bf16[1216,1,2048]{2,0,1:T(8,128)(2,1)}, bf16[1216,1,2048]{2,0,1:T(8,128)(2,1)}, bf16[1216,2048]{1,0:T(8,128)(2,1)}) fusion(f32[1216,2,2048]{2,0,1:T(8,128)} %fusion.56, bf16[1216,2048]{1,0:T(8,128)(2,1)} %constant_dynamic-update-slice_fusion.14, bf16[2048,2048]{1,0:T(8,128)(2,1)} %all-gather.14.cloned.1.call-done), kind=kOutput, calls=%fused_computation.114 | convolution fusion | flops 10237902848 | bytes 48234496 | tf_op jit(solution)/shard_map/dot_general | solution.py:162
  998.0 27.8 %convolution_bitcast_fusion = bf16[1216,2048]{1,0:T(8,128)(2,1)} fusion(bf16[2048,2,2048]{2,0,1:T(8,128)(2,1)} %all-gather.12.cloned.1.call-done, bf16[1216,1,2048]{2,0,1:T(8,128)(2,1)} %get-tuple-element.328, bf16[1216,1,2048]{2,0,1:T(8,128)(2,1)} %get-tuple-element.327), kind=kOutput, calls=%fused_computation.80 | convolution fusion | flops 20406075392 | bytes 31719424 | tf_op jit(solution)/shard_map/rcf,dcf->rd/dot_general | solution.py:316
  1025.9 16.1 fusion.234
  1042.1 71.5 %reduce-scatter.27.cloned.1.call-done = bf16[304,2048]{1,0:T(8,128)(2,1)} async-done(((bf16[1216,2048]{1,0:T(8,128)(2,1)}), bf16[304,2048]{1,0:T(8,128)(2,1)}) %reduce-scatter.27.cloned.1.call-update) | async-done | bytes 1245200 | tf_op jit(solution)/shard_map/reduce_scatter | solution.py:378
  1118.8 87.1 %reduce-scatter.21.cloned.1.call-done = bf16[304,2048]{1,0:T(8,128)(2,1)} async-done(((bf16[1216,2048]{1,0:T(8,128)(2,1)}), bf16[304,2048]{1,0:T(8,128)(2,1)}) %reduce-scatter.21.cloned.1.call-update) | async-done | bytes 1245200 | tf_op jit(solution)/shard_map/reduce_scatter | solution.py:378
  1218.6 23.8 %collective-permute-done.36 = bf16[304,2048]{1,0:T(8,128)(2,1)S(1)} collective-permute-done((bf16[304,2048]{1,0:T(8,128)(2,1)S(1)}, bf16[304,2048]{1,0:T(8,128)(2,1)S(1)}, u32[]{:S(2)}, u32[]{:S(2)}) %collective-permute-start.36) | collective-permute-done | bytes 1245216 | tf_op jit(solution)/shard_map/ppermute | solution.py:175
  1244.1 18.2 fusion.237
  1265.4 17.0 add_convert_fusion.1
  1282.4 13.8 collective-permute-done.39
  1303.5 22.2 %collective-permute-done.41 = bf16[304,2048]{1,0:T(8,128)(2,1)S(1)} collective-permute-done((bf16[304,2048]{1,0:T(8,128)(2,1)}, bf16[304,2048]{1,0:T(8,128)(2,1)S(1)}, u32[]{:S(2)}, u32[]{:S(2)}) %collective-permute-start.41) | collective-permute-done | bytes 1245216 | tf_op jit(solution)/shard_map/ppermute | solution.py:178
  1333.7 7.1 fusion.143
  1340.9 9.6 fusion.19
  1350.8 10.2 fusion.21
  1366.2 21.2 fusion.3
  1387.3 17.0 fusion.5
  1415.3 12.0 fusion.125
  1434.1 24.4 %collective-permute-done.45 = bf16[304,2048]{1,0:T(8,128)(2,1)S(1)} collective-permute-done((bf16[304,2048]{1,0:T(8,128)(2,1)}, bf16[304,2048]{1,0:T(8,128)(2,1)S(1)}, u32[]{:S(2)}, u32[]{:S(2)}) %collective-permute-start.45) | collective-permute-done | bytes 1245216 | tf_op jit(solution)/shard_map/ppermute | solution.py:178
  1463.9 22.6 %collective-permute-done.47 = bf16[304,2048]{1,0:T(8,128)(2,1)S(1)} collective-permute-done((bf16[304,2048]{1,0:T(8,128)(2,1)S(1)}, bf16[304,2048]{1,0:T(8,128)(2,1)S(1)}, u32[]{:S(2)}, u32[]{:S(2)}) %collective-permute-start.47) | collective-permute-done | bytes 1245216 | tf_op jit(solution)/shard_map/ppermute | solution.py:178
  1492.5 11.6 fusion.16
  1516.7 18.0 fusion
  1534.7 17.2 fusion.2
  1561.7 8.5 fusion.118
  1574.6 11.2 fusion.122
  1602.6 29.4 %fusion.42 = f32[2048,2,2048]{0,2,1:T(8,128)} fusion(bf16[1216,1,2048]{2,0,1:T(8,128)(2,1)} %get-tuple-element.328, bf16[1216,1,2048]{2,0,1:T(8,128)(2,1)} %get-tuple-element.327, bf16[1216,2048]{1,0:T(8,128)(2,1)} %copy-done.43), kind=kOutput, calls=%fused_computation.84 | convolution fusion | flops 20421017600 | bytes 48496640 | tf_op jit(solution)/shard_map/rd,rcf->dcf/dot_general | solution.py:311
  1644.1 31.0 %add_convert_fusion = bf16[2048,2,2048]{0,2,1:T(8,128)(2,1)} fusion(f32[2048,2,2048]{0,2,1:T(8,128)} %fusion.42, bf16[1216,1,2048]{2,0,1:T(8,128)(2,1)} %get-tuple-element.330, bf16[1216,1,2048]{2,0,1:T(8,128)(2,1)} %get-tuple-element.329, bf16[1216,2048]{1,0:T(8,128)(2,1)} %copy-done.42), kind=kOutput, calls=%fused_computation | convolution fusion | flops 20437794816 | bytes 65273856 | tf_op jit(solution)/shard_map/rd,rcf->dcf/dot_general | solution.py:311
  1690.8 16.0 fusion.235
  1708.6 7.2 multiply_reduce_fusion.1
  1735.4 100.5 %reduce-scatter.39.cloned.1.call-done = bf16[256,4096]{0,1:T(8,128)(2,1)} async-done(((bf16[2048,4096]{0,1:T(8,128)(2,1)}), bf16[256,4096]{0,1:T(8,128)(2,1)}) %reduce-scatter.39.cloned.1.call-update) | async-done | bytes 2097168 | tf_op jit(solution)/shard_map/reduce_scatter | solution.py:406
  1842.5 18.4 multiply_reduce_fusion
  1860.9 67.3 %reduce-scatter.31.cloned.1.call-done = bf16[304,2048]{1,0:T(8,128)(2,1)} async-done(((bf16[1216,2048]{1,0:T(8,128)(2,1)}), bf16[304,2048]{1,0:T(8,128)(2,1)}) %reduce-scatter.31.cloned.1.call-update) | async-done | bytes 1245200 | tf_op jit(solution)/shard_map/reduce_scatter | solution.py:378
  1928.2 92.2 %reduce-scatter.29.cloned.1.call-done = bf16[304,2048]{1,0:T(8,128)(2,1)} async-done(((bf16[1216,2048]{1,0:T(8,128)(2,1)}), bf16[304,2048]{1,0:T(8,128)(2,1)}) %reduce-scatter.29.cloned.1.call-update) | async-done | bytes 1245200 | tf_op jit(solution)/shard_map/reduce_scatter | solution.py:378
  2025.0 20.3 psum.14
  2054.5 58.7 %reduce-scatter.23.cloned.1.call-done = bf16[304,2048]{1,0:T(8,128)(2,1)} async-done(((bf16[1216,2048]{1,0:T(8,128)(2,1)}), bf16[304,2048]{1,0:T(8,128)(2,1)}) %reduce-scatter.23.cloned.1.call-update) | async-done | bytes 1245200 | tf_op jit(solution)/shard_map/reduce_scatter | solution.py:378
  2121.0 30.4 %reduce-scatter.43.cloned.1.call-done = bf16[256,2]{1,0:T(8,128)(2,1)} async-done(((bf16[2048,2]{1,0:T(8,128)(2,1)}), bf16[256,2]{1,0:T(8,128)(2,1)}) %reduce-scatter.43.cloned.1.call-update) | async-done | bytes 1040
  2160.0 39.4 %psum.15 = f32[2,7]{1,0:T(2,128)S(1)} all-reduce(f32[2,7]{1,0:T(2,128)S(1)} %pad_maximum_fusion.26), channel_id=1, replica_groups=mesh['dp'=8,'tensor'=4] {'dp','tensor'}, use_global_device_ids=true, to_apply=%region_57.58 | all-reduce | flops 14 | bytes 112 | tf_op jit(solution)/shard_map/psum | solution.py:441
  (669 shorter events, 457.7 us)
Async XLA Ops:
  7.2 129.9 %all-gather.8.cloned.1.call-start = ((), (), s32[]{:S(2)}) async-start(), calls=%async_computation.15 | async-start | bytes 2359296 | tf_op jit(solution)/shard_map/all_gather | solution.py:244
  10.0 147.1 %all-gather.6.cloned.1.call-start = ((), (), s32[]{:S(2)}) async-start(), calls=%async_computation.14 | async-start | bytes 1179648 | tf_op jit(solution)/shard_map/all_gather | solution.py:245
  11.8 286.1 %all-gather.10.cloned.1.call-start = ((), (), s32[]{:S(2)}) async-start(), calls=%async_computation.16 | async-start | bytes 2359296 | tf_op jit(solution)/shard_map/all_gather | solution.py:246
  28.6 30.9 %collective-permute-start = (bf16[304,2048]{1,0:T(8,128)(2,1)}, bf16[304,2048]{1,0:T(8,128)(2,1)}, u32[]{:S(2)}, u32[]{:S(2)}) collective-permute-start(bf16[304,2048]{1,0:T(8,128)(2,1)} %get-tuple-element.349), channel_id=1, source_target_pairs={{0,1},{1,2},{2,3},{4,5},{5,6},{6,7},{8,9},{9,10},{10,11},{12,13},{... | collective-permute-start | bytes 3735560 | tf_op jit(solution)/shard_map/ppermute | solution.py:175
  33.1 31.5 %collective-permute-start.1 = (bf16[304,2048]{1,0:T(8,128)(2,1)}, bf16[304,2048]{1,0:T(8,128)(2,1)}, u32[]{:S(2)}, u32[]{:S(2)}) collective-permute-start(bf16[304,2048]{1,0:T(8,128)(2,1)} %get-tuple-element.349), channel_id=1, source_target_pairs={{1,0},{2,1},{3,2},{5,4},{6,5},{7,6},{9,8},{10,9},{11,10},{13,12},{... | collective-permute-start | bytes 3735560 | tf_op jit(solution)/shard_map/ppermute | solution.py:178
  35.8 356.1 %reduce-scatter.19.cloned.1.call-start = ((), (), s32[]{:S(2)}) async-start(), calls=%async_computation.18 | async-start | bytes 6225920 | tf_op jit(solution)/shard_map/reduce_scatter | solution.py:378
  59.5 8.5 collective-permute-start.2
  64.7 32.9 %collective-permute-start.3 = (bf16[304,2048]{1,0:T(8,128)(2,1)}, bf16[304,2048]{1,0:T(8,128)(2,1)S(1)}, u32[]{:S(2)}, u32[]{:S(2)}) collective-permute-start(bf16[304,2048]{1,0:T(8,128)(2,1)} %collective-permute-done.1), channel_id=1, source_target_pairs={{1,0},{2,1},{5,4},{6,5},{9,8},{10,9},{13,12},{14,13},{17,16},{18,1... | collective-permute-start | bytes 3735560 | tf_op jit(solution)/shard_map/ppermute | solution.py:178
  68.1 35.9 %collective-permute-start.4 = (bf16[304,2048]{1,0:T(8,128)(2,1)}, bf16[304,2048]{1,0:T(8,128)(2,1)S(1)}, u32[]{:S(2)}, u32[]{:S(2)}) collective-permute-start(bf16[304,2048]{1,0:T(8,128)(2,1)} %collective-permute-done.2), channel_id=1, source_target_pairs={{2,3},{6,7},{10,11},{14,15},{18,19},{22,23},{26,27},{30,31}} | collective-permute-start | bytes 3735560 | tf_op jit(solution)/shard_map/ppermute | solution.py:175
  97.6 29.8 %collective-permute-start.5 = (bf16[304,2048]{1,0:T(8,128)(2,1)S(1)}, bf16[304,2048]{1,0:T(8,128)(2,1)S(1)}, u32[]{:S(2)}, u32[]{:S(2)}) collective-permute-start(bf16[304,2048]{1,0:T(8,128)(2,1)S(1)} %collective-permute-done.3), channel_id=1, source_target_pairs={{1,0},{5,4},{9,8},{13,12},{17,16},{21,20},{25,24},{29,28}} | collective-permute-start | bytes 3735560 | tf_op jit(solution)/shard_map/ppermute | solution.py:178
  129.0 26.5 %collective-permute-start.6 = (bf16[304,2048]{1,0:T(8,128)(2,1)}, bf16[304,2048]{1,0:T(8,128)(2,1)}, u32[]{:S(2)}, u32[]{:S(2)}) collective-permute-start(bf16[304,2048]{1,0:T(8,128)(2,1)} %get-tuple-element.164), channel_id=1, source_target_pairs={{0,1},{1,2},{2,3},{4,5},{5,6},{6,7},{8,9},{9,10},{10,11},{12,13},{... | collective-permute-start | bytes 3735560 | tf_op jit(solution)/shard_map/ppermute | solution.py:175
  135.6 29.3 %collective-permute-start.7 = (bf16[304,2048]{1,0:T(8,128)(2,1)}, bf16[304,2048]{1,0:T(8,128)(2,1)}, u32[]{:S(2)}, u32[]{:S(2)}) collective-permute-start(bf16[304,2048]{1,0:T(8,128)(2,1)} %get-tuple-element.164), channel_id=1, source_target_pairs={{1,0},{2,1},{3,2},{5,4},{6,5},{7,6},{9,8},{10,9},{11,10},{13,12},{... | collective-permute-start | bytes 3735560 | tf_op jit(solution)/shard_map/ppermute | solution.py:178
  155.4 19.5 collective-permute-start.8
  164.9 28.4 %collective-permute-start.9 = (bf16[304,2048]{1,0:T(8,128)(2,1)}, bf16[304,2048]{1,0:T(8,128)(2,1)}, u32[]{:S(2)}, u32[]{:S(2)}) collective-permute-start(bf16[304,2048]{1,0:T(8,128)(2,1)} %collective-permute-done.7), channel_id=1, source_target_pairs={{1,0},{2,1},{5,4},{6,5},{9,8},{10,9},{13,12},{14,13},{17,16},{18,1... | collective-permute-start | bytes 3735560 | tf_op jit(solution)/shard_map/ppermute | solution.py:178
  174.9 26.3 %collective-permute-start.10 = (bf16[304,2048]{1,0:T(8,128)(2,1)}, bf16[304,2048]{1,0:T(8,128)(2,1)S(1)}, u32[]{:S(2)}, u32[]{:S(2)}) collective-permute-start(bf16[304,2048]{1,0:T(8,128)(2,1)} %collective-permute-done.8), channel_id=1, source_target_pairs={{2,3},{6,7},{10,11},{14,15},{18,19},{22,23},{26,27},{30,31}} | collective-permute-start | bytes 3735560 | tf_op jit(solution)/shard_map/ppermute | solution.py:175
  193.3 27.4 %collective-permute-start.11 = (bf16[304,2048]{1,0:T(8,128)(2,1)}, bf16[304,2048]{1,0:T(8,128)(2,1)S(1)}, u32[]{:S(2)}, u32[]{:S(2)}) collective-permute-start(bf16[304,2048]{1,0:T(8,128)(2,1)} %collective-permute-done.9), channel_id=1, source_target_pairs={{1,0},{5,4},{9,8},{13,12},{17,16},{21,20},{25,24},{29,28}} | collective-permute-start | bytes 3735560 | tf_op jit(solution)/shard_map/ppermute | solution.py:178
  305.0 179.2 %reduce-scatter.17.cloned.1.call-start = ((), (), s32[]{:S(2)}) async-start(), calls=%async_computation.17 | async-start | bytes 6225920 | tf_op jit(solution)/shard_map/reduce_scatter | solution.py:378
  352.3 403.0 %all-gather.12.cloned.1.call-start = ((), (), s32[]{:S(2)}) async-start(), calls=%async_computation.19 | async-start | bytes 18874368 | tf_op jit(solution)/shard_map/all_gather | solution.py:247
  358.3 424.3 %all-gather.14.cloned.1.call-start = ((), (), s32[]{:S(2)}) async-start(), calls=%async_computation.20 | async-start | bytes 9437184 | tf_op jit(solution)/shard_map/all_gather | solution.py:248
  489.6 30.0 %collective-permute-start.12 = (bf16[304,2048]{1,0:T(8,128)(2,1)S(1)}, bf16[304,2048]{1,0:T(8,128)(2,1)S(1)}, u32[]{:S(2)}, u32[]{:S(2)}) collective-permute-start(bf16[304,2048]{1,0:T(8,128)(2,1)S(1)} %get-tuple-element.167), channel_id=1, source_target_pairs={{0,1},{1,2},{2,3},{4,5},{5,6},{6,7},{8,9},{9,10},{10,11},{12,13},{... | collective-permute-start | bytes 3735560 | tf_op jit(solution)/shard_map/ppermute | solution.py:175
  493.1 30.9 %collective-permute-start.13 = (bf16[304,2048]{1,0:T(8,128)(2,1)S(1)}, bf16[304,2048]{1,0:T(8,128)(2,1)S(1)}, u32[]{:S(2)}, u32[]{:S(2)}) collective-permute-start(bf16[304,2048]{1,0:T(8,128)(2,1)S(1)} %get-tuple-element.167), channel_id=1, source_target_pairs={{1,0},{2,1},{3,2},{5,4},{6,5},{7,6},{9,8},{10,9},{11,10},{13,12},{... | collective-permute-start | bytes 3735560 | tf_op jit(solution)/shard_map/ppermute | solution.py:178
  524.0 31.3 %collective-permute-start.15 = (bf16[304,2048]{1,0:T(8,128)(2,1)S(1)}, bf16[304,2048]{1,0:T(8,128)(2,1)}, u32[]{:S(2)}, u32[]{:S(2)}) collective-permute-start(bf16[304,2048]{1,0:T(8,128)(2,1)S(1)} %collective-permute-done.13), channel_id=1, source_target_pairs={{1,0},{2,1},{5,4},{6,5},{9,8},{10,9},{13,12},{14,13},{17,16},{18,1... | collective-permute-start | bytes 3735560 | tf_op jit(solution)/shard_map/ppermute | solution.py:178
  525.3 35.3 %collective-permute-start.16 = (bf16[304,2048]{1,0:T(8,128)(2,1)}, bf16[304,2048]{1,0:T(8,128)(2,1)}, u32[]{:S(2)}, u32[]{:S(2)}) collective-permute-start(bf16[304,2048]{1,0:T(8,128)(2,1)} %collective-permute-done.14), channel_id=1, source_target_pairs={{2,3},{6,7},{10,11},{14,15},{18,19},{22,23},{26,27},{30,31}} | collective-permute-start | bytes 3735560 | tf_op jit(solution)/shard_map/ppermute | solution.py:175
  529.1 513.0 %reduce-scatter.25.cloned.1.call-start = ((), (), s32[]{:S(2)}) async-start(), calls=%async_computation.23 | async-start | bytes 6225920 | tf_op jit(solution)/shard_map/reduce_scatter | solution.py:378
  555.3 29.5 %collective-permute-start.17 = (bf16[304,2048]{1,0:T(8,128)(2,1)}, bf16[304,2048]{1,0:T(8,128)(2,1)S(1)}, u32[]{:S(2)}, u32[]{:S(2)}) collective-permute-start(bf16[304,2048]{1,0:T(8,128)(2,1)} %collective-permute-done.15), channel_id=1, source_target_pairs={{1,0},{5,4},{9,8},{13,12},{17,16},{21,20},{25,24},{29,28}} | collective-permute-start | bytes 3735560 | tf_op jit(solution)/shard_map/ppermute | solution.py:178
  585.2 25.7 %collective-permute-start.18 = (bf16[304,2048]{1,0:T(8,128)(2,1)S(1)}, bf16[304,2048]{1,0:T(8,128)(2,1)S(1)}, u32[]{:S(2)}, u32[]{:S(2)}) collective-permute-start(bf16[304,2048]{1,0:T(8,128)(2,1)S(1)} %copy-done.48), channel_id=1, source_target_pairs={{0,1},{1,2},{2,3},{4,5},{5,6},{6,7},{8,9},{9,10},{10,11},{12,13},{... | collective-permute-start | bytes 3735560 | tf_op jit(solution)/shard_map/ppermute | solution.py:175
  586.8 28.2 %collective-permute-start.19 = (bf16[304,2048]{1,0:T(8,128)(2,1)S(1)}, bf16[304,2048]{1,0:T(8,128)(2,1)S(1)}, u32[]{:S(2)}, u32[]{:S(2)}) collective-permute-start(bf16[304,2048]{1,0:T(8,128)(2,1)S(1)} %copy-done.48), channel_id=1, source_target_pairs={{1,0},{2,1},{3,2},{5,4},{6,5},{7,6},{9,8},{10,9},{11,10},{13,12},{... | collective-permute-start | bytes 3735560 | tf_op jit(solution)/shard_map/ppermute | solution.py:178
  615.0 27.5 %collective-permute-start.21 = (bf16[304,2048]{1,0:T(8,128)(2,1)S(1)}, bf16[304,2048]{1,0:T(8,128)(2,1)S(1)}, u32[]{:S(2)}, u32[]{:S(2)}) collective-permute-start(bf16[304,2048]{1,0:T(8,128)(2,1)S(1)} %collective-permute-done.19), channel_id=1, source_target_pairs={{1,0},{2,1},{5,4},{6,5},{9,8},{10,9},{13,12},{14,13},{17,16},{18,1... | collective-permute-start | bytes 3735560 | tf_op jit(solution)/shard_map/ppermute | solution.py:178
  616.3 28.8 %collective-permute-start.22 = (bf16[304,2048]{1,0:T(8,128)(2,1)S(1)}, bf16[304,2048]{1,0:T(8,128)(2,1)S(1)}, u32[]{:S(2)}, u32[]{:S(2)}) collective-permute-start(bf16[304,2048]{1,0:T(8,128)(2,1)S(1)} %collective-permute-done.20), channel_id=1, source_target_pairs={{2,3},{6,7},{10,11},{14,15},{18,19},{22,23},{26,27},{30,31}} | collective-permute-start | bytes 3735560 | tf_op jit(solution)/shard_map/ppermute | solution.py:175
  642.6 26.6 %collective-permute-start.23 = (bf16[304,2048]{1,0:T(8,128)(2,1)S(1)}, bf16[304,2048]{1,0:T(8,128)(2,1)S(1)}, u32[]{:S(2)}, u32[]{:S(2)}) collective-permute-start(bf16[304,2048]{1,0:T(8,128)(2,1)S(1)} %collective-permute-done.21), channel_id=1, source_target_pairs={{1,0},{5,4},{9,8},{13,12},{17,16},{21,20},{25,24},{29,28}} | collective-permute-start | bytes 3735560 | tf_op jit(solution)/shard_map/ppermute | solution.py:178
  669.5 22.9 %collective-permute-start.24 = (bf16[304,2048]{1,0:T(8,128)(2,1)S(1)}, bf16[304,2048]{1,0:T(8,128)(2,1)S(1)}, u32[]{:S(2)}, u32[]{:S(2)}) collective-permute-start(bf16[304,2048]{1,0:T(8,128)(2,1)S(1)} %get-tuple-element.169), channel_id=1, source_target_pairs={{0,1},{1,2},{2,3},{4,5},{5,6},{6,7},{8,9},{9,10},{10,11},{12,13},{... | collective-permute-start | bytes 3735560 | tf_op jit(solution)/shard_map/ppermute | solution.py:175
  671.0 27.6 %collective-permute-start.25 = (bf16[304,2048]{1,0:T(8,128)(2,1)S(1)}, bf16[304,2048]{1,0:T(8,128)(2,1)S(1)}, u32[]{:S(2)}, u32[]{:S(2)}) collective-permute-start(bf16[304,2048]{1,0:T(8,128)(2,1)S(1)} %get-tuple-element.169), channel_id=1, source_target_pairs={{1,0},{2,1},{3,2},{5,4},{6,5},{7,6},{9,8},{10,9},{11,10},{13,12},{... | collective-permute-start | bytes 3735560 | tf_op jit(solution)/shard_map/ppermute | solution.py:178
  692.4 7.4 collective-permute-start.26
  698.6 27.5 %collective-permute-start.27 = (bf16[304,2048]{1,0:T(8,128)(2,1)S(1)}, bf16[304,2048]{1,0:T(8,128)(2,1)S(1)}, u32[]{:S(2)}, u32[]{:S(2)}) collective-permute-start(bf16[304,2048]{1,0:T(8,128)(2,1)S(1)} %collective-permute-done.25), channel_id=1, source_target_pairs={{1,0},{2,1},{5,4},{6,5},{9,8},{10,9},{13,12},{14,13},{17,16},{18,1... | collective-permute-start | bytes 3735560 | tf_op jit(solution)/shard_map/ppermute | solution.py:178
  699.9 34.9 %collective-permute-start.28 = (bf16[304,2048]{1,0:T(8,128)(2,1)S(1)}, bf16[304,2048]{1,0:T(8,128)(2,1)S(1)}, u32[]{:S(2)}, u32[]{:S(2)}) collective-permute-start(bf16[304,2048]{1,0:T(8,128)(2,1)S(1)} %collective-permute-done.26), channel_id=1, source_target_pairs={{2,3},{6,7},{10,11},{14,15},{18,19},{22,23},{26,27},{30,31}} | collective-permute-start | bytes 3735560 | tf_op jit(solution)/shard_map/ppermute | solution.py:175
  726.1 23.9 %collective-permute-start.29 = (bf16[304,2048]{1,0:T(8,128)(2,1)S(1)}, bf16[304,2048]{1,0:T(8,128)(2,1)S(1)}, u32[]{:S(2)}, u32[]{:S(2)}) collective-permute-start(bf16[304,2048]{1,0:T(8,128)(2,1)S(1)} %collective-permute-done.27), channel_id=1, source_target_pairs={{1,0},{5,4},{9,8},{13,12},{17,16},{21,20},{25,24},{29,28}} | collective-permute-start | bytes 3735560 | tf_op jit(solution)/shard_map/ppermute | solution.py:178
  752.3 55.9 %collective-permute-start.30 = (bf16[304,2048]{1,0:T(8,128)(2,1)S(1)}, bf16[304,2048]{1,0:T(8,128)(2,1)S(1)}, u32[]{:S(2)}, u32[]{:S(2)}) collective-permute-start(bf16[304,2048]{1,0:T(8,128)(2,1)S(1)} %get-tuple-element.170), channel_id=1, source_target_pairs={{0,1},{1,2},{2,3},{4,5},{5,6},{6,7},{8,9},{9,10},{10,11},{12,13},{... | collective-permute-start | bytes 3735560 | tf_op jit(solution)/shard_map/ppermute | solution.py:175
  753.8 84.2 %collective-permute-start.31 = (bf16[304,2048]{1,0:T(8,128)(2,1)S(1)}, bf16[304,2048]{1,0:T(8,128)(2,1)}, u32[]{:S(2)}, u32[]{:S(2)}) collective-permute-start(bf16[304,2048]{1,0:T(8,128)(2,1)S(1)} %get-tuple-element.170), channel_id=1, source_target_pairs={{1,0},{2,1},{3,2},{5,4},{6,5},{7,6},{9,8},{10,9},{11,10},{13,12},{... | collective-permute-start | bytes 3735560 | tf_op jit(solution)/shard_map/ppermute | solution.py:178
  808.2 31.1 %collective-permute-start.32 = (bf16[304,2048]{1,0:T(8,128)(2,1)S(1)}, bf16[304,2048]{1,0:T(8,128)(2,1)}, u32[]{:S(2)}, u32[]{:S(2)}) collective-permute-start(bf16[304,2048]{1,0:T(8,128)(2,1)S(1)} %collective-permute-done.30), channel_id=1, source_target_pairs={{1,2},{2,3},{5,6},{6,7},{9,10},{10,11},{13,14},{14,15},{17,18},{18... | collective-permute-start | bytes 3735560 | tf_op jit(solution)/shard_map/ppermute | solution.py:175
  837.9 275.7 %reduce-scatter.27.cloned.1.call-start = ((), (), s32[]{:S(2)}) async-start(), calls=%async_computation.24 | async-start | bytes 6225920 | tf_op jit(solution)/shard_map/reduce_scatter | solution.py:378
  838.0 97.5 %collective-permute-start.33 = (bf16[304,2048]{1,0:T(8,128)(2,1)}, bf16[304,2048]{1,0:T(8,128)(2,1)S(1)}, u32[]{:S(2)}, u32[]{:S(2)}) collective-permute-start(bf16[304,2048]{1,0:T(8,128)(2,1)} %collective-permute-done.31), channel_id=1, source_target_pairs={{1,0},{2,1},{5,4},{6,5},{9,8},{10,9},{13,12},{14,13},{17,16},{18,1... | collective-permute-start | bytes 3735560 | tf_op jit(solution)/shard_map/ppermute | solution.py:178
  839.3 107.8 %collective-permute-start.34 = (bf16[304,2048]{1,0:T(8,128)(2,1)}, bf16[304,2048]{1,0:T(8,128)(2,1)S(1)}, u32[]{:S(2)}, u32[]{:S(2)}) collective-permute-start(bf16[304,2048]{1,0:T(8,128)(2,1)} %collective-permute-done.32), channel_id=1, source_target_pairs={{2,3},{6,7},{10,11},{14,15},{18,19},{22,23},{26,27},{30,31}} | collective-permute-start | bytes 3735560 | tf_op jit(solution)/shard_map/ppermute | solution.py:175
  935.5 34.1 %collective-permute-start.35 = (bf16[304,2048]{1,0:T(8,128)(2,1)S(1)}, bf16[304,2048]{1,0:T(8,128)(2,1)S(1)}, u32[]{:S(2)}, u32[]{:S(2)}) collective-permute-start(bf16[304,2048]{1,0:T(8,128)(2,1)S(1)} %collective-permute-done.33), channel_id=1, source_target_pairs={{1,0},{5,4},{9,8},{13,12},{17,16},{21,20},{25,24},{29,28}} | collective-permute-start | bytes 3735560 | tf_op jit(solution)/shard_map/ppermute | solution.py:178
  1025.8 180.1 %reduce-scatter.21.cloned.1.call-start = ((), (), s32[]{:S(2)}) async-start(), calls=%async_computation.21 | async-start | bytes 6225920 | tf_op jit(solution)/shard_map/reduce_scatter | solution.py:378
  1042.0 677.7 %reduce-scatter.41.cloned.1.call-start = ((), (), s32[]{:S(2)}) async-start(), calls=%async_computation.31 | async-start | bytes 9437184 | tf_op jit(solution)/shard_map/reduce_scatter | solution.py:411
  1212.5 29.9 %collective-permute-start.36 = (bf16[304,2048]{1,0:T(8,128)(2,1)S(1)}, bf16[304,2048]{1,0:T(8,128)(2,1)S(1)}, u32[]{:S(2)}, u32[]{:S(2)}) collective-permute-start(bf16[304,2048]{1,0:T(8,128)(2,1)S(1)} %get-tuple-element.175), channel_id=1, source_target_pairs={{0,1},{1,2},{2,3},{4,5},{5,6},{6,7},{8,9},{9,10},{10,11},{12,13},{... | collective-permute-start | bytes 3735560 | tf_op jit(solution)/shard_map/ppermute | solution.py:175
  1217.3 45.0 %collective-permute-start.37 = (bf16[304,2048]{1,0:T(8,128)(2,1)S(1)}, bf16[304,2048]{1,0:T(8,128)(2,1)S(1)}, u32[]{:S(2)}, u32[]{:S(2)}) collective-permute-start(bf16[304,2048]{1,0:T(8,128)(2,1)S(1)} %get-tuple-element.175), channel_id=1, source_target_pairs={{1,0},{2,1},{3,2},{5,4},{6,5},{7,6},{9,8},{10,9},{11,10},{13,12},{... | collective-permute-start | bytes 3735560 | tf_op jit(solution)/shard_map/ppermute | solution.py:178
  1242.4 21.2 collective-permute-start.38
  1262.3 33.9 %collective-permute-start.39 = (bf16[304,2048]{1,0:T(8,128)(2,1)S(1)}, bf16[304,2048]{1,0:T(8,128)(2,1)}, u32[]{:S(2)}, u32[]{:S(2)}) collective-permute-start(bf16[304,2048]{1,0:T(8,128)(2,1)S(1)} %collective-permute-done.37), channel_id=1, source_target_pairs={{1,0},{2,1},{5,4},{6,5},{9,8},{10,9},{13,12},{14,13},{17,16},{18,1... | collective-permute-start | bytes 3735560 | tf_op jit(solution)/shard_map/ppermute | solution.py:178
  1263.6 37.9 %collective-permute-start.40 = (bf16[304,2048]{1,0:T(8,128)(2,1)}, bf16[304,2048]{1,0:T(8,128)(2,1)}, u32[]{:S(2)}, u32[]{:S(2)}) collective-permute-start(bf16[304,2048]{1,0:T(8,128)(2,1)} %collective-permute-done.38), channel_id=1, source_target_pairs={{2,3},{6,7},{10,11},{14,15},{18,19},{22,23},{26,27},{30,31}} | collective-permute-start | bytes 3735560 | tf_op jit(solution)/shard_map/ppermute | solution.py:175
  1282.4 443.3 %reduce-scatter.35.cloned.1.call-start = ((), (), s32[]{:S(2)}) async-start(), calls=%async_computation.28 | async-start | bytes 1179648 | tf_op jit(solution)/shard_map/reduce_scatter | solution.py:398
  1296.3 29.4 %collective-permute-start.41 = (bf16[304,2048]{1,0:T(8,128)(2,1)}, bf16[304,2048]{1,0:T(8,128)(2,1)S(1)}, u32[]{:S(2)}, u32[]{:S(2)}) collective-permute-start(bf16[304,2048]{1,0:T(8,128)(2,1)} %collective-permute-done.39), channel_id=1, source_target_pairs={{1,0},{5,4},{9,8},{13,12},{17,16},{21,20},{25,24},{29,28}} | collective-permute-start | bytes 3735560 | tf_op jit(solution)/shard_map/ppermute | solution.py:178
  1326.0 101.3 %collective-permute-start.42 = (bf16[304,2048]{1,0:T(8,128)(2,1)}, bf16[304,2048]{1,0:T(8,128)(2,1)}, u32[]{:S(2)}, u32[]{:S(2)}) collective-permute-start(bf16[304,2048]{1,0:T(8,128)(2,1)} %get-tuple-element.176), channel_id=1, source_target_pairs={{0,1},{1,2},{2,3},{4,5},{5,6},{6,7},{8,9},{9,10},{10,11},{12,13},{... | collective-permute-start | bytes 3735560 | tf_op jit(solution)/shard_map/ppermute | solution.py:175
  1328.8 99.4 %collective-permute-start.43 = (bf16[304,2048]{1,0:T(8,128)(2,1)}, bf16[304,2048]{1,0:T(8,128)(2,1)}, u32[]{:S(2)}, u32[]{:S(2)}) collective-permute-start(bf16[304,2048]{1,0:T(8,128)(2,1)} %get-tuple-element.176), channel_id=1, source_target_pairs={{1,0},{2,1},{3,2},{5,4},{6,5},{7,6},{9,8},{10,9},{11,10},{13,12},{... | collective-permute-start | bytes 3735560 | tf_op jit(solution)/shard_map/ppermute | solution.py:178
  1428.2 30.3 %collective-permute-start.45 = (bf16[304,2048]{1,0:T(8,128)(2,1)}, bf16[304,2048]{1,0:T(8,128)(2,1)S(1)}, u32[]{:S(2)}, u32[]{:S(2)}) collective-permute-start(bf16[304,2048]{1,0:T(8,128)(2,1)} %collective-permute-done.43), channel_id=1, source_target_pairs={{1,0},{2,1},{5,4},{6,5},{9,8},{10,9},{13,12},{14,13},{17,16},{18,1... | collective-permute-start | bytes 3735560 | tf_op jit(solution)/shard_map/ppermute | solution.py:178
  1432.2 31.5 %collective-permute-start.46 = (bf16[304,2048]{1,0:T(8,128)(2,1)S(1)}, bf16[304,2048]{1,0:T(8,128)(2,1)S(1)}, u32[]{:S(2)}, u32[]{:S(2)}) collective-permute-start(bf16[304,2048]{1,0:T(8,128)(2,1)S(1)} %collective-permute-done.44), channel_id=1, source_target_pairs={{2,3},{6,7},{10,11},{14,15},{18,19},{22,23},{26,27},{30,31}} | collective-permute-start | bytes 3735560 | tf_op jit(solution)/shard_map/ppermute | solution.py:175
  1458.6 27.9 %collective-permute-start.47 = (bf16[304,2048]{1,0:T(8,128)(2,1)S(1)}, bf16[304,2048]{1,0:T(8,128)(2,1)S(1)}, u32[]{:S(2)}, u32[]{:S(2)}) collective-permute-start(bf16[304,2048]{1,0:T(8,128)(2,1)S(1)} %collective-permute-done.45), channel_id=1, source_target_pairs={{1,0},{5,4},{9,8},{13,12},{17,16},{21,20},{25,24},{29,28}} | collective-permute-start | bytes 3735560 | tf_op jit(solution)/shard_map/ppermute | solution.py:178
  1592.6 136.4 %reduce-scatter.33.cloned.1.call-start = ((), (), s32[]{:S(2)}) async-start(), calls=%async_computation.27 | async-start | bytes 2359296 | tf_op jit(solution)/shard_map/reduce_scatter | solution.py:395
  1602.6 129.7 %reduce-scatter.37.cloned.1.call-start = ((), (), s32[]{:S(2)}) async-start(), calls=%async_computation.29 | async-start | bytes 2359296 | tf_op jit(solution)/shard_map/reduce_scatter | solution.py:403
  1644.1 191.8 %reduce-scatter.39.cloned.1.call-start = ((), (), s32[]{:S(2)}) async-start(), calls=%async_computation.30 | async-start | bytes 18874368 | tf_op jit(solution)/shard_map/reduce_scatter | solution.py:406
  1675.2 253.0 %reduce-scatter.31.cloned.1.call-start = ((), (), s32[]{:S(2)}) async-start(), calls=%async_computation.26 | async-start | bytes 6225920 | tf_op jit(solution)/shard_map/reduce_scatter | solution.py:378
  1684.0 336.4 %reduce-scatter.29.cloned.1.call-start = ((), (), s32[]{:S(2)}) async-start(), calls=%async_computation.25 | async-start | bytes 6225920 | tf_op jit(solution)/shard_map/reduce_scatter | solution.py:378
  1690.7 422.4 %reduce-scatter.23.cloned.1.call-start = ((), (), s32[]{:S(2)}) async-start(), calls=%async_computation.22 | async-start | bytes 6225920 | tf_op jit(solution)/shard_map/reduce_scatter | solution.py:378
  1706.8 444.6 %reduce-scatter.43.cloned.1.call-start = ((), (), s32[]{:S(2)}) async-start(), calls=%async_computation.32 | async-start | bytes 589824
  (174 other events, 5423.4 us)
Sparse Core Ops, SparseCore 0:
  10.5 30.4 all-gather.7
  43.5 23.3 all-gather.5
  69.3 28.0 all-gather.9
  305.1 86.8 reduce-scatter.18
  394.1 90.0 reduce-scatter.16
  486.5 90.2 all-gather.11
  579.3 55.8 all-gather.13
  838.0 125.7 reduce-scatter.24
  1025.9 87.6 reduce-scatter.26
  1115.8 90.0 reduce-scatter.20
  1282.5 83.4 reduce-scatter.40
  1592.7 33.8 reduce-scatter.34
  1630.4 41.1 reduce-scatter.32
  1675.3 41.1 reduce-scatter.36
  1719.9 115.9 reduce-scatter.38
  1838.6 89.5 reduce-scatter.30
  1930.4 90.0 reduce-scatter.28
  2022.6 90.5 reduce-scatter.22
  2116.8 34.5 reduce-scatter.42

commit v11 on v10

--- a/solution.py
+++ b/solution.py
@@ -280,9 +280,10 @@
         values = keyval_raw[:, :, HD:].astype(jnp.bfloat16)
         mixed_full, log_totals = attend(queries, key_rows, values, visible, block_rows)
         mixed = mixed_full.astype(jnp.bfloat16).reshape(group_rows, query_heads * HD)
-        attn_branch = yield (
-            "scatter", jnp.dot(mixed, full_output, preferred_element_type=jnp.float32)
-        )
+        attn_partial, _, _ = lax.optimization_barrier(
+            (jnp.dot(mixed, full_output, preferred_element_type=jnp.float32), full_gateup, full_down)
+        )
+        attn_branch = yield ("offload_scatter", attn_partial)
         middle = start_rows + branch_scale * attn_branch
         scale_two = lax.rsqrt(jnp.mean(middle * middle, axis=1, keepdims=True) + norm_eps)
         hat_two = middle * scale_two
@@ -300,7 +301,7 @@
         ffn_grad = (branch_scale * upstream).astype(jnp.bfloat16)
         ffn_grad_all = yield ("gather", ffn_grad)
         ffn_branch = yield (
-            "scatter", jnp.dot(hidden_state, full_down, preferred_element_type=jnp.float32)
+            "offload_scatter", jnp.dot(hidden_state, full_down, preferred_element_type=jnp.float32)
         )
         layer_rows = (middle + branch_scale * ffn_branch).astype(jnp.bfloat16)
         grad_down = contract_rows(hidden_state, ffn_grad_all)
@@ -312,7 +313,7 @@
             "rd,rcf->dcf", rows_two, gateup_grad, preferred_element_type=jnp.float32
         )
         normed_two_grad = yield (
-            "scatter",
+            "offload_scatter",
             jnp.einsum(
                 "rcf,dcf->rd", gateup_grad, full_gateup, preferred_element_type=jnp.float32
             ),
@@ -374,6 +375,8 @@
                 previous, value = lax.optimization_barrier((previous, value))
             if kind == "gather":
                 previous = line_gather(value, tensor_count)
+            elif kind == "scatter":
+                previous = line_scatter(value, tensor_count)
             else:
                 previous = lax.psum_scatter(
                     value.astype(jnp.bfloat16), "tensor", scatter_dimension=0, tiled=True

time: 2230 us -> 2090 us (0.937)
  waiting for transfers between devices: 1170 us -> 982 us
  starting transfers between devices: 73.4 us -> 109 us
  other arithmetic: 196 us -> 219 us
    reduce_scatter x8 -> x6, waiting for transfers between devices: 502 us -> 291 us  [per_device(): lax.psum_scatter(value.astype(jnp.bfloat16), 'tensor', scatter_dimension=...]
    ppermute x0 -> x12, waiting for transfers between devices: none -> 154 us  [the longest x6 118 us: line_scatter(): lax.ppermute(send.astype(jnp.bfloat16), 'tensor', [(i, i + 1) for i in ra...]
    reduce_scatter x1, waiting for transfers between devices: 100 us -> 0.01 us  [per_device(): lax.psum_scatter(totals[3].reshape(width, -1).astype(jnp.bfloat16), 'dp',...]
    ppermute x0 -> x12, starting transfers between devices: none -> 36.8 us  [the longest x6 27.5 us: line_scatter(): lax.ppermute(send.astype(jnp.bfloat16), 'tensor', [(i, i + 1) for i in ra...]
    ppermute x24, waiting for transfers between devices: 412 us -> 389 us  [line_gather(): lax.ppermute(from_right, 'tensor', [(i, i - 1) for i in range(1, count -...]
  transfers between devices with their start and end apart: 67 -> 77, of which waited for: 36 -> 38; matrix products, arithmetic and copies ran while one was open for 37% -> 40% of each run, Pallas kernels for 0% -> 0%
where the time goes in v11:
time: 2090 us; the launch traced here: 2080 us
  waiting for transfers between devices  982 us (47%)
  matrix products  542 us (26%)
  other arithmetic  219 us (10%)
  local copies, waits for them, and re-layouts  131 us (6%)
  starting transfers between devices  109 us (5%)
  blocking collectives  71.7 us (3%)
  between operations  21 us (1%)
    ppermute x24, waiting for transfers between devices, line_gather(): lax.ppermute(from_right, 'tensor', [(i, i - 1) for i in range(1, count -...  389 us
    reduce_scatter x6, waiting for transfers between devices, per_device(): lax.psum_scatter(value.astype(jnp.bfloat16), 'tensor', scatter_dimension=...  291 us
    ppermute x24, waiting for transfers between devices, line_gather(): lax.ppermute(from_left, 'tensor', [(i, i + 1) for i in range(step - 1, co...  126 us
    ppermute x6, waiting for transfers between devices, line_scatter(): lax.ppermute(send.astype(jnp.bfloat16), 'tensor', [(i, i + 1) for i in ra...  118 us
    dot_general x6, matrix products, contract_cols(): lax.dot_general(left, right, (((1,), (1,)), ((), ())), preferred_element_...  63.5 us
    dot_general x2, matrix products, micro_step(): jnp.einsum('rd,rcf->dcf', rows_two, gateup_grad, preferred_element_type=j...  60.4 us
    dot_general x4, matrix products, attend_back(): jnp.einsum('ikrd,jkd->krij', grad_block, values[:stop], preferred_element...  60.2 us
    dot_general x6, matrix products, contract_rows(): lax.dot_general(left, right, (((0,), (0,)), ((), ())), preferred_element_...  59.2 us
  transfers between devices with their start and end apart: 77, of which 38 were waited for; matrix products, arithmetic and copies ran while one was open for 40% of the time, Pallas kernels for 0%

profile of v11, /device:TPU:0, one launch (start us, length us, event | category | flops | bytes accessed | tf_op | source)
XLA Modules:
  0.0 2075.8 jit_solution(8875062472662617211)
XLA Ops:
  25.4 10.4 all_gather.18
  44.5 25.5 %collective-permute-done = bf16[304,2048]{1,0:T(8,128)(2,1)S(1)} collective-permute-done((bf16[304,2048]{1,0:T(8,128)(2,1)}, bf16[304,2048]{1,0:T(8,128)(2,1)S(1)}, u32[]{:S(2)}, u32[]{:S(2)}) %collective-permute-start) | collective-permute-done | bytes 1245216 | tf_op jit(solution)/shard_map/ppermute | solution.py:175
  78.4 29.6 %collective-permute-done.3 = bf16[304,2048]{1,0:T(8,128)(2,1)S(1)} collective-permute-done((bf16[304,2048]{1,0:T(8,128)(2,1)}, bf16[304,2048]{1,0:T(8,128)(2,1)S(1)}, u32[]{:S(2)}, u32[]{:S(2)}) %collective-permute-start.3) | collective-permute-done | bytes 1245216 | tf_op jit(solution)/shard_map/ppermute | solution.py:178
  113.3 24.6 %collective-permute-done.5 = bf16[304,2048]{1,0:T(8,128)(2,1)S(1)} collective-permute-done((bf16[304,2048]{1,0:T(8,128)(2,1)S(1)}, bf16[304,2048]{1,0:T(8,128)(2,1)S(1)}, u32[]{:S(2)}, u32[]{:S(2)}) %collective-permute-start.5) | collective-permute-done | bytes 1245216 | tf_op jit(solution)/shard_map/ppermute | solution.py:178
  149.5 7.5 fusion.232
  157.0 9.1 collective-permute-done.6
  189.2 17.1 collective-permute-done.9
  214.3 19.6 collective-permute-done.11
  279.8 12.2 fusion.135
  328.6 12.3 fusion.136
  347.0 39.8 %reduce-scatter.17.cloned.1.call-done = bf16[304,2048]{1,0:T(8,128)(2,1)} async-done(((bf16[1216,2048]{1,0:T(8,128)(2,1)}), bf16[304,2048]{1,0:T(8,128)(2,1)}) %reduce-scatter.17.cloned.1.call-update) | async-done | bytes 1245200 | tf_op jit(solution)/shard_map/reduce_scatter | solution.py:381
  386.8 92.4 %reduce-scatter.15.cloned.1.call-done = bf16[304,2048]{1,0:T(8,128)(2,1)} async-done(((bf16[1216,2048]{1,0:T(8,128)(2,1)}), bf16[304,2048]{1,0:T(8,128)(2,1)}) %reduce-scatter.15.cloned.1.call-update) | async-done | bytes 1245200 | tf_op jit(solution)/shard_map/reduce_scatter | solution.py:381
  488.4 25.2 %collective-permute-done.12 = bf16[304,2048]{1,0:T(8,128)(2,1)S(1)} collective-permute-done((bf16[304,2048]{1,0:T(8,128)(2,1)S(1)}, bf16[304,2048]{1,0:T(8,128)(2,1)S(1)}, u32[]{:S(2)}, u32[]{:S(2)}) %collective-permute-start.12) | collective-permute-done | bytes 1245216 | tf_op jit(solution)/shard_map/ppermute | solution.py:175
  520.0 28.1 %collective-permute-done.15 = bf16[304,2048]{1,0:T(8,128)(2,1)S(1)} collective-permute-done((bf16[304,2048]{1,0:T(8,128)(2,1)S(1)}, bf16[304,2048]{1,0:T(8,128)(2,1)S(1)}, u32[]{:S(2)}, u32[]{:S(2)}) %collective-permute-start.15) | collective-permute-done | bytes 1245216 | tf_op jit(solution)/shard_map/ppermute | solution.py:178
  551.3 26.0 %collective-permute-done.17 = bf16[304,2048]{1,0:T(8,128)(2,1)S(1)} collective-permute-done((bf16[304,2048]{1,0:T(8,128)(2,1)S(1)}, bf16[304,2048]{1,0:T(8,128)(2,1)S(1)}, u32[]{:S(2)}, u32[]{:S(2)}) %collective-permute-start.17) | collective-permute-done | bytes 1245216 | tf_op jit(solution)/shard_map/ppermute | solution.py:178
  580.5 22.7 %collective-permute-done.18 = bf16[304,2048]{1,0:T(8,128)(2,1)S(1)} collective-permute-done((bf16[304,2048]{1,0:T(8,128)(2,1)S(1)}, bf16[304,2048]{1,0:T(8,128)(2,1)S(1)}, u32[]{:S(2)}, u32[]{:S(2)}) %collective-permute-start.18) | collective-permute-done | bytes 1245216 | tf_op jit(solution)/shard_map/ppermute | solution.py:175
  609.9 25.0 %collective-permute-done.21 = bf16[304,2048]{1,0:T(8,128)(2,1)S(1)} collective-permute-done((bf16[304,2048]{1,0:T(8,128)(2,1)S(1)}, bf16[304,2048]{1,0:T(8,128)(2,1)S(1)}, u32[]{:S(2)}, u32[]{:S(2)}) %collective-permute-start.21) | collective-permute-done | bytes 1245216 | tf_op jit(solution)/shard_map/ppermute | solution.py:178
  637.7 23.7 %collective-permute-done.23 = bf16[304,2048]{1,0:T(8,128)(2,1)S(1)} collective-permute-done((bf16[304,2048]{1,0:T(8,128)(2,1)S(1)}, bf16[304,2048]{1,0:T(8,128)(2,1)S(1)}, u32[]{:S(2)}, u32[]{:S(2)}) %collective-permute-start.23) | collective-permute-done | bytes 1245216 | tf_op jit(solution)/shard_map/ppermute | solution.py:178
  664.6 20.0 collective-permute-done.24
  692.9 26.0 %fusion.59 = f32[1216,2,2048]{2,0,1:T(8,128)} fusion(bf16[2048,2,2048]{2,0,1:T(8,128)(2,1)} %all-gather.12.cloned.1.call-done, bf16[1216,2048]{1,0:T(8,128)(2,1)S(1)} %constant_dynamic-update-slice_fusion.35), kind=kOutput, calls=%fused_computation.103 | convolution fusion | flops 20401094656 | bytes 41680896 | tf_op jit(solution)/shard_map/rd,dcf->rcf/dot_general | solution.py:292
  728.9 31.1 %collective-permute-done.29 = bf16[304,2048]{1,0:T(8,128)(2,1)S(1)} collective-permute-done((bf16[304,2048]{1,0:T(8,128)(2,1)S(1)}, bf16[304,2048]{1,0:T(8,128)(2,1)S(1)}, u32[]{:S(2)}, u32[]{:S(2)}) %collective-permute-start.29) | collective-permute-done | bytes 1245216 | tf_op jit(solution)/shard_map/ppermute | solution.py:178
  764.2 26.0 %fusion.56 = f32[1216,2,2048]{2,0,1:T(8,128)} fusion(bf16[2048,2,2048]{2,0,1:T(8,128)(2,1)} %all-gather.12.cloned.1.call-done, bf16[1216,2048]{1,0:T(8,128)(2,1)S(1)} %constant_dynamic-update-slice_fusion.28), kind=kOutput, calls=%fused_computation.100 | convolution fusion | flops 20401094656 | bytes 41680896 | tf_op jit(solution)/shard_map/rd,dcf->rcf/dot_general | solution.py:292
  793.2 25.6 %fusion.69 = (bf16[1216,1,2048]{2,0,1:T(8,128)(2,1)}, bf16[1216,1,2048]{2,0,1:T(8,128)(2,1)}, bf16[1216,2048]{1,0:T(8,128)(2,1)}) fusion(f32[1216,2,2048]{2,0,1:T(8,128)} %fusion.59, bf16[1216,2048]{1,0:T(8,128)(2,1)} %constant_dynamic-update-slice_fusion.21, bf16[2048,2048]{1,0:T(8,128)(2,1)} %all-gather.14.cloned.1.call-done), kind=kOutput, calls=%fused_computation.113 | convolution fusion | flops 10237902848 | bytes 48234496 | tf_op jit(solution)/shard_map/dot_general | solution.py:162
  821.8 27.7 %convolution_bitcast_fusion.1 = bf16[1216,2048]{1,0:T(8,128)(2,1)} fusion(bf16[2048,2,2048]{2,0,1:T(8,128)(2,1)} %all-gather.12.cloned.1.call-done, bf16[1216,1,2048]{2,0,1:T(8,128)(2,1)} %get-tuple-element.335, bf16[1216,1,2048]{2,0,1:T(8,128)(2,1)} %get-tuple-element.334), kind=kOutput, calls=%fused_computation.81 | convolution fusion | flops 20406075392 | bytes 31719424 | tf_op jit(solution)/shard_map/rcf,dcf->rd/dot_general | solution.py:317
  865.2 64.0 %collective-permute-done.35 = bf16[304,2048]{1,0:T(8,128)(2,1)S(1)} collective-permute-done((bf16[304,2048]{1,0:T(8,128)(2,1)}, bf16[304,2048]{1,0:T(8,128)(2,1)S(1)}, u32[]{:S(2)}, u32[]{:S(2)}) %collective-permute-start.35) | collective-permute-done | bytes 1245216 | tf_op jit(solution)/shard_map/ppermute | solution.py:178
  931.4 26.0 %fusion.70 = (bf16[1216,1,2048]{2,0,1:T(8,128)(2,1)}, bf16[1216,1,2048]{2,0,1:T(8,128)(2,1)}, bf16[1216,2048]{1,0:T(8,128)(2,1)}) fusion(f32[1216,2,2048]{2,0,1:T(8,128)} %fusion.56, bf16[1216,2048]{1,0:T(8,128)(2,1)} %constant_dynamic-update-slice_fusion.14, bf16[2048,2048]{1,0:T(8,128)(2,1)} %all-gather.14.cloned.1.call-done), kind=kOutput, calls=%fused_computation.114 | convolution fusion | flops 10237902848 | bytes 48234496 | tf_op jit(solution)/shard_map/dot_general | solution.py:162
  957.5 27.8 %convolution_bitcast_fusion = bf16[1216,2048]{1,0:T(8,128)(2,1)} fusion(bf16[2048,2,2048]{2,0,1:T(8,128)(2,1)} %all-gather.12.cloned.1.call-done, bf16[1216,1,2048]{2,0,1:T(8,128)(2,1)} %get-tuple-element.333, bf16[1216,1,2048]{2,0,1:T(8,128)(2,1)} %get-tuple-element.332), kind=kOutput, calls=%fused_computation.80 | convolution fusion | flops 20406075392 | bytes 31719424 | tf_op jit(solution)/shard_map/rcf,dcf->rd/dot_general | solution.py:317
  985.3 16.3 fusion.234
  1001.7 71.6 %reduce-scatter.25.cloned.1.call-done = bf16[304,2048]{1,0:T(8,128)(2,1)} async-done(((bf16[1216,2048]{1,0:T(8,128)(2,1)}), bf16[304,2048]{1,0:T(8,128)(2,1)}) %reduce-scatter.25.cloned.1.call-update) | async-done | bytes 1245200 | tf_op jit(solution)/shard_map/reduce_scatter | solution.py:381
  1078.5 87.1 %reduce-scatter.19.cloned.1.call-done = bf16[304,2048]{1,0:T(8,128)(2,1)} async-done(((bf16[1216,2048]{1,0:T(8,128)(2,1)}), bf16[304,2048]{1,0:T(8,128)(2,1)}) %reduce-scatter.19.cloned.1.call-update) | async-done | bytes 1245200 | tf_op jit(solution)/shard_map/reduce_scatter | solution.py:381
  1178.3 23.9 %collective-permute-done.36 = bf16[304,2048]{1,0:T(8,128)(2,1)S(1)} collective-permute-done((bf16[304,2048]{1,0:T(8,128)(2,1)S(1)}, bf16[304,2048]{1,0:T(8,128)(2,1)S(1)}, u32[]{:S(2)}, u32[]{:S(2)}) %collective-permute-start.36) | collective-permute-done | bytes 1245216 | tf_op jit(solution)/shard_map/ppermute | solution.py:175
  1203.9 18.2 fusion.237
  1225.1 17.0 add_convert_fusion.1
  1242.2 13.8 collective-permute-done.39
  1263.2 22.3 %collective-permute-done.41 = bf16[304,2048]{1,0:T(8,128)(2,1)S(1)} collective-permute-done((bf16[304,2048]{1,0:T(8,128)(2,1)}, bf16[304,2048]{1,0:T(8,128)(2,1)S(1)}, u32[]{:S(2)}, u32[]{:S(2)}) %collective-permute-start.41) | collective-permute-done | bytes 1245216 | tf_op jit(solution)/shard_map/ppermute | solution.py:178
  1293.3 7.1 fusion.143
  1300.4 9.6 fusion.19
  1310.3 10.3 fusion.21
  1325.9 21.1 %fusion.3 = (f32[2,4,608]{2,1,0:T(4,128)S(1)}, f32[2,1216,608,4]{2,1,3,0:T(8,128)}) fusion(f32[2,1216,608,4]{2,1,3,0:T(8,128)} %copy-done.1, f32[2,4,608]{2,1,0:T(4,128)S(1)} %bitcast.680, pred[608,1216]{0,1:T(8,128)(4,1)S(1)} %copy-done.16, bf16[608,2,4,64]{0,3,2,1:T(8,128)(2,1)S(1)} %bitcast.653, bf16[1216,2,128]{2,0,1:T(8,128)(2,1)S(1)} %copy-done.87), kind=kOutput, calls=%fused_computation.8 | convolution fusion | flops 786640128 | bytes 49340416 | tf_op jit(solution)/shard_map/ikrd,jkd->krij/dot_general | solution.py:119
  1347.1 17.2 fusion.5
  1375.3 12.0 fusion.125
  1394.1 24.3 %collective-permute-done.45 = bf16[304,2048]{1,0:T(8,128)(2,1)S(1)} collective-permute-done((bf16[304,2048]{1,0:T(8,128)(2,1)}, bf16[304,2048]{1,0:T(8,128)(2,1)S(1)}, u32[]{:S(2)}, u32[]{:S(2)}) %collective-permute-start.45) | collective-permute-done | bytes 1245216 | tf_op jit(solution)/shard_map/ppermute | solution.py:178
  1423.7 22.6 %collective-permute-done.47 = bf16[304,2048]{1,0:T(8,128)(2,1)S(1)} collective-permute-done((bf16[304,2048]{1,0:T(8,128)(2,1)S(1)}, bf16[304,2048]{1,0:T(8,128)(2,1)S(1)}, u32[]{:S(2)}, u32[]{:S(2)}) %collective-permute-start.47) | collective-permute-done | bytes 1245216 | tf_op jit(solution)/shard_map/ppermute | solution.py:178
  1452.3 11.5 fusion.16
  1476.7 18.0 fusion
  1494.7 17.0 fusion.2
  1521.5 8.5 fusion.118
  1534.4 11.3 fusion.122
  1564.5 29.6 %fusion.42 = f32[2048,2,2048]{0,2,1:T(8,128)} fusion(bf16[1216,1,2048]{2,0,1:T(8,128)(2,1)} %get-tuple-element.333, bf16[1216,1,2048]{2,0,1:T(8,128)(2,1)} %get-tuple-element.332, bf16[1216,2048]{1,0:T(8,128)(2,1)} %copy-done.54), kind=kOutput, calls=%fused_computation.84 | convolution fusion | flops 20421017600 | bytes 48496640 | tf_op jit(solution)/shard_map/rd,rcf->dcf/dot_general | solution.py:312
  1599.2 7.0 add_convert_fusion.2
  1606.3 30.8 %add_convert_fusion = bf16[2048,2,2048]{0,2,1:T(8,128)(2,1)} fusion(f32[2048,2,2048]{0,2,1:T(8,128)} %fusion.42, bf16[1216,1,2048]{2,0,1:T(8,128)(2,1)} %get-tuple-element.335, bf16[1216,1,2048]{2,0,1:T(8,128)(2,1)} %get-tuple-element.334, bf16[1216,2048]{1,0:T(8,128)(2,1)} %copy-done.53), kind=kOutput, calls=%fused_computation | convolution fusion | flops 20437794816 | bytes 65273856 | tf_op jit(solution)/shard_map/rd,rcf->dcf/dot_general | solution.py:312
  1651.5 20.8 %collective-permute-done.48 = bf16[304,2048]{1,0:T(8,128)(2,1)S(1)} collective-permute-done((bf16[304,2048]{1,0:T(8,128)(2,1)S(1)}, bf16[304,2048]{1,0:T(8,128)(2,1)S(1)}, u32[]{:S(2)}, u32[]{:S(2)}) %collective-permute-start.48) | collective-permute-done | bytes 1245216 | tf_op jit(solution)/shard_map/ppermute | solution.py:201
  1679.0 21.4 %collective-permute-done.49 = bf16[304,2048]{1,0:T(8,128)(2,1)S(1)} collective-permute-done((bf16[304,2048]{1,0:T(8,128)(2,1)S(1)}, bf16[304,2048]{1,0:T(8,128)(2,1)S(1)}, u32[]{:S(2)}, u32[]{:S(2)}) %collective-permute-start.49) | collective-permute-done | bytes 1245216 | tf_op jit(solution)/shard_map/ppermute | solution.py:201
  1707.3 15.9 fusion.235
  1739.3 12.2 collective-permute-done.50
  1751.5 8.4 collective-permute-done.53
  1771.1 19.6 collective-permute-done.54
  1807.5 28.0 %collective-permute-done.55 = bf16[304,2048]{1,0:T(8,128)(2,1)} collective-permute-done((bf16[304,2048]{1,0:T(8,128)(2,1)}, bf16[304,2048]{1,0:T(8,128)(2,1)}, u32[]{:S(2)}, u32[]{:S(2)}) %collective-permute-start.55) | collective-permute-done | bytes 1245216 | tf_op jit(solution)/shard_map/ppermute | solution.py:201
  1874.7 17.7 multiply_reduce_fusion
  1892.4 15.5 collective-permute-done.56
  1907.9 28.1 %collective-permute-done.59 = bf16[304,2048]{1,0:T(8,128)(2,1)S(1)} collective-permute-done((bf16[304,2048]{1,0:T(8,128)(2,1)S(1)}, bf16[304,2048]{1,0:T(8,128)(2,1)S(1)}, u32[]{:S(2)}, u32[]{:S(2)}) %collective-permute-start.59) | collective-permute-done | bytes 1245216 | tf_op jit(solution)/shard_map/ppermute | solution.py:207
  1942.4 21.9 %psum.14 = bf16[2,2048]{1,0:T(2,128)(2,1)} all-reduce(f32[2,2048]{1,0:T(2,128)} %maximum_add_fusion), channel_id=1, replica_groups=mesh['dp'=8,'tensor'=4] {'tensor'}, use_global_device_ids=true, to_apply=%region_52.53 | all-reduce | flops 4096 | bytes 24576 | tf_op jit(solution)/shard_map/psum | solution.py:396
  1981.6 21.7 %reduce-scatter.37.cloned.1.call-done = bf16[256,2]{1,0:T(8,128)(2,1)} async-done(((bf16[2048,2]{1,0:T(8,128)(2,1)}), bf16[256,2]{1,0:T(8,128)(2,1)}) %reduce-scatter.37.cloned.1.call-update) | async-done | bytes 1040
  2011.8 39.4 %psum.15 = f32[2,7]{1,0:T(2,128)S(1)} all-reduce(f32[2,7]{1,0:T(2,128)S(1)} %pad_maximum_fusion.26), channel_id=1, replica_groups=mesh['dp'=8,'tensor'=4] {'dp','tensor'}, use_global_device_ids=true, to_apply=%region_55.56 | all-reduce | flops 14 | bytes 112 | tf_op jit(solution)/shard_map/psum | solution.py:444
  (694 shorter events, 531.0 us)
Async XLA Ops:
  7.2 142.3 %all-gather.8.cloned.1.call-start = ((), (), s32[]{:S(2)}) async-start(), calls=%async_computation.13 | async-start | bytes 2359296 | tf_op jit(solution)/shard_map/all_gather | solution.py:244
  9.9 158.0 %all-gather.6.cloned.1.call-start = ((), (), s32[]{:S(2)}) async-start(), calls=%async_computation.12 | async-start | bytes 1179648 | tf_op jit(solution)/shard_map/all_gather | solution.py:245
  11.6 280.5 %all-gather.10.cloned.1.call-start = ((), (), s32[]{:S(2)}) async-start(), calls=%async_computation.14 | async-start | bytes 2359296 | tf_op jit(solution)/shard_map/all_gather | solution.py:246
  14.3 285.4 %all-gather.14.cloned.1.call-start = ((), (), s32[]{:S(2)}) async-start(), calls=%async_computation.16 | async-start | bytes 9437184 | tf_op jit(solution)/shard_map/all_gather | solution.py:248
  18.6 281.0 %all-gather.12.cloned.1.call-start = ((), (), s32[]{:S(2)}) async-start(), calls=%async_computation.15 | async-start | bytes 18874368 | tf_op jit(solution)/shard_map/all_gather | solution.py:247
  24.8 362.1 %reduce-scatter.17.cloned.1.call-start = ((), (), s32[]{:S(2)}) async-start(), calls=%async_computation.18 | async-start | bytes 6225920 | tf_op jit(solution)/shard_map/reduce_scatter | solution.py:381
  39.1 30.9 %collective-permute-start = (bf16[304,2048]{1,0:T(8,128)(2,1)}, bf16[304,2048]{1,0:T(8,128)(2,1)S(1)}, u32[]{:S(2)}, u32[]{:S(2)}) collective-permute-start(bf16[304,2048]{1,0:T(8,128)(2,1)} %get-tuple-element.362), channel_id=1, source_target_pairs={{0,1},{1,2},{2,3},{4,5},{5,6},{6,7},{8,9},{9,10},{10,11},{12,13},{... | collective-permute-start | bytes 3735560 | tf_op jit(solution)/shard_map/ppermute | solution.py:175
  42.6 31.6 %collective-permute-start.1 = (bf16[304,2048]{1,0:T(8,128)(2,1)}, bf16[304,2048]{1,0:T(8,128)(2,1)}, u32[]{:S(2)}, u32[]{:S(2)}) collective-permute-start(bf16[304,2048]{1,0:T(8,128)(2,1)} %get-tuple-element.362), channel_id=1, source_target_pairs={{1,0},{2,1},{3,2},{5,4},{6,5},{7,6},{9,8},{10,9},{11,10},{13,12},{... | collective-permute-start | bytes 3735560 | tf_op jit(solution)/shard_map/ppermute | solution.py:178
  74.2 33.8 %collective-permute-start.3 = (bf16[304,2048]{1,0:T(8,128)(2,1)}, bf16[304,2048]{1,0:T(8,128)(2,1)S(1)}, u32[]{:S(2)}, u32[]{:S(2)}) collective-permute-start(bf16[304,2048]{1,0:T(8,128)(2,1)} %collective-permute-done.1), channel_id=1, source_target_pairs={{1,0},{2,1},{5,4},{6,5},{9,8},{10,9},{13,12},{14,13},{17,16},{18,1... | collective-permute-start | bytes 3735560 | tf_op jit(solution)/shard_map/ppermute | solution.py:178
  77.6 35.5 %collective-permute-start.4 = (bf16[304,2048]{1,0:T(8,128)(2,1)}, bf16[304,2048]{1,0:T(8,128)(2,1)S(1)}, u32[]{:S(2)}, u32[]{:S(2)}) collective-permute-start(bf16[304,2048]{1,0:T(8,128)(2,1)} %collective-permute-done.2), channel_id=1, source_target_pairs={{2,3},{6,7},{10,11},{14,15},{18,19},{22,23},{26,27},{30,31}} | collective-permute-start | bytes 3735560 | tf_op jit(solution)/shard_map/ppermute | solution.py:175
  108.0 29.9 %collective-permute-start.5 = (bf16[304,2048]{1,0:T(8,128)(2,1)S(1)}, bf16[304,2048]{1,0:T(8,128)(2,1)S(1)}, u32[]{:S(2)}, u32[]{:S(2)}) collective-permute-start(bf16[304,2048]{1,0:T(8,128)(2,1)S(1)} %collective-permute-done.3), channel_id=1, source_target_pairs={{1,0},{5,4},{9,8},{13,12},{17,16},{21,20},{25,24},{29,28}} | collective-permute-start | bytes 3735560 | tf_op jit(solution)/shard_map/ppermute | solution.py:178
  139.5 26.7 %collective-permute-start.6 = (bf16[304,2048]{1,0:T(8,128)(2,1)}, bf16[304,2048]{1,0:T(8,128)(2,1)}, u32[]{:S(2)}, u32[]{:S(2)}) collective-permute-start(bf16[304,2048]{1,0:T(8,128)(2,1)} %get-tuple-element.166), channel_id=1, source_target_pairs={{0,1},{1,2},{2,3},{4,5},{5,6},{6,7},{8,9},{9,10},{10,11},{12,13},{... | collective-permute-start | bytes 3735560 | tf_op jit(solution)/shard_map/ppermute | solution.py:175
  148.2 29.5 %collective-permute-start.7 = (bf16[304,2048]{1,0:T(8,128)(2,1)}, bf16[304,2048]{1,0:T(8,128)(2,1)}, u32[]{:S(2)}, u32[]{:S(2)}) collective-permute-start(bf16[304,2048]{1,0:T(8,128)(2,1)} %get-tuple-element.166), channel_id=1, source_target_pairs={{1,0},{2,1},{3,2},{5,4},{6,5},{7,6},{9,8},{10,9},{11,10},{13,12},{... | collective-permute-start | bytes 3735560 | tf_op jit(solution)/shard_map/ppermute | solution.py:178
  177.7 28.6 %collective-permute-start.9 = (bf16[304,2048]{1,0:T(8,128)(2,1)}, bf16[304,2048]{1,0:T(8,128)(2,1)}, u32[]{:S(2)}, u32[]{:S(2)}) collective-permute-start(bf16[304,2048]{1,0:T(8,128)(2,1)} %collective-permute-done.7), channel_id=1, source_target_pairs={{1,0},{2,1},{5,4},{6,5},{9,8},{10,9},{13,12},{14,13},{17,16},{18,1... | collective-permute-start | bytes 3735560 | tf_op jit(solution)/shard_map/ppermute | solution.py:178
  186.2 28.0 %collective-permute-start.10 = (bf16[304,2048]{1,0:T(8,128)(2,1)}, bf16[304,2048]{1,0:T(8,128)(2,1)S(1)}, u32[]{:S(2)}, u32[]{:S(2)}) collective-permute-start(bf16[304,2048]{1,0:T(8,128)(2,1)} %collective-permute-done.8), channel_id=1, source_target_pairs={{2,3},{6,7},{10,11},{14,15},{18,19},{22,23},{26,27},{30,31}} | collective-permute-start | bytes 3735560 | tf_op jit(solution)/shard_map/ppermute | solution.py:175
  206.3 27.6 %collective-permute-start.11 = (bf16[304,2048]{1,0:T(8,128)(2,1)}, bf16[304,2048]{1,0:T(8,128)(2,1)S(1)}, u32[]{:S(2)}, u32[]{:S(2)}) collective-permute-start(bf16[304,2048]{1,0:T(8,128)(2,1)} %collective-permute-done.9), channel_id=1, source_target_pairs={{1,0},{5,4},{9,8},{13,12},{17,16},{21,20},{25,24},{29,28}} | collective-permute-start | bytes 3735560 | tf_op jit(solution)/shard_map/ppermute | solution.py:178
  299.7 179.5 %reduce-scatter.15.cloned.1.call-start = ((), (), s32[]{:S(2)}) async-start(), calls=%async_computation.17 | async-start | bytes 6225920 | tf_op jit(solution)/shard_map/reduce_scatter | solution.py:381
  347.0 654.8 %reduce-scatter.23.cloned.1.call-start = ((), (), s32[]{:S(2)}) async-start(), calls=%async_computation.21 | async-start | bytes 6225920 | tf_op jit(solution)/shard_map/reduce_scatter | solution.py:381
  483.6 29.9 %collective-permute-start.12 = (bf16[304,2048]{1,0:T(8,128)(2,1)S(1)}, bf16[304,2048]{1,0:T(8,128)(2,1)S(1)}, u32[]{:S(2)}, u32[]{:S(2)}) collective-permute-start(bf16[304,2048]{1,0:T(8,128)(2,1)S(1)} %get-tuple-element.171), channel_id=1, source_target_pairs={{0,1},{1,2},{2,3},{4,5},{5,6},{6,7},{8,9},{9,10},{10,11},{12,13},{... | collective-permute-start | bytes 3735560 | tf_op jit(solution)/shard_map/ppermute | solution.py:175
  487.1 30.9 %collective-permute-start.13 = (bf16[304,2048]{1,0:T(8,128)(2,1)S(1)}, bf16[304,2048]{1,0:T(8,128)(2,1)S(1)}, u32[]{:S(2)}, u32[]{:S(2)}) collective-permute-start(bf16[304,2048]{1,0:T(8,128)(2,1)S(1)} %get-tuple-element.171), channel_id=1, source_target_pairs={{1,0},{2,1},{3,2},{5,4},{6,5},{7,6},{9,8},{10,9},{11,10},{13,12},{... | collective-permute-start | bytes 3735560 | tf_op jit(solution)/shard_map/ppermute | solution.py:178
  517.9 30.1 %collective-permute-start.15 = (bf16[304,2048]{1,0:T(8,128)(2,1)S(1)}, bf16[304,2048]{1,0:T(8,128)(2,1)S(1)}, u32[]{:S(2)}, u32[]{:S(2)}) collective-permute-start(bf16[304,2048]{1,0:T(8,128)(2,1)S(1)} %collective-permute-done.13), channel_id=1, source_target_pairs={{1,0},{2,1},{5,4},{6,5},{9,8},{10,9},{13,12},{14,13},{17,16},{18,1... | collective-permute-start | bytes 3735560 | tf_op jit(solution)/shard_map/ppermute | solution.py:178
  519.2 31.9 %collective-permute-start.16 = (bf16[304,2048]{1,0:T(8,128)(2,1)S(1)}, bf16[304,2048]{1,0:T(8,128)(2,1)S(1)}, u32[]{:S(2)}, u32[]{:S(2)}) collective-permute-start(bf16[304,2048]{1,0:T(8,128)(2,1)S(1)} %collective-permute-done.14), channel_id=1, source_target_pairs={{2,3},{6,7},{10,11},{14,15},{18,19},{22,23},{26,27},{30,31}} | collective-permute-start | bytes 3735560 | tf_op jit(solution)/shard_map/ppermute | solution.py:175
  548.1 29.2 %collective-permute-start.17 = (bf16[304,2048]{1,0:T(8,128)(2,1)S(1)}, bf16[304,2048]{1,0:T(8,128)(2,1)S(1)}, u32[]{:S(2)}, u32[]{:S(2)}) collective-permute-start(bf16[304,2048]{1,0:T(8,128)(2,1)S(1)} %collective-permute-done.15), channel_id=1, source_target_pairs={{1,0},{5,4},{9,8},{13,12},{17,16},{21,20},{25,24},{29,28}} | collective-permute-start | bytes 3735560 | tf_op jit(solution)/shard_map/ppermute | solution.py:178
  579.2 28.2 %collective-permute-start.19 = (bf16[304,2048]{1,0:T(8,128)(2,1)S(1)}, bf16[304,2048]{1,0:T(8,128)(2,1)S(1)}, u32[]{:S(2)}, u32[]{:S(2)}) collective-permute-start(bf16[304,2048]{1,0:T(8,128)(2,1)S(1)} %get-tuple-element.172), channel_id=1, source_target_pairs={{1,0},{2,1},{3,2},{5,4},{6,5},{7,6},{9,8},{10,9},{11,10},{13,12},{... | collective-permute-start | bytes 3735560 | tf_op jit(solution)/shard_map/ppermute | solution.py:178
  607.4 27.5 %collective-permute-start.21 = (bf16[304,2048]{1,0:T(8,128)(2,1)S(1)}, bf16[304,2048]{1,0:T(8,128)(2,1)S(1)}, u32[]{:S(2)}, u32[]{:S(2)}) collective-permute-start(bf16[304,2048]{1,0:T(8,128)(2,1)S(1)} %collective-permute-done.19), channel_id=1, source_target_pairs={{1,0},{2,1},{5,4},{6,5},{9,8},{10,9},{13,12},{14,13},{17,16},{18,1... | collective-permute-start | bytes 3735560 | tf_op jit(solution)/shard_map/ppermute | solution.py:178
  608.7 28.8 %collective-permute-start.22 = (bf16[304,2048]{1,0:T(8,128)(2,1)S(1)}, bf16[304,2048]{1,0:T(8,128)(2,1)S(1)}, u32[]{:S(2)}, u32[]{:S(2)}) collective-permute-start(bf16[304,2048]{1,0:T(8,128)(2,1)S(1)} %collective-permute-done.20), channel_id=1, source_target_pairs={{2,3},{6,7},{10,11},{14,15},{18,19},{22,23},{26,27},{30,31}} | collective-permute-start | bytes 3735560 | tf_op jit(solution)/shard_map/ppermute | solution.py:175
  634.9 26.5 %collective-permute-start.23 = (bf16[304,2048]{1,0:T(8,128)(2,1)S(1)}, bf16[304,2048]{1,0:T(8,128)(2,1)S(1)}, u32[]{:S(2)}, u32[]{:S(2)}) collective-permute-start(bf16[304,2048]{1,0:T(8,128)(2,1)S(1)} %collective-permute-done.21), channel_id=1, source_target_pairs={{1,0},{5,4},{9,8},{13,12},{17,16},{21,20},{25,24},{29,28}} | collective-permute-start | bytes 3735560 | tf_op jit(solution)/shard_map/ppermute | solution.py:178
  663.3 27.6 %collective-permute-start.25 = (bf16[304,2048]{1,0:T(8,128)(2,1)S(1)}, bf16[304,2048]{1,0:T(8,128)(2,1)S(1)}, u32[]{:S(2)}, u32[]{:S(2)}) collective-permute-start(bf16[304,2048]{1,0:T(8,128)(2,1)S(1)} %get-tuple-element.173), channel_id=1, source_target_pairs={{1,0},{2,1},{3,2},{5,4},{6,5},{7,6},{9,8},{10,9},{11,10},{13,12},{... | collective-permute-start | bytes 3735560 | tf_op jit(solution)/shard_map/ppermute | solution.py:178
  690.8 28.1 %collective-permute-start.27 = (bf16[304,2048]{1,0:T(8,128)(2,1)S(1)}, bf16[304,2048]{1,0:T(8,128)(2,1)S(1)}, u32[]{:S(2)}, u32[]{:S(2)}) collective-permute-start(bf16[304,2048]{1,0:T(8,128)(2,1)S(1)} %collective-permute-done.25), channel_id=1, source_target_pairs={{1,0},{2,1},{5,4},{6,5},{9,8},{10,9},{13,12},{14,13},{17,16},{18,1... | collective-permute-start | bytes 3735560 | tf_op jit(solution)/shard_map/ppermute | solution.py:178
  692.1 35.6 %collective-permute-start.28 = (bf16[304,2048]{1,0:T(8,128)(2,1)S(1)}, bf16[304,2048]{1,0:T(8,128)(2,1)S(1)}, u32[]{:S(2)}, u32[]{:S(2)}) collective-permute-start(bf16[304,2048]{1,0:T(8,128)(2,1)S(1)} %collective-permute-done.26), channel_id=1, source_target_pairs={{2,3},{6,7},{10,11},{14,15},{18,19},{22,23},{26,27},{30,31}} | collective-permute-start | bytes 3735560 | tf_op jit(solution)/shard_map/ppermute | solution.py:175
  718.9 41.1 %collective-permute-start.29 = (bf16[304,2048]{1,0:T(8,128)(2,1)S(1)}, bf16[304,2048]{1,0:T(8,128)(2,1)S(1)}, u32[]{:S(2)}, u32[]{:S(2)}) collective-permute-start(bf16[304,2048]{1,0:T(8,128)(2,1)S(1)} %collective-permute-done.27), channel_id=1, source_target_pairs={{1,0},{5,4},{9,8},{13,12},{17,16},{21,20},{25,24},{29,28}} | collective-permute-start | bytes 3735560 | tf_op jit(solution)/shard_map/ppermute | solution.py:178
  762.3 29.1 %collective-permute-start.30 = (bf16[304,2048]{1,0:T(8,128)(2,1)S(1)}, bf16[304,2048]{1,0:T(8,128)(2,1)S(1)}, u32[]{:S(2)}, u32[]{:S(2)}) collective-permute-start(bf16[304,2048]{1,0:T(8,128)(2,1)S(1)} %get-tuple-element.174), channel_id=1, source_target_pairs={{0,1},{1,2},{2,3},{4,5},{5,6},{6,7},{8,9},{9,10},{10,11},{12,13},{... | collective-permute-start | bytes 3735560 | tf_op jit(solution)/shard_map/ppermute | solution.py:175
  790.1 28.6 %collective-permute-start.31 = (bf16[304,2048]{1,0:T(8,128)(2,1)S(1)}, bf16[304,2048]{1,0:T(8,128)(2,1)}, u32[]{:S(2)}, u32[]{:S(2)}) collective-permute-start(bf16[304,2048]{1,0:T(8,128)(2,1)S(1)} %get-tuple-element.174), channel_id=1, source_target_pairs={{1,0},{2,1},{3,2},{5,4},{6,5},{7,6},{9,8},{10,9},{11,10},{13,12},{... | collective-permute-start | bytes 3735560 | tf_op jit(solution)/shard_map/ppermute | solution.py:178
  791.4 28.6 %collective-permute-start.32 = (bf16[304,2048]{1,0:T(8,128)(2,1)S(1)}, bf16[304,2048]{1,0:T(8,128)(2,1)}, u32[]{:S(2)}, u32[]{:S(2)}) collective-permute-start(bf16[304,2048]{1,0:T(8,128)(2,1)S(1)} %collective-permute-done.30), channel_id=1, source_target_pairs={{1,2},{2,3},{5,6},{6,7},{9,10},{10,11},{13,14},{14,15},{17,18},{18... | collective-permute-start | bytes 3735560 | tf_op jit(solution)/shard_map/ppermute | solution.py:175
  818.8 30.8 %collective-permute-start.33 = (bf16[304,2048]{1,0:T(8,128)(2,1)}, bf16[304,2048]{1,0:T(8,128)(2,1)}, u32[]{:S(2)}, u32[]{:S(2)}) collective-permute-start(bf16[304,2048]{1,0:T(8,128)(2,1)} %collective-permute-done.31), channel_id=1, source_target_pairs={{1,0},{2,1},{5,4},{6,5},{9,8},{10,9},{13,12},{14,13},{17,16},{18,1... | collective-permute-start | bytes 3735560 | tf_op jit(solution)/shard_map/ppermute | solution.py:178
  820.1 42.6 %collective-permute-start.34 = (bf16[304,2048]{1,0:T(8,128)(2,1)}, bf16[304,2048]{1,0:T(8,128)(2,1)}, u32[]{:S(2)}, u32[]{:S(2)}) collective-permute-start(bf16[304,2048]{1,0:T(8,128)(2,1)} %collective-permute-done.32), channel_id=1, source_target_pairs={{2,3},{6,7},{10,11},{14,15},{18,19},{22,23},{26,27},{30,31}} | collective-permute-start | bytes 3735560 | tf_op jit(solution)/shard_map/ppermute | solution.py:175
  849.6 223.8 %reduce-scatter.25.cloned.1.call-start = ((), (), s32[]{:S(2)}) async-start(), calls=%async_computation.22 | async-start | bytes 6225920 | tf_op jit(solution)/shard_map/reduce_scatter | solution.py:381
  849.6 79.5 %collective-permute-start.35 = (bf16[304,2048]{1,0:T(8,128)(2,1)}, bf16[304,2048]{1,0:T(8,128)(2,1)S(1)}, u32[]{:S(2)}, u32[]{:S(2)}) collective-permute-start(bf16[304,2048]{1,0:T(8,128)(2,1)} %collective-permute-done.33), channel_id=1, source_target_pairs={{1,0},{5,4},{9,8},{13,12},{17,16},{21,20},{25,24},{29,28}} | collective-permute-start | bytes 3735560 | tf_op jit(solution)/shard_map/ppermute | solution.py:178
  985.3 180.3 %reduce-scatter.19.cloned.1.call-start = ((), (), s32[]{:S(2)}) async-start(), calls=%async_computation.19 | async-start | bytes 6225920 | tf_op jit(solution)/shard_map/reduce_scatter | solution.py:381
  1001.7 841.2 %reduce-scatter.35.cloned.1.call-start = ((), (), s32[]{:S(2)}) async-start(), calls=%async_computation.27 | async-start | bytes 9437184 | tf_op jit(solution)/shard_map/reduce_scatter | solution.py:414
  1172.2 29.9 %collective-permute-start.36 = (bf16[304,2048]{1,0:T(8,128)(2,1)S(1)}, bf16[304,2048]{1,0:T(8,128)(2,1)S(1)}, u32[]{:S(2)}, u32[]{:S(2)}) collective-permute-start(bf16[304,2048]{1,0:T(8,128)(2,1)S(1)} %get-tuple-element.179), channel_id=1, source_target_pairs={{0,1},{1,2},{2,3},{4,5},{5,6},{6,7},{8,9},{9,10},{10,11},{12,13},{... | collective-permute-start | bytes 3735560 | tf_op jit(solution)/shard_map/ppermute | solution.py:175
  1177.0 45.1 %collective-permute-start.37 = (bf16[304,2048]{1,0:T(8,128)(2,1)S(1)}, bf16[304,2048]{1,0:T(8,128)(2,1)S(1)}, u32[]{:S(2)}, u32[]{:S(2)}) collective-permute-start(bf16[304,2048]{1,0:T(8,128)(2,1)S(1)} %get-tuple-element.179), channel_id=1, source_target_pairs={{1,0},{2,1},{3,2},{5,4},{6,5},{7,6},{9,8},{10,9},{11,10},{13,12},{... | collective-permute-start | bytes 3735560 | tf_op jit(solution)/shard_map/ppermute | solution.py:178
  1222.1 33.9 %collective-permute-start.39 = (bf16[304,2048]{1,0:T(8,128)(2,1)S(1)}, bf16[304,2048]{1,0:T(8,128)(2,1)}, u32[]{:S(2)}, u32[]{:S(2)}) collective-permute-start(bf16[304,2048]{1,0:T(8,128)(2,1)S(1)} %collective-permute-done.37), channel_id=1, source_target_pairs={{1,0},{2,1},{5,4},{6,5},{9,8},{10,9},{13,12},{14,13},{17,16},{18,1... | collective-permute-start | bytes 3735560 | tf_op jit(solution)/shard_map/ppermute | solution.py:178
  1223.4 37.9 %collective-permute-start.40 = (bf16[304,2048]{1,0:T(8,128)(2,1)}, bf16[304,2048]{1,0:T(8,128)(2,1)}, u32[]{:S(2)}, u32[]{:S(2)}) collective-permute-start(bf16[304,2048]{1,0:T(8,128)(2,1)} %collective-permute-done.38), channel_id=1, source_target_pairs={{2,3},{6,7},{10,11},{14,15},{18,19},{22,23},{26,27},{30,31}} | collective-permute-start | bytes 3735560 | tf_op jit(solution)/shard_map/ppermute | solution.py:175
  1242.2 606.7 %reduce-scatter.29.cloned.1.call-start = ((), (), s32[]{:S(2)}) async-start(), calls=%async_computation.24 | async-start | bytes 1179648 | tf_op jit(solution)/shard_map/reduce_scatter | solution.py:401
  1256.0 29.4 %collective-permute-start.41 = (bf16[304,2048]{1,0:T(8,128)(2,1)}, bf16[304,2048]{1,0:T(8,128)(2,1)S(1)}, u32[]{:S(2)}, u32[]{:S(2)}) collective-permute-start(bf16[304,2048]{1,0:T(8,128)(2,1)} %collective-permute-done.39), channel_id=1, source_target_pairs={{1,0},{5,4},{9,8},{13,12},{17,16},{21,20},{25,24},{29,28}} | collective-permute-start | bytes 3735560 | tf_op jit(solution)/shard_map/ppermute | solution.py:178
  1285.8 101.5 %collective-permute-start.42 = (bf16[304,2048]{1,0:T(8,128)(2,1)}, bf16[304,2048]{1,0:T(8,128)(2,1)}, u32[]{:S(2)}, u32[]{:S(2)}) collective-permute-start(bf16[304,2048]{1,0:T(8,128)(2,1)} %get-tuple-element.180), channel_id=1, source_target_pairs={{0,1},{1,2},{2,3},{4,5},{5,6},{6,7},{8,9},{9,10},{10,11},{12,13},{... | collective-permute-start | bytes 3735560 | tf_op jit(solution)/shard_map/ppermute | solution.py:175
  1288.6 99.6 %collective-permute-start.43 = (bf16[304,2048]{1,0:T(8,128)(2,1)}, bf16[304,2048]{1,0:T(8,128)(2,1)}, u32[]{:S(2)}, u32[]{:S(2)}) collective-permute-start(bf16[304,2048]{1,0:T(8,128)(2,1)} %get-tuple-element.180), channel_id=1, source_target_pairs={{1,0},{2,1},{3,2},{5,4},{6,5},{7,6},{9,8},{10,9},{11,10},{13,12},{... | collective-permute-start | bytes 3735560 | tf_op jit(solution)/shard_map/ppermute | solution.py:178
  1388.2 30.2 %collective-permute-start.45 = (bf16[304,2048]{1,0:T(8,128)(2,1)}, bf16[304,2048]{1,0:T(8,128)(2,1)S(1)}, u32[]{:S(2)}, u32[]{:S(2)}) collective-permute-start(bf16[304,2048]{1,0:T(8,128)(2,1)} %collective-permute-done.43), channel_id=1, source_target_pairs={{1,0},{2,1},{5,4},{6,5},{9,8},{10,9},{13,12},{14,13},{17,16},{18,1... | collective-permute-start | bytes 3735560 | tf_op jit(solution)/shard_map/ppermute | solution.py:178
  1392.2 31.3 %collective-permute-start.46 = (bf16[304,2048]{1,0:T(8,128)(2,1)S(1)}, bf16[304,2048]{1,0:T(8,128)(2,1)S(1)}, u32[]{:S(2)}, u32[]{:S(2)}) collective-permute-start(bf16[304,2048]{1,0:T(8,128)(2,1)S(1)} %collective-permute-done.44), channel_id=1, source_target_pairs={{2,3},{6,7},{10,11},{14,15},{18,19},{22,23},{26,27},{30,31}} | collective-permute-start | bytes 3735560 | tf_op jit(solution)/shard_map/ppermute | solution.py:175
  1418.4 27.9 %collective-permute-start.47 = (bf16[304,2048]{1,0:T(8,128)(2,1)S(1)}, bf16[304,2048]{1,0:T(8,128)(2,1)S(1)}, u32[]{:S(2)}, u32[]{:S(2)}) collective-permute-start(bf16[304,2048]{1,0:T(8,128)(2,1)S(1)} %collective-permute-done.45), channel_id=1, source_target_pairs={{1,0},{5,4},{9,8},{13,12},{17,16},{21,20},{25,24},{29,28}} | collective-permute-start | bytes 3735560 | tf_op jit(solution)/shard_map/ppermute | solution.py:178
  1552.4 299.8 %reduce-scatter.27.cloned.1.call-start = ((), (), s32[]{:S(2)}) async-start(), calls=%async_computation.23 | async-start | bytes 2359296 | tf_op jit(solution)/shard_map/reduce_scatter | solution.py:398
  1564.4 290.8 %reduce-scatter.31.cloned.1.call-start = ((), (), s32[]{:S(2)}) async-start(), calls=%async_computation.25 | async-start | bytes 2359296 | tf_op jit(solution)/shard_map/reduce_scatter | solution.py:406
  1606.2 257.7 %reduce-scatter.33.cloned.1.call-start = ((), (), s32[]{:S(2)}) async-start(), calls=%async_computation.26 | async-start | bytes 18874368 | tf_op jit(solution)/shard_map/reduce_scatter | solution.py:409
  1637.1 336.5 %reduce-scatter.21.cloned.1.call-start = ((), (), s32[]{:S(2)}) async-start(), calls=%async_computation.20 | async-start | bytes 6225920 | tf_op jit(solution)/shard_map/reduce_scatter | solution.py:381
  1649.7 29.3 %collective-permute-start.51 = (bf16[304,2048]{1,0:T(8,128)(2,1)}, bf16[304,2048]{1,0:T(8,128)(2,1)}, u32[]{:S(2)}, u32[]{:S(2)}) collective-permute-start(bf16[304,2048]{1,0:T(8,128)(2,1)} %get-tuple-element.345), channel_id=1, source_target_pairs={{3,2},{7,6},{11,10},{15,14},{19,18},{23,22},{27,26},{31,30}} | collective-permute-start | bytes 3735560 | tf_op jit(solution)/shard_map/ppermute | solution.py:207
  1723.2 280.1 %reduce-scatter.37.cloned.1.call-start = ((), (), s32[]{:S(2)}) async-start(), calls=%async_computation.28 | async-start | bytes 589824
  1724.5 27.0 %collective-permute-start.50 = (bf16[304,2048]{1,0:T(8,128)(2,1)S(1)}, bf16[304,2048]{1,0:T(8,128)(2,1)}, u32[]{:S(2)}, u32[]{:S(2)}) collective-permute-start(bf16[304,2048]{1,0:T(8,128)(2,1)S(1)} %copy-done.90), channel_id=1, source_target_pairs={{0,1},{1,2},{2,3},{4,5},{5,6},{6,7},{8,9},{9,10},{10,11},{12,13},{... | collective-permute-start | bytes 3735560 | tf_op jit(solution)/shard_map/ppermute | solution.py:201
  1732.9 27.0 %collective-permute-start.53 = (bf16[304,2048]{1,0:T(8,128)(2,1)S(1)}, bf16[304,2048]{1,0:T(8,128)(2,1)S(1)}, u32[]{:S(2)}, u32[]{:S(2)}) collective-permute-start(bf16[304,2048]{1,0:T(8,128)(2,1)S(1)} %add_convert_fusion.8), channel_id=1, source_target_pairs={{1,0},{2,1},{3,2},{5,4},{6,5},{7,6},{9,8},{10,9},{11,10},{13,12},{... | collective-permute-start | bytes 3735560 | tf_op jit(solution)/shard_map/ppermute | solution.py:207
  1769.3 38.2 %collective-permute-start.57 = (bf16[304,2048]{1,0:T(8,128)(2,1)}, bf16[304,2048]{1,0:T(8,128)(2,1)}, u32[]{:S(2)}, u32[]{:S(2)}) collective-permute-start(bf16[304,2048]{1,0:T(8,128)(2,1)} %get-tuple-element.341), channel_id=1, source_target_pairs={{3,2},{7,6},{11,10},{15,14},{19,18},{23,22},{27,26},{31,30}} | collective-permute-start | bytes 3735560 | tf_op jit(solution)/shard_map/ppermute | solution.py:207
  1792.1 43.5 %collective-permute-start.55 = (bf16[304,2048]{1,0:T(8,128)(2,1)}, bf16[304,2048]{1,0:T(8,128)(2,1)}, u32[]{:S(2)}, u32[]{:S(2)}) collective-permute-start(bf16[304,2048]{1,0:T(8,128)(2,1)} %add_convert_fusion.7), channel_id=1, source_target_pairs={{0,1},{1,2},{4,5},{5,6},{8,9},{9,10},{12,13},{13,14},{16,17},{17,1... | collective-permute-start | bytes 3735560 | tf_op jit(solution)/shard_map/ppermute | solution.py:201
  1841.0 29.3 %collective-permute-start.58 = (bf16[304,2048]{1,0:T(8,128)(2,1)}, bf16[304,2048]{1,0:T(8,128)(2,1)}, u32[]{:S(2)}, u32[]{:S(2)}) collective-permute-start(bf16[304,2048]{1,0:T(8,128)(2,1)} %get-tuple-element.339), channel_id=1, source_target_pairs={{2,1},{3,2},{6,5},{7,6},{10,9},{11,10},{14,13},{15,14},{18,17},{19... | collective-permute-start | bytes 3735560 | tf_op jit(solution)/shard_map/ppermute | solution.py:207
  1858.3 49.7 %collective-permute-start.56 = (bf16[304,2048]{1,0:T(8,128)(2,1)}, bf16[304,2048]{1,0:T(8,128)(2,1)}, u32[]{:S(2)}, u32[]{:S(2)}) collective-permute-start(bf16[304,2048]{1,0:T(8,128)(2,1)} %get-tuple-element.338), channel_id=1, source_target_pairs={{0,1},{1,2},{2,3},{4,5},{5,6},{6,7},{8,9},{9,10},{10,11},{12,13},{... | collective-permute-start | bytes 3735560 | tf_op jit(solution)/shard_map/ppermute | solution.py:201
  1873.0 63.1 %collective-permute-start.59 = (bf16[304,2048]{1,0:T(8,128)(2,1)S(1)}, bf16[304,2048]{1,0:T(8,128)(2,1)S(1)}, u32[]{:S(2)}, u32[]{:S(2)}) collective-permute-start(bf16[304,2048]{1,0:T(8,128)(2,1)S(1)} %add_convert_fusion.4), channel_id=1, source_target_pairs={{1,0},{2,1},{3,2},{5,4},{6,5},{7,6},{9,8},{10,9},{11,10},{13,12},{... | collective-permute-start | bytes 3735560 | tf_op jit(solution)/shard_map/ppermute | solution.py:207
  (184 other events, 4826.8 us)
Sparse Core Ops, SparseCore 0:
  10.5 30.5 all-gather.7
  43.5 23.3 all-gather.5
  69.4 28.0 all-gather.9
  99.8 55.8 all-gather.13
  158.0 89.7 all-gather.11
  299.8 86.9 reduce-scatter.16
  389.1 90.0 reduce-scatter.14
  849.7 106.8 reduce-scatter.22
  985.4 87.8 reduce-scatter.24
  1075.5 90.0 reduce-scatter.18
  1242.3 83.4 reduce-scatter.34
  1552.5 33.9 reduce-scatter.28
  1590.3 41.0 reduce-scatter.26
  1635.1 41.0 reduce-scatter.30
  1679.7 115.9 reduce-scatter.32
  1798.4 125.0 reduce-scatter.20
  1968.8 34.5 reduce-scatter.36

commit v12 on v5

--- a/solution.py
+++ b/solution.py
@@ -161,6 +161,13 @@
 def contract_cols(left, right):
     return lax.dot_general(
         left, right, (((1,), (1,)), ((), ())), preferred_element_type=jnp.float32
+    )
+
+
+def by_row_blocks(operation, rows_in, count):
+    size = rows_in.shape[0] // count
+    return jnp.concatenate(
+        [operation(rows_in[index * size : (index + 1) * size]) for index in range(count)], axis=0
     )
 
 
@@ -288,8 +295,12 @@
         hat_two = middle * scale_two
         normed_two = (hat_two * gain_values[1][None, :]).astype(jnp.bfloat16)
         rows_two = yield ("gather", normed_two)
-        gate_up = jnp.einsum(
-            "rd,dcf->rcf", rows_two, full_gateup, preferred_element_type=jnp.float32
+        gate_up = by_row_blocks(
+            lambda part: jnp.einsum(
+                "rd,dcf->rcf", part, full_gateup, preferred_element_type=jnp.float32
+            ),
+            rows_two,
+            tensor_count,
         )
         gate_part = gate_up[:, 0]
         up_part = gate_up[:, 1]
@@ -300,11 +311,18 @@
         ffn_grad = (branch_scale * upstream).astype(jnp.bfloat16)
         ffn_grad_all = yield ("gather", ffn_grad)
         ffn_branch = yield (
-            "scatter", jnp.dot(hidden_state, full_down, preferred_element_type=jnp.float32)
+            "scatter",
+            by_row_blocks(
+                lambda part: jnp.dot(part, full_down, preferred_element_type=jnp.float32),
+                hidden_state,
+                tensor_count,
+            ),
         )
         layer_rows = (middle + branch_scale * ffn_branch).astype(jnp.bfloat16)
         grad_down = contract_rows(hidden_state, ffn_grad_all)
-        hidden_grad = contract_cols(ffn_grad_all, full_down)
+        hidden_grad = by_row_blocks(
+            lambda part: contract_cols(part, full_down), ffn_grad_all, tensor_count
+        )
         gate_grad = hidden_grad * up_part * sigmoid_gate * (1.0 + gate_part * (1.0 - sigmoid_gate))
         up_grad = hidden_grad * silu_gate
         gateup_grad = jnp.stack([gate_grad, up_grad], axis=1).astype(jnp.bfloat16)
@@ -313,8 +331,12 @@
         )
         normed_two_grad = yield (
             "scatter",
-            jnp.einsum(
-                "rcf,dcf->rd", gateup_grad, full_gateup, preferred_element_type=jnp.float32
+            by_row_blocks(
+                lambda part: jnp.einsum(
+                    "rcf,dcf->rd", part, full_gateup, preferred_element_type=jnp.float32
+                ),
+                gateup_grad,
+                tensor_count,
             ),
         )
         middle_back, gain_two = norm_back(normed_two_grad, hat_two, scale_two, gain_values[1])

time: 2010 us -> 2130 us (1.060)
  other arithmetic: 242 us -> 324 us
  matrix products: 543 us -> 624 us
  waiting for transfers between devices: 763 us -> 700 us
    ppermute x24, waiting for transfers between devices: 258 us -> 183 us  [line_scatter(): lax.ppermute(send.astype(jnp.bfloat16), 'tensor', [(i, i + 1) for i in ra...]
    dot_general x6 -> x24, matrix products: 137 us -> 207 us  [the longest x8 82.7 us: micro_step(): jnp.einsum('rd,dcf->rcf', part, full_gateup, preferred_element_type=jnp.f...]
    reduce_scatter x1, waiting for transfers between devices: 0.01 us -> 34.3 us  [per_device(): lax.psum_scatter(totals[0].astype(jnp.bfloat16), 'dp', scatter_dimension=...]
    concatenate x0 -> x6, other arithmetic: none -> 33.3 us  [by_row_blocks(): jnp.concatenate([operation(rows_in[index * size:(index + 1) * size]) for...]
    reduce_scatter x1, waiting for transfers between devices: 23.9 us -> 0.01 us  [per_device(): lax.psum_scatter(totals[2].astype(jnp.bfloat16), 'dp', scatter_dimension=...]
    dot_general x6 -> x12, matrix products: 65.8 us -> 72 us  [contract_cols(): lax.dot_general(left, right, (((1,), (1,)), ((), ())), preferred_element_...]
  transfers between devices with their start and end apart: 107 -> 107, of which waited for: 47 -> 46; matrix products, arithmetic and copies ran while one was open for 42% -> 47% of each run, Pallas kernels for 0% -> 0%
where the time goes in v12:
time: 2130 us; the launch traced here: 2110 us
  waiting for transfers between devices  700 us (33%)
  matrix products  624 us (29%)
  other arithmetic  324 us (15%)
  starting transfers between devices  234 us (11%)
  local copies, waits for them, and re-layouts  141 us (7%)
  blocking collectives  69.8 us (3%)
    ppermute x24, waiting for transfers between devices, line_gather(): lax.ppermute(from_right, 'tensor', [(i, i - 1) for i in range(1, count -...  342 us
    ppermute x24, waiting for transfers between devices, line_scatter(): lax.ppermute(send.astype(jnp.bfloat16), 'tensor', [(i, i + 1) for i in ra...  183 us
    ppermute x24, starting transfers between devices, line_scatter(): lax.ppermute(send.astype(jnp.bfloat16), 'tensor', [(i, i + 1) for i in ra...  116 us
    dot_general x8, matrix products, micro_step(): jnp.einsum('rd,dcf->rcf', part, full_gateup, preferred_element_type=jnp.f...  82.7 us
    dot_general x8, matrix products, micro_step(): jnp.einsum('rcf,dcf->rd', part, full_gateup, preferred_element_type=jnp.f...  82.2 us
    dot_general x12, matrix products, contract_cols(): lax.dot_general(left, right, (((1,), (1,)), ((), ())), preferred_element_...  72 us
    dot_general x4, matrix products, attend_back(): jnp.einsum('ikrd,jkd->krij', grad_block, values[:stop], preferred_element...  64.4 us
    ppermute x24, waiting for transfers between devices, line_scatter(): lax.ppermute(send.astype(jnp.bfloat16), 'tensor', [(i, i - 1) for i in ra...  61.5 us
  transfers between devices with their start and end apart: 107, of which 46 were waited for; matrix products, arithmetic and copies ran while one was open for 47% of the time, Pallas kernels for 0%

profile of v12, /device:TPU:0, one launch (start us, length us, event | category | flops | bytes accessed | tf_op | source)
XLA Modules:
  0.0 2113.7 jit_solution(17514390562074563545)
XLA Ops:
  19.5 10.4 all_gather.18
  44.5 19.7 collective-permute-done
  82.0 18.2 collective-permute-done.3
  115.8 17.9 collective-permute-done.5
  174.1 12.9 fusion.150
  209.7 14.1 collective-permute-done.9
  231.7 27.1 %collective-permute-done.11 = bf16[304,2048]{1,0:T(8,128)(2,1)S(1)} collective-permute-done((bf16[304,2048]{1,0:T(8,128)(2,1)}, bf16[304,2048]{1,0:T(8,128)(2,1)S(1)}, u32[]{:S(2)}, u32[]{:S(2)}) %collective-permute-start.11) | collective-permute-done | bytes 1245216 | tf_op jit(solution)/shard_map/ppermute | solution.py:185
  302.1 13.8 fusion.149
  360.8 22.6 %collective-permute-done.17 = bf16[304,2048]{1,0:T(8,128)(2,1)S(1)} collective-permute-done((bf16[304,2048]{1,0:T(8,128)(2,1)S(1)}, bf16[304,2048]{1,0:T(8,128)(2,1)S(1)}, u32[]{:S(2)}, u32[]{:S(2)}) %collective-permute-start.17) | collective-permute-done | bytes 1245216 | tf_op jit(solution)/shard_map/ppermute | solution.py:214
  390.8 21.9 %collective-permute-done.18 = bf16[304,2048]{1,0:T(8,128)(2,1)S(1)} collective-permute-done((bf16[304,2048]{1,0:T(8,128)(2,1)S(1)}, bf16[304,2048]{1,0:T(8,128)(2,1)S(1)}, u32[]{:S(2)}, u32[]{:S(2)}) %collective-permute-start.18) | collective-permute-done | bytes 1245216 | tf_op jit(solution)/shard_map/ppermute | solution.py:208
  417.6 20.8 collective-permute-done.19
  446.8 16.9 collective-permute-done.20
  463.7 22.4 %collective-permute-done.23 = bf16[304,2048]{1,0:T(8,128)(2,1)S(1)} collective-permute-done((bf16[304,2048]{1,0:T(8,128)(2,1)S(1)}, bf16[304,2048]{1,0:T(8,128)(2,1)S(1)}, u32[]{:S(2)}, u32[]{:S(2)}) %collective-permute-start.23) | collective-permute-done | bytes 1245216 | tf_op jit(solution)/shard_map/ppermute | solution.py:214
  498.2 13.0 collective-permute-done.24
  512.0 11.8 collective-permute-done.25
  525.9 26.0 %collective-permute-done.27 = bf16[304,2048]{1,0:T(8,128)(2,1)S(1)} collective-permute-done((bf16[304,2048]{1,0:T(8,128)(2,1)S(1)}, bf16[304,2048]{1,0:T(8,128)(2,1)S(1)}, u32[]{:S(2)}, u32[]{:S(2)}) %collective-permute-start.27) | collective-permute-done | bytes 1245216 | tf_op jit(solution)/shard_map/ppermute | solution.py:185
  554.8 24.3 %collective-permute-done.29 = bf16[304,2048]{1,0:T(8,128)(2,1)S(1)} collective-permute-done((bf16[304,2048]{1,0:T(8,128)(2,1)S(1)}, bf16[304,2048]{1,0:T(8,128)(2,1)S(1)}, u32[]{:S(2)}, u32[]{:S(2)}) %collective-permute-start.29) | collective-permute-done | bytes 1245216 | tf_op jit(solution)/shard_map/ppermute | solution.py:185
  582.2 13.0 collective-permute-done.30
  596.0 18.2 collective-permute-done.31
  617.0 28.6 %collective-permute-done.33 = bf16[304,2048]{1,0:T(8,128)(2,1)S(1)} collective-permute-done((bf16[304,2048]{1,0:T(8,128)(2,1)S(1)}, bf16[304,2048]{1,0:T(8,128)(2,1)S(1)}, u32[]{:S(2)}, u32[]{:S(2)}) %collective-permute-start.33) | collective-permute-done | bytes 1245216 | tf_op jit(solution)/shard_map/ppermute | solution.py:185
  648.3 29.0 %collective-permute-done.35 = bf16[304,2048]{1,0:T(8,128)(2,1)S(1)} collective-permute-done((bf16[304,2048]{1,0:T(8,128)(2,1)S(1)}, bf16[304,2048]{1,0:T(8,128)(2,1)S(1)}, u32[]{:S(2)}, u32[]{:S(2)}) %collective-permute-start.35) | collective-permute-done | bytes 1245216 | tf_op jit(solution)/shard_map/ppermute | solution.py:185
  680.5 13.0 collective-permute-done.36
  694.2 14.0 collective-permute-done.37
  710.3 26.1 %collective-permute-done.39 = bf16[304,2048]{1,0:T(8,128)(2,1)S(1)} collective-permute-done((bf16[304,2048]{1,0:T(8,128)(2,1)S(1)}, bf16[304,2048]{1,0:T(8,128)(2,1)S(1)}, u32[]{:S(2)}, u32[]{:S(2)}) %collective-permute-start.39) | collective-permute-done | bytes 1245216 | tf_op jit(solution)/shard_map/ppermute | solution.py:185
  746.3 22.0 %collective-permute-done.41 = bf16[304,2048]{1,0:T(8,128)(2,1)S(1)} collective-permute-done((bf16[304,2048]{1,0:T(8,128)(2,1)S(1)}, bf16[304,2048]{1,0:T(8,128)(2,1)S(1)}, u32[]{:S(2)}, u32[]{:S(2)}) %collective-permute-start.41) | collective-permute-done | bytes 1245216 | tf_op jit(solution)/shard_map/ppermute | solution.py:185
  799.3 13.5 fusion.181
  849.7 15.0 fusion.169
  864.7 13.1 fusion.170
  877.8 11.4 fusion.171
  919.3 12.8 collective-permute-done.45
  987.8 12.9 collective-permute-done.49
  1057.3 10.8 multiply_convert_fusion.2
  1068.0 10.8 convolution_bitcast_fusion.11
  1085.7 10.4 convolution_bitcast_fusion.10
  1096.1 10.4 convolution_bitcast_fusion.9
  1117.6 10.4 convolution_bitcast_fusion.8
  1239.4 10.4 convolution_bitcast_fusion.1
  1260.8 10.4 convolution_bitcast_fusion
  1283.7 11.7 collective-permute-start.66
  1296.5 18.8 collective-permute-done.66
  1320.7 23.0 %collective-permute-done.67 = bf16[304,2048]{1,0:T(8,128)(2,1)S(1)} collective-permute-done((bf16[304,2048]{1,0:T(8,128)(2,1)S(1)}, bf16[304,2048]{1,0:T(8,128)(2,1)S(1)}, u32[]{:S(2)}, u32[]{:S(2)}) %collective-permute-start.67) | collective-permute-done | bytes 1245216 | tf_op jit(solution)/shard_map/ppermute | solution.py:208
  1359.9 17.8 fusion.287
  1377.6 10.6 collective-permute-done.71
  1399.2 19.0 add_convert_fusion.1
  1421.4 29.1 %fusion.36 = f32[2048,2,2048]{0,2,1:T(8,128)} fusion(bf16[1216,1,2048]{2,0,1:T(8,128)(2,1)} %get-tuple-element.336, bf16[1216,1,2048]{2,0,1:T(8,128)(2,1)} %get-tuple-element.337, bf16[1216,2048]{1,0:T(8,128)(2,1)} %copy-done.60), kind=kOutput, calls=%fused_computation.80 | convolution fusion | flops 20421017600 | bytes 48496640 | tf_op jit(solution)/shard_map/rd,rcf->dcf/dot_general | solution.py:329
  1453.7 30.9 %add_convert_fusion = bf16[2048,2,2048]{0,2,1:T(8,128)(2,1)} fusion(f32[2048,2,2048]{0,2,1:T(8,128)} %fusion.36, bf16[1216,1,2048]{2,0,1:T(8,128)(2,1)} %get-tuple-element.338, bf16[1216,1,2048]{2,0,1:T(8,128)(2,1)} %get-tuple-element.339, bf16[1216,2048]{1,0:T(8,128)(2,1)} %copy-done.59), kind=kOutput, calls=%fused_computation | convolution fusion | flops 20437794816 | bytes 65273856 | tf_op jit(solution)/shard_map/rd,rcf->dcf/dot_general | solution.py:329
  1492.7 16.3 collective-permute-done.77
  1517.5 12.8 fusion.19
  1537.6 22.4 %fusion.3 = (f32[2,4,608]{2,1,0:T(4,128)S(1)}, f32[2,1216,608,4]{2,1,3,0:T(8,128)}) fusion(f32[2,1216,608,4]{2,1,3,0:T(8,128)} %copy-done.1, f32[2,4,608]{2,1,0:T(4,128)S(1)} %bitcast.730, pred[608,1216]{0,1:T(8,128)(4,1)S(1)} %copy-done.24, bf16[608,2,4,64]{0,3,2,1:T(8,128)(2,1)S(1)} %bitcast.701, bf16[1216,2,128]{2,0,1:T(8,128)(2,1)S(1)} %copy-done.101), kind=kOutput, calls=%fused_computation.8 | convolution fusion | flops 786640128 | bytes 49340416 | tf_op jit(solution)/shard_map/ikrd,jkd->krij/dot_general | solution.py:119
  1560.0 18.4 fusion.5
  1581.8 10.1 fusion.21
  1602.9 11.9 fusion.139
  1644.1 14.5 collective-permute-done.83
  1673.1 11.2 fusion.16
  1695.4 18.1 fusion
  1713.5 17.0 fusion.2
  1757.8 14.8 collective-permute-done.85
  1778.5 12.4 fusion.136
  1845.5 11.2 collective-permute-done.90
  1917.9 17.8 multiply_reduce_fusion
  1941.4 34.3 %reduce-scatter.9.cloned.1.call-done = bf16[256,512]{1,0:T(8,128)(2,1)} async-done(((bf16[2048,512]{1,0:T(8,128)(2,1)}), bf16[256,512]{1,0:T(8,128)(2,1)}) %reduce-scatter.9.cloned.1.call-update) | async-done | bytes 262160 | tf_op jit(solution)/shard_map/reduce_scatter | solution.py:415
  1987.3 20.0 psum.14
  2020.7 19.9 reduce-scatter.19.cloned.1.call-done
  2051.1 39.5 %psum.15 = f32[2,7]{1,0:T(2,128)S(1)} all-reduce(f32[2,7]{1,0:T(2,128)S(1)} %pad_maximum_fusion.32), channel_id=1, replica_groups=mesh['dp'=8,'tensor'=4] {'dp','tensor'}, use_global_device_ids=true, to_apply=%region_49.50 | all-reduce | flops 14 | bytes 112 | tf_op jit(solution)/shard_map/psum | solution.py:461
  (942 shorter events, 979.0 us)
Async XLA Ops:
  7.2 134.2 %all-gather.6.cloned.1.call-start = ((), (), s32[]{:S(2)}) async-start(), calls=%async_computation.6 | async-start | bytes 1179648 | tf_op jit(solution)/shard_map/all_gather | solution.py:252
  8.9 139.6 %all-gather.8.cloned.1.call-start = ((), (), s32[]{:S(2)}) async-start(), calls=%async_computation.7 | async-start | bytes 2359296 | tf_op jit(solution)/shard_map/all_gather | solution.py:251
  11.6 189.4 %all-gather.10.cloned.1.call-start = ((), (), s32[]{:S(2)}) async-start(), calls=%async_computation.8 | async-start | bytes 2359296 | tf_op jit(solution)/shard_map/all_gather | solution.py:253
  14.4 760.2 %all-gather.14.cloned.1.call-start = ((), (), s32[]{:S(2)}) async-start(), calls=%async_computation.10 | async-start | bytes 9437184 | tf_op jit(solution)/shard_map/all_gather | solution.py:255
  18.8 780.5 %all-gather.12.cloned.1.call-start = ((), (), s32[]{:S(2)}) async-start(), calls=%async_computation.9 | async-start | bytes 18874368 | tf_op jit(solution)/shard_map/all_gather | solution.py:254
  33.2 31.1 %collective-permute-start = (bf16[304,2048]{1,0:T(8,128)(2,1)}, bf16[304,2048]{1,0:T(8,128)(2,1)S(1)}, u32[]{:S(2)}, u32[]{:S(2)}) collective-permute-start(bf16[304,2048]{1,0:T(8,128)(2,1)} %get-tuple-element.383), channel_id=1, source_target_pairs={{0,1},{1,2},{2,3},{4,5},{5,6},{6,7},{8,9},{9,10},{10,11},{12,13},{... | collective-permute-start | bytes 3735560 | tf_op jit(solution)/shard_map/ppermute | solution.py:182
  36.9 31.6 %collective-permute-start.1 = (bf16[304,2048]{1,0:T(8,128)(2,1)}, bf16[304,2048]{1,0:T(8,128)(2,1)}, u32[]{:S(2)}, u32[]{:S(2)}) collective-permute-start(bf16[304,2048]{1,0:T(8,128)(2,1)} %get-tuple-element.383), channel_id=1, source_target_pairs={{1,0},{2,1},{3,2},{5,4},{6,5},{7,6},{9,8},{10,9},{11,10},{13,12},{... | collective-permute-start | bytes 3735560 | tf_op jit(solution)/shard_map/ppermute | solution.py:185
  41.8 1838.4 %reduce-scatter.17.cloned.1.call-start = ((), (), s32[]{:S(2)}) async-start(), calls=%async_computation.15 | async-start | bytes 9437184 | tf_op jit(solution)/shard_map/reduce_scatter | solution.py:431
  68.5 31.8 %collective-permute-start.3 = (bf16[304,2048]{1,0:T(8,128)(2,1)}, bf16[304,2048]{1,0:T(8,128)(2,1)}, u32[]{:S(2)}, u32[]{:S(2)}) collective-permute-start(bf16[304,2048]{1,0:T(8,128)(2,1)} %collective-permute-done.1), channel_id=1, source_target_pairs={{1,0},{2,1},{5,4},{6,5},{9,8},{10,9},{13,12},{14,13},{17,16},{18,1... | collective-permute-start | bytes 3735560 | tf_op jit(solution)/shard_map/ppermute | solution.py:185
  72.7 40.6 %collective-permute-start.4 = (bf16[304,2048]{1,0:T(8,128)(2,1)}, bf16[304,2048]{1,0:T(8,128)(2,1)}, u32[]{:S(2)}, u32[]{:S(2)}) collective-permute-start(bf16[304,2048]{1,0:T(8,128)(2,1)} %collective-permute-done.2), channel_id=1, source_target_pairs={{2,3},{6,7},{10,11},{14,15},{18,19},{22,23},{26,27},{30,31}} | collective-permute-start | bytes 3735560 | tf_op jit(solution)/shard_map/ppermute | solution.py:182
  100.2 33.4 %collective-permute-start.5 = (bf16[304,2048]{1,0:T(8,128)(2,1)}, bf16[304,2048]{1,0:T(8,128)(2,1)S(1)}, u32[]{:S(2)}, u32[]{:S(2)}) collective-permute-start(bf16[304,2048]{1,0:T(8,128)(2,1)} %collective-permute-done.3), channel_id=1, source_target_pairs={{1,0},{5,4},{9,8},{13,12},{17,16},{21,20},{25,24},{29,28}} | collective-permute-start | bytes 3735560 | tf_op jit(solution)/shard_map/ppermute | solution.py:185
  137.3 54.7 %collective-permute-start.6 = (bf16[304,2048]{1,0:T(8,128)(2,1)}, bf16[304,2048]{1,0:T(8,128)(2,1)}, u32[]{:S(2)}, u32[]{:S(2)}) collective-permute-start(bf16[304,2048]{1,0:T(8,128)(2,1)} %get-tuple-element.164), channel_id=1, source_target_pairs={{0,1},{1,2},{2,3},{4,5},{5,6},{6,7},{8,9},{9,10},{10,11},{12,13},{... | collective-permute-start | bytes 3735560 | tf_op jit(solution)/shard_map/ppermute | solution.py:182
  139.9 52.8 %collective-permute-start.7 = (bf16[304,2048]{1,0:T(8,128)(2,1)}, bf16[304,2048]{1,0:T(8,128)(2,1)}, u32[]{:S(2)}, u32[]{:S(2)}) collective-permute-start(bf16[304,2048]{1,0:T(8,128)(2,1)} %get-tuple-element.164), channel_id=1, source_target_pairs={{1,0},{2,1},{3,2},{5,4},{6,5},{7,6},{9,8},{10,9},{11,10},{13,12},{... | collective-permute-start | bytes 3735560 | tf_op jit(solution)/shard_map/ppermute | solution.py:185
  192.7 31.1 %collective-permute-start.9 = (bf16[304,2048]{1,0:T(8,128)(2,1)}, bf16[304,2048]{1,0:T(8,128)(2,1)}, u32[]{:S(2)}, u32[]{:S(2)}) collective-permute-start(bf16[304,2048]{1,0:T(8,128)(2,1)} %collective-permute-done.7), channel_id=1, source_target_pairs={{1,0},{2,1},{5,4},{6,5},{9,8},{10,9},{13,12},{14,13},{17,16},{18,1... | collective-permute-start | bytes 3735560 | tf_op jit(solution)/shard_map/ppermute | solution.py:185
  198.9 31.3 %collective-permute-start.10 = (bf16[304,2048]{1,0:T(8,128)(2,1)S(1)}, bf16[304,2048]{1,0:T(8,128)(2,1)}, u32[]{:S(2)}, u32[]{:S(2)}) collective-permute-start(bf16[304,2048]{1,0:T(8,128)(2,1)S(1)} %collective-permute-done.8), channel_id=1, source_target_pairs={{2,3},{6,7},{10,11},{14,15},{18,19},{22,23},{26,27},{30,31}} | collective-permute-start | bytes 3735560 | tf_op jit(solution)/shard_map/ppermute | solution.py:182
  223.8 35.0 %collective-permute-start.11 = (bf16[304,2048]{1,0:T(8,128)(2,1)}, bf16[304,2048]{1,0:T(8,128)(2,1)S(1)}, u32[]{:S(2)}, u32[]{:S(2)}) collective-permute-start(bf16[304,2048]{1,0:T(8,128)(2,1)} %collective-permute-done.9), channel_id=1, source_target_pairs={{1,0},{5,4},{9,8},{13,12},{17,16},{21,20},{25,24},{29,28}} | collective-permute-start | bytes 3735560 | tf_op jit(solution)/shard_map/ppermute | solution.py:185
  271.8 44.2 %collective-permute-start.15 = (bf16[304,2048]{1,0:T(8,128)(2,1)}, bf16[304,2048]{1,0:T(8,128)(2,1)}, u32[]{:S(2)}, u32[]{:S(2)}) collective-permute-start(bf16[304,2048]{1,0:T(8,128)(2,1)} %get-tuple-element.371), channel_id=1, source_target_pairs={{3,2},{7,6},{11,10},{15,14},{19,18},{23,22},{27,26},{31,30}} | collective-permute-start | bytes 3735560 | tf_op jit(solution)/shard_map/ppermute | solution.py:214
  333.7 27.1 %collective-permute-start.14 = (bf16[304,2048]{1,0:T(8,128)(2,1)S(1)}, bf16[304,2048]{1,0:T(8,128)(2,1)S(1)}, u32[]{:S(2)}, u32[]{:S(2)}) collective-permute-start(bf16[304,2048]{1,0:T(8,128)(2,1)S(1)} %get-tuple-element.368), channel_id=1, source_target_pairs={{0,1},{1,2},{2,3},{4,5},{5,6},{6,7},{8,9},{9,10},{10,11},{12,13},{... | collective-permute-start | bytes 3735560 | tf_op jit(solution)/shard_map/ppermute | solution.py:208
  340.8 42.5 %collective-permute-start.17 = (bf16[304,2048]{1,0:T(8,128)(2,1)S(1)}, bf16[304,2048]{1,0:T(8,128)(2,1)S(1)}, u32[]{:S(2)}, u32[]{:S(2)}) collective-permute-start(bf16[304,2048]{1,0:T(8,128)(2,1)S(1)} %add_convert_fusion.34), channel_id=1, source_target_pairs={{1,0},{2,1},{3,2},{5,4},{6,5},{7,6},{9,8},{10,9},{11,10},{13,12},{... | collective-permute-start | bytes 3735560 | tf_op jit(solution)/shard_map/ppermute | solution.py:214
  390.0 27.5 %collective-permute-start.21 = (bf16[304,2048]{1,0:T(8,128)(2,1)S(1)}, bf16[304,2048]{1,0:T(8,128)(2,1)S(1)}, u32[]{:S(2)}, u32[]{:S(2)}) collective-permute-start(bf16[304,2048]{1,0:T(8,128)(2,1)S(1)} %get-tuple-element.367), channel_id=1, source_target_pairs={{3,2},{7,6},{11,10},{15,14},{19,18},{23,22},{27,26},{31,30}} | collective-permute-start | bytes 3735560 | tf_op jit(solution)/shard_map/ppermute | solution.py:214
  445.5 40.6 %collective-permute-start.23 = (bf16[304,2048]{1,0:T(8,128)(2,1)S(1)}, bf16[304,2048]{1,0:T(8,128)(2,1)S(1)}, u32[]{:S(2)}, u32[]{:S(2)}) collective-permute-start(bf16[304,2048]{1,0:T(8,128)(2,1)S(1)} %add_convert_fusion.30), channel_id=1, source_target_pairs={{1,0},{2,1},{3,2},{5,4},{6,5},{7,6},{9,8},{10,9},{11,10},{13,12},{... | collective-permute-start | bytes 3735560 | tf_op jit(solution)/shard_map/ppermute | solution.py:214
  523.8 28.0 %collective-permute-start.27 = (bf16[304,2048]{1,0:T(8,128)(2,1)S(1)}, bf16[304,2048]{1,0:T(8,128)(2,1)S(1)}, u32[]{:S(2)}, u32[]{:S(2)}) collective-permute-start(bf16[304,2048]{1,0:T(8,128)(2,1)S(1)} %collective-permute-done.25), channel_id=1, source_target_pairs={{1,0},{2,1},{5,4},{6,5},{9,8},{10,9},{13,12},{14,13},{17,16},{18,1... | collective-permute-start | bytes 3735560 | tf_op jit(solution)/shard_map/ppermute | solution.py:185
  525.1 29.5 %collective-permute-start.28 = (bf16[304,2048]{1,0:T(8,128)(2,1)S(1)}, bf16[304,2048]{1,0:T(8,128)(2,1)S(1)}, u32[]{:S(2)}, u32[]{:S(2)}) collective-permute-start(bf16[304,2048]{1,0:T(8,128)(2,1)S(1)} %collective-permute-done.26), channel_id=1, source_target_pairs={{2,3},{6,7},{10,11},{14,15},{18,19},{22,23},{26,27},{30,31}} | collective-permute-start | bytes 3735560 | tf_op jit(solution)/shard_map/ppermute | solution.py:182
  551.8 27.2 %collective-permute-start.29 = (bf16[304,2048]{1,0:T(8,128)(2,1)S(1)}, bf16[304,2048]{1,0:T(8,128)(2,1)S(1)}, u32[]{:S(2)}, u32[]{:S(2)}) collective-permute-start(bf16[304,2048]{1,0:T(8,128)(2,1)S(1)} %collective-permute-done.27), channel_id=1, source_target_pairs={{1,0},{5,4},{9,8},{13,12},{17,16},{21,20},{25,24},{29,28}} | collective-permute-start | bytes 3735560 | tf_op jit(solution)/shard_map/ppermute | solution.py:185
  580.9 33.2 %collective-permute-start.31 = (bf16[304,2048]{1,0:T(8,128)(2,1)S(1)}, bf16[304,2048]{1,0:T(8,128)(2,1)S(1)}, u32[]{:S(2)}, u32[]{:S(2)}) collective-permute-start(bf16[304,2048]{1,0:T(8,128)(2,1)S(1)} %get-tuple-element.168), channel_id=1, source_target_pairs={{1,0},{2,1},{3,2},{5,4},{6,5},{7,6},{9,8},{10,9},{11,10},{13,12},{... | collective-permute-start | bytes 3735560 | tf_op jit(solution)/shard_map/ppermute | solution.py:185
  614.2 31.4 %collective-permute-start.33 = (bf16[304,2048]{1,0:T(8,128)(2,1)S(1)}, bf16[304,2048]{1,0:T(8,128)(2,1)S(1)}, u32[]{:S(2)}, u32[]{:S(2)}) collective-permute-start(bf16[304,2048]{1,0:T(8,128)(2,1)S(1)} %collective-permute-done.31), channel_id=1, source_target_pairs={{1,0},{2,1},{5,4},{6,5},{9,8},{10,9},{13,12},{14,13},{17,16},{18,1... | collective-permute-start | bytes 3735560 | tf_op jit(solution)/shard_map/ppermute | solution.py:185
  615.5 32.6 %collective-permute-start.34 = (bf16[304,2048]{1,0:T(8,128)(2,1)S(1)}, bf16[304,2048]{1,0:T(8,128)(2,1)S(1)}, u32[]{:S(2)}, u32[]{:S(2)}) collective-permute-start(bf16[304,2048]{1,0:T(8,128)(2,1)S(1)} %collective-permute-done.32), channel_id=1, source_target_pairs={{2,3},{6,7},{10,11},{14,15},{18,19},{22,23},{26,27},{30,31}} | collective-permute-start | bytes 3735560 | tf_op jit(solution)/shard_map/ppermute | solution.py:182
  645.5 31.8 %collective-permute-start.35 = (bf16[304,2048]{1,0:T(8,128)(2,1)S(1)}, bf16[304,2048]{1,0:T(8,128)(2,1)S(1)}, u32[]{:S(2)}, u32[]{:S(2)}) collective-permute-start(bf16[304,2048]{1,0:T(8,128)(2,1)S(1)} %collective-permute-done.33), channel_id=1, source_target_pairs={{1,0},{5,4},{9,8},{13,12},{17,16},{21,20},{25,24},{29,28}} | collective-permute-start | bytes 3735560 | tf_op jit(solution)/shard_map/ppermute | solution.py:185
  679.2 29.0 %collective-permute-start.37 = (bf16[304,2048]{1,0:T(8,128)(2,1)S(1)}, bf16[304,2048]{1,0:T(8,128)(2,1)S(1)}, u32[]{:S(2)}, u32[]{:S(2)}) collective-permute-start(bf16[304,2048]{1,0:T(8,128)(2,1)S(1)} %get-tuple-element.169), channel_id=1, source_target_pairs={{1,0},{2,1},{3,2},{5,4},{6,5},{7,6},{9,8},{10,9},{11,10},{13,12},{... | collective-permute-start | bytes 3735560 | tf_op jit(solution)/shard_map/ppermute | solution.py:185
  708.2 28.2 %collective-permute-start.39 = (bf16[304,2048]{1,0:T(8,128)(2,1)S(1)}, bf16[304,2048]{1,0:T(8,128)(2,1)S(1)}, u32[]{:S(2)}, u32[]{:S(2)}) collective-permute-start(bf16[304,2048]{1,0:T(8,128)(2,1)S(1)} %collective-permute-done.37), channel_id=1, source_target_pairs={{1,0},{2,1},{5,4},{6,5},{9,8},{10,9},{13,12},{14,13},{17,16},{18,1... | collective-permute-start | bytes 3735560 | tf_op jit(solution)/shard_map/ppermute | solution.py:185
  709.5 35.7 %collective-permute-start.40 = (bf16[304,2048]{1,0:T(8,128)(2,1)S(1)}, bf16[304,2048]{1,0:T(8,128)(2,1)S(1)}, u32[]{:S(2)}, u32[]{:S(2)}) collective-permute-start(bf16[304,2048]{1,0:T(8,128)(2,1)S(1)} %collective-permute-done.38), channel_id=1, source_target_pairs={{2,3},{6,7},{10,11},{14,15},{18,19},{22,23},{26,27},{30,31}} | collective-permute-start | bytes 3735560 | tf_op jit(solution)/shard_map/ppermute | solution.py:182
  736.4 32.0 %collective-permute-start.41 = (bf16[304,2048]{1,0:T(8,128)(2,1)S(1)}, bf16[304,2048]{1,0:T(8,128)(2,1)S(1)}, u32[]{:S(2)}, u32[]{:S(2)}) collective-permute-start(bf16[304,2048]{1,0:T(8,128)(2,1)S(1)} %collective-permute-done.39), channel_id=1, source_target_pairs={{1,0},{5,4},{9,8},{13,12},{17,16},{21,20},{25,24},{29,28}} | collective-permute-start | bytes 3735560 | tf_op jit(solution)/shard_map/ppermute | solution.py:185
  770.7 136.2 %collective-permute-start.42 = (bf16[304,2048]{1,0:T(8,128)(2,1)S(1)}, bf16[304,2048]{1,0:T(8,128)(2,1)}, u32[]{:S(2)}, u32[]{:S(2)}) collective-permute-start(bf16[304,2048]{1,0:T(8,128)(2,1)S(1)} %get-tuple-element.170), channel_id=1, source_target_pairs={{0,1},{1,2},{2,3},{4,5},{5,6},{6,7},{8,9},{9,10},{10,11},{12,13},{... | collective-permute-start | bytes 3735560 | tf_op jit(solution)/shard_map/ppermute | solution.py:182
  773.1 138.6 %collective-permute-start.43 = (bf16[304,2048]{1,0:T(8,128)(2,1)S(1)}, bf16[304,2048]{1,0:T(8,128)(2,1)}, u32[]{:S(2)}, u32[]{:S(2)}) collective-permute-start(bf16[304,2048]{1,0:T(8,128)(2,1)S(1)} %get-tuple-element.170), channel_id=1, source_target_pairs={{1,0},{2,1},{3,2},{5,4},{6,5},{7,6},{9,8},{10,9},{11,10},{13,12},{... | collective-permute-start | bytes 3735560 | tf_op jit(solution)/shard_map/ppermute | solution.py:185
  972.2 28.5 %collective-permute-start.49 = (bf16[304,2048]{1,0:T(8,128)(2,1)S(1)}, bf16[304,2048]{1,0:T(8,128)(2,1)}, u32[]{:S(2)}, u32[]{:S(2)}) collective-permute-start(bf16[304,2048]{1,0:T(8,128)(2,1)S(1)} %add_convert_fusion.29), channel_id=1, source_target_pairs={{0,1},{1,2},{4,5},{5,6},{8,9},{9,10},{12,13},{13,14},{16,17},{17,1... | collective-permute-start | bytes 3735560 | tf_op jit(solution)/shard_map/ppermute | solution.py:208
  1052.1 28.5 %collective-permute-start.54 = (bf16[304,2048]{1,0:T(8,128)(2,1)}, bf16[304,2048]{1,0:T(8,128)(2,1)}, u32[]{:S(2)}, u32[]{:S(2)}) collective-permute-start(bf16[304,2048]{1,0:T(8,128)(2,1)} %get-tuple-element.358), channel_id=1, source_target_pairs={{0,1},{4,5},{8,9},{12,13},{16,17},{20,21},{24,25},{28,29}} | collective-permute-start | bytes 3735560 | tf_op jit(solution)/shard_map/ppermute | solution.py:208
  1078.8 27.7 %collective-permute-start.57 = (bf16[304,2048]{1,0:T(8,128)(2,1)}, bf16[304,2048]{1,0:T(8,128)(2,1)}, u32[]{:S(2)}, u32[]{:S(2)}) collective-permute-start(bf16[304,2048]{1,0:T(8,128)(2,1)} %get-tuple-element.359), channel_id=1, source_target_pairs={{3,2},{7,6},{11,10},{15,14},{19,18},{23,22},{27,26},{31,30}} | collective-permute-start | bytes 3735560 | tf_op jit(solution)/shard_map/ppermute | solution.py:214
  1083.4 28.3 %collective-permute-start.55 = (bf16[304,2048]{1,0:T(8,128)(2,1)}, bf16[304,2048]{1,0:T(8,128)(2,1)}, u32[]{:S(2)}, u32[]{:S(2)}) collective-permute-start(bf16[304,2048]{1,0:T(8,128)(2,1)} %add_convert_fusion.24), channel_id=1, source_target_pairs={{0,1},{1,2},{4,5},{5,6},{8,9},{9,10},{12,13},{13,14},{16,17},{17,1... | collective-permute-start | bytes 3735560 | tf_op jit(solution)/shard_map/ppermute | solution.py:208
  1132.4 28.2 %collective-permute-start.56 = (bf16[304,2048]{1,0:T(8,128)(2,1)}, bf16[304,2048]{1,0:T(8,128)(2,1)S(1)}, u32[]{:S(2)}, u32[]{:S(2)}) collective-permute-start(bf16[304,2048]{1,0:T(8,128)(2,1)} %get-tuple-element.356), channel_id=1, source_target_pairs={{0,1},{1,2},{2,3},{4,5},{5,6},{6,7},{8,9},{9,10},{10,11},{12,13},{... | collective-permute-start | bytes 3735560 | tf_op jit(solution)/shard_map/ppermute | solution.py:208
  1194.8 28.2 %collective-permute-start.61 = (bf16[304,2048]{1,0:T(8,128)(2,1)S(1)}, bf16[304,2048]{1,0:T(8,128)(2,1)}, u32[]{:S(2)}, u32[]{:S(2)}) collective-permute-start(bf16[304,2048]{1,0:T(8,128)(2,1)S(1)} %add_convert_fusion.19), channel_id=1, source_target_pairs={{0,1},{1,2},{4,5},{5,6},{8,9},{9,10},{12,13},{13,14},{16,17},{17,1... | collective-permute-start | bytes 3735560 | tf_op jit(solution)/shard_map/ppermute | solution.py:208
  1228.0 29.0 %collective-permute-start.64 = (bf16[304,2048]{1,0:T(8,128)(2,1)S(1)}, bf16[304,2048]{1,0:T(8,128)(2,1)}, u32[]{:S(2)}, u32[]{:S(2)}) collective-permute-start(bf16[304,2048]{1,0:T(8,128)(2,1)S(1)} %get-tuple-element.353), channel_id=1, source_target_pairs={{2,1},{3,2},{6,5},{7,6},{10,9},{11,10},{14,13},{15,14},{18,17},{19... | collective-permute-start | bytes 3735560 | tf_op jit(solution)/shard_map/ppermute | solution.py:214
  1249.8 29.2 %collective-permute-start.62 = (bf16[304,2048]{1,0:T(8,128)(2,1)}, bf16[304,2048]{1,0:T(8,128)(2,1)}, u32[]{:S(2)}, u32[]{:S(2)}) collective-permute-start(bf16[304,2048]{1,0:T(8,128)(2,1)} %get-tuple-element.352), channel_id=1, source_target_pairs={{0,1},{1,2},{2,3},{4,5},{5,6},{6,7},{8,9},{9,10},{10,11},{12,13},{... | collective-permute-start | bytes 3735560 | tf_op jit(solution)/shard_map/ppermute | solution.py:208
  1283.7 31.6 %collective-permute-start.66 = (bf16[304,2048]{1,0:T(8,128)(2,1)S(1)}, bf16[304,2048]{1,0:T(8,128)(2,1)S(1)}, u32[]{:S(2)}, u32[]{:S(2)}) collective-permute-start(bf16[304,2048]{1,0:T(8,128)(2,1)S(1)} %get-tuple-element.350), channel_id=1, source_target_pairs={{0,1},{4,5},{8,9},{12,13},{16,17},{20,21},{24,25},{28,29}} | collective-permute-start | bytes 3735560 | tf_op jit(solution)/shard_map/ppermute | solution.py:208
  1315.7 28.0 %collective-permute-start.67 = (bf16[304,2048]{1,0:T(8,128)(2,1)S(1)}, bf16[304,2048]{1,0:T(8,128)(2,1)S(1)}, u32[]{:S(2)}, u32[]{:S(2)}) collective-permute-start(bf16[304,2048]{1,0:T(8,128)(2,1)S(1)} %add_convert_fusion.15), channel_id=1, source_target_pairs={{0,1},{1,2},{4,5},{5,6},{8,9},{9,10},{12,13},{13,14},{16,17},{17,1... | collective-permute-start | bytes 3735560 | tf_op jit(solution)/shard_map/ppermute | solution.py:208
  1358.6 29.7 %collective-permute-start.71 = (bf16[304,2048]{1,0:T(8,128)(2,1)S(1)}, bf16[304,2048]{1,0:T(8,128)(2,1)S(1)}, u32[]{:S(2)}, u32[]{:S(2)}) collective-permute-start(bf16[304,2048]{1,0:T(8,128)(2,1)S(1)} %add_convert_fusion.12), channel_id=1, source_target_pairs={{1,0},{2,1},{3,2},{5,4},{6,5},{7,6},{9,8},{10,9},{11,10},{13,12},{... | collective-permute-start | bytes 3735560 | tf_op jit(solution)/shard_map/ppermute | solution.py:214
  1392.4 27.2 %collective-permute-start.72 = (bf16[304,2048]{1,0:T(8,128)(2,1)S(1)}, bf16[304,2048]{1,0:T(8,128)(2,1)S(1)}, u32[]{:S(2)}, u32[]{:S(2)}) collective-permute-start(bf16[304,2048]{1,0:T(8,128)(2,1)S(1)} %get-tuple-element.175), channel_id=1, source_target_pairs={{0,1},{1,2},{2,3},{4,5},{5,6},{6,7},{8,9},{9,10},{10,11},{12,13},{... | collective-permute-start | bytes 3735560 | tf_op jit(solution)/shard_map/ppermute | solution.py:182
  1418.3 468.6 %reduce-scatter.15.cloned.1.call-start = ((), (), s32[]{:S(2)}) async-start(), calls=%async_computation.14 | async-start | bytes 18874368 | tf_op jit(solution)/shard_map/reduce_scatter | solution.py:426
  1418.3 32.2 %collective-permute-start.73 = (bf16[304,2048]{1,0:T(8,128)(2,1)S(1)}, bf16[304,2048]{1,0:T(8,128)(2,1)}, u32[]{:S(2)}, u32[]{:S(2)}) collective-permute-start(bf16[304,2048]{1,0:T(8,128)(2,1)S(1)} %get-tuple-element.175), channel_id=1, source_target_pairs={{1,0},{2,1},{3,2},{5,4},{6,5},{7,6},{9,8},{10,9},{11,10},{13,12},{... | collective-permute-start | bytes 3735560 | tf_op jit(solution)/shard_map/ppermute | solution.py:185
  1419.6 32.2 %collective-permute-start.74 = (bf16[304,2048]{1,0:T(8,128)(2,1)S(1)}, bf16[304,2048]{1,0:T(8,128)(2,1)}, u32[]{:S(2)}, u32[]{:S(2)}) collective-permute-start(bf16[304,2048]{1,0:T(8,128)(2,1)S(1)} %collective-permute-done.72), channel_id=1, source_target_pairs={{1,2},{2,3},{5,6},{6,7},{9,10},{10,11},{13,14},{14,15},{17,18},{18... | collective-permute-start | bytes 3735560 | tf_op jit(solution)/shard_map/ppermute | solution.py:182
  1450.5 34.2 %collective-permute-start.75 = (bf16[304,2048]{1,0:T(8,128)(2,1)}, bf16[304,2048]{1,0:T(8,128)(2,1)}, u32[]{:S(2)}, u32[]{:S(2)}) collective-permute-start(bf16[304,2048]{1,0:T(8,128)(2,1)} %collective-permute-done.73), channel_id=1, source_target_pairs={{1,0},{2,1},{5,4},{6,5},{9,8},{10,9},{13,12},{14,13},{17,16},{18,1... | collective-permute-start | bytes 3735560 | tf_op jit(solution)/shard_map/ppermute | solution.py:185
  1451.8 39.3 %collective-permute-start.76 = (bf16[304,2048]{1,0:T(8,128)(2,1)}, bf16[304,2048]{1,0:T(8,128)(2,1)}, u32[]{:S(2)}, u32[]{:S(2)}) collective-permute-start(bf16[304,2048]{1,0:T(8,128)(2,1)} %collective-permute-done.74), channel_id=1, source_target_pairs={{2,3},{6,7},{10,11},{14,15},{18,19},{22,23},{26,27},{30,31}} | collective-permute-start | bytes 3735560 | tf_op jit(solution)/shard_map/ppermute | solution.py:182
  1484.7 451.0 %reduce-scatter.11.cloned.1.call-start = ((), (), s32[]{:S(2)}) async-start(), calls=%async_computation.12 | async-start | bytes 1179648 | tf_op jit(solution)/shard_map/reduce_scatter | solution.py:418
  1509.3 108.4 %collective-permute-start.78 = (bf16[304,2048]{1,0:T(8,128)(2,1)}, bf16[304,2048]{1,0:T(8,128)(2,1)}, u32[]{:S(2)}, u32[]{:S(2)}) collective-permute-start(bf16[304,2048]{1,0:T(8,128)(2,1)} %get-tuple-element.176), channel_id=1, source_target_pairs={{0,1},{1,2},{2,3},{4,5},{5,6},{6,7},{8,9},{9,10},{10,11},{12,13},{... | collective-permute-start | bytes 3735560 | tf_op jit(solution)/shard_map/ppermute | solution.py:182
  1511.9 106.7 %collective-permute-start.79 = (bf16[304,2048]{1,0:T(8,128)(2,1)}, bf16[304,2048]{1,0:T(8,128)(2,1)}, u32[]{:S(2)}, u32[]{:S(2)}) collective-permute-start(bf16[304,2048]{1,0:T(8,128)(2,1)} %get-tuple-element.176), channel_id=1, source_target_pairs={{1,0},{2,1},{3,2},{5,4},{6,5},{7,6},{9,8},{10,9},{11,10},{13,12},{... | collective-permute-start | bytes 3735560 | tf_op jit(solution)/shard_map/ppermute | solution.py:185
  1668.9 79.8 %collective-permute-start.84 = (bf16[304,2048]{1,0:T(8,128)(2,1)}, bf16[304,2048]{1,0:T(8,128)(2,1)}, u32[]{:S(2)}, u32[]{:S(2)}) collective-permute-start(bf16[304,2048]{1,0:T(8,128)(2,1)} %get-tuple-element.346), channel_id=1, source_target_pairs={{0,1},{4,5},{8,9},{12,13},{16,17},{20,21},{24,25},{28,29}} | collective-permute-start | bytes 3735560 | tf_op jit(solution)/shard_map/ppermute | solution.py:208
  1671.4 86.5 %collective-permute-start.87 = (bf16[304,2048]{1,0:T(8,128)(2,1)}, bf16[304,2048]{1,0:T(8,128)(2,1)}, u32[]{:S(2)}, u32[]{:S(2)}) collective-permute-start(bf16[304,2048]{1,0:T(8,128)(2,1)} %get-tuple-element.347), channel_id=1, source_target_pairs={{3,2},{7,6},{11,10},{15,14},{19,18},{23,22},{27,26},{31,30}} | collective-permute-start | bytes 3735560 | tf_op jit(solution)/shard_map/ppermute | solution.py:214
  1824.0 32.7 %collective-permute-start.90 = (bf16[304,2048]{1,0:T(8,128)(2,1)}, bf16[304,2048]{1,0:T(8,128)(2,1)S(1)}, u32[]{:S(2)}, u32[]{:S(2)}) collective-permute-start(bf16[304,2048]{1,0:T(8,128)(2,1)} %get-tuple-element.342), channel_id=1, source_target_pairs={{0,1},{4,5},{8,9},{12,13},{16,17},{20,21},{24,25},{28,29}} | collective-permute-start | bytes 3735560 | tf_op jit(solution)/shard_map/ppermute | solution.py:208
  1838.3 100.7 %reduce-scatter.13.cloned.1.call-start = ((), (), s32[]{:S(2)}) async-start(), calls=%async_computation.13 | async-start | bytes 2359296 | tf_op jit(solution)/shard_map/reduce_scatter | solution.py:423
  1843.6 49.8 %collective-permute-start.93 = (bf16[304,2048]{1,0:T(8,128)(2,1)}, bf16[304,2048]{1,0:T(8,128)(2,1)}, u32[]{:S(2)}, u32[]{:S(2)}) collective-permute-start(bf16[304,2048]{1,0:T(8,128)(2,1)} %get-tuple-element.343), channel_id=1, source_target_pairs={{3,2},{7,6},{11,10},{15,14},{19,18},{23,22},{27,26},{31,30}} | collective-permute-start | bytes 3735560 | tf_op jit(solution)/shard_map/ppermute | solution.py:214
  1859.9 33.5 %collective-permute-start.91 = (bf16[304,2048]{1,0:T(8,128)(2,1)}, bf16[304,2048]{1,0:T(8,128)(2,1)}, u32[]{:S(2)}, u32[]{:S(2)}) collective-permute-start(bf16[304,2048]{1,0:T(8,128)(2,1)} %add_convert_fusion.7), channel_id=1, source_target_pairs={{0,1},{1,2},{4,5},{5,6},{8,9},{9,10},{12,13},{13,14},{16,17},{17,1... | collective-permute-start | bytes 3735560 | tf_op jit(solution)/shard_map/ppermute | solution.py:208
  1872.1 103.6 %reduce-scatter.9.cloned.1.call-start = ((), (), s32[]{:S(2)}) async-start(), calls=%async_computation.11 | async-start | bytes 2359296 | tf_op jit(solution)/shard_map/reduce_scatter | solution.py:415
  1911.1 129.5 %reduce-scatter.19.cloned.1.call-start = ((), (), s32[]{:S(2)}) async-start(), calls=%async_computation.16 | async-start | bytes 589824
  1911.2 67.8 %collective-permute-start.92 = (bf16[304,2048]{1,0:T(8,128)(2,1)S(1)}, bf16[304,2048]{1,0:T(8,128)(2,1)}, u32[]{:S(2)}, u32[]{:S(2)}) collective-permute-start(bf16[304,2048]{1,0:T(8,128)(2,1)S(1)} %copy-done.104), channel_id=1, source_target_pairs={{0,1},{1,2},{2,3},{4,5},{5,6},{6,7},{8,9},{9,10},{10,11},{12,13},{... | collective-permute-start | bytes 3735560 | tf_op jit(solution)/shard_map/ppermute | solution.py:208
  1916.2 62.7 %collective-permute-start.95 = (bf16[304,2048]{1,0:T(8,128)(2,1)S(1)}, bf16[304,2048]{1,0:T(8,128)(2,1)}, u32[]{:S(2)}, u32[]{:S(2)}) collective-permute-start(bf16[304,2048]{1,0:T(8,128)(2,1)S(1)} %add_convert_fusion.4), channel_id=1, source_target_pairs={{1,0},{2,1},{3,2},{5,4},{6,5},{7,6},{9,8},{10,9},{11,10},{13,12},{... | collective-permute-start | bytes 3735560 | tf_op jit(solution)/shard_map/ppermute | solution.py:214
  (273 other events, 4683.0 us)
Sparse Core Ops, SparseCore 0:
  10.5 26.0 all-gather.5
  39.1 27.7 all-gather.7
  69.3 28.0 all-gather.9
  99.8 55.8 all-gather.13
  158.0 89.7 all-gather.11
  1418.4 81.8 reduce-scatter.16
  1503.8 115.9 reduce-scatter.14
  1838.4 47.9 reduce-scatter.10
  1889.8 41.0 reduce-scatter.12
  1934.6 41.0 reduce-scatter.8
  2009.2 31.3 reduce-scatter.18
